TPU v7x, 32 devices: a whole 2x2x4 slice. The times are simulated.
32 devices in a mesh: groups: 2 (over y), sec: 4 (over z), tile: 2 (over x), sub: 2 (over core).
Axes of the slice: x: 2, y: 2, z: 4, core: 2. Of those that a mesh axis runs over, the one named last changes fastest.
Arguments:
- images: bfloat16 [8, 2048, 2048], P(('groups', 'sec'), 'sub', 'tile'), parts along dimension 0, may hold values from -8 to 8
- skipped: int32 [8, 16, 16], P(('groups', 'sec'), 'sub', 'tile'), parts along dimension 0, may hold values from 0 to 1, as said below
- patch_mask: int32 [8, 16, 16], P(('groups', 'sec'), 'sub', 'tile'), parts along dimension 0, may hold values 0 or 1
Outputs:
- flow_field: float32 [2, 8, 16, 16], P(None, ('groups', 'sec'), 'sub', 'tile'), parts along dimension 1
- positions: float32 [2, 8, 16, 16], P(None, ('groups', 'sec'), 'sub', 'tile'), parts along dimension 1
There are 2 independent parts, one for each index of `groups`. A program takes and returns all parts, laid end to end along the dimension named above; each array names one. Nothing has to cross between parts.
Inputs may be any that keep to these rules, and one draw needn't show every extreme that they name: `skipped`: of patch columns 2k and 2k + 1 of a section and patch row, exactly one is 1.
All inputs are finite; a program needn't handle non-finite values. No bound on the sum of `patch_mask` on one device may be relied on, other than what follows from the above.
Results may differ from a plain program's by a relative error of at most 0.012.
The roundings to bfloat16 on the way count: a program that leaves them out, or rounds other values in their place, can miss the bound.
Values may be sent and summed in bfloat16 or wider, within the bound.
No kernel may reach another device: no remote copies, remote signals or barrier semaphores. Data moves between devices by JAX's collectives and lax.ppermute only.
A program may use at most 128 MiB of HBM per device.

v0:
```python
import functools
import math

import jax
import jax.numpy as jnp
from jax import lax
from jax.experimental import pallas as pl
from jax.experimental.pallas import tpu as pltpu
from jax.sharding import PartitionSpec as P

PATCH = 160
STRIDE = 128
RELAX = 6
RIM = 16


SHARPNESS = 48.0
STIFFNESS = 0.25
RELAXATION = 0.8
EPSILON = 1e-05


def shifted(value, axis, steps):
    count = lax.axis_size(axis)
    first, last = (max(0, -steps), min(count, count - steps))
    return lax.ppermute(value, axis, [(source, source + steps) for source in range(first, last)])


def extended(block, sides, width):
    for axis, dim in sides:
        count = lax.axis_size(axis)
        forward = [(i, i + 1) for i in range(count - 1)]
        backward = [(target, source) for source, target in forward]
        low = lax.ppermute(
            lax.slice_in_dim(block, block.shape[dim] - width, None, axis=dim), axis, forward
        )
        high = lax.ppermute(lax.slice_in_dim(block, 0, width, axis=dim), axis, backward)
        block = jnp.concatenate([low, block, high], axis=dim)
    return block


def dft_tables(patch):
    index = jnp.arange(patch, dtype=jnp.int32)
    product = index[:, None] * index[None, :] % patch
    angle = product.astype(jnp.float32) * (2.0 * math.pi / patch)
    return (jnp.cos(angle).astype(jnp.bfloat16), (-jnp.sin(angle)).astype(jnp.bfloat16))


def _sum_all(x):
    return jnp.sum(jnp.sum(x, axis=1, keepdims=True), axis=0, keepdims=True)


def _flow_kernel(
    skip_ref, skip_next_ref, flag_ref, own_ref, prev_ref, next_ref, cs_ref, c_ref, s_ref, out_ref,
    *, cols,
):
    f32, bf16 = jnp.float32, jnp.bfloat16
    p = PATCH
    i = pl.program_id(0)
    cos_t = c_ref[...]
    sin_t = s_ref[...]
    both_t = cs_ref[...]
    size = float(p * p)

    def spectrum(blk):
        x = blk.astype(f32)
        centered = x - _sum_all(x) / size
        spread = _sum_all(centered * centered) / size
        normed = (centered * lax.rsqrt(spread + EPSILON)).astype(bf16)
        half = jnp.dot(both_t, normed, preferred_element_type=f32).astype(bf16)
        h_re, h_im = half[:p], half[p:]
        re = jnp.dot(h_re, cos_t, preferred_element_type=f32) - jnp.dot(
            h_im, sin_t, preferred_element_type=f32
        )
        im = jnp.dot(h_re, sin_t, preferred_element_type=f32) + jnp.dot(
            h_im, cos_t, preferred_element_type=f32
        )
        return re, im

    u_col = lax.broadcasted_iota(jnp.int32, (p, 1), 0)
    off_col = jnp.where(u_col < p // 2, u_col, u_col - p).astype(f32)
    u_row = lax.broadcasted_iota(jnp.int32, (1, p), 1)
    off_row = jnp.where(u_row < p // 2, u_row, u_row - p).astype(f32)

    def moments(own_blk, other_blk):
        o_re, o_im = spectrum(own_blk)
        t_re, t_im = spectrum(other_blk)
        c_re = (o_re * t_re + o_im * t_im).astype(bf16)
        c_im = (o_re * t_im - o_im * t_re).astype(bf16)
        a = jnp.dot(both_t, c_re, preferred_element_type=f32)
        b = jnp.dot(both_t, c_im, preferred_element_type=f32)
        b_re = (a[:p] + b[p:]).astype(bf16)
        b_im = (b[:p] - a[p:]).astype(bf16)
        corr = (
            jnp.dot(b_re, cos_t, preferred_element_type=f32)
            + jnp.dot(b_im, sin_t, preferred_element_type=f32)
        ) / float(p) ** 4
        w = jnp.exp(SHARPNESS * corr)
        total = _sum_all(w)
        rows_sum = jnp.sum(w, axis=1, keepdims=True)
        cols_sum = jnp.sum(w, axis=0, keepdims=True)
        along_rows = jnp.sum(rows_sum * off_col, axis=0, keepdims=True)
        along_cols = jnp.sum(cols_sum * off_row, axis=1, keepdims=True)
        return along_rows / total / float(RIM), along_cols / total / float(RIM)

    def window(ref, j):
        return ref[:, j * STRIDE : j * STRIDE + p]

    lane = lax.broadcasted_iota(jnp.int32, (1, 128), 1)
    acc = [jnp.zeros((1, 128), f32) for _ in range(4)]
    use_own = flag_ref[0] == 1
    for k in range(cols // 2):
        left, right = 2 * k, 2 * k + 1
        first_near = skip_ref[i * cols + left] == 0
        own_a = jnp.where(first_near, window(own_ref, left), window(own_ref, right))
        oth_a = jnp.where(first_near, window(prev_ref, left), window(prev_ref, right))
        ra, ca = moments(own_a, oth_a)
        second_far = skip_next_ref[i * cols + right] == 1
        own_b = jnp.where(second_far, window(next_ref, right), window(next_ref, left))
        col_b_prev = jnp.where(second_far, window(prev_ref, right), window(prev_ref, left))
        col_b_own = jnp.where(second_far, window(own_ref, right), window(own_ref, left))
        oth_b = jnp.where(use_own, col_b_own, col_b_prev)
        rb, cb = moments(own_b, oth_b)
        sel = lane == k
        acc = [jnp.where(sel, v, a) for v, a in zip((ra, ca, rb, cb), acc)]
    out_ref[0] = jnp.concatenate(acc + [jnp.zeros((4, 128), f32)], axis=0)


def pair_flows(own_pad, prev_pad, next_pad, skip, skip_next, use_own):
    tall, broad = own_pad.shape
    rows = (tall - (PATCH - STRIDE)) // STRIDE
    cols = (broad - (PATCH - STRIDE)) // STRIDE
    assert cols % 2 == 0 and cols // 2 <= 128
    cos_t, sin_t = dft_tables(PATCH)
    both_t = jnp.concatenate([cos_t, sin_t], axis=0)
    band = pl.BlockSpec((pl.Element(PATCH), pl.Element(broad)), lambda i, *_: (i * STRIDE, 0))
    table = pl.BlockSpec((PATCH, PATCH), lambda i, *_: (0, 0))
    grid_spec = pltpu.PrefetchScalarGridSpec(
        num_scalar_prefetch=3,
        grid=(rows,),
        in_specs=[band, band, band, pl.BlockSpec((2 * PATCH, PATCH), lambda i, *_: (0, 0)), table, table],
        out_specs=pl.BlockSpec((1, 8, 128), lambda i, *_: (i, 0, 0)),
    )
    out = pl.pallas_call(
        functools.partial(_flow_kernel, cols=cols),
        grid_spec=grid_spec,
        out_shape=jax.ShapeDtypeStruct((rows, 8, 128), jnp.float32),
        compiler_params=pltpu.CompilerParams(dimension_semantics=("arbitrary",)),
    )(
        skip.reshape(-1),
        skip_next.reshape(-1),
        use_own.reshape(1),
        own_pad,
        prev_pad,
        next_pad,
        both_t,
        cos_t,
        sin_t,
    )
    half = cols // 2
    first = jnp.repeat(jnp.transpose(out[:, 0:2, :half], (1, 0, 2)), 2, axis=2)
    second = jnp.repeat(jnp.transpose(out[:, 2:4, :half], (1, 0, 2)), 2, axis=2)
    return first, second


def gather_sections(value, axis):
    count = lax.axis_size(axis)
    spread = jnp.broadcast_to(value[None], (count,) + value.shape)
    return lax.all_to_all(spread, axis, 0, 0, tiled=True)


def earlier(values, steps, axis):
    width = values.shape[axis]
    widths = [(0, 0)] * values.ndim
    widths[axis] = (steps, 0)
    return lax.slice_in_dim(jnp.pad(values, widths), 0, width, axis=axis)


def later(values, steps, axis):
    width = values.shape[axis]
    widths = [(0, 0)] * values.ndim
    widths[axis] = (0, steps)
    return lax.slice_in_dim(jnp.pad(values, widths), steps, steps + width, axis=axis)


def relax(flow_field, weight, distance):
    near = (distance == 1).astype(jnp.float32)
    far = 1.0 - near
    diag = STIFFNESS + weight + later(weight * near, 1, 0) + later(weight * far, 2, 0)
    positions = jnp.zeros_like(flow_field)
    for sweep in range(RELAX):
        partner = near * earlier(positions, 1, 1) + far * earlier(positions, 2, 1)
        error = weight * (positions - partner - flow_field)
        gradient = (
            STIFFNESS * positions + error - later(error * near, 1, 1) - later(error * far, 2, 1)
        )
        positions = positions - RELAXATION * gradient / diag
    return positions


def body(images, skipped, patch_mask):
    index = lax.axis_index("sec")
    own_distance = jnp.where(index >= 2, 1 + skipped, 1)
    own_pad = extended(images, (("sub", 1), ("tile", 2)), RIM)
    prev_pad = shifted(own_pad, "sec", 1)
    next_pad = shifted(own_pad, "sec", -1)
    skip_next = shifted(skipped, "sec", -1)
    use_own = (index == 0).astype(jnp.int32)
    first, second = pair_flows(
        own_pad[0], prev_pad[0], next_pad[0], skipped[0], skip_next[0], use_own
    )
    first = jnp.where(skipped[0] == 0, first, 0.0)
    second = jnp.where(skip_next[0] == 1, second, 0.0)
    weight = patch_mask.astype(jnp.float32) * (index >= 1).astype(jnp.float32)
    stacked = jnp.concatenate(
        [first, second, weight, own_distance.astype(jnp.float32)], axis=0
    )
    every = jnp.moveaxis(gather_sections(stacked, "sec"), 0, 1)
    raw_all = every[0:2] + earlier(every[2:4], 1, 1)
    flow_all = raw_all * every[4]
    positions_all = relax(flow_all, every[4], every[5])
    flow_field = lax.dynamic_slice_in_dim(flow_all, index, 1, 1)
    positions = lax.dynamic_slice_in_dim(positions_all, index, 1, 1)
    return (flow_field, positions)


def solution(mesh):
    placed = (
        P(("groups", "sec"), "sub", "tile"),
        P(("groups", "sec"), "sub", "tile"),
        P(("groups", "sec"), "sub", "tile"),
    )
    return jax.shard_map(
        body,
        mesh=mesh,
        in_specs=placed,
        out_specs=(
            P(None, ("groups", "sec"), "sub", "tile"),
            P(None, ("groups", "sec"), "sub", "tile"),
        ),
        check_vma=False,
    )
```

profile of v0, /device:TPU:0, one launch (start us, length us, event | category | flops | bytes accessed | tf_op | source)
XLA Modules:
  0.0 165.7 jit_solution(12058711712001178193)
XLA Ops:
  0.6 0.8 fusion.82
  1.4 2.3 %collective-permute-start.1 = (bf16[1,16,1024]{2,1,0:T(8,128)(2,1)S(1)}, bf16[1,16,1024]{2,1,0:T(8,128)(2,1)S(1)}, u32[]{:S(2)}, u32[]{:S(2)}) collective-permute-start(bf16[1,16,1024]{2,1,0:T(8,128)(2,1)S(1)} %get-tuple-element.23), channel_id=1, source_target_pairs={{0,1},{2,3},{4,5},{6,7},{8,9},{10,11},{12,13},{14,15},{16,17},{18,... | collective-permute-start | bytes 98312 | tf_op jit(solution)/shard_map/ppermute | solution.py:34
  3.8 1.3 collective-permute-start.2
  5.1 1.8 %constant_dynamic-update-slice_fusion.1 = bf16[1,1056,1024]{2,1,0:T(8,128)(2,1)S(1)} fusion(bf16[1,1056,1024]{2,1,0:T(8,128)(2,1)S(1)} %constant_dynamic-update-slice_fusion.2, bf16[1,1024,1024]{2,1,0:T(8,128)(2,1)} %param.3), kind=kLoop, calls=%fused_computation.133 | loop fusion | bytes 4194304
  6.9 0.2 fusion.81
  7.1 4.2 %collective-permute-start.3 = (bf16[1,1056,16]{2,1,0:T(8,128)(2,1)S(1)}, bf16[1,1056,16]{2,1,0:T(8,128)(2,1)S(1)}, u32[]{:S(2)}, u32[]{:S(2)}) collective-permute-start(bf16[1,1056,16]{2,1,0:T(8,128)(2,1)S(1)} %get-tuple-element.21), channel_id=1, source_target_pairs={{0,2},{1,3},{4,6},{5,7},{8,10},{9,11},{12,14},{13,15},{16,18},{17,... | collective-permute-start | bytes 101384 | tf_op jit(solution)/shard_map/ppermute | solution.py:34
  11.3 1.3 collective-permute-start.4
  12.6 5.4 %collective-permute-done.3 = bf16[1,1056,16]{2,1,0:T(8,128)(2,1)S(1)} collective-permute-done((bf16[1,1056,16]{2,1,0:T(8,128)(2,1)S(1)}, bf16[1,1056,16]{2,1,0:T(8,128)(2,1)S(1)}, u32[]{:S(2)}, u32[]{:S(2)}) %collective-permute-start.3) | collective-permute-done | bytes 33824 | tf_op jit(solution)/shard_map/ppermute | solution.py:34
  18.0 4.5 %collective-permute-done.4 = bf16[1,1056,16]{2,1,0:T(8,128)(2,1)S(1)} collective-permute-done((bf16[1,1056,16]{2,1,0:T(8,128)(2,1)S(1)}, bf16[1,1056,16]{2,1,0:T(8,128)(2,1)S(1)}, u32[]{:S(2)}, u32[]{:S(2)}) %collective-permute-start.4) | collective-permute-done | bytes 33824 | tf_op jit(solution)/shard_map/ppermute | solution.py:37
  22.5 4.5 %concatenate.13 = bf16[1,1056,1056]{2,1,0:T(8,128)(2,1)S(1)} concatenate(bf16[1,1056,16]{2,1,0:T(8,128)(2,1)S(1)} %collective-permute-done.3, bf16[1,1056,1024]{2,1,0:T(8,128)(2,1)} %copy-done.1, bf16[1,1056,16]{2,1,0:T(8,128)(2,1)S(1)} %collective-permute-done.4), dimensions={2} | concatenate | bytes 4460544 | tf_op jit(solution)/shard_map/concatenate | solution.py:38
  27.0 5.0 %collective-permute-start.5 = (bf16[1,1056,1056]{2,1,0:T(8,128)(2,1)S(1)}, bf16[1,1056,1056]{2,1,0:T(8,128)(2,1)}, u32[]{:S(2)}, u32[]{:S(2)}) collective-permute-start(bf16[1,1056,1056]{2,1,0:T(8,128)(2,1)S(1)} %concatenate.13), channel_id=1, source_target_pairs={{0,4},{4,8},{8,12},{1,5},{5,9},{9,13},{2,6},{6,10},{10,14},{3,7},{... | collective-permute-start | bytes 6690824 | tf_op jit(solution)/shard_map/ppermute | solution.py:26
  31.9 1.3 collective-permute-start.6
  33.3 1.3 collective-permute-start
  34.7 0.7 negate_convert_fusion
  35.4 0.7 pad_maximum_fusion.cs_ref
  36.1 0.6 reshape_squeeze.6.skip_ref
  36.7 0.1 copy.15
  36.8 51.6 %collective-permute-done = s32[1,8,8]{1,2,0:T(8,128)S(1)} collective-permute-done((s32[1,8,8]{1,2,0:T(8,128)S(1)}, s32[1,8,8]{1,2,0:T(8,128)S(1)}, u32[]{:S(2)}, u32[]{:S(2)}) %collective-permute-start) | collective-permute-done | bytes 288 | tf_op jit(solution)/shard_map/ppermute | solution.py:26
  88.5 0.6 reshape_squeeze.7.skip_next_ref
  89.1 63.0 %shard_map.50 = f32[8,8,128]{2,1,0:T(8,128)} custom-call(s32[64]{0:T(128)} %reshape_squeeze.6.skip_ref, s32[64]{0:T(128)} %reshape_squeeze.7.skip_next_ref, s32[1]{0:T(128)} %bitcast.1.flag_ref, bf16[1056,1056]{1,0:T(8,128)(2,1)} %bitcast.36, bf16[1056,1056]{1,0:T(8,128)(2,1)} %bitcast.3.prev_ref, bf16[1056,1056]{1,0:T(8,128)(2,1)} %bitcast.4.next_ref, ...), custom_call_target="tpu_custom_call" | custom-call | tf_op jit(solution)/shard_map/pallas_call | solution.py:144
  152.1 0.8 slice_bitcast_fusion.2
  152.9 0.1 copy.21
  153.0 0.1 copy.18
  153.1 0.1 copy.24
  153.2 0.7 reshape.29
  153.9 3.2 %all-to-all-start = ((f32[4,1,384]{2,1,0:T(1,128)}), f32[4,1,384]{2,1,0:T(1,128)S(1)}, u32[]{:S(2)}, u32[]{:S(2)}) async-start(f32[4,1,384]{2,1,0:T(1,128)} %reshape.29), calls=%async_computation | async-start | bytes 12288 | tf_op jit(solution)/shard_map/all_to_all | solution.py:169
  157.2 5.6 %all-to-all-done = f32[4,1,384]{2,1,0:T(1,128)S(1)} async-done(((f32[4,1,384]{2,1,0:T(1,128)}), f32[4,1,384]{2,1,0:T(1,128)S(1)}, u32[]{:S(2)}, u32[]{:S(2)}) %all-to-all-start) | async-done | bytes 6176 | tf_op jit(solution)/shard_map/all_to_all | solution.py:169
  162.7 0.5 broadcast.105
  163.2 0.7 reduce
  163.9 0.1 reshape.30
  164.2 0.6 dynamic-slice_bitcast_fusion
  165.1 0.6 fusion.71
  (59 shorter events, 0.6 us)
Async XLA Ops:
  1.4 3.7 %collective-permute-start.1 = (bf16[1,16,1024]{2,1,0:T(8,128)(2,1)S(1)}, bf16[1,16,1024]{2,1,0:T(8,128)(2,1)S(1)}, u32[]{:S(2)}, u32[]{:S(2)}) collective-permute-start(bf16[1,16,1024]{2,1,0:T(8,128)(2,1)S(1)} %get-tuple-element.23), channel_id=1, source_target_pairs={{0,1},{2,3},{4,5},{6,7},{8,9},{10,11},{12,13},{14,15},{16,17},{18,... | collective-permute-start | bytes 98312 | tf_op jit(solution)/shard_map/ppermute | solution.py:34
  3.8 3.1 %collective-permute-start.2 = (bf16[1,16,1024]{2,1,0:T(8,128)(2,1)S(1)}, bf16[1,16,1024]{2,1,0:T(8,128)(2,1)S(1)}, u32[]{:S(2)}, u32[]{:S(2)}) collective-permute-start(bf16[1,16,1024]{2,1,0:T(8,128)(2,1)S(1)} %get-tuple-element.22), channel_id=1, source_target_pairs={{1,0},{3,2},{5,4},{7,6},{9,8},{11,10},{13,12},{15,14},{17,16},{19,... | collective-permute-start | bytes 98312 | tf_op jit(solution)/shard_map/ppermute | solution.py:37
  6.9 11.1 %copy-start.1 = (bf16[1,1056,1024]{2,1,0:T(8,128)(2,1)}, bf16[1,1056,1024]{2,1,0:T(8,128)(2,1)S(1)}, u32[]{:S(2)}) copy-start(bf16[1,1056,1024]{2,1,0:T(8,128)(2,1)S(1)} %constant_dynamic-update-slice_fusion) | copy-start | bytes 6488068
  7.1 10.9 %collective-permute-start.3 = (bf16[1,1056,16]{2,1,0:T(8,128)(2,1)S(1)}, bf16[1,1056,16]{2,1,0:T(8,128)(2,1)S(1)}, u32[]{:S(2)}, u32[]{:S(2)}) collective-permute-start(bf16[1,1056,16]{2,1,0:T(8,128)(2,1)S(1)} %get-tuple-element.21), channel_id=1, source_target_pairs={{0,2},{1,3},{4,6},{5,7},{8,10},{9,11},{12,14},{13,15},{16,18},{17,... | collective-permute-start | bytes 101384 | tf_op jit(solution)/shard_map/ppermute | solution.py:34
  11.3 21.9 %copy-start.4 = (s32[1,8,8]{2,1,0:T(8,128)S(1)}, s32[1,8,8]{2,1,0:T(8,128)}, u32[]{:S(2)}) copy-start(s32[1,8,8]{2,1,0:T(8,128)} %param.4) | copy-start | bytes 772
  11.3 23.3 %copy-start.5 = (s32[1,8,8]{2,1,0:T(8,128)S(1)}, s32[1,8,8]{2,1,0:T(8,128)}, u32[]{:S(2)}) copy-start(s32[1,8,8]{2,1,0:T(8,128)} %param.5) | copy-start | bytes 772
  11.3 11.1 %collective-permute-start.4 = (bf16[1,1056,16]{2,1,0:T(8,128)(2,1)S(1)}, bf16[1,1056,16]{2,1,0:T(8,128)(2,1)S(1)}, u32[]{:S(2)}, u32[]{:S(2)}) collective-permute-start(bf16[1,1056,16]{2,1,0:T(8,128)(2,1)S(1)} %get-tuple-element.20), channel_id=1, source_target_pairs={{2,0},{3,1},{6,4},{7,5},{10,8},{11,9},{14,12},{15,13},{18,16},{19,... | collective-permute-start | bytes 101384 | tf_op jit(solution)/shard_map/ppermute | solution.py:37
  27.0 62.1 %copy-start = (bf16[1,1056,1056]{2,1,0:T(8,128)(2,1)}, bf16[1,1056,1056]{2,1,0:T(8,128)(2,1)S(1)}, u32[]{:S(2)}) copy-start(bf16[1,1056,1056]{2,1,0:T(8,128)(2,1)S(1)} %concatenate.13) | copy-start | bytes 6690820
  27.0 62.1 %collective-permute-start.5 = (bf16[1,1056,1056]{2,1,0:T(8,128)(2,1)S(1)}, bf16[1,1056,1056]{2,1,0:T(8,128)(2,1)}, u32[]{:S(2)}, u32[]{:S(2)}) collective-permute-start(bf16[1,1056,1056]{2,1,0:T(8,128)(2,1)S(1)} %concatenate.13), channel_id=1, source_target_pairs={{0,4},{4,8},{8,12},{1,5},{5,9},{9,13},{2,6},{6,10},{10,14},{3,7},{... | collective-permute-start | bytes 6690824 | tf_op jit(solution)/shard_map/ppermute | solution.py:26
  31.9 57.1 %collective-permute-start.6 = (bf16[1,1056,1056]{2,1,0:T(8,128)(2,1)S(1)}, bf16[1,1056,1056]{2,1,0:T(8,128)(2,1)}, u32[]{:S(2)}, u32[]{:S(2)}) collective-permute-start(bf16[1,1056,1056]{2,1,0:T(8,128)(2,1)S(1)} %concatenate.13), channel_id=1, source_target_pairs={{4,0},{8,4},{12,8},{5,1},{9,5},{13,9},{6,2},{10,6},{14,10},{7,3},{... | collective-permute-start | bytes 6690824 | tf_op jit(solution)/shard_map/ppermute | solution.py:26
  33.3 55.1 %collective-permute-start = (s32[1,8,8]{1,2,0:T(8,128)S(1)}, s32[1,8,8]{1,2,0:T(8,128)S(1)}, u32[]{:S(2)}, u32[]{:S(2)}) collective-permute-start(s32[1,8,8]{1,2,0:T(8,128)S(1)} %copy.16), channel_id=1, source_target_pairs={{4,0},{8,4},{12,8},{5,1},{9,5},{13,9},{6,2},{10,6},{14,10},{7,3},{... | collective-permute-start | bytes 776 | tf_op jit(solution)/shard_map/ppermute | solution.py:26
  35.4 53.7 %copy-start.2 = (bf16[160,160]{1,0:T(8,128)(2,1)}, bf16[160,160]{1,0:T(8,128)(2,1)S(1)}, u32[]{:S(2)}) copy-start(bf16[160,160]{1,0:T(8,128)(2,1)S(1)} %get-tuple-element.26.s_ref) | copy-start | bytes 153604
  35.4 53.7 %copy-start.3 = (bf16[160,160]{1,0:T(8,128)(2,1)}, bf16[160,160]{1,0:T(8,128)(2,1)S(1)}, u32[]{:S(2)}) copy-start(bf16[160,160]{1,0:T(8,128)(2,1)S(1)} %get-tuple-element.27.c_ref) | copy-start | bytes 153604
  153.9 8.8 %all-to-all-start = ((f32[4,1,384]{2,1,0:T(1,128)}), f32[4,1,384]{2,1,0:T(1,128)S(1)}, u32[]{:S(2)}, u32[]{:S(2)}) async-start(f32[4,1,384]{2,1,0:T(1,128)} %reshape.29), calls=%async_computation | async-start | bytes 12288 | tf_op jit(solution)/shard_map/all_to_all | solution.py:169
where the time goes:
time: 166 us
  waiting for transfers between devices  67 us (40%)
  Pallas kernels  63 us (38%)
  starting transfers between devices  19.9 us (12%)
  local copies, waits for them, and re-layouts  11.8 us (7%)
  other arithmetic  3 us (2%)
    pallas_call x1, Pallas kernels, pair_flows(): pl.pallas_call(functools.partial(_flow_kernel, cols=cols), grid_spec=grid...  63 us
    ppermute x3, waiting for transfers between devices, shifted(): lax.ppermute(value, axis, [(source, source + steps) for source in range(f...  51.6 us
    ppermute x3, starting transfers between devices, shifted(): lax.ppermute(value, axis, [(source, source + steps) for source in range(f...  7.51 us
    ppermute x2, starting transfers between devices, extended(): lax.ppermute(lax.slice_in_dim(block, block.shape[dim] - width, None, axis...  6.59 us
    all_to_all x1, waiting for transfers between devices, gather_sections(): return lax.all_to_all(spread, axis, 0, 0, tiled=True)  5.55 us
    ppermute x2, waiting for transfers between devices, extended(): lax.ppermute(lax.slice_in_dim(block, block.shape[dim] - width, None, axis...  5.36 us
    concatenate x2, local copies, waits for them, and re-layouts, extended(): block = jnp.concatenate([low, block, high], axis=dim)  4.49 us
    ppermute x2, waiting for transfers between devices, extended(): lax.ppermute(lax.slice_in_dim(block, 0, width, axis=dim), axis, backward)  4.48 us
  transfers between devices with their start and end apart: 8, of which 4 were waited for; matrix products, arithmetic and copies ran while one was open for 3% of the time, Pallas kernels for 0%

commit v1 on v0

--- a/solution.py
+++ b/solution.py
@@ -201,14 +201,26 @@
 def body(images, skipped, patch_mask):
     index = lax.axis_index("sec")
     own_distance = jnp.where(index >= 2, 1 + skipped, 1)
-    own_pad = extended(images, (("sub", 1), ("tile", 2)), RIM)
-    prev_pad = shifted(own_pad, "sec", 1)
-    next_pad = shifted(own_pad, "sec", -1)
+    own_pad = extended(images, (("sub", 1), ("tile", 2)), RIM)[0]
     skip_next = shifted(skipped, "sec", -1)
     use_own = (index == 0).astype(jnp.int32)
-    first, second = pair_flows(
-        own_pad[0], prev_pad[0], next_pad[0], skipped[0], skip_next[0], use_own
-    )
+    rows_count = (own_pad.shape[0] - (PATCH - STRIDE)) // STRIDE
+    chunks = max(n for n in (1, 2, 4) if rows_count % n == 0)
+    per = rows_count // chunks
+    firsts, seconds = [], []
+    for c in range(chunks):
+        start = c * per * STRIDE
+        own_c = own_pad[start : start + per * STRIDE + PATCH - STRIDE]
+        prev_c = shifted(own_c, "sec", 1)
+        next_c = shifted(own_c, "sec", -1)
+        part = slice(c * per, (c + 1) * per)
+        first_c, second_c = pair_flows(
+            own_c, prev_c, next_c, skipped[0, part], skip_next[0, part], use_own
+        )
+        firsts.append(first_c)
+        seconds.append(second_c)
+    first = jnp.concatenate(firsts, axis=1)
+    second = jnp.concatenate(seconds, axis=1)
     first = jnp.where(skipped[0] == 0, first, 0.0)
     second = jnp.where(skip_next[0] == 1, second, 0.0)
     weight = patch_mask.astype(jnp.float32) * (index >= 1).astype(jnp.float32)

time: 166 us -> 156 us (0.940)
  waiting for transfers between devices: 67 us -> 16.1 us
  starting transfers between devices: 19.9 us -> 38 us
  local copies, waits for them, and re-layouts: 11.8 us -> 24.1 us
  Pallas kernels: 63 us -> 71.6 us
    ppermute x3 -> x9, waiting for transfers between devices: 51.6 us -> 0.7 us  [shifted(): lax.ppermute(value, axis, [(source, source + steps) for source in range(f...]
    ppermute x3 -> x9, starting transfers between devices: 7.51 us -> 24 us  [shifted(): lax.ppermute(value, axis, [(source, source + steps) for source in range(f...]
    pallas_call x1 -> x4, Pallas kernels: 63 us -> 71.6 us  [pair_flows(): pl.pallas_call(functools.partial(_flow_kernel, cols=cols), grid_spec=grid...]
    unnamed x19 -> x29, local copies, waits for them, and re-layouts: 3.36 us -> 6.65 us
    transpose x2 -> x8, local copies, waits for them, and re-layouts: 0.93 us -> 3.11 us  [pair_flows(): first = jnp.repeat(jnp.transpose(out[:, 0:2, :half], (1, 0, 2)), 2, axis=2)]
    slice x0 -> x3, local copies, waits for them, and re-layouts: none -> 2.17 us  [the longest x1 1.33 us: body(): own_c = own_pad[start:start + per * STRIDE + PATCH - STRIDE]]
    another operation x1 -> x4, local copies, waits for them, and re-layouts: 0.59 us -> 2.5 us  [pair_flows(): skip_next.reshape(-1)]
    another operation x1 -> x4, local copies, waits for them, and re-layouts: 0.59 us -> 2.45 us  [pair_flows(): skip.reshape(-1)]
  transfers between devices with their start and end apart: 8 -> 14, of which waited for: 4 -> 4; matrix products, arithmetic and copies ran while one was open for 3% -> 12% of each run, Pallas kernels for 0% -> 35%
where the time goes in v1:
time: 156 us; the launch traced here: 155 us
  Pallas kernels  71.6 us (46%)
  starting transfers between devices  38 us (24%)
  local copies, waits for them, and re-layouts  24.1 us (15%)
  waiting for transfers between devices  16.1 us (10%)
  other arithmetic  3.7 us (2%)
    pallas_call x4, Pallas kernels, pair_flows(): pl.pallas_call(functools.partial(_flow_kernel, cols=cols), grid_spec=grid...  71.6 us
    ppermute x9, starting transfers between devices, shifted(): lax.ppermute(value, axis, [(source, source + steps) for source in range(f...  24 us
    unnamed x29, local copies, waits for them, and re-layouts  6.65 us
    ppermute x2, starting transfers between devices, extended(): lax.ppermute(lax.slice_in_dim(block, block.shape[dim] - width, None, axis...  6.59 us
    all_to_all x1, waiting for transfers between devices, gather_sections(): return lax.all_to_all(spread, axis, 0, 0, tiled=True)  5.58 us
    ppermute x2, waiting for transfers between devices, extended(): lax.ppermute(lax.slice_in_dim(block, block.shape[dim] - width, None, axis...  5.36 us
    all_to_all x1, starting transfers between devices, gather_sections(): return lax.all_to_all(spread, axis, 0, 0, tiled=True)  4.85 us
    concatenate x2, local copies, waits for them, and re-layouts, extended(): block = jnp.concatenate([low, block, high], axis=dim)  4.48 us
  transfers between devices with their start and end apart: 14, of which 4 were waited for; matrix products, arithmetic and copies ran while one was open for 12% of the time, Pallas kernels for 35%

profile of v1, /device:TPU:0, one launch (start us, length us, event | category | flops | bytes accessed | tf_op | source)
XLA Modules:
  0.0 154.7 jit_solution(8810564023527733445)
XLA Ops:
  0.6 0.8 fusion.82
  1.4 2.3 %collective-permute-start.1 = (bf16[1,16,1024]{2,1,0:T(8,128)(2,1)S(1)}, bf16[1,16,1024]{2,1,0:T(8,128)(2,1)S(1)}, u32[]{:S(2)}, u32[]{:S(2)}) collective-permute-start(bf16[1,16,1024]{2,1,0:T(8,128)(2,1)S(1)} %get-tuple-element.27), channel_id=1, source_target_pairs={{0,1},{2,3},{4,5},{6,7},{8,9},{10,11},{12,13},{14,15},{16,17},{18,... | collective-permute-start | bytes 98312 | tf_op jit(solution)/shard_map/ppermute | solution.py:34
  3.8 1.3 collective-permute-start.2
  5.1 1.3 collective-permute-start
  6.4 0.8 fusion.84
  7.9 1.8 %constant_dynamic-update-slice_fusion.1 = bf16[1,1056,1024]{2,1,0:T(8,128)(2,1)S(1)} fusion(bf16[1,1056,1024]{2,1,0:T(8,128)(2,1)S(1)} %constant_dynamic-update-slice_fusion.2, bf16[1,1024,1024]{2,1,0:T(8,128)(2,1)} %param.3), kind=kLoop, calls=%fused_computation.135 | loop fusion | bytes 4194304
  9.9 4.2 %collective-permute-start.3 = (bf16[1,1056,16]{2,1,0:T(8,128)(2,1)S(1)}, bf16[1,1056,16]{2,1,0:T(8,128)(2,1)S(1)}, u32[]{:S(2)}, u32[]{:S(2)}) collective-permute-start(bf16[1,1056,16]{2,1,0:T(8,128)(2,1)S(1)} %get-tuple-element.25), channel_id=1, source_target_pairs={{0,2},{1,3},{4,6},{5,7},{8,10},{9,11},{12,14},{13,15},{16,18},{17,... | collective-permute-start | bytes 101384 | tf_op jit(solution)/shard_map/ppermute | solution.py:34
  14.1 1.3 collective-permute-start.4
  15.5 5.4 %collective-permute-done.3 = bf16[1,1056,16]{2,1,0:T(8,128)(2,1)S(1)} collective-permute-done((bf16[1,1056,16]{2,1,0:T(8,128)(2,1)S(1)}, bf16[1,1056,16]{2,1,0:T(8,128)(2,1)S(1)}, u32[]{:S(2)}, u32[]{:S(2)}) %collective-permute-start.3) | collective-permute-done | bytes 33824 | tf_op jit(solution)/shard_map/ppermute | solution.py:34
  20.8 4.4 %collective-permute-done.4 = bf16[1,1056,16]{2,1,0:T(8,128)(2,1)S(1)} collective-permute-done((bf16[1,1056,16]{2,1,0:T(8,128)(2,1)S(1)}, bf16[1,1056,16]{2,1,0:T(8,128)(2,1)S(1)}, u32[]{:S(2)}, u32[]{:S(2)}) %collective-permute-start.4) | collective-permute-done | bytes 33824 | tf_op jit(solution)/shard_map/ppermute | solution.py:37
  25.3 4.5 %concatenate.22 = bf16[1,1056,1056]{2,1,0:T(8,128)(2,1)S(1)} concatenate(bf16[1,1056,16]{2,1,0:T(8,128)(2,1)S(1)} %collective-permute-done.3, bf16[1,1056,1024]{2,1,0:T(8,128)(2,1)} %copy-done, bf16[1,1056,16]{2,1,0:T(8,128)(2,1)S(1)} %collective-permute-done.4), dimensions={2} | concatenate | bytes 4460544 | tf_op jit(solution)/shard_map/concatenate | solution.py:38
  29.8 1.3 slice_bitcast_fusion.3
  31.1 4.3 %collective-permute-start.5 = (bf16[288,1056]{1,0:T(8,128)(2,1)}, bf16[288,1056]{1,0:T(8,128)(2,1)S(1)}, u32[]{:S(2)}, u32[]{:S(2)}) collective-permute-start(bf16[288,1056]{1,0:T(8,128)(2,1)} %get-tuple-element.20.own_ref), channel_id=1, source_target_pairs={{0,4},{4,8},{8,12},{1,5},{5,9},{9,13},{2,6},{6,10},{10,14},{3,7},{... | collective-permute-start | bytes 1824776 | tf_op jit(solution)/shard_map/ppermute | solution.py:26
  35.4 1.3 collective-permute-start.6
  36.7 4.6 %collective-permute-start.7 = (bf16[288,1056]{1,0:T(8,128)(2,1)}, bf16[288,1056]{1,0:T(8,128)(2,1)S(1)}, u32[]{:S(2)}, u32[]{:S(2)}) collective-permute-start(bf16[288,1056]{1,0:T(8,128)(2,1)} %get-tuple-element.23.own_ref), channel_id=1, source_target_pairs={{0,4},{4,8},{8,12},{1,5},{5,9},{9,13},{2,6},{6,10},{10,14},{3,7},{... | collective-permute-start | bytes 1824776 | tf_op jit(solution)/shard_map/ppermute | solution.py:26
  45.2 1.3 collective-permute-start.8
  49.0 1.3 collective-permute-start.10
  50.9 5.4 %collective-permute-start.9 = (bf16[288,1056]{1,0:T(8,128)(2,1)}, bf16[288,1056]{1,0:T(8,128)(2,1)}, u32[]{:S(2)}, u32[]{:S(2)}) collective-permute-start(bf16[288,1056]{1,0:T(8,128)(2,1)} %get-tuple-element.22.own_ref), channel_id=1, source_target_pairs={{0,4},{4,8},{8,12},{1,5},{5,9},{9,13},{2,6},{6,10},{10,14},{3,7},{... | collective-permute-start | bytes 1824776 | tf_op jit(solution)/shard_map/ppermute | solution.py:26
  56.3 0.9 copy-done.8
  57.2 3.1 %collective-permute-start.11 = (bf16[288,1056]{1,0:T(8,128)(2,1)S(1)}, bf16[288,1056]{1,0:T(8,128)(2,1)S(1)}, u32[]{:S(2)}, u32[]{:S(2)}) collective-permute-start(bf16[288,1056]{1,0:T(8,128)(2,1)S(1)} %get-tuple-element.21.own_ref), channel_id=1, source_target_pairs={{0,4},{4,8},{8,12},{1,5},{5,9},{9,13},{2,6},{6,10},{10,14},{3,7},{... | collective-permute-start | bytes 1824776 | tf_op jit(solution)/shard_map/ppermute | solution.py:26
  60.4 17.9 %shard_map.50 = f32[2,8,128]{2,1,0:T(8,128)} custom-call(s32[16]{0:T(128)} %reshape_squeeze.24.skip_ref, s32[16]{0:T(128)} %reshape_squeeze.25.skip_next_ref, s32[1]{0:T(128)} %bitcast.1.flag_ref, bf16[288,1056]{1,0:T(8,128)(2,1)} %get-tuple-element.20.own_ref, bf16[288,1056]{1,0:T(8,128)(2,1)} %copy-done.6, bf16[288,1056]{1,0:T(8,128)(2,1)} %copy-done.8, ...), custom_call_target="tpu_custom_call" | custom-call | tf_op jit(solution)/shard_map/pallas_call | solution.py:144
  78.2 1.5 collective-permute-start.12
  79.7 0.8 slice_bitcast_fusion.12
  80.7 17.8 %shard_map.51 = f32[2,8,128]{2,1,0:T(8,128)} custom-call(s32[16]{0:T(128)} %reshape_squeeze.26.skip_ref, s32[16]{0:T(128)} %reshape_squeeze.27.skip_next_ref, s32[1]{0:T(128)} %bitcast.1.flag_ref, bf16[288,1056]{1,0:T(8,128)(2,1)} %get-tuple-element.23.own_ref, bf16[288,1056]{1,0:T(8,128)(2,1)} %copy-done.4, ...), custom_call_target="tpu_custom_call" | custom-call | tf_op jit(solution)/shard_map/pallas_call | solution.py:144
  98.5 0.8 slice_bitcast_fusion.11
  99.4 0.8 copy-done.7
  100.3 17.8 %shard_map.52 = f32[2,8,128]{2,1,0:T(8,128)} custom-call(s32[16]{0:T(128)} %reshape_squeeze.28.skip_ref, s32[16]{0:T(128)} %reshape_squeeze.29.skip_next_ref, s32[1]{0:T(128)} %bitcast.1.flag_ref, bf16[288,1056]{1,0:T(8,128)(2,1)} %get-tuple-element.22.own_ref, bf16[288,1056]{1,0:T(8,128)(2,1)} %collective-permute-done.9.prev_ref, ...), custom_call_target="tpu_custom_call" | custom-call | tf_op jit(solution)/shard_map/pallas_call | solution.py:144
  119.1 0.9 copy-done.5
  120.0 0.8 copy-done.9
  120.8 18.1 %shard_map.53 = f32[2,8,128]{2,1,0:T(8,128)} custom-call(s32[16]{0:T(128)} %reshape_squeeze.30.skip_ref, s32[16]{0:T(128)} %reshape_squeeze.31.skip_next_ref, s32[1]{0:T(128)} %bitcast.1.flag_ref, bf16[288,1056]{1,0:T(8,128)(2,1)} %copy-done.3, bf16[288,1056]{1,0:T(8,128)(2,1)} %copy-done.5, bf16[288,1056]{1,0:T(8,128)(2,1)} %copy-done.9, ...), custom_call_target="tpu_custom_call" | custom-call | tf_op jit(solution)/shard_map/pallas_call | solution.py:144
  141.2 4.9 %all-to-all-start = ((f32[4,1,384]{2,1,0:T(1,128)}), f32[4,1,384]{2,1,0:T(1,128)S(1)}, u32[]{:S(2)}, u32[]{:S(2)}) async-start(f32[4,1,384]{2,1,0:T(1,128)} %reshape.60), calls=%async_computation | async-start | bytes 12288 | tf_op jit(solution)/shard_map/all_to_all | solution.py:169
  146.1 5.6 %all-to-all-done = f32[4,1,384]{2,1,0:T(1,128)S(1)} async-done(((f32[4,1,384]{2,1,0:T(1,128)}), f32[4,1,384]{2,1,0:T(1,128)S(1)}, u32[]{:S(2)}, u32[]{:S(2)}) %all-to-all-start) | async-done | bytes 6176 | tf_op jit(solution)/shard_map/all_to_all | solution.py:169
  (113 shorter events, 14.4 us)
Async XLA Ops:
  1.4 6.5 %collective-permute-start.1 = (bf16[1,16,1024]{2,1,0:T(8,128)(2,1)S(1)}, bf16[1,16,1024]{2,1,0:T(8,128)(2,1)S(1)}, u32[]{:S(2)}, u32[]{:S(2)}) collective-permute-start(bf16[1,16,1024]{2,1,0:T(8,128)(2,1)S(1)} %get-tuple-element.27), channel_id=1, source_target_pairs={{0,1},{2,3},{4,5},{6,7},{8,9},{10,11},{12,13},{14,15},{16,17},{18,... | collective-permute-start | bytes 98312 | tf_op jit(solution)/shard_map/ppermute | solution.py:34
  3.8 5.9 %collective-permute-start.2 = (bf16[1,16,1024]{2,1,0:T(8,128)(2,1)S(1)}, bf16[1,16,1024]{2,1,0:T(8,128)(2,1)S(1)}, u32[]{:S(2)}, u32[]{:S(2)}) collective-permute-start(bf16[1,16,1024]{2,1,0:T(8,128)(2,1)S(1)} %get-tuple-element.26), channel_id=1, source_target_pairs={{1,0},{3,2},{5,4},{7,6},{9,8},{11,10},{13,12},{15,14},{17,16},{19,... | collective-permute-start | bytes 98312 | tf_op jit(solution)/shard_map/ppermute | solution.py:37
  5.1 41.4 %collective-permute-start = (s32[1,8,8]{2,1,0:T(8,128)}, s32[1,8,8]{2,1,0:T(8,128)S(1)}, u32[]{:S(2)}, u32[]{:S(2)}) collective-permute-start(s32[1,8,8]{2,1,0:T(8,128)} %param.4), channel_id=1, source_target_pairs={{4,0},{8,4},{12,8},{5,1},{9,5},{13,9},{6,2},{10,6},{14,10},{7,3},{... | collective-permute-start | bytes 776 | tf_op jit(solution)/shard_map/ppermute | solution.py:26
  7.9 7.5 %copy-start.11 = (s32[1,8,8]{2,1,0:T(8,128)S(1)}, s32[1,8,8]{2,1,0:T(8,128)}, u32[]{:S(2)}) copy-start(s32[1,8,8]{2,1,0:T(8,128)} %param.5) | copy-start | bytes 772
  9.7 11.1 %copy-start = (bf16[1,1056,1024]{2,1,0:T(8,128)(2,1)}, bf16[1,1056,1024]{2,1,0:T(8,128)(2,1)S(1)}, u32[]{:S(2)}) copy-start(bf16[1,1056,1024]{2,1,0:T(8,128)(2,1)S(1)} %constant_dynamic-update-slice_fusion) | copy-start | bytes 6488068
  9.9 10.9 %collective-permute-start.3 = (bf16[1,1056,16]{2,1,0:T(8,128)(2,1)S(1)}, bf16[1,1056,16]{2,1,0:T(8,128)(2,1)S(1)}, u32[]{:S(2)}, u32[]{:S(2)}) collective-permute-start(bf16[1,1056,16]{2,1,0:T(8,128)(2,1)S(1)} %get-tuple-element.25), channel_id=1, source_target_pairs={{0,2},{1,3},{4,6},{5,7},{8,10},{9,11},{12,14},{13,15},{16,18},{17,... | collective-permute-start | bytes 101384 | tf_op jit(solution)/shard_map/ppermute | solution.py:34
  14.1 11.1 %collective-permute-start.4 = (bf16[1,1056,16]{2,1,0:T(8,128)(2,1)S(1)}, bf16[1,1056,16]{2,1,0:T(8,128)(2,1)S(1)}, u32[]{:S(2)}, u32[]{:S(2)}) collective-permute-start(bf16[1,1056,16]{2,1,0:T(8,128)(2,1)S(1)} %get-tuple-element.24), channel_id=1, source_target_pairs={{2,0},{3,1},{6,4},{7,5},{10,8},{11,9},{14,12},{15,13},{18,16},{19,... | collective-permute-start | bytes 101384 | tf_op jit(solution)/shard_map/ppermute | solution.py:37
  29.8 5.6 %copy-start.10 = (s32[1,8,8]{2,1,0:T(8,128)S(1)}, s32[1,8,8]{2,1,0:T(8,128)}, u32[]{:S(2)}) copy-start(s32[1,8,8]{2,1,0:T(8,128)} %param.4) | copy-start | bytes 772
  31.1 88.0 %copy-start.3 = (bf16[288,1056]{1,0:T(8,128)(2,1)}, bf16[288,1056]{1,0:T(8,128)(2,1)S(1)}, u32[]{:S(2)}) copy-start(bf16[288,1056]{1,0:T(8,128)(2,1)S(1)} %get-tuple-element.21.own_ref) | copy-start | bytes 1824772
  31.1 19.8 %collective-permute-start.5 = (bf16[288,1056]{1,0:T(8,128)(2,1)}, bf16[288,1056]{1,0:T(8,128)(2,1)S(1)}, u32[]{:S(2)}, u32[]{:S(2)}) collective-permute-start(bf16[288,1056]{1,0:T(8,128)(2,1)} %get-tuple-element.20.own_ref), channel_id=1, source_target_pairs={{0,4},{4,8},{8,12},{1,5},{5,9},{9,13},{2,6},{6,10},{10,14},{3,7},{... | collective-permute-start | bytes 1824776 | tf_op jit(solution)/shard_map/ppermute | solution.py:26
  35.4 20.9 %collective-permute-start.6 = (bf16[288,1056]{1,0:T(8,128)(2,1)}, bf16[288,1056]{1,0:T(8,128)(2,1)S(1)}, u32[]{:S(2)}, u32[]{:S(2)}) collective-permute-start(bf16[288,1056]{1,0:T(8,128)(2,1)} %get-tuple-element.20.own_ref), channel_id=1, source_target_pairs={{4,0},{8,4},{12,8},{5,1},{9,5},{13,9},{6,2},{10,6},{14,10},{7,3},{... | collective-permute-start | bytes 1824776 | tf_op jit(solution)/shard_map/ppermute | solution.py:26
  36.7 41.5 %collective-permute-start.7 = (bf16[288,1056]{1,0:T(8,128)(2,1)}, bf16[288,1056]{1,0:T(8,128)(2,1)S(1)}, u32[]{:S(2)}, u32[]{:S(2)}) collective-permute-start(bf16[288,1056]{1,0:T(8,128)(2,1)} %get-tuple-element.23.own_ref), channel_id=1, source_target_pairs={{0,4},{4,8},{8,12},{1,5},{5,9},{9,13},{2,6},{6,10},{10,14},{3,7},{... | collective-permute-start | bytes 1824776 | tf_op jit(solution)/shard_map/ppermute | solution.py:26
  42.0 18.4 %copy-start.1 = (bf16[160,160]{1,0:T(8,128)(2,1)}, bf16[160,160]{1,0:T(8,128)(2,1)S(1)}, u32[]{:S(2)}) copy-start(bf16[160,160]{1,0:T(8,128)(2,1)S(1)} %get-tuple-element.44.s_ref) | copy-start | bytes 153604
  42.0 18.4 %copy-start.2 = (bf16[160,160]{1,0:T(8,128)(2,1)}, bf16[160,160]{1,0:T(8,128)(2,1)S(1)}, u32[]{:S(2)}) copy-start(bf16[160,160]{1,0:T(8,128)(2,1)S(1)} %get-tuple-element.45.c_ref) | copy-start | bytes 153604
  45.2 35.5 %collective-permute-start.8 = (bf16[288,1056]{1,0:T(8,128)(2,1)}, bf16[288,1056]{1,0:T(8,128)(2,1)}, u32[]{:S(2)}, u32[]{:S(2)}) collective-permute-start(bf16[288,1056]{1,0:T(8,128)(2,1)} %get-tuple-element.23.own_ref), channel_id=1, source_target_pairs={{4,0},{8,4},{12,8},{5,1},{9,5},{13,9},{6,2},{10,6},{14,10},{7,3},{... | collective-permute-start | bytes 1824776 | tf_op jit(solution)/shard_map/ppermute | solution.py:26
  49.0 50.5 %collective-permute-start.10 = (bf16[288,1056]{1,0:T(8,128)(2,1)}, bf16[288,1056]{1,0:T(8,128)(2,1)S(1)}, u32[]{:S(2)}, u32[]{:S(2)}) collective-permute-start(bf16[288,1056]{1,0:T(8,128)(2,1)} %get-tuple-element.22.own_ref), channel_id=1, source_target_pairs={{4,0},{8,4},{12,8},{5,1},{9,5},{13,9},{6,2},{10,6},{14,10},{7,3},{... | collective-permute-start | bytes 1824776 | tf_op jit(solution)/shard_map/ppermute | solution.py:26
  50.9 9.4 %copy-start.6 = (bf16[288,1056]{1,0:T(8,128)(2,1)}, bf16[288,1056]{1,0:T(8,128)(2,1)S(1)}, u32[]{:S(2)}) copy-start(bf16[288,1056]{1,0:T(8,128)(2,1)S(1)} %collective-permute-done.5.prev_ref) | copy-start | bytes 1824772
  50.9 48.5 %collective-permute-start.9 = (bf16[288,1056]{1,0:T(8,128)(2,1)}, bf16[288,1056]{1,0:T(8,128)(2,1)}, u32[]{:S(2)}, u32[]{:S(2)}) collective-permute-start(bf16[288,1056]{1,0:T(8,128)(2,1)} %get-tuple-element.22.own_ref), channel_id=1, source_target_pairs={{0,4},{4,8},{8,12},{1,5},{5,9},{9,13},{2,6},{6,10},{10,14},{3,7},{... | collective-permute-start | bytes 1824776 | tf_op jit(solution)/shard_map/ppermute | solution.py:26
  56.3 0.9 copy-start.8
  57.2 61.9 %collective-permute-start.11 = (bf16[288,1056]{1,0:T(8,128)(2,1)S(1)}, bf16[288,1056]{1,0:T(8,128)(2,1)S(1)}, u32[]{:S(2)}, u32[]{:S(2)}) collective-permute-start(bf16[288,1056]{1,0:T(8,128)(2,1)S(1)} %get-tuple-element.21.own_ref), channel_id=1, source_target_pairs={{0,4},{4,8},{8,12},{1,5},{5,9},{9,13},{2,6},{6,10},{10,14},{3,7},{... | collective-permute-start | bytes 1824776 | tf_op jit(solution)/shard_map/ppermute | solution.py:26
  78.2 2.4 %copy-start.4 = (bf16[288,1056]{1,0:T(8,128)(2,1)}, bf16[288,1056]{1,0:T(8,128)(2,1)S(1)}, u32[]{:S(2)}) copy-start(bf16[288,1056]{1,0:T(8,128)(2,1)S(1)} %collective-permute-done.7.prev_ref) | copy-start | bytes 1824772
  78.2 40.9 %collective-permute-start.12 = (bf16[288,1056]{1,0:T(8,128)(2,1)S(1)}, bf16[288,1056]{1,0:T(8,128)(2,1)S(1)}, u32[]{:S(2)}, u32[]{:S(2)}) collective-permute-start(bf16[288,1056]{1,0:T(8,128)(2,1)S(1)} %get-tuple-element.21.own_ref), channel_id=1, source_target_pairs={{4,0},{8,4},{12,8},{5,1},{9,5},{13,9},{6,2},{10,6},{14,10},{7,3},{... | collective-permute-start | bytes 1824776 | tf_op jit(solution)/shard_map/ppermute | solution.py:26
  99.4 0.8 copy-start.7
  119.1 0.9 copy-start.5
  120.0 0.8 copy-start.9
  141.2 10.4 %all-to-all-start = ((f32[4,1,384]{2,1,0:T(1,128)}), f32[4,1,384]{2,1,0:T(1,128)S(1)}, u32[]{:S(2)}, u32[]{:S(2)}) async-start(f32[4,1,384]{2,1,0:T(1,128)} %reshape.60), calls=%async_computation | async-start | bytes 12288 | tf_op jit(solution)/shard_map/all_to_all | solution.py:169

commit v2 on v1

--- a/solution.py
+++ b/solution.py
@@ -52,114 +52,121 @@
 
 def _flow_kernel(
     skip_ref, skip_next_ref, flag_ref, own_ref, prev_ref, next_ref, cs_ref, c_ref, s_ref, out_ref,
-    *, cols,
+    half_ref, x_ref, y_ref, br_ref, bi_ref,
+    *, cols, row0,
 ):
     f32, bf16 = jnp.float32, jnp.bfloat16
     p = PATCH
-    i = pl.program_id(0)
+    pairs = cols // 2
+    i = pl.program_id(0) + row0
     cos_t = c_ref[...]
     sin_t = s_ref[...]
     both_t = cs_ref[...]
     size = float(p * p)
 
-    def spectrum(blk):
+    def window(ref, j):
+        return ref[:, j * STRIDE : j * STRIDE + p]
+
+    use_own = flag_ref[0] == 1
+    blocks = []
+    for k in range(pairs):
+        left, right = 2 * k, 2 * k + 1
+        first_near = skip_ref[i * cols + left] == 0
+        blocks.append(jnp.where(first_near, window(own_ref, left), window(own_ref, right)))
+        blocks.append(jnp.where(first_near, window(prev_ref, left), window(prev_ref, right)))
+    for k in range(pairs):
+        left, right = 2 * k, 2 * k + 1
+        second_far = skip_next_ref[i * cols + right] == 1
+        blocks.append(jnp.where(second_far, window(next_ref, right), window(next_ref, left)))
+        col_prev = jnp.where(second_far, window(prev_ref, right), window(prev_ref, left))
+        col_own = jnp.where(second_far, window(own_ref, right), window(own_ref, left))
+        blocks.append(jnp.where(use_own, col_own, col_prev))
+
+    for t, blk in enumerate(blocks):
         x = blk.astype(f32)
         centered = x - _sum_all(x) / size
         spread = _sum_all(centered * centered) / size
         normed = (centered * lax.rsqrt(spread + EPSILON)).astype(bf16)
-        half = jnp.dot(both_t, normed, preferred_element_type=f32).astype(bf16)
-        h_re, h_im = half[:p], half[p:]
-        re = jnp.dot(h_re, cos_t, preferred_element_type=f32) - jnp.dot(
-            h_im, sin_t, preferred_element_type=f32
-        )
-        im = jnp.dot(h_re, sin_t, preferred_element_type=f32) + jnp.dot(
-            h_im, cos_t, preferred_element_type=f32
-        )
+        half_ref[2 * p * t : 2 * p * (t + 1), :] = jnp.dot(
+            both_t, normed, preferred_element_type=f32
+        ).astype(bf16)
+    halves = half_ref[...]
+    x_ref[...] = jnp.dot(halves, cos_t, preferred_element_type=f32)
+    y_ref[...] = jnp.dot(halves, sin_t, preferred_element_type=f32)
+
+    def spectrum(t):
+        base = 2 * p * t
+        re = x_ref[base : base + p, :] - y_ref[base + p : base + 2 * p, :]
+        im = y_ref[base : base + p, :] + x_ref[base + p : base + 2 * p, :]
         return re, im
 
-    u_col = lax.broadcasted_iota(jnp.int32, (p, 1), 0)
-    off_col = jnp.where(u_col < p // 2, u_col, u_col - p).astype(f32)
-    u_row = lax.broadcasted_iota(jnp.int32, (1, p), 1)
-    off_row = jnp.where(u_row < p // 2, u_row, u_row - p).astype(f32)
-
-    def moments(own_blk, other_blk):
-        o_re, o_im = spectrum(own_blk)
-        t_re, t_im = spectrum(other_blk)
+    for c in range(cols):
+        o_re, o_im = spectrum(2 * c)
+        t_re, t_im = spectrum(2 * c + 1)
         c_re = (o_re * t_re + o_im * t_im).astype(bf16)
         c_im = (o_re * t_im - o_im * t_re).astype(bf16)
         a = jnp.dot(both_t, c_re, preferred_element_type=f32)
         b = jnp.dot(both_t, c_im, preferred_element_type=f32)
-        b_re = (a[:p] + b[p:]).astype(bf16)
-        b_im = (b[:p] - a[p:]).astype(bf16)
-        corr = (
-            jnp.dot(b_re, cos_t, preferred_element_type=f32)
-            + jnp.dot(b_im, sin_t, preferred_element_type=f32)
-        ) / float(p) ** 4
-        w = jnp.exp(SHARPNESS * corr)
-        total = _sum_all(w)
-        rows_sum = jnp.sum(w, axis=1, keepdims=True)
-        cols_sum = jnp.sum(w, axis=0, keepdims=True)
-        along_rows = jnp.sum(rows_sum * off_col, axis=0, keepdims=True)
-        along_cols = jnp.sum(cols_sum * off_row, axis=1, keepdims=True)
-        return along_rows / total / float(RIM), along_cols / total / float(RIM)
-
-    def window(ref, j):
-        return ref[:, j * STRIDE : j * STRIDE + p]
-
-    lane = lax.broadcasted_iota(jnp.int32, (1, 128), 1)
-    acc = [jnp.zeros((1, 128), f32) for _ in range(4)]
-    use_own = flag_ref[0] == 1
-    for k in range(cols // 2):
-        left, right = 2 * k, 2 * k + 1
-        first_near = skip_ref[i * cols + left] == 0
-        own_a = jnp.where(first_near, window(own_ref, left), window(own_ref, right))
-        oth_a = jnp.where(first_near, window(prev_ref, left), window(prev_ref, right))
-        ra, ca = moments(own_a, oth_a)
-        second_far = skip_next_ref[i * cols + right] == 1
-        own_b = jnp.where(second_far, window(next_ref, right), window(next_ref, left))
-        col_b_prev = jnp.where(second_far, window(prev_ref, right), window(prev_ref, left))
-        col_b_own = jnp.where(second_far, window(own_ref, right), window(own_ref, left))
-        oth_b = jnp.where(use_own, col_b_own, col_b_prev)
-        rb, cb = moments(own_b, oth_b)
-        sel = lane == k
-        acc = [jnp.where(sel, v, a) for v, a in zip((ra, ca, rb, cb), acc)]
-    out_ref[0] = jnp.concatenate(acc + [jnp.zeros((4, 128), f32)], axis=0)
-
-
-def pair_flows(own_pad, prev_pad, next_pad, skip, skip_next, use_own):
+        br_ref[p * c : p * (c + 1), :] = (a[:p] + b[p:]).astype(bf16)
+        bi_ref[p * c : p * (c + 1), :] = (b[:p] - a[p:]).astype(bf16)
+
+    corr = (
+        jnp.dot(br_ref[...], cos_t, preferred_element_type=f32)
+        + jnp.dot(bi_ref[...], sin_t, preferred_element_type=f32)
+    ) / float(p) ** 4
+    w = jnp.exp(SHARPNESS * corr)
+    u_col = lax.broadcasted_iota(jnp.int32, (cols * p, 1), 0) % p
+    off_col = jnp.where(u_col < p // 2, u_col, u_col - p).astype(f32)
+    u_row = lax.broadcasted_iota(jnp.int32, (1, p), 1)
+    off_row = jnp.where(u_row < p // 2, u_row, u_row - p).astype(f32)
+    rows_sum = jnp.sum(w, axis=1, keepdims=True)
+    total = jnp.sum(rows_sum.reshape(cols, p, 1), axis=1)
+    along_rows = jnp.sum((rows_sum * off_col).reshape(cols, p, 1), axis=1)
+    cols_sum = jnp.sum(w.reshape(cols, p, p), axis=1)
+    along_cols = jnp.sum(cols_sum * off_row, axis=1, keepdims=True)
+    ar = along_rows / total / float(RIM)
+    ac = along_cols / total / float(RIM)
+    lane = lax.broadcasted_iota(jnp.int32, (cols, 128), 1)
+    res = jnp.where(lane == 0, ar, jnp.where(lane == 1, ac, 0.0))
+    height = out_ref.shape[1]
+    if height > cols:
+        res = jnp.concatenate([res, jnp.zeros((height - cols, 128), f32)], axis=0)
+    out_ref[0] = res
+
+
+def pair_flows(own_pad, prev_pad, next_pad, skip_flat, skip_next_flat, use_own, row0, tables):
     tall, broad = own_pad.shape
     rows = (tall - (PATCH - STRIDE)) // STRIDE
     cols = (broad - (PATCH - STRIDE)) // STRIDE
-    assert cols % 2 == 0 and cols // 2 <= 128
-    cos_t, sin_t = dft_tables(PATCH)
-    both_t = jnp.concatenate([cos_t, sin_t], axis=0)
+    assert cols % 2 == 0
+    height = max(8, -(-cols // 8) * 8)
+    both_t, cos_t, sin_t = tables
     band = pl.BlockSpec((pl.Element(PATCH), pl.Element(broad)), lambda i, *_: (i * STRIDE, 0))
     table = pl.BlockSpec((PATCH, PATCH), lambda i, *_: (0, 0))
     grid_spec = pltpu.PrefetchScalarGridSpec(
         num_scalar_prefetch=3,
         grid=(rows,),
         in_specs=[band, band, band, pl.BlockSpec((2 * PATCH, PATCH), lambda i, *_: (0, 0)), table, table],
-        out_specs=pl.BlockSpec((1, 8, 128), lambda i, *_: (i, 0, 0)),
+        out_specs=pl.BlockSpec((1, height, 128), lambda i, *_: (i, 0, 0)),
+        scratch_shapes=[
+            pltpu.VMEM((4 * cols * PATCH, PATCH), jnp.bfloat16),
+            pltpu.VMEM((4 * cols * PATCH, PATCH), jnp.float32),
+            pltpu.VMEM((4 * cols * PATCH, PATCH), jnp.float32),
+            pltpu.VMEM((cols * PATCH, PATCH), jnp.bfloat16),
+            pltpu.VMEM((cols * PATCH, PATCH), jnp.bfloat16),
+        ],
     )
     out = pl.pallas_call(
-        functools.partial(_flow_kernel, cols=cols),
+        functools.partial(_flow_kernel, cols=cols, row0=row0),
         grid_spec=grid_spec,
-        out_shape=jax.ShapeDtypeStruct((rows, 8, 128), jnp.float32),
-        compiler_params=pltpu.CompilerParams(dimension_semantics=("arbitrary",)),
-    )(
-        skip.reshape(-1),
-        skip_next.reshape(-1),
-        use_own.reshape(1),
-        own_pad,
-        prev_pad,
-        next_pad,
-        both_t,
-        cos_t,
-        sin_t,
-    )
+        out_shape=jax.ShapeDtypeStruct((rows, height, 128), jnp.float32),
+        compiler_params=pltpu.CompilerParams(
+            dimension_semantics=("arbitrary",), vmem_limit_bytes=48 * 1024 * 1024
+        ),
+    )(skip_flat, skip_next_flat, use_own.reshape(1), own_pad, prev_pad, next_pad, both_t, cos_t, sin_t)
     half = cols // 2
-    first = jnp.repeat(jnp.transpose(out[:, 0:2, :half], (1, 0, 2)), 2, axis=2)
-    second = jnp.repeat(jnp.transpose(out[:, 2:4, :half], (1, 0, 2)), 2, axis=2)
+    first = jnp.repeat(jnp.transpose(out[:, :half, 0:2], (2, 0, 1)), 2, axis=2)
+    second = jnp.repeat(jnp.transpose(out[:, half:cols, 0:2], (2, 0, 1)), 2, axis=2)
     return first, second
 
 
@@ -207,15 +214,18 @@
     rows_count = (own_pad.shape[0] - (PATCH - STRIDE)) // STRIDE
     chunks = max(n for n in (1, 2, 4) if rows_count % n == 0)
     per = rows_count // chunks
+    cos_t, sin_t = dft_tables(PATCH)
+    tables = (jnp.concatenate([cos_t, sin_t], axis=0), cos_t, sin_t)
+    skip_flat = skipped.reshape(-1)
+    skip_next_flat = skip_next.reshape(-1)
     firsts, seconds = [], []
     for c in range(chunks):
         start = c * per * STRIDE
         own_c = own_pad[start : start + per * STRIDE + PATCH - STRIDE]
         prev_c = shifted(own_c, "sec", 1)
         next_c = shifted(own_c, "sec", -1)
-        part = slice(c * per, (c + 1) * per)
         first_c, second_c = pair_flows(
-            own_c, prev_c, next_c, skipped[0, part], skip_next[0, part], use_own
+            own_c, prev_c, next_c, skip_flat, skip_next_flat, use_own, c * per, tables
         )
         firsts.append(first_c)
         seconds.append(second_c)

time: 156 us -> 124 us (0.79)
  Pallas kernels: 71.6 us -> 48.6 us
  local copies, waits for them, and re-layouts: 24.1 us -> 12.6 us
  waiting for transfers between devices: 16.1 us -> 19.7 us
    pallas_call x4, Pallas kernels: 71.6 us -> 48.6 us  [pair_flows(): pl.pallas_call(functools.partial(_flow_kernel, cols=cols, row0=row0), gri...]
    another operation x8 -> x0, local copies, waits for them, and re-layouts: 4.95 us -> none  [the longest x4 2.5 us: pair_flows(): skip_next.reshape(-1)]
    ppermute x9, waiting for transfers between devices: 0.7 us -> 4.31 us  [shifted(): lax.ppermute(value, axis, [(source, source + steps) for source in range(f...]
    unnamed x29 -> x9, local copies, waits for them, and re-layouts: 6.65 us -> 3.2 us
    transpose x12, local copies, waits for them, and re-layouts: 3.12 us -> 0.81 us  [the longest x8 0.42 us: pair_flows(): first = jnp.repeat(jnp.transpose(out[:, :half, 0:2], (2, 0, 1)), 2, axis=2)]
    ppermute x9, starting transfers between devices: 24 us -> 26 us  [shifted(): lax.ppermute(value, axis, [(source, source + steps) for source in range(f...]
  transfers between devices with their start and end apart: 14 -> 14, of which waited for: 4 -> 4; matrix products, arithmetic and copies ran while one was open for 12% -> 8% of each run, Pallas kernels for 35% -> 29%
where the time goes in v2:
time: 124 us
  Pallas kernels  48.6 us (39%)
  starting transfers between devices  39.3 us (32%)
  waiting for transfers between devices  19.7 us (16%)
  local copies, waits for them, and re-layouts  12.6 us (10%)
  other arithmetic  2.34 us (2%)
    pallas_call x4, Pallas kernels, pair_flows(): pl.pallas_call(functools.partial(_flow_kernel, cols=cols, row0=row0), gri...  48.6 us
    ppermute x9, starting transfers between devices, shifted(): lax.ppermute(value, axis, [(source, source + steps) for source in range(f...  26 us
    ppermute x2, starting transfers between devices, extended(): lax.ppermute(lax.slice_in_dim(block, block.shape[dim] - width, None, axis...  6.59 us
    all_to_all x1, waiting for transfers between devices, gather_sections(): return lax.all_to_all(spread, axis, 0, 0, tiled=True)  5.58 us
    ppermute x2, waiting for transfers between devices, extended(): lax.ppermute(lax.slice_in_dim(block, block.shape[dim] - width, None, axis...  5.35 us
    ppermute x2, waiting for transfers between devices, extended(): lax.ppermute(lax.slice_in_dim(block, 0, width, axis=dim), axis, backward)  4.44 us
    ppermute x9, waiting for transfers between devices, shifted(): lax.ppermute(value, axis, [(source, source + steps) for source in range(f...  4.31 us
    all_to_all x1, starting transfers between devices, gather_sections(): return lax.all_to_all(spread, axis, 0, 0, tiled=True)  4.1 us
  transfers between devices with their start and end apart: 14, of which 4 were waited for; matrix products, arithmetic and copies ran while one was open for 8% of the time, Pallas kernels for 29%

profile of v2, /device:TPU:0, one launch (start us, length us, event | category | flops | bytes accessed | tf_op | source)
XLA Modules:
  0.0 123.6 jit_solution(5117408950672441364)
XLA Ops:
  0.6 0.8 fusion.82
  1.4 2.3 %collective-permute-start.1 = (bf16[1,16,1024]{2,1,0:T(8,128)(2,1)S(1)}, bf16[1,16,1024]{2,1,0:T(8,128)(2,1)S(1)}, u32[]{:S(2)}, u32[]{:S(2)}) collective-permute-start(bf16[1,16,1024]{2,1,0:T(8,128)(2,1)S(1)} %get-tuple-element.27), channel_id=1, source_target_pairs={{0,1},{2,3},{4,5},{6,7},{8,9},{10,11},{12,13},{14,15},{16,17},{18,... | collective-permute-start | bytes 98312 | tf_op jit(solution)/shard_map/ppermute | solution.py:34
  3.8 1.3 %collective-permute-start.2 = (bf16[1,16,1024]{2,1,0:T(8,128)(2,1)S(1)}, bf16[1,16,1024]{2,1,0:T(8,128)(2,1)S(1)}, u32[]{:S(2)}, u32[]{:S(2)}) collective-permute-start(bf16[1,16,1024]{2,1,0:T(8,128)(2,1)S(1)} %get-tuple-element.26), channel_id=1, source_target_pairs={{1,0},{3,2},{5,4},{7,6},{9,8},{11,10},{13,12},{15,14},{17,16},{19,... | collective-permute-start | bytes 98312 | tf_op jit(solution)/shard_map/ppermute | solution.py:37
  5.1 1.3 %collective-permute-start = (s32[1,8,8]{2,1,0:T(8,128)}, s32[1,8,8]{2,1,0:T(8,128)S(1)}, u32[]{:S(2)}, u32[]{:S(2)}) collective-permute-start(s32[1,8,8]{2,1,0:T(8,128)} %param.4), channel_id=1, source_target_pairs={{4,0},{8,4},{12,8},{5,1},{9,5},{13,9},{6,2},{10,6},{14,10},{7,3},{... | collective-permute-start | bytes 776 | tf_op jit(solution)/shard_map/ppermute | solution.py:26
  6.4 1.8 %constant_dynamic-update-slice_fusion.1 = bf16[1,1056,1024]{2,1,0:T(8,128)(2,1)S(1)} fusion(bf16[1,1056,1024]{2,1,0:T(8,128)(2,1)S(1)} %constant_dynamic-update-slice_fusion.2, bf16[1,1024,1024]{2,1,0:T(8,128)(2,1)} %param.3), kind=kLoop, calls=%fused_computation.135 | loop fusion | bytes 4194304
  8.4 4.2 %collective-permute-start.3 = (bf16[1,1056,16]{2,1,0:T(8,128)(2,1)S(1)}, bf16[1,1056,16]{2,1,0:T(8,128)(2,1)S(1)}, u32[]{:S(2)}, u32[]{:S(2)}) collective-permute-start(bf16[1,1056,16]{2,1,0:T(8,128)(2,1)S(1)} %get-tuple-element.25), channel_id=1, source_target_pairs={{0,2},{1,3},{4,6},{5,7},{8,10},{9,11},{12,14},{13,15},{16,18},{17,... | collective-permute-start | bytes 101384 | tf_op jit(solution)/shard_map/ppermute | solution.py:34
  12.6 1.3 %collective-permute-start.4 = (bf16[1,1056,16]{2,1,0:T(8,128)(2,1)S(1)}, bf16[1,1056,16]{2,1,0:T(8,128)(2,1)S(1)}, u32[]{:S(2)}, u32[]{:S(2)}) collective-permute-start(bf16[1,1056,16]{2,1,0:T(8,128)(2,1)S(1)} %get-tuple-element.24), channel_id=1, source_target_pairs={{2,0},{3,1},{6,4},{7,5},{10,8},{11,9},{14,12},{15,13},{18,16},{19,... | collective-permute-start | bytes 101384 | tf_op jit(solution)/shard_map/ppermute | solution.py:37
  14.0 5.4 %collective-permute-done.3 = bf16[1,1056,16]{2,1,0:T(8,128)(2,1)S(1)} collective-permute-done((bf16[1,1056,16]{2,1,0:T(8,128)(2,1)S(1)}, bf16[1,1056,16]{2,1,0:T(8,128)(2,1)S(1)}, u32[]{:S(2)}, u32[]{:S(2)}) %collective-permute-start.3) | collective-permute-done | bytes 33824 | tf_op jit(solution)/shard_map/ppermute | solution.py:34
  19.3 4.4 %collective-permute-done.4 = bf16[1,1056,16]{2,1,0:T(8,128)(2,1)S(1)} collective-permute-done((bf16[1,1056,16]{2,1,0:T(8,128)(2,1)S(1)}, bf16[1,1056,16]{2,1,0:T(8,128)(2,1)S(1)}, u32[]{:S(2)}, u32[]{:S(2)}) %collective-permute-start.4) | collective-permute-done | bytes 33824 | tf_op jit(solution)/shard_map/ppermute | solution.py:37
  23.7 3.8 %concatenate.19 = bf16[1,1056,1056]{2,1,0:T(8,128)(2,1)} concatenate(bf16[1,1056,16]{2,1,0:T(8,128)(2,1)S(1)} %collective-permute-done.3, bf16[1,1056,1024]{2,1,0:T(8,128)(2,1)S(1)} %constant_dynamic-update-slice_fusion, bf16[1,1056,16]{2,1,0:T(8,128)(2,1)S(1)} %collective-permute-done.4), dimensions={2} | concatenate | bytes 4460544 | tf_op jit(solution)/shard_map/concatenate | solution.py:38
  27.5 1.9 %slice_bitcast_fusion.3 = (bf16[288,1056]{1,0:T(8,128)(2,1)S(1)}, bf16[288,1056]{1,0:T(8,128)(2,1)S(1)}, bf16[288,1056]{1,0:T(8,128)(2,1)S(1)}, bf16[288,1056]{1,0:T(8,128)(2,1)S(1)}) fusion(bf16[1,1056,1056]{2,1,0:T(8,128)(2,1)} %concatenate.19), kind=kLoop, calls=%fused_computation.3 | loop fusion | bytes 4866048 | tf_op jit(solution)/shard_map/slice | solution.py:224
  29.4 5.1 %collective-permute-start.5 = (bf16[288,1056]{1,0:T(8,128)(2,1)S(1)}, bf16[288,1056]{1,0:T(8,128)(2,1)}, u32[]{:S(2)}, u32[]{:S(2)}) collective-permute-start(bf16[288,1056]{1,0:T(8,128)(2,1)S(1)} %get-tuple-element.20.own_ref), channel_id=1, source_target_pairs={{0,4},{4,8},{8,12},{1,5},{5,9},{9,13},{2,6},{6,10},{10,14},{3,7},{... | collective-permute-start | bytes 1824776 | tf_op jit(solution)/shard_map/ppermute | solution.py:26
  34.6 1.3 %collective-permute-start.6 = (bf16[288,1056]{1,0:T(8,128)(2,1)S(1)}, bf16[288,1056]{1,0:T(8,128)(2,1)}, u32[]{:S(2)}, u32[]{:S(2)}) collective-permute-start(bf16[288,1056]{1,0:T(8,128)(2,1)S(1)} %get-tuple-element.20.own_ref), channel_id=1, source_target_pairs={{4,0},{8,4},{12,8},{5,1},{9,5},{13,9},{6,2},{10,6},{14,10},{7,3},{... | collective-permute-start | bytes 1824776 | tf_op jit(solution)/shard_map/ppermute | solution.py:26
  35.8 5.4 %collective-permute-start.7 = (bf16[288,1056]{1,0:T(8,128)(2,1)S(1)}, bf16[288,1056]{1,0:T(8,128)(2,1)}, u32[]{:S(2)}, u32[]{:S(2)}) collective-permute-start(bf16[288,1056]{1,0:T(8,128)(2,1)S(1)} %get-tuple-element.23.own_ref), channel_id=1, source_target_pairs={{0,4},{4,8},{8,12},{1,5},{5,9},{9,13},{2,6},{6,10},{10,14},{3,7},{... | collective-permute-start | bytes 1824776 | tf_op jit(solution)/shard_map/ppermute | solution.py:26
  41.3 1.3 %collective-permute-start.8 = (bf16[288,1056]{1,0:T(8,128)(2,1)S(1)}, bf16[288,1056]{1,0:T(8,128)(2,1)}, u32[]{:S(2)}, u32[]{:S(2)}) collective-permute-start(bf16[288,1056]{1,0:T(8,128)(2,1)S(1)} %get-tuple-element.23.own_ref), channel_id=1, source_target_pairs={{4,0},{8,4},{12,8},{5,1},{9,5},{13,9},{6,2},{10,6},{14,10},{7,3},{... | collective-permute-start | bytes 1824776 | tf_op jit(solution)/shard_map/ppermute | solution.py:26
  42.5 0.7 negate_convert_fusion
  43.4 1.3 %collective-permute-start.10 = (bf16[288,1056]{1,0:T(8,128)(2,1)S(1)}, bf16[288,1056]{1,0:T(8,128)(2,1)}, u32[]{:S(2)}, u32[]{:S(2)}) collective-permute-start(bf16[288,1056]{1,0:T(8,128)(2,1)S(1)} %get-tuple-element.22.own_ref), channel_id=1, source_target_pairs={{4,0},{8,4},{12,8},{5,1},{9,5},{13,9},{6,2},{10,6},{14,10},{7,3},{... | collective-permute-start | bytes 1824776 | tf_op jit(solution)/shard_map/ppermute | solution.py:26
  44.7 4.3 %collective-permute-done.5.prev_ref = bf16[288,1056]{1,0:T(8,128)(2,1)} collective-permute-done((bf16[288,1056]{1,0:T(8,128)(2,1)S(1)}, bf16[288,1056]{1,0:T(8,128)(2,1)}, u32[]{:S(2)}, u32[]{:S(2)}) %collective-permute-start.5) | collective-permute-done | bytes 608288 | tf_op jit(solution)/shard_map/ppermute | solution.py:26
  49.0 5.4 %collective-permute-start.9 = (bf16[288,1056]{1,0:T(8,128)(2,1)S(1)}, bf16[288,1056]{1,0:T(8,128)(2,1)}, u32[]{:S(2)}, u32[]{:S(2)}) collective-permute-start(bf16[288,1056]{1,0:T(8,128)(2,1)S(1)} %get-tuple-element.22.own_ref), channel_id=1, source_target_pairs={{0,4},{4,8},{8,12},{1,5},{5,9},{9,13},{2,6},{6,10},{10,14},{3,7},{... | collective-permute-start | bytes 1824776 | tf_op jit(solution)/shard_map/ppermute | solution.py:26
  54.4 3.5 %collective-permute-start.11 = (bf16[288,1056]{1,0:T(8,128)(2,1)S(1)}, bf16[288,1056]{1,0:T(8,128)(2,1)}, u32[]{:S(2)}, u32[]{:S(2)}) collective-permute-start(bf16[288,1056]{1,0:T(8,128)(2,1)S(1)} %get-tuple-element.21.own_ref), channel_id=1, source_target_pairs={{0,4},{4,8},{8,12},{1,5},{5,9},{9,13},{2,6},{6,10},{10,14},{3,7},{... | collective-permute-start | bytes 1824776 | tf_op jit(solution)/shard_map/ppermute | solution.py:26
  57.9 12.1 %shard_map.50 = f32[2,8,128]{2,1,0:T(8,128)S(1)} custom-call(s32[64]{0:T(128)S(1)} %reshape.54.skip_ref, s32[64]{0:T(128)S(1)} %reshape.55.skip_next_ref, s32[1]{0:T(128)} %bitcast.1.flag_ref, bf16[288,1056]{1,0:T(8,128)(2,1)S(1)} %get-tuple-element.20.own_ref, bf16[288,1056]{1,0:T(8,128)(2,1)} %collective-permute-done.5.prev_ref, ...), custom_call_target="tpu_custom_call" | custom-call | tf_op jit(solution)/shard_map/pallas_call | solution.py:159
  70.0 1.5 %collective-permute-start.12 = (bf16[288,1056]{1,0:T(8,128)(2,1)S(1)}, bf16[288,1056]{1,0:T(8,128)(2,1)S(1)}, u32[]{:S(2)}, u32[]{:S(2)}) collective-permute-start(bf16[288,1056]{1,0:T(8,128)(2,1)S(1)} %get-tuple-element.21.own_ref), channel_id=1, source_target_pairs={{4,0},{8,4},{12,8},{5,1},{9,5},{13,9},{6,2},{10,6},{14,10},{7,3},{... | collective-permute-start | bytes 1824776 | tf_op jit(solution)/shard_map/ppermute | solution.py:26
  71.8 12.1 %shard_map.51 = f32[2,8,128]{2,1,0:T(8,128)S(1)} custom-call(s32[64]{0:T(128)S(1)} %reshape.54.skip_ref, s32[64]{0:T(128)S(1)} %reshape.55.skip_next_ref, s32[1]{0:T(128)} %bitcast.1.flag_ref, bf16[288,1056]{1,0:T(8,128)(2,1)S(1)} %get-tuple-element.23.own_ref, bf16[288,1056]{1,0:T(8,128)(2,1)} %collective-permute-done.7.prev_ref, ...), custom_call_target="tpu_custom_call" | custom-call | tf_op jit(solution)/shard_map/pallas_call | solution.py:159
  84.2 12.1 %shard_map.52 = f32[2,8,128]{2,1,0:T(8,128)S(1)} custom-call(s32[64]{0:T(128)S(1)} %reshape.54.skip_ref, s32[64]{0:T(128)S(1)} %reshape.55.skip_next_ref, s32[1]{0:T(128)} %bitcast.1.flag_ref, bf16[288,1056]{1,0:T(8,128)(2,1)S(1)} %get-tuple-element.22.own_ref, bf16[288,1056]{1,0:T(8,128)(2,1)} %collective-permute-done.9.prev_ref, ...), custom_call_target="tpu_custom_call" | custom-call | tf_op jit(solution)/shard_map/pallas_call | solution.py:159
  96.6 12.2 %shard_map.53 = f32[2,8,128]{2,1,0:T(8,128)S(1)} custom-call(s32[64]{0:T(128)S(1)} %reshape.54.skip_ref, s32[64]{0:T(128)S(1)} %reshape.55.skip_next_ref, s32[1]{0:T(128)} %bitcast.1.flag_ref, bf16[288,1056]{1,0:T(8,128)(2,1)S(1)} %get-tuple-element.21.own_ref, bf16[288,1056]{1,0:T(8,128)(2,1)} %collective-permute-done.11.prev_ref, ...), custom_call_target="tpu_custom_call" | custom-call | tf_op jit(solution)/shard_map/pallas_call | solution.py:159
  110.2 0.7 reshape.68
  110.9 4.1 %all-to-all-start = ((f32[4,1,384]{2,1,0:T(1,128)}), f32[4,1,384]{2,1,0:T(1,128)S(1)}, u32[]{:S(2)}, u32[]{:S(2)}) async-start(f32[4,1,384]{2,1,0:T(1,128)} %reshape.68), calls=%async_computation | async-start | bytes 12288 | tf_op jit(solution)/shard_map/all_to_all | solution.py:176
  115.0 5.6 %all-to-all-done = f32[4,1,384]{2,1,0:T(1,128)S(1)} async-done(((f32[4,1,384]{2,1,0:T(1,128)}), f32[4,1,384]{2,1,0:T(1,128)S(1)}, u32[]{:S(2)}, u32[]{:S(2)}) %all-to-all-start) | async-done | bytes 6176 | tf_op jit(solution)/shard_map/all_to_all | solution.py:176
  120.6 0.5 broadcast.105
  121.1 0.7 reduce
  122.0 0.6 dynamic-slice_bitcast_fusion
  123.0 0.6 fusion.71
  (85 shorter events, 3.0 us)
Async XLA Ops:
  1.4 5.0 %collective-permute-start.1 = (bf16[1,16,1024]{2,1,0:T(8,128)(2,1)S(1)}, bf16[1,16,1024]{2,1,0:T(8,128)(2,1)S(1)}, u32[]{:S(2)}, u32[]{:S(2)}) collective-permute-start(bf16[1,16,1024]{2,1,0:T(8,128)(2,1)S(1)} %get-tuple-element.27), channel_id=1, source_target_pairs={{0,1},{2,3},{4,5},{6,7},{8,9},{10,11},{12,13},{14,15},{16,17},{18,... | collective-permute-start | bytes 98312 | tf_op jit(solution)/shard_map/ppermute | solution.py:34
  3.8 4.4 %collective-permute-start.2 = (bf16[1,16,1024]{2,1,0:T(8,128)(2,1)S(1)}, bf16[1,16,1024]{2,1,0:T(8,128)(2,1)S(1)}, u32[]{:S(2)}, u32[]{:S(2)}) collective-permute-start(bf16[1,16,1024]{2,1,0:T(8,128)(2,1)S(1)} %get-tuple-element.26), channel_id=1, source_target_pairs={{1,0},{3,2},{5,4},{7,6},{9,8},{11,10},{13,12},{15,14},{17,16},{19,... | collective-permute-start | bytes 98312 | tf_op jit(solution)/shard_map/ppermute | solution.py:37
  5.1 38.3 %collective-permute-start = (s32[1,8,8]{2,1,0:T(8,128)}, s32[1,8,8]{2,1,0:T(8,128)S(1)}, u32[]{:S(2)}, u32[]{:S(2)}) collective-permute-start(s32[1,8,8]{2,1,0:T(8,128)} %param.4), channel_id=1, source_target_pairs={{4,0},{8,4},{12,8},{5,1},{9,5},{13,9},{6,2},{10,6},{14,10},{7,3},{... | collective-permute-start | bytes 776 | tf_op jit(solution)/shard_map/ppermute | solution.py:26
  6.4 7.5 %copy-start = (s32[1,8,8]{2,1,0:T(8,128)S(1)}, s32[1,8,8]{2,1,0:T(8,128)}, u32[]{:S(2)}) copy-start(s32[1,8,8]{2,1,0:T(8,128)} %param.4) | copy-start | bytes 772
  8.4 10.9 %collective-permute-start.3 = (bf16[1,1056,16]{2,1,0:T(8,128)(2,1)S(1)}, bf16[1,1056,16]{2,1,0:T(8,128)(2,1)S(1)}, u32[]{:S(2)}, u32[]{:S(2)}) collective-permute-start(bf16[1,1056,16]{2,1,0:T(8,128)(2,1)S(1)} %get-tuple-element.25), channel_id=1, source_target_pairs={{0,2},{1,3},{4,6},{5,7},{8,10},{9,11},{12,14},{13,15},{16,18},{17,... | collective-permute-start | bytes 101384 | tf_op jit(solution)/shard_map/ppermute | solution.py:34
  12.6 11.1 %collective-permute-start.4 = (bf16[1,1056,16]{2,1,0:T(8,128)(2,1)S(1)}, bf16[1,1056,16]{2,1,0:T(8,128)(2,1)S(1)}, u32[]{:S(2)}, u32[]{:S(2)}) collective-permute-start(bf16[1,1056,16]{2,1,0:T(8,128)(2,1)S(1)} %get-tuple-element.24), channel_id=1, source_target_pairs={{2,0},{3,1},{6,4},{7,5},{10,8},{11,9},{14,12},{15,13},{18,16},{19,... | collective-permute-start | bytes 101384 | tf_op jit(solution)/shard_map/ppermute | solution.py:37
  27.5 7.0 %copy-start.1 = (s32[1,8,8]{2,1,0:T(8,128)S(1)}, s32[1,8,8]{2,1,0:T(8,128)}, u32[]{:S(2)}) copy-start(s32[1,8,8]{2,1,0:T(8,128)} %param.5) | copy-start | bytes 772
  29.4 19.6 %collective-permute-start.5 = (bf16[288,1056]{1,0:T(8,128)(2,1)S(1)}, bf16[288,1056]{1,0:T(8,128)(2,1)}, u32[]{:S(2)}, u32[]{:S(2)}) collective-permute-start(bf16[288,1056]{1,0:T(8,128)(2,1)S(1)} %get-tuple-element.20.own_ref), channel_id=1, source_target_pairs={{0,4},{4,8},{8,12},{1,5},{5,9},{9,13},{2,6},{6,10},{10,14},{3,7},{... | collective-permute-start | bytes 1824776 | tf_op jit(solution)/shard_map/ppermute | solution.py:26
  34.6 19.8 %collective-permute-start.6 = (bf16[288,1056]{1,0:T(8,128)(2,1)S(1)}, bf16[288,1056]{1,0:T(8,128)(2,1)}, u32[]{:S(2)}, u32[]{:S(2)}) collective-permute-start(bf16[288,1056]{1,0:T(8,128)(2,1)S(1)} %get-tuple-element.20.own_ref), channel_id=1, source_target_pairs={{4,0},{8,4},{12,8},{5,1},{9,5},{13,9},{6,2},{10,6},{14,10},{7,3},{... | collective-permute-start | bytes 1824776 | tf_op jit(solution)/shard_map/ppermute | solution.py:26
  35.8 34.2 %collective-permute-start.7 = (bf16[288,1056]{1,0:T(8,128)(2,1)S(1)}, bf16[288,1056]{1,0:T(8,128)(2,1)}, u32[]{:S(2)}, u32[]{:S(2)}) collective-permute-start(bf16[288,1056]{1,0:T(8,128)(2,1)S(1)} %get-tuple-element.23.own_ref), channel_id=1, source_target_pairs={{0,4},{4,8},{8,12},{1,5},{5,9},{9,13},{2,6},{6,10},{10,14},{3,7},{... | collective-permute-start | bytes 1824776 | tf_op jit(solution)/shard_map/ppermute | solution.py:26
  41.3 30.5 %collective-permute-start.8 = (bf16[288,1056]{1,0:T(8,128)(2,1)S(1)}, bf16[288,1056]{1,0:T(8,128)(2,1)}, u32[]{:S(2)}, u32[]{:S(2)}) collective-permute-start(bf16[288,1056]{1,0:T(8,128)(2,1)S(1)} %get-tuple-element.23.own_ref), channel_id=1, source_target_pairs={{4,0},{8,4},{12,8},{5,1},{9,5},{13,9},{6,2},{10,6},{14,10},{7,3},{... | collective-permute-start | bytes 1824776 | tf_op jit(solution)/shard_map/ppermute | solution.py:26
  43.4 40.7 %collective-permute-start.10 = (bf16[288,1056]{1,0:T(8,128)(2,1)S(1)}, bf16[288,1056]{1,0:T(8,128)(2,1)}, u32[]{:S(2)}, u32[]{:S(2)}) collective-permute-start(bf16[288,1056]{1,0:T(8,128)(2,1)S(1)} %get-tuple-element.22.own_ref), channel_id=1, source_target_pairs={{4,0},{8,4},{12,8},{5,1},{9,5},{13,9},{6,2},{10,6},{14,10},{7,3},{... | collective-permute-start | bytes 1824776 | tf_op jit(solution)/shard_map/ppermute | solution.py:26
  49.0 35.2 %collective-permute-start.9 = (bf16[288,1056]{1,0:T(8,128)(2,1)S(1)}, bf16[288,1056]{1,0:T(8,128)(2,1)}, u32[]{:S(2)}, u32[]{:S(2)}) collective-permute-start(bf16[288,1056]{1,0:T(8,128)(2,1)S(1)} %get-tuple-element.22.own_ref), channel_id=1, source_target_pairs={{0,4},{4,8},{8,12},{1,5},{5,9},{9,13},{2,6},{6,10},{10,14},{3,7},{... | collective-permute-start | bytes 1824776 | tf_op jit(solution)/shard_map/ppermute | solution.py:26
  54.4 42.2 %collective-permute-start.11 = (bf16[288,1056]{1,0:T(8,128)(2,1)S(1)}, bf16[288,1056]{1,0:T(8,128)(2,1)}, u32[]{:S(2)}, u32[]{:S(2)}) collective-permute-start(bf16[288,1056]{1,0:T(8,128)(2,1)S(1)} %get-tuple-element.21.own_ref), channel_id=1, source_target_pairs={{0,4},{4,8},{8,12},{1,5},{5,9},{9,13},{2,6},{6,10},{10,14},{3,7},{... | collective-permute-start | bytes 1824776 | tf_op jit(solution)/shard_map/ppermute | solution.py:26
  70.0 26.6 %collective-permute-start.12 = (bf16[288,1056]{1,0:T(8,128)(2,1)S(1)}, bf16[288,1056]{1,0:T(8,128)(2,1)S(1)}, u32[]{:S(2)}, u32[]{:S(2)}) collective-permute-start(bf16[288,1056]{1,0:T(8,128)(2,1)S(1)} %get-tuple-element.21.own_ref), channel_id=1, source_target_pairs={{4,0},{8,4},{12,8},{5,1},{9,5},{13,9},{6,2},{10,6},{14,10},{7,3},{... | collective-permute-start | bytes 1824776 | tf_op jit(solution)/shard_map/ppermute | solution.py:26
  110.9 9.7 %all-to-all-start = ((f32[4,1,384]{2,1,0:T(1,128)}), f32[4,1,384]{2,1,0:T(1,128)S(1)}, u32[]{:S(2)}, u32[]{:S(2)}) async-start(f32[4,1,384]{2,1,0:T(1,128)} %reshape.68), calls=%async_computation | async-start | bytes 12288 | tf_op jit(solution)/shard_map/all_to_all | solution.py:176

commit v3 on v2

--- a/solution.py
+++ b/solution.py
@@ -26,15 +26,30 @@
     return lax.ppermute(value, axis, [(source, source + steps) for source in range(first, last)])
 
 
+def _strip_send(strip, dim):
+    return jnp.swapaxes(strip, 1, 2) if dim == 2 else strip
+
+
+def _strip_recv(strip, dim):
+    return jnp.swapaxes(strip, 1, 2) if dim == 2 else strip
+
+
 def extended(block, sides, width):
     for axis, dim in sides:
         count = lax.axis_size(axis)
-        forward = [(i, i + 1) for i in range(count - 1)]
-        backward = [(target, source) for source, target in forward]
-        low = lax.ppermute(
-            lax.slice_in_dim(block, block.shape[dim] - width, None, axis=dim), axis, forward
-        )
-        high = lax.ppermute(lax.slice_in_dim(block, 0, width, axis=dim), axis, backward)
+        top = lax.slice_in_dim(block, 0, width, axis=dim)
+        bottom = lax.slice_in_dim(block, block.shape[dim] - width, None, axis=dim)
+        if count == 2:
+            index = lax.axis_index(axis)
+            send = _strip_send(jnp.where(index == 0, bottom, top), dim)
+            got = _strip_recv(lax.ppermute(send, axis, [(0, 1), (1, 0)]), dim)
+            low = jnp.where(index == 1, got, jnp.zeros_like(got))
+            high = jnp.where(index == 0, got, jnp.zeros_like(got))
+        else:
+            forward = [(i, i + 1) for i in range(count - 1)]
+            backward = [(target, source) for source, target in forward]
+            low = _strip_recv(lax.ppermute(_strip_send(bottom, dim), axis, forward), dim)
+            high = _strip_recv(lax.ppermute(_strip_send(top, dim), axis, backward), dim)
         block = jnp.concatenate([low, block, high], axis=dim)
     return block
 

time: 124 us -> 116 us (0.935)
  starting transfers between devices: 39.3 us -> 34.2 us
  waiting for transfers between devices: 19.7 us -> 16.9 us
  other arithmetic: 2.34 us -> 5.1 us
  local copies, waits for them, and re-layouts: 12.6 us -> 9.93 us
    ppermute x4 -> x2, starting transfers between devices: 9.17 us -> 3.02 us  [extended(): got = _strip_recv(lax.ppermute(send, axis, [(0, 1), (1, 0)]), dim)]
    ppermute x4 -> x2, waiting for transfers between devices: 9.8 us -> 7.13 us  [extended(): got = _strip_recv(lax.ppermute(send, axis, [(0, 1), (1, 0)]), dim)]
    concatenate x0 -> x1, other arithmetic: none -> 1.78 us  [extended(): block = jnp.concatenate([low, block, high], axis=dim)]
    unnamed x9 -> x7, local copies, waits for them, and re-layouts: 3.2 us -> 1.42 us
    concatenate x2 -> x1, local copies, waits for them, and re-layouts: 3.78 us -> 3.8 us  [extended(): block = jnp.concatenate([low, block, high], axis=dim)]
  transfers between devices with their start and end apart: 14 -> 12, of which waited for: 4 -> 4; matrix products, arithmetic and copies ran while one was open for 8% -> 8% of each run, Pallas kernels for 29% -> 31%
where the time goes in v3:
time: 116 us
  Pallas kernels  48.6 us (42%)
  starting transfers between devices  34.2 us (29%)
  waiting for transfers between devices  16.9 us (15%)
  local copies, waits for them, and re-layouts  9.93 us (9%)
  other arithmetic  5.1 us (4%)
    pallas_call x4, Pallas kernels, pair_flows(): pl.pallas_call(functools.partial(_flow_kernel, cols=cols, row0=row0), gri...  48.6 us
    ppermute x9, starting transfers between devices, shifted(): lax.ppermute(value, axis, [(source, source + steps) for source in range(f...  27.2 us
    ppermute x2, waiting for transfers between devices, extended(): got = _strip_recv(lax.ppermute(send, axis, [(0, 1), (1, 0)]), dim)  7.13 us
    all_to_all x1, waiting for transfers between devices, gather_sections(): return lax.all_to_all(spread, axis, 0, 0, tiled=True)  5.58 us
    ppermute x9, waiting for transfers between devices, shifted(): lax.ppermute(value, axis, [(source, source + steps) for source in range(f...  4.21 us
    all_to_all x1, starting transfers between devices, gather_sections(): return lax.all_to_all(spread, axis, 0, 0, tiled=True)  3.99 us
    concatenate x1, local copies, waits for them, and re-layouts, extended(): block = jnp.concatenate([low, block, high], axis=dim)  3.8 us
    ppermute x2, starting transfers between devices, extended(): got = _strip_recv(lax.ppermute(send, axis, [(0, 1), (1, 0)]), dim)  3.02 us
  transfers between devices with their start and end apart: 12, of which 4 were waited for; matrix products, arithmetic and copies ran while one was open for 8% of the time, Pallas kernels for 31%

profile of v3, /device:TPU:0, one launch (start us, length us, event | category | flops | bytes accessed | tf_op | source)
XLA Modules:
  0.0 115.8 jit_solution(7479898358189358383)
XLA Ops:
  0.6 0.8 slice_select_fusion.1
  1.4 0.5 collective-permute-start.1
  1.9 1.3 %collective-permute-start = (s32[1,8,8]{2,1,0:T(8,128)}, s32[1,8,8]{2,1,0:T(8,128)S(1)}, u32[]{:S(2)}, u32[]{:S(2)}) collective-permute-start(s32[1,8,8]{2,1,0:T(8,128)} %param.4), channel_id=1, source_target_pairs={{4,0},{8,4},{12,8},{5,1},{9,5},{13,9},{6,2},{10,6},{14,10},{7,3},{... | collective-permute-start | bytes 776 | tf_op jit(solution)/shard_map/ppermute | solution.py:26
  3.2 1.8 %pad_maximum_fusion = bf16[1,1056,1024]{2,1,0:T(8,128)(2,1)S(1)} fusion(bf16[1,16,1024]{2,1,0:T(8,128)(2,1)S(1)} %get-tuple-element.27, bf16[1,1024,1024]{2,1,0:T(8,128)(2,1)} %param.3, bf16[1,16,1024]{2,1,0:T(8,128)(2,1)S(1)} %get-tuple-element.26), kind=kLoop, calls=%fused_computation | loop fusion | flops 6488064 | bytes 4325376 | tf_op jit(solution)/shard_map/concatenate | solution.py:53
  5.0 0.1 fusion
  5.1 2.6 %collective-permute-start.2 = (bf16[1,16,1056]{1,2,0:T(8,128)(2,1)S(1)}, bf16[1,16,1056]{1,2,0:T(8,128)(2,1)S(1)}, u32[]{:S(2)}, u32[]{:S(2)}) collective-permute-start(bf16[1,16,1056]{1,2,0:T(8,128)(2,1)S(1)} %fusion), channel_id=1, source_target_pairs={{0,2},{2,0},{1,3},{3,1},{4,6},{6,4},{5,7},{7,5},{8,10},{10,8},{9,1... | collective-permute-start | bytes 101384 | tf_op jit(solution)/shard_map/ppermute | solution.py:45
  7.7 7.1 %collective-permute-done.2 = bf16[1,16,1056]{1,2,0:T(8,128)(2,1)S(1)} collective-permute-done((bf16[1,16,1056]{1,2,0:T(8,128)(2,1)S(1)}, bf16[1,16,1056]{1,2,0:T(8,128)(2,1)S(1)}, u32[]{:S(2)}, u32[]{:S(2)}) %collective-permute-start.2) | collective-permute-done | bytes 33824 | tf_op jit(solution)/shard_map/ppermute | solution.py:45
  14.9 3.8 %concatenate.19 = bf16[1,1056,1056]{2,1,0:T(8,128)(2,1)} concatenate(bf16[1,1056,16]{2,1,0:T(8,128)(2,1)S(1)} %get-tuple-element.25, bf16[1,1056,1024]{2,1,0:T(8,128)(2,1)S(1)} %pad_maximum_fusion, bf16[1,1056,16]{2,1,0:T(8,128)(2,1)S(1)} %get-tuple-element.24), dimensions={2} | concatenate | bytes 4460544 | tf_op jit(solution)/shard_map/concatenate | solution.py:53
  18.7 1.9 %slice_bitcast_fusion.3 = (bf16[288,1056]{1,0:T(8,128)(2,1)S(1)}, bf16[288,1056]{1,0:T(8,128)(2,1)S(1)}, bf16[288,1056]{1,0:T(8,128)(2,1)S(1)}, bf16[288,1056]{1,0:T(8,128)(2,1)S(1)}) fusion(bf16[1,1056,1056]{2,1,0:T(8,128)(2,1)} %concatenate.19), kind=kLoop, calls=%fused_computation.4 | loop fusion | bytes 4866048 | tf_op jit(solution)/shard_map/slice | solution.py:239
  20.6 5.2 %collective-permute-start.3 = (bf16[288,1056]{1,0:T(8,128)(2,1)S(1)}, bf16[288,1056]{1,0:T(8,128)(2,1)}, u32[]{:S(2)}, u32[]{:S(2)}) collective-permute-start(bf16[288,1056]{1,0:T(8,128)(2,1)S(1)} %get-tuple-element.20.own_ref), channel_id=1, source_target_pairs={{0,4},{4,8},{8,12},{1,5},{5,9},{9,13},{2,6},{6,10},{10,14},{3,7},{... | collective-permute-start | bytes 1824776 | tf_op jit(solution)/shard_map/ppermute | solution.py:26
  25.8 1.3 %collective-permute-start.4 = (bf16[288,1056]{1,0:T(8,128)(2,1)S(1)}, bf16[288,1056]{1,0:T(8,128)(2,1)}, u32[]{:S(2)}, u32[]{:S(2)}) collective-permute-start(bf16[288,1056]{1,0:T(8,128)(2,1)S(1)} %get-tuple-element.20.own_ref), channel_id=1, source_target_pairs={{4,0},{8,4},{12,8},{5,1},{9,5},{13,9},{6,2},{10,6},{14,10},{7,3},{... | collective-permute-start | bytes 1824776 | tf_op jit(solution)/shard_map/ppermute | solution.py:26
  27.1 5.4 %collective-permute-start.5 = (bf16[288,1056]{1,0:T(8,128)(2,1)S(1)}, bf16[288,1056]{1,0:T(8,128)(2,1)}, u32[]{:S(2)}, u32[]{:S(2)}) collective-permute-start(bf16[288,1056]{1,0:T(8,128)(2,1)S(1)} %get-tuple-element.23.own_ref), channel_id=1, source_target_pairs={{0,4},{4,8},{8,12},{1,5},{5,9},{9,13},{2,6},{6,10},{10,14},{3,7},{... | collective-permute-start | bytes 1824776 | tf_op jit(solution)/shard_map/ppermute | solution.py:26
  32.5 1.3 %collective-permute-start.6 = (bf16[288,1056]{1,0:T(8,128)(2,1)S(1)}, bf16[288,1056]{1,0:T(8,128)(2,1)}, u32[]{:S(2)}, u32[]{:S(2)}) collective-permute-start(bf16[288,1056]{1,0:T(8,128)(2,1)S(1)} %get-tuple-element.23.own_ref), channel_id=1, source_target_pairs={{4,0},{8,4},{12,8},{5,1},{9,5},{13,9},{6,2},{10,6},{14,10},{7,3},{... | collective-permute-start | bytes 1824776 | tf_op jit(solution)/shard_map/ppermute | solution.py:26
  33.8 0.7 negate_convert_fusion
  34.7 5.4 %collective-permute-start.7 = (bf16[288,1056]{1,0:T(8,128)(2,1)S(1)}, bf16[288,1056]{1,0:T(8,128)(2,1)}, u32[]{:S(2)}, u32[]{:S(2)}) collective-permute-start(bf16[288,1056]{1,0:T(8,128)(2,1)S(1)} %get-tuple-element.22.own_ref), channel_id=1, source_target_pairs={{0,4},{4,8},{8,12},{1,5},{5,9},{9,13},{2,6},{6,10},{10,14},{3,7},{... | collective-permute-start | bytes 1824776 | tf_op jit(solution)/shard_map/ppermute | solution.py:26
  40.2 0.1 collective-permute-done.3.prev_ref
  40.3 1.3 %collective-permute-start.8 = (bf16[288,1056]{1,0:T(8,128)(2,1)S(1)}, bf16[288,1056]{1,0:T(8,128)(2,1)}, u32[]{:S(2)}, u32[]{:S(2)}) collective-permute-start(bf16[288,1056]{1,0:T(8,128)(2,1)S(1)} %get-tuple-element.22.own_ref), channel_id=1, source_target_pairs={{4,0},{8,4},{12,8},{5,1},{9,5},{13,9},{6,2},{10,6},{14,10},{7,3},{... | collective-permute-start | bytes 1824776 | tf_op jit(solution)/shard_map/ppermute | solution.py:26
  41.6 4.1 %collective-permute-done.4.next_ref = bf16[288,1056]{1,0:T(8,128)(2,1)} collective-permute-done((bf16[288,1056]{1,0:T(8,128)(2,1)S(1)}, bf16[288,1056]{1,0:T(8,128)(2,1)}, u32[]{:S(2)}, u32[]{:S(2)}) %collective-permute-start.4) | collective-permute-done | bytes 608288 | tf_op jit(solution)/shard_map/ppermute | solution.py:26
  45.7 1.3 %collective-permute-start.10 = (bf16[288,1056]{1,0:T(8,128)(2,1)S(1)}, bf16[288,1056]{1,0:T(8,128)(2,1)}, u32[]{:S(2)}, u32[]{:S(2)}) collective-permute-start(bf16[288,1056]{1,0:T(8,128)(2,1)S(1)} %get-tuple-element.21.own_ref), channel_id=1, source_target_pairs={{4,0},{8,4},{12,8},{5,1},{9,5},{13,9},{6,2},{10,6},{14,10},{7,3},{... | collective-permute-start | bytes 1824776 | tf_op jit(solution)/shard_map/ppermute | solution.py:26
  47.0 12.1 %shard_map.50 = f32[2,8,128]{2,1,0:T(8,128)S(1)} custom-call(s32[64]{0:T(128)S(1)} %reshape.54.skip_ref, s32[64]{0:T(128)S(1)} %reshape.55.skip_next_ref, s32[1]{0:T(128)} %bitcast.1.flag_ref, bf16[288,1056]{1,0:T(8,128)(2,1)S(1)} %get-tuple-element.20.own_ref, bf16[288,1056]{1,0:T(8,128)(2,1)} %collective-permute-done.3.prev_ref, ...), custom_call_target="tpu_custom_call" | custom-call | tf_op jit(solution)/shard_map/pallas_call | solution.py:174
  59.1 4.8 %collective-permute-start.9 = (bf16[288,1056]{1,0:T(8,128)(2,1)S(1)}, bf16[288,1056]{1,0:T(8,128)(2,1)S(1)}, u32[]{:S(2)}, u32[]{:S(2)}) collective-permute-start(bf16[288,1056]{1,0:T(8,128)(2,1)S(1)} %get-tuple-element.21.own_ref), channel_id=1, source_target_pairs={{0,4},{4,8},{8,12},{1,5},{5,9},{9,13},{2,6},{6,10},{10,14},{3,7},{... | collective-permute-start | bytes 1824776 | tf_op jit(solution)/shard_map/ppermute | solution.py:26
  64.1 12.1 %shard_map.51 = f32[2,8,128]{2,1,0:T(8,128)S(1)} custom-call(s32[64]{0:T(128)S(1)} %reshape.54.skip_ref, s32[64]{0:T(128)S(1)} %reshape.55.skip_next_ref, s32[1]{0:T(128)} %bitcast.1.flag_ref, bf16[288,1056]{1,0:T(8,128)(2,1)S(1)} %get-tuple-element.23.own_ref, bf16[288,1056]{1,0:T(8,128)(2,1)} %collective-permute-done.5.prev_ref, ...), custom_call_target="tpu_custom_call" | custom-call | tf_op jit(solution)/shard_map/pallas_call | solution.py:174
  76.5 12.1 %shard_map.52 = f32[2,8,128]{2,1,0:T(8,128)S(1)} custom-call(s32[64]{0:T(128)S(1)} %reshape.54.skip_ref, s32[64]{0:T(128)S(1)} %reshape.55.skip_next_ref, s32[1]{0:T(128)} %bitcast.1.flag_ref, bf16[288,1056]{1,0:T(8,128)(2,1)S(1)} %get-tuple-element.22.own_ref, bf16[288,1056]{1,0:T(8,128)(2,1)} %collective-permute-done.7.prev_ref, ...), custom_call_target="tpu_custom_call" | custom-call | tf_op jit(solution)/shard_map/pallas_call | solution.py:174
  89.0 12.2 %shard_map.53 = f32[2,8,128]{2,1,0:T(8,128)S(1)} custom-call(s32[64]{0:T(128)S(1)} %reshape.54.skip_ref, s32[64]{0:T(128)S(1)} %reshape.55.skip_next_ref, s32[1]{0:T(128)} %bitcast.1.flag_ref, bf16[288,1056]{1,0:T(8,128)(2,1)S(1)} %get-tuple-element.21.own_ref, bf16[288,1056]{1,0:T(8,128)(2,1)S(1)} %collective-permute-done.9.prev_ref, ...), custom_call_target="tpu_custom_call" | custom-call | tf_op jit(solution)/shard_map/pallas_call | solution.py:174
  102.6 0.7 reshape.68
  103.3 4.0 %all-to-all-start = ((f32[4,1,384]{2,1,0:T(1,128)}), f32[4,1,384]{2,1,0:T(1,128)S(1)}, u32[]{:S(2)}, u32[]{:S(2)}) async-start(f32[4,1,384]{2,1,0:T(1,128)} %reshape.68), calls=%async_computation | async-start | bytes 12288 | tf_op jit(solution)/shard_map/all_to_all | solution.py:191
  107.2 5.6 %all-to-all-done = f32[4,1,384]{2,1,0:T(1,128)S(1)} async-done(((f32[4,1,384]{2,1,0:T(1,128)}), f32[4,1,384]{2,1,0:T(1,128)S(1)}, u32[]{:S(2)}, u32[]{:S(2)}) %all-to-all-start) | async-done | bytes 6176 | tf_op jit(solution)/shard_map/all_to_all | solution.py:191
  112.8 0.5 broadcast.124
  113.3 0.7 reduce
  114.0 0.1 reshape.69
  114.3 0.6 dynamic-slice_bitcast_fusion
  115.2 0.6 fusion.72
  (81 shorter events, 2.7 us)
Async XLA Ops:
  1.4 1.8 %collective-permute-start.1 = (bf16[1,16,1024]{2,1,0:T(8,128)(2,1)S(1)}, bf16[1,16,1024]{2,1,0:T(8,128)(2,1)S(1)}, u32[]{:S(2)}, u32[]{:S(2)}) collective-permute-start(bf16[1,16,1024]{2,1,0:T(8,128)(2,1)S(1)} %slice_select_fusion.1), channel_id=1, source_target_pairs={{0,1},{1,0},{2,3},{3,2},{4,5},{5,4},{6,7},{7,6},{8,9},{9,8},{10,11... | collective-permute-start | bytes 98312 | tf_op jit(solution)/shard_map/ppermute | solution.py:45
  1.9 32.8 %collective-permute-start = (s32[1,8,8]{2,1,0:T(8,128)}, s32[1,8,8]{2,1,0:T(8,128)S(1)}, u32[]{:S(2)}, u32[]{:S(2)}) collective-permute-start(s32[1,8,8]{2,1,0:T(8,128)} %param.4), channel_id=1, source_target_pairs={{4,0},{8,4},{12,8},{5,1},{9,5},{13,9},{6,2},{10,6},{14,10},{7,3},{... | collective-permute-start | bytes 776 | tf_op jit(solution)/shard_map/ppermute | solution.py:26
  3.2 4.5 %copy-start = (s32[1,8,8]{2,1,0:T(8,128)S(1)}, s32[1,8,8]{2,1,0:T(8,128)}, u32[]{:S(2)}) copy-start(s32[1,8,8]{2,1,0:T(8,128)} %param.4) | copy-start | bytes 772
  5.1 9.7 %collective-permute-start.2 = (bf16[1,16,1056]{1,2,0:T(8,128)(2,1)S(1)}, bf16[1,16,1056]{1,2,0:T(8,128)(2,1)S(1)}, u32[]{:S(2)}, u32[]{:S(2)}) collective-permute-start(bf16[1,16,1056]{1,2,0:T(8,128)(2,1)S(1)} %fusion), channel_id=1, source_target_pairs={{0,2},{2,0},{1,3},{3,1},{4,6},{6,4},{5,7},{7,5},{8,10},{10,8},{9,1... | collective-permute-start | bytes 101384 | tf_op jit(solution)/shard_map/ppermute | solution.py:45
  18.7 7.1 %copy-start.1 = (s32[1,8,8]{2,1,0:T(8,128)S(1)}, s32[1,8,8]{2,1,0:T(8,128)}, u32[]{:S(2)}) copy-start(s32[1,8,8]{2,1,0:T(8,128)} %param.5) | copy-start | bytes 772
  20.6 19.7 %collective-permute-start.3 = (bf16[288,1056]{1,0:T(8,128)(2,1)S(1)}, bf16[288,1056]{1,0:T(8,128)(2,1)}, u32[]{:S(2)}, u32[]{:S(2)}) collective-permute-start(bf16[288,1056]{1,0:T(8,128)(2,1)S(1)} %get-tuple-element.20.own_ref), channel_id=1, source_target_pairs={{0,4},{4,8},{8,12},{1,5},{5,9},{9,13},{2,6},{6,10},{10,14},{3,7},{... | collective-permute-start | bytes 1824776 | tf_op jit(solution)/shard_map/ppermute | solution.py:26
  25.8 19.8 %collective-permute-start.4 = (bf16[288,1056]{1,0:T(8,128)(2,1)S(1)}, bf16[288,1056]{1,0:T(8,128)(2,1)}, u32[]{:S(2)}, u32[]{:S(2)}) collective-permute-start(bf16[288,1056]{1,0:T(8,128)(2,1)S(1)} %get-tuple-element.20.own_ref), channel_id=1, source_target_pairs={{4,0},{8,4},{12,8},{5,1},{9,5},{13,9},{6,2},{10,6},{14,10},{7,3},{... | collective-permute-start | bytes 1824776 | tf_op jit(solution)/shard_map/ppermute | solution.py:26
  27.1 32.0 %collective-permute-start.5 = (bf16[288,1056]{1,0:T(8,128)(2,1)S(1)}, bf16[288,1056]{1,0:T(8,128)(2,1)}, u32[]{:S(2)}, u32[]{:S(2)}) collective-permute-start(bf16[288,1056]{1,0:T(8,128)(2,1)S(1)} %get-tuple-element.23.own_ref), channel_id=1, source_target_pairs={{0,4},{4,8},{8,12},{1,5},{5,9},{9,13},{2,6},{6,10},{10,14},{3,7},{... | collective-permute-start | bytes 1824776 | tf_op jit(solution)/shard_map/ppermute | solution.py:26
  32.5 31.6 %collective-permute-start.6 = (bf16[288,1056]{1,0:T(8,128)(2,1)S(1)}, bf16[288,1056]{1,0:T(8,128)(2,1)}, u32[]{:S(2)}, u32[]{:S(2)}) collective-permute-start(bf16[288,1056]{1,0:T(8,128)(2,1)S(1)} %get-tuple-element.23.own_ref), channel_id=1, source_target_pairs={{4,0},{8,4},{12,8},{5,1},{9,5},{13,9},{6,2},{10,6},{14,10},{7,3},{... | collective-permute-start | bytes 1824776 | tf_op jit(solution)/shard_map/ppermute | solution.py:26
  34.7 41.8 %collective-permute-start.7 = (bf16[288,1056]{1,0:T(8,128)(2,1)S(1)}, bf16[288,1056]{1,0:T(8,128)(2,1)}, u32[]{:S(2)}, u32[]{:S(2)}) collective-permute-start(bf16[288,1056]{1,0:T(8,128)(2,1)S(1)} %get-tuple-element.22.own_ref), channel_id=1, source_target_pairs={{0,4},{4,8},{8,12},{1,5},{5,9},{9,13},{2,6},{6,10},{10,14},{3,7},{... | collective-permute-start | bytes 1824776 | tf_op jit(solution)/shard_map/ppermute | solution.py:26
  40.3 36.2 %collective-permute-start.8 = (bf16[288,1056]{1,0:T(8,128)(2,1)S(1)}, bf16[288,1056]{1,0:T(8,128)(2,1)}, u32[]{:S(2)}, u32[]{:S(2)}) collective-permute-start(bf16[288,1056]{1,0:T(8,128)(2,1)S(1)} %get-tuple-element.22.own_ref), channel_id=1, source_target_pairs={{4,0},{8,4},{12,8},{5,1},{9,5},{13,9},{6,2},{10,6},{14,10},{7,3},{... | collective-permute-start | bytes 1824776 | tf_op jit(solution)/shard_map/ppermute | solution.py:26
  45.7 43.3 %collective-permute-start.10 = (bf16[288,1056]{1,0:T(8,128)(2,1)S(1)}, bf16[288,1056]{1,0:T(8,128)(2,1)}, u32[]{:S(2)}, u32[]{:S(2)}) collective-permute-start(bf16[288,1056]{1,0:T(8,128)(2,1)S(1)} %get-tuple-element.21.own_ref), channel_id=1, source_target_pairs={{4,0},{8,4},{12,8},{5,1},{9,5},{13,9},{6,2},{10,6},{14,10},{7,3},{... | collective-permute-start | bytes 1824776 | tf_op jit(solution)/shard_map/ppermute | solution.py:26
  59.1 29.9 %collective-permute-start.9 = (bf16[288,1056]{1,0:T(8,128)(2,1)S(1)}, bf16[288,1056]{1,0:T(8,128)(2,1)S(1)}, u32[]{:S(2)}, u32[]{:S(2)}) collective-permute-start(bf16[288,1056]{1,0:T(8,128)(2,1)S(1)} %get-tuple-element.21.own_ref), channel_id=1, source_target_pairs={{0,4},{4,8},{8,12},{1,5},{5,9},{9,13},{2,6},{6,10},{10,14},{3,7},{... | collective-permute-start | bytes 1824776 | tf_op jit(solution)/shard_map/ppermute | solution.py:26
  103.3 9.6 %all-to-all-start = ((f32[4,1,384]{2,1,0:T(1,128)}), f32[4,1,384]{2,1,0:T(1,128)S(1)}, u32[]{:S(2)}, u32[]{:S(2)}) async-start(f32[4,1,384]{2,1,0:T(1,128)} %reshape.68), calls=%async_computation | async-start | bytes 12288 | tf_op jit(solution)/shard_map/all_to_all | solution.py:191

commit v4 on v3

--- a/solution.py
+++ b/solution.py
@@ -227,7 +227,7 @@
     skip_next = shifted(skipped, "sec", -1)
     use_own = (index == 0).astype(jnp.int32)
     rows_count = (own_pad.shape[0] - (PATCH - STRIDE)) // STRIDE
-    chunks = max(n for n in (1, 2, 4) if rows_count % n == 0)
+    chunks = 2 if rows_count % 2 == 0 else 1
     per = rows_count // chunks
     cos_t, sin_t = dft_tables(PATCH)
     tables = (jnp.concatenate([cos_t, sin_t], axis=0), cos_t, sin_t)

time: 116 us -> 118 us (1.017)
  waiting for transfers between devices: 16.9 us -> 36.5 us
  starting transfers between devices: 34.2 us -> 21.5 us
  Pallas kernels: 48.6 us -> 45.2 us
  local copies, waits for them, and re-layouts: 9.93 us -> 8.65 us
    ppermute x9 -> x5, waiting for transfers between devices: 4.21 us -> 23.2 us  [shifted(): lax.ppermute(value, axis, [(source, source + steps) for source in range(f...]
    ppermute x9 -> x5, starting transfers between devices: 27.2 us -> 14.9 us  [shifted(): lax.ppermute(value, axis, [(source, source + steps) for source in range(f...]
    pallas_call x4 -> x2, Pallas kernels: 48.6 us -> 45.2 us  [pair_flows(): pl.pallas_call(functools.partial(_flow_kernel, cols=cols, row0=row0), gri...]
  transfers between devices with their start and end apart: 12 -> 8, of which waited for: 4 -> 5; matrix products, arithmetic and copies ran while one was open for 8% -> 1% of each run, Pallas kernels for 31% -> 19%
where the time goes in v4:
time: 118 us
  Pallas kernels  45.2 us (38%)
  waiting for transfers between devices  36.5 us (31%)
  starting transfers between devices  21.5 us (18%)
  local copies, waits for them, and re-layouts  8.65 us (7%)
  other arithmetic  5.21 us (4%)
    pallas_call x2, Pallas kernels, pair_flows(): pl.pallas_call(functools.partial(_flow_kernel, cols=cols, row0=row0), gri...  45.2 us
    ppermute x5, waiting for transfers between devices, shifted(): lax.ppermute(value, axis, [(source, source + steps) for source in range(f...  23.2 us
    ppermute x5, starting transfers between devices, shifted(): lax.ppermute(value, axis, [(source, source + steps) for source in range(f...  14.9 us
    ppermute x2, waiting for transfers between devices, extended(): got = _strip_recv(lax.ppermute(send, axis, [(0, 1), (1, 0)]), dim)  7.67 us
    all_to_all x1, waiting for transfers between devices, gather_sections(): return lax.all_to_all(spread, axis, 0, 0, tiled=True)  5.55 us
    concatenate x1, local copies, waits for them, and re-layouts, extended(): block = jnp.concatenate([low, block, high], axis=dim)  3.79 us
    ppermute x2, starting transfers between devices, extended(): got = _strip_recv(lax.ppermute(send, axis, [(0, 1), (1, 0)]), dim)  3.35 us
    all_to_all x1, starting transfers between devices, gather_sections(): return lax.all_to_all(spread, axis, 0, 0, tiled=True)  3.25 us
  transfers between devices with their start and end apart: 8, of which 5 were waited for; matrix products, arithmetic and copies ran while one was open for 1% of the time, Pallas kernels for 19%

profile of v4, /device:TPU:0, one launch (start us, length us, event | category | flops | bytes accessed | tf_op | source)
XLA Modules:
  0.0 118.0 jit_solution(13224871944195142234)
XLA Ops:
  0.6 0.8 slice_select_fusion.1
  1.4 0.5 collective-permute-start.1
  1.9 0.9 collective-permute-done.1
  2.7 1.8 %pad_maximum_fusion = bf16[1,1056,1024]{2,1,0:T(8,128)(2,1)S(1)} fusion(bf16[1,16,1024]{2,1,0:T(8,128)(2,1)S(1)} %get-tuple-element.25, bf16[1,1024,1024]{2,1,0:T(8,128)(2,1)} %param.3, bf16[1,16,1024]{2,1,0:T(8,128)(2,1)S(1)} %get-tuple-element.24), kind=kLoop, calls=%fused_computation | loop fusion | flops 6488064 | bytes 4325376 | tf_op jit(solution)/shard_map/concatenate | solution.py:53
  4.5 0.1 fusion
  4.7 2.9 %collective-permute-start.2 = (bf16[1,16,1056]{1,2,0:T(8,128)(2,1)S(1)}, bf16[1,16,1056]{1,2,0:T(8,128)(2,1)S(1)}, u32[]{:S(2)}, u32[]{:S(2)}) collective-permute-start(bf16[1,16,1056]{1,2,0:T(8,128)(2,1)S(1)} %fusion), channel_id=1, source_target_pairs={{0,2},{2,0},{1,3},{3,1},{4,6},{6,4},{5,7},{7,5},{8,10},{10,8},{9,1... | collective-permute-start | bytes 101384 | tf_op jit(solution)/shard_map/ppermute | solution.py:45
  7.6 6.8 %collective-permute-done.2 = bf16[1,16,1056]{1,2,0:T(8,128)(2,1)S(1)} collective-permute-done((bf16[1,16,1056]{1,2,0:T(8,128)(2,1)S(1)}, bf16[1,16,1056]{1,2,0:T(8,128)(2,1)S(1)}, u32[]{:S(2)}, u32[]{:S(2)}) %collective-permute-start.2) | collective-permute-done | bytes 33824 | tf_op jit(solution)/shard_map/ppermute | solution.py:45
  14.4 3.8 %concatenate.19 = bf16[1,1056,1056]{2,1,0:T(8,128)(2,1)} concatenate(bf16[1,1056,16]{2,1,0:T(8,128)(2,1)S(1)} %get-tuple-element.23, bf16[1,1056,1024]{2,1,0:T(8,128)(2,1)S(1)} %pad_maximum_fusion, bf16[1,1056,16]{2,1,0:T(8,128)(2,1)S(1)} %get-tuple-element.22), dimensions={2} | concatenate | bytes 4460544 | tf_op jit(solution)/shard_map/concatenate | solution.py:53
  18.2 1.9 %slice_bitcast_fusion.1 = (bf16[544,1056]{1,0:T(8,128)(2,1)S(1)}, bf16[544,1056]{1,0:T(8,128)(2,1)S(1)}) fusion(bf16[1,1056,1056]{2,1,0:T(8,128)(2,1)} %concatenate.19), kind=kLoop, calls=%fused_computation.2 | loop fusion | bytes 4595712 | tf_op jit(solution)/shard_map/slice | solution.py:239
  20.1 4.8 %collective-permute-start.3 = (bf16[544,1056]{1,0:T(8,128)(2,1)S(1)}, bf16[544,1056]{1,0:T(8,128)(2,1)}, u32[]{:S(2)}, u32[]{:S(2)}) collective-permute-start(bf16[544,1056]{1,0:T(8,128)(2,1)S(1)} %get-tuple-element.20.own_ref), channel_id=1, source_target_pairs={{0,4},{4,8},{8,12},{1,5},{5,9},{9,13},{2,6},{6,10},{10,14},{3,7},{... | collective-permute-start | bytes 3446792 | tf_op jit(solution)/shard_map/ppermute | solution.py:26
  24.9 1.3 %collective-permute-start.4 = (bf16[544,1056]{1,0:T(8,128)(2,1)S(1)}, bf16[544,1056]{1,0:T(8,128)(2,1)}, u32[]{:S(2)}, u32[]{:S(2)}) collective-permute-start(bf16[544,1056]{1,0:T(8,128)(2,1)S(1)} %get-tuple-element.20.own_ref), channel_id=1, source_target_pairs={{4,0},{8,4},{12,8},{5,1},{9,5},{13,9},{6,2},{10,6},{14,10},{7,3},{... | collective-permute-start | bytes 3446792 | tf_op jit(solution)/shard_map/ppermute | solution.py:26
  26.3 1.3 %collective-permute-start = (s32[1,8,8]{1,2,0:T(8,128)S(1)}, s32[1,8,8]{1,2,0:T(8,128)S(1)}, u32[]{:S(2)}, u32[]{:S(2)}) collective-permute-start(s32[1,8,8]{1,2,0:T(8,128)S(1)} %copy.18), channel_id=1, source_target_pairs={{4,0},{8,4},{12,8},{5,1},{9,5},{13,9},{6,2},{10,6},{14,10},{7,3},{... | collective-permute-start | bytes 776 | tf_op jit(solution)/shard_map/ppermute | solution.py:26
  27.6 6.3 %collective-permute-start.5 = (bf16[544,1056]{1,0:T(8,128)(2,1)S(1)}, bf16[544,1056]{1,0:T(8,128)(2,1)}, u32[]{:S(2)}, u32[]{:S(2)}) collective-permute-start(bf16[544,1056]{1,0:T(8,128)(2,1)S(1)} %get-tuple-element.21.own_ref), channel_id=1, source_target_pairs={{0,4},{4,8},{8,12},{1,5},{5,9},{9,13},{2,6},{6,10},{10,14},{3,7},{... | collective-permute-start | bytes 3446792 | tf_op jit(solution)/shard_map/ppermute | solution.py:26
  33.8 1.3 %collective-permute-start.6 = (bf16[544,1056]{1,0:T(8,128)(2,1)S(1)}, bf16[544,1056]{1,0:T(8,128)(2,1)}, u32[]{:S(2)}, u32[]{:S(2)}) collective-permute-start(bf16[544,1056]{1,0:T(8,128)(2,1)S(1)} %get-tuple-element.21.own_ref), channel_id=1, source_target_pairs={{4,0},{8,4},{12,8},{5,1},{9,5},{13,9},{6,2},{10,6},{14,10},{7,3},{... | collective-permute-start | bytes 3446792 | tf_op jit(solution)/shard_map/ppermute | solution.py:26
  35.2 0.7 negate_convert_fusion
  36.0 0.1 copy.17
  36.1 21.2 %collective-permute-done = s32[1,8,8]{1,2,0:T(8,128)S(1)} collective-permute-done((s32[1,8,8]{1,2,0:T(8,128)S(1)}, s32[1,8,8]{1,2,0:T(8,128)S(1)}, u32[]{:S(2)}, u32[]{:S(2)}) %collective-permute-start) | collective-permute-done | bytes 288 | tf_op jit(solution)/shard_map/ppermute | solution.py:26
  57.5 22.7 %shard_map.50 = f32[4,8,128]{2,1,0:T(8,128)S(1)} custom-call(s32[64]{0:T(128)S(1)} %reshape.38.skip_ref, s32[64]{0:T(128)S(1)} %reshape.39.skip_next_ref, s32[1]{0:T(128)} %bitcast.1.flag_ref, bf16[544,1056]{1,0:T(8,128)(2,1)S(1)} %get-tuple-element.20.own_ref, bf16[544,1056]{1,0:T(8,128)(2,1)} %collective-permute-done.3.prev_ref, ...), custom_call_target="tpu_custom_call" | custom-call | tf_op jit(solution)/shard_map/pallas_call | solution.py:174
  80.2 0.1 copy.20
  80.3 2.0 %collective-permute-done.6.next_ref = bf16[544,1056]{1,0:T(8,128)(2,1)} collective-permute-done((bf16[544,1056]{1,0:T(8,128)(2,1)S(1)}, bf16[544,1056]{1,0:T(8,128)(2,1)}, u32[]{:S(2)}, u32[]{:S(2)}) %collective-permute-start.6) | collective-permute-done | bytes 1148960 | tf_op jit(solution)/shard_map/ppermute | solution.py:26
  82.3 22.6 %shard_map.51 = f32[4,8,128]{2,1,0:T(8,128)S(1)} custom-call(s32[64]{0:T(128)S(1)} %reshape.38.skip_ref, s32[64]{0:T(128)S(1)} %reshape.39.skip_next_ref, s32[1]{0:T(128)} %bitcast.1.flag_ref, bf16[544,1056]{1,0:T(8,128)(2,1)S(1)} %get-tuple-element.21.own_ref, bf16[544,1056]{1,0:T(8,128)(2,1)} %collective-permute-done.5.prev_ref, ...), custom_call_target="tpu_custom_call" | custom-call | tf_op jit(solution)/shard_map/pallas_call | solution.py:174
  104.9 0.1 copy.21
  105.0 0.1 copy.24
  105.1 0.1 copy.25
  105.5 0.7 reshape.48
  106.2 3.2 %all-to-all-start = ((f32[4,1,384]{2,1,0:T(1,128)}), f32[4,1,384]{2,1,0:T(1,128)S(1)}, u32[]{:S(2)}, u32[]{:S(2)}) async-start(f32[4,1,384]{2,1,0:T(1,128)} %reshape.48), calls=%async_computation | async-start | bytes 12288 | tf_op jit(solution)/shard_map/all_to_all | solution.py:191
  109.5 5.6 %all-to-all-done = f32[4,1,384]{2,1,0:T(1,128)S(1)} async-done(((f32[4,1,384]{2,1,0:T(1,128)}), f32[4,1,384]{2,1,0:T(1,128)S(1)}, u32[]{:S(2)}, u32[]{:S(2)}) %all-to-all-start) | async-done | bytes 6176 | tf_op jit(solution)/shard_map/all_to_all | solution.py:191
  115.0 0.5 broadcast.124
  115.5 0.7 reduce
  116.2 0.1 reshape.49
  116.5 0.6 dynamic-slice_bitcast_fusion
  117.4 0.6 fusion.72
  (58 shorter events, 1.1 us)
Async XLA Ops:
  1.4 1.3 %collective-permute-start.1 = (bf16[1,16,1024]{2,1,0:T(8,128)(2,1)S(1)}, bf16[1,16,1024]{2,1,0:T(8,128)(2,1)S(1)}, u32[]{:S(2)}, u32[]{:S(2)}) collective-permute-start(bf16[1,16,1024]{2,1,0:T(8,128)(2,1)S(1)} %slice_select_fusion.1), channel_id=1, source_target_pairs={{0,1},{1,0},{2,3},{3,2},{4,5},{5,4},{6,7},{7,6},{8,9},{9,8},{10,11... | collective-permute-start | bytes 98312 | tf_op jit(solution)/shard_map/ppermute | solution.py:45
  4.7 9.7 %collective-permute-start.2 = (bf16[1,16,1056]{1,2,0:T(8,128)(2,1)S(1)}, bf16[1,16,1056]{1,2,0:T(8,128)(2,1)S(1)}, u32[]{:S(2)}, u32[]{:S(2)}) collective-permute-start(bf16[1,16,1056]{1,2,0:T(8,128)(2,1)S(1)} %fusion), channel_id=1, source_target_pairs={{0,2},{2,0},{1,3},{3,1},{4,6},{6,4},{5,7},{7,5},{8,10},{10,8},{9,1... | collective-permute-start | bytes 101384 | tf_op jit(solution)/shard_map/ppermute | solution.py:45
  18.2 8.0 %copy-start = (s32[1,8,8]{2,1,0:T(8,128)S(1)}, s32[1,8,8]{2,1,0:T(8,128)}, u32[]{:S(2)}) copy-start(s32[1,8,8]{2,1,0:T(8,128)} %param.4) | copy-start | bytes 772
  18.2 16.9 %copy-start.1 = (s32[1,8,8]{2,1,0:T(8,128)S(1)}, s32[1,8,8]{2,1,0:T(8,128)}, u32[]{:S(2)}) copy-start(s32[1,8,8]{2,1,0:T(8,128)} %param.5) | copy-start | bytes 772
  20.1 37.4 %collective-permute-start.3 = (bf16[544,1056]{1,0:T(8,128)(2,1)S(1)}, bf16[544,1056]{1,0:T(8,128)(2,1)}, u32[]{:S(2)}, u32[]{:S(2)}) collective-permute-start(bf16[544,1056]{1,0:T(8,128)(2,1)S(1)} %get-tuple-element.20.own_ref), channel_id=1, source_target_pairs={{0,4},{4,8},{8,12},{1,5},{5,9},{9,13},{2,6},{6,10},{10,14},{3,7},{... | collective-permute-start | bytes 3446792 | tf_op jit(solution)/shard_map/ppermute | solution.py:26
  24.9 32.6 %collective-permute-start.4 = (bf16[544,1056]{1,0:T(8,128)(2,1)S(1)}, bf16[544,1056]{1,0:T(8,128)(2,1)}, u32[]{:S(2)}, u32[]{:S(2)}) collective-permute-start(bf16[544,1056]{1,0:T(8,128)(2,1)S(1)} %get-tuple-element.20.own_ref), channel_id=1, source_target_pairs={{4,0},{8,4},{12,8},{5,1},{9,5},{13,9},{6,2},{10,6},{14,10},{7,3},{... | collective-permute-start | bytes 3446792 | tf_op jit(solution)/shard_map/ppermute | solution.py:26
  26.3 31.1 %collective-permute-start = (s32[1,8,8]{1,2,0:T(8,128)S(1)}, s32[1,8,8]{1,2,0:T(8,128)S(1)}, u32[]{:S(2)}, u32[]{:S(2)}) collective-permute-start(s32[1,8,8]{1,2,0:T(8,128)S(1)} %copy.18), channel_id=1, source_target_pairs={{4,0},{8,4},{12,8},{5,1},{9,5},{13,9},{6,2},{10,6},{14,10},{7,3},{... | collective-permute-start | bytes 776 | tf_op jit(solution)/shard_map/ppermute | solution.py:26
  27.6 52.8 %collective-permute-start.5 = (bf16[544,1056]{1,0:T(8,128)(2,1)S(1)}, bf16[544,1056]{1,0:T(8,128)(2,1)}, u32[]{:S(2)}, u32[]{:S(2)}) collective-permute-start(bf16[544,1056]{1,0:T(8,128)(2,1)S(1)} %get-tuple-element.21.own_ref), channel_id=1, source_target_pairs={{0,4},{4,8},{8,12},{1,5},{5,9},{9,13},{2,6},{6,10},{10,14},{3,7},{... | collective-permute-start | bytes 3446792 | tf_op jit(solution)/shard_map/ppermute | solution.py:26
  33.8 48.5 %collective-permute-start.6 = (bf16[544,1056]{1,0:T(8,128)(2,1)S(1)}, bf16[544,1056]{1,0:T(8,128)(2,1)}, u32[]{:S(2)}, u32[]{:S(2)}) collective-permute-start(bf16[544,1056]{1,0:T(8,128)(2,1)S(1)} %get-tuple-element.21.own_ref), channel_id=1, source_target_pairs={{4,0},{8,4},{12,8},{5,1},{9,5},{13,9},{6,2},{10,6},{14,10},{7,3},{... | collective-permute-start | bytes 3446792 | tf_op jit(solution)/shard_map/ppermute | solution.py:26
  106.2 8.8 %all-to-all-start = ((f32[4,1,384]{2,1,0:T(1,128)}), f32[4,1,384]{2,1,0:T(1,128)S(1)}, u32[]{:S(2)}, u32[]{:S(2)}) async-start(f32[4,1,384]{2,1,0:T(1,128)} %reshape.48), calls=%async_computation | async-start | bytes 12288 | tf_op jit(solution)/shard_map/all_to_all | solution.py:191

commit v5 on v3

--- a/solution.py
+++ b/solution.py
@@ -52,6 +52,36 @@
             high = _strip_recv(lax.ppermute(_strip_send(top, dim), axis, backward), dim)
         block = jnp.concatenate([low, block, high], axis=dim)
     return block
+
+
+def extended_pairs(block, width):
+    sub = lax.axis_index("sub")
+    tile = lax.axis_index("tile")
+    swap = [(0, 1), (1, 0)]
+    rows_send = jnp.where(
+        sub == 0, block[:, -width:, :], block[:, :width, :]
+    )
+    cols_send = jnp.swapaxes(jnp.where(tile == 0, block[:, :, -width:], block[:, :, :width]), 1, 2)
+    corner_rows = jnp.where(sub == 0, block[:, -width:, :], block[:, :width, :])
+    corner_send = jnp.where(tile == 0, corner_rows[:, :, -width:], corner_rows[:, :, :width])
+    rows_got = lax.ppermute(rows_send, "sub", swap)
+    cols_got = jnp.swapaxes(lax.ppermute(cols_send, "tile", swap), 1, 2)
+    corner_got = lax.ppermute(corner_send, ("tile", "sub"), [(0, 3), (3, 0), (1, 2), (2, 1)])
+
+    def keep(flag, value):
+        return jnp.where(flag, value, jnp.zeros_like(value))
+
+    top, bottom = sub == 1, sub == 0
+    left, right = tile == 1, tile == 0
+    middle = jnp.concatenate([keep(left, cols_got), block, keep(right, cols_got)], axis=2)
+    upper = jnp.concatenate(
+        [keep(top & left, corner_got), keep(top, rows_got), keep(top & right, corner_got)], axis=2
+    )
+    lower = jnp.concatenate(
+        [keep(bottom & left, corner_got), keep(bottom, rows_got), keep(bottom & right, corner_got)],
+        axis=2,
+    )
+    return jnp.concatenate([upper, middle, lower], axis=1)
 
 
 def dft_tables(patch):
@@ -223,7 +253,10 @@
 def body(images, skipped, patch_mask):
     index = lax.axis_index("sec")
     own_distance = jnp.where(index >= 2, 1 + skipped, 1)
-    own_pad = extended(images, (("sub", 1), ("tile", 2)), RIM)[0]
+    if lax.axis_size("sub") == 2 and lax.axis_size("tile") == 2:
+        own_pad = extended_pairs(images, RIM)[0]
+    else:
+        own_pad = extended(images, (("sub", 1), ("tile", 2)), RIM)[0]
     skip_next = shifted(skipped, "sec", -1)
     use_own = (index == 0).astype(jnp.int32)
     rows_count = (own_pad.shape[0] - (PATCH - STRIDE)) // STRIDE

time: 116 us -> 111 us (0.957)
  waiting for transfers between devices: 16.9 us -> 11.7 us
    ppermute x2 -> x3, waiting for transfers between devices: 7.13 us -> 1.9 us  [the longest x1 1.89 us: extended_pairs(): cols_got = jnp.swapaxes(lax.ppermute(cols_send, 'tile', swap), 1, 2)]
    ppermute x9, starting transfers between devices: 27.2 us -> 25.3 us  [shifted(): lax.ppermute(value, axis, [(source, source + steps) for source in range(f...]
    slice x0 -> x1, other arithmetic: none -> 1.88 us  [body(): own_c = own_pad[start:start + per * STRIDE + PATCH - STRIDE]]
    concatenate x1 -> x0, other arithmetic: 1.78 us -> none  [extended(): block = jnp.concatenate([low, block, high], axis=dim)]
    concatenate x1 -> x3, local copies, waits for them, and re-layouts: 3.8 us -> 4.18 us  [the longest x1 3.98 us: extended_pairs(): jnp.concatenate([keep(left, cols_got), block, keep(right, cols_got)], axi...]
    ppermute x2 -> x3, starting transfers between devices: 3.02 us -> 3.12 us  [the longest x1 2.6 us: extended_pairs(): lax.ppermute(corner_send, ('tile', 'sub'), [(0, 3), (3, 0), (1, 2), (2, 1)])]
  transfers between devices with their start and end apart: 12 -> 13, of which waited for: 4 -> 4; matrix products, arithmetic and copies ran while one was open for 8% -> 9% of each run, Pallas kernels for 31% -> 33%
where the time goes in v5:
time: 111 us
  Pallas kernels  48.6 us (44%)
  starting transfers between devices  33.2 us (30%)
  waiting for transfers between devices  11.7 us (11%)
  local copies, waits for them, and re-layouts  10.1 us (9%)
  other arithmetic  5.96 us (5%)
    pallas_call x4, Pallas kernels, pair_flows(): pl.pallas_call(functools.partial(_flow_kernel, cols=cols, row0=row0), gri...  48.6 us
    ppermute x9, starting transfers between devices, shifted(): lax.ppermute(value, axis, [(source, source + steps) for source in range(f...  25.3 us
    all_to_all x1, waiting for transfers between devices, gather_sections(): return lax.all_to_all(spread, axis, 0, 0, tiled=True)  5.58 us
    all_to_all x1, starting transfers between devices, gather_sections(): return lax.all_to_all(spread, axis, 0, 0, tiled=True)  4.81 us
    ppermute x9, waiting for transfers between devices, shifted(): lax.ppermute(value, axis, [(source, source + steps) for source in range(f...  4.23 us
    concatenate x1, local copies, waits for them, and re-layouts, extended_pairs(): jnp.concatenate([keep(left, cols_got), block, keep(right, cols_got)], axi...  3.98 us
    ppermute x1, starting transfers between devices, extended_pairs(): lax.ppermute(corner_send, ('tile', 'sub'), [(0, 3), (3, 0), (1, 2), (2, 1)])  2.6 us
  transfers between devices with their start and end apart: 13, of which 4 were waited for; matrix products, arithmetic and copies ran while one was open for 9% of the time, Pallas kernels for 33%

profile of v5, /device:TPU:0, one launch (start us, length us, event | category | flops | bytes accessed | tf_op | source)
XLA Modules:
  0.0 110.7 jit_solution(801468543257922435)
XLA Ops:
  0.6 0.9 slice_select_fusion
  1.6 0.5 collective-permute-start.2
  2.1 2.6 %collective-permute-start.1 = (bf16[1,16,16]{2,1,0:T(8,128)(2,1)S(1)}, bf16[1,16,16]{2,1,0:T(8,128)(2,1)S(1)}, u32[]{:S(2)}, u32[]{:S(2)}) collective-permute-start(bf16[1,16,16]{2,1,0:T(8,128)(2,1)S(1)} %slice_select_fusion.1), channel_id=1, source_target_pairs={{0,3},{3,0},{1,2},{2,1},{4,7},{7,4},{5,6},{6,5},{8,11},{11,8},{9,1... | collective-permute-start | bytes 1544 | tf_op jit(solution)/shard_map/ppermute | solution.py:69
  4.7 1.2 %fusion.83 = (bf16[1,1024,16]{2,1,0:T(8,128)(2,1)S(1)}, bf16[1,1024,16]{2,1,0:T(8,128)(2,1)S(1)}) fusion(bf16[1,1024,1024]{2,1,0:T(8,128)(2,1)} %param.3), kind=kLoop, calls=%fused_computation.163 | loop fusion | bytes 131072 | tf_op jit(solution)/shard_map/slice | solution.py:64
  6.2 1.3 %collective-permute-start = (s32[1,8,8]{2,1,0:T(8,128)}, s32[1,8,8]{2,1,0:T(8,128)S(1)}, u32[]{:S(2)}, u32[]{:S(2)}) collective-permute-start(s32[1,8,8]{2,1,0:T(8,128)} %param.4), channel_id=1, source_target_pairs={{4,0},{8,4},{12,8},{5,1},{9,5},{13,9},{6,2},{10,6},{14,10},{7,3},{... | collective-permute-start | bytes 776 | tf_op jit(solution)/shard_map/ppermute | solution.py:26
  7.5 0.7 select_convert_fusion
  8.2 1.9 %collective-permute-done.3 = bf16[1,16,1024]{2,1,0:T(8,128)(2,1)S(1)} collective-permute-done((bf16[1,16,1024]{2,1,0:T(8,128)(2,1)S(1)}, bf16[1,16,1024]{2,1,0:T(8,128)(2,1)S(1)}, u32[]{:S(2)}, u32[]{:S(2)}) %collective-permute-start.3) | collective-permute-done | bytes 32800 | tf_op jit(solution)/shard_map/ppermute | solution.py:68
  10.3 0.2 copy.32
  10.5 4.0 %concatenate.29 = bf16[1,1024,1056]{2,1,0:T(8,128)(2,1)} concatenate(bf16[1,1024,16]{2,1,0:T(8,128)(2,1)S(1)} %copy.31, bf16[1,1024,1024]{2,1,0:T(8,128)(2,1)S(1)} %copy-done, bf16[1,1024,16]{2,1,0:T(8,128)(2,1)S(1)} %copy.32), dimensions={2} | concatenate | bytes 4325376 | tf_op jit(solution)/shard_map/concatenate | solution.py:76
  14.7 1.9 %fusion.1 = (bf16[288,1056]{1,0:T(8,128)(2,1)S(1)}, bf16[288,1056]{1,0:T(8,128)(2,1)S(1)}, bf16[288,1056]{1,0:T(8,128)(2,1)S(1)}, bf16[288,1056]{1,0:T(8,128)(2,1)S(1)}) fusion(bf16[1,1024,1056]{2,1,0:T(8,128)(2,1)} %concatenate.29, bf16[1,16,1056]{2,1,0:T(8,128)(2,1)S(1)} %concatenate.28, bf16[1,16,1056]{2,1,0:T(8,128)(2,1)S(1)} %concatenate.32), kind=kLoop, calls=%fused_computation.5 | loop fusion | flops 2433024 | bytes 6187008 | tf_op jit(solution)/shard_map/slice | solution.py:272
  16.6 4.3 %collective-permute-start.4 = (bf16[288,1056]{1,0:T(8,128)(2,1)S(1)}, bf16[288,1056]{1,0:T(8,128)(2,1)}, u32[]{:S(2)}, u32[]{:S(2)}) collective-permute-start(bf16[288,1056]{1,0:T(8,128)(2,1)S(1)} %get-tuple-element.20.own_ref), channel_id=1, source_target_pairs={{0,4},{4,8},{8,12},{1,5},{5,9},{9,13},{2,6},{6,10},{10,14},{3,7},{... | collective-permute-start | bytes 1824776 | tf_op jit(solution)/shard_map/ppermute | solution.py:26
  20.9 1.3 %collective-permute-start.5 = (bf16[288,1056]{1,0:T(8,128)(2,1)S(1)}, bf16[288,1056]{1,0:T(8,128)(2,1)}, u32[]{:S(2)}, u32[]{:S(2)}) collective-permute-start(bf16[288,1056]{1,0:T(8,128)(2,1)S(1)} %get-tuple-element.20.own_ref), channel_id=1, source_target_pairs={{4,0},{8,4},{12,8},{5,1},{9,5},{13,9},{6,2},{10,6},{14,10},{7,3},{... | collective-permute-start | bytes 1824776 | tf_op jit(solution)/shard_map/ppermute | solution.py:26
  22.2 5.4 %collective-permute-start.6 = (bf16[288,1056]{1,0:T(8,128)(2,1)S(1)}, bf16[288,1056]{1,0:T(8,128)(2,1)}, u32[]{:S(2)}, u32[]{:S(2)}) collective-permute-start(bf16[288,1056]{1,0:T(8,128)(2,1)S(1)} %get-tuple-element.22.own_ref), channel_id=1, source_target_pairs={{0,4},{4,8},{8,12},{1,5},{5,9},{9,13},{2,6},{6,10},{10,14},{3,7},{... | collective-permute-start | bytes 1824776 | tf_op jit(solution)/shard_map/ppermute | solution.py:26
  27.6 1.3 %collective-permute-start.7 = (bf16[288,1056]{1,0:T(8,128)(2,1)S(1)}, bf16[288,1056]{1,0:T(8,128)(2,1)}, u32[]{:S(2)}, u32[]{:S(2)}) collective-permute-start(bf16[288,1056]{1,0:T(8,128)(2,1)S(1)} %get-tuple-element.22.own_ref), channel_id=1, source_target_pairs={{4,0},{8,4},{12,8},{5,1},{9,5},{13,9},{6,2},{10,6},{14,10},{7,3},{... | collective-permute-start | bytes 1824776 | tf_op jit(solution)/shard_map/ppermute | solution.py:26
  28.9 0.7 negate_convert_fusion
  29.8 5.4 %collective-permute-start.8 = (bf16[288,1056]{1,0:T(8,128)(2,1)S(1)}, bf16[288,1056]{1,0:T(8,128)(2,1)}, u32[]{:S(2)}, u32[]{:S(2)}) collective-permute-start(bf16[288,1056]{1,0:T(8,128)(2,1)S(1)} %get-tuple-element.21.own_ref), channel_id=1, source_target_pairs={{0,4},{4,8},{8,12},{1,5},{5,9},{9,13},{2,6},{6,10},{10,14},{3,7},{... | collective-permute-start | bytes 1824776 | tf_op jit(solution)/shard_map/ppermute | solution.py:26
  35.2 0.2 collective-permute-done.4.prev_ref
  35.4 1.3 %collective-permute-start.9 = (bf16[288,1056]{1,0:T(8,128)(2,1)S(1)}, bf16[288,1056]{1,0:T(8,128)(2,1)}, u32[]{:S(2)}, u32[]{:S(2)}) collective-permute-start(bf16[288,1056]{1,0:T(8,128)(2,1)S(1)} %get-tuple-element.21.own_ref), channel_id=1, source_target_pairs={{4,0},{8,4},{12,8},{5,1},{9,5},{13,9},{6,2},{10,6},{14,10},{7,3},{... | collective-permute-start | bytes 1824776 | tf_op jit(solution)/shard_map/ppermute | solution.py:26
  36.7 4.0 %collective-permute-done.5.next_ref = bf16[288,1056]{1,0:T(8,128)(2,1)} collective-permute-done((bf16[288,1056]{1,0:T(8,128)(2,1)S(1)}, bf16[288,1056]{1,0:T(8,128)(2,1)}, u32[]{:S(2)}, u32[]{:S(2)}) %collective-permute-start.5) | collective-permute-done | bytes 608288 | tf_op jit(solution)/shard_map/ppermute | solution.py:26
  40.8 3.5 %collective-permute-start.10 = (bf16[288,1056]{1,0:T(8,128)(2,1)S(1)}, bf16[288,1056]{1,0:T(8,128)(2,1)}, u32[]{:S(2)}, u32[]{:S(2)}) collective-permute-start(bf16[288,1056]{1,0:T(8,128)(2,1)S(1)} %get-tuple-element.23.own_ref), channel_id=1, source_target_pairs={{0,4},{4,8},{8,12},{1,5},{5,9},{9,13},{2,6},{6,10},{10,14},{3,7},{... | collective-permute-start | bytes 1824776 | tf_op jit(solution)/shard_map/ppermute | solution.py:26
  44.3 12.1 %shard_map.50 = f32[2,8,128]{2,1,0:T(8,128)S(1)} custom-call(s32[64]{0:T(128)S(1)} %reshape.54.skip_ref, s32[64]{0:T(128)S(1)} %reshape.55.skip_next_ref, s32[1]{0:T(128)} %bitcast.1.flag_ref, bf16[288,1056]{1,0:T(8,128)(2,1)S(1)} %get-tuple-element.20.own_ref, bf16[288,1056]{1,0:T(8,128)(2,1)} %collective-permute-done.4.prev_ref, ...), custom_call_target="tpu_custom_call" | custom-call | tf_op jit(solution)/shard_map/pallas_call | solution.py:204
  56.4 1.5 %collective-permute-start.11 = (bf16[288,1056]{1,0:T(8,128)(2,1)S(1)}, bf16[288,1056]{1,0:T(8,128)(2,1)S(1)}, u32[]{:S(2)}, u32[]{:S(2)}) collective-permute-start(bf16[288,1056]{1,0:T(8,128)(2,1)S(1)} %get-tuple-element.23.own_ref), channel_id=1, source_target_pairs={{4,0},{8,4},{12,8},{5,1},{9,5},{13,9},{6,2},{10,6},{14,10},{7,3},{... | collective-permute-start | bytes 1824776 | tf_op jit(solution)/shard_map/ppermute | solution.py:26
  58.1 12.1 %shard_map.51 = f32[2,8,128]{2,1,0:T(8,128)S(1)} custom-call(s32[64]{0:T(128)S(1)} %reshape.54.skip_ref, s32[64]{0:T(128)S(1)} %reshape.55.skip_next_ref, s32[1]{0:T(128)} %bitcast.1.flag_ref, bf16[288,1056]{1,0:T(8,128)(2,1)S(1)} %get-tuple-element.22.own_ref, bf16[288,1056]{1,0:T(8,128)(2,1)} %collective-permute-done.6.prev_ref, ...), custom_call_target="tpu_custom_call" | custom-call | tf_op jit(solution)/shard_map/pallas_call | solution.py:204
  70.6 12.1 %shard_map.52 = f32[2,8,128]{2,1,0:T(8,128)S(1)} custom-call(s32[64]{0:T(128)S(1)} %reshape.54.skip_ref, s32[64]{0:T(128)S(1)} %reshape.55.skip_next_ref, s32[1]{0:T(128)} %bitcast.1.flag_ref, bf16[288,1056]{1,0:T(8,128)(2,1)S(1)} %get-tuple-element.21.own_ref, bf16[288,1056]{1,0:T(8,128)(2,1)} %collective-permute-done.8.prev_ref, ...), custom_call_target="tpu_custom_call" | custom-call | tf_op jit(solution)/shard_map/pallas_call | solution.py:204
  83.0 12.2 %shard_map.53 = f32[2,8,128]{2,1,0:T(8,128)S(1)} custom-call(s32[64]{0:T(128)S(1)} %reshape.54.skip_ref, s32[64]{0:T(128)S(1)} %reshape.55.skip_next_ref, s32[1]{0:T(128)} %bitcast.1.flag_ref, bf16[288,1056]{1,0:T(8,128)(2,1)S(1)} %get-tuple-element.23.own_ref, bf16[288,1056]{1,0:T(8,128)(2,1)} %collective-permute-done.10.prev_ref, ...), custom_call_target="tpu_custom_call" | custom-call | tf_op jit(solution)/shard_map/pallas_call | solution.py:204
  96.6 0.7 reshape.68
  97.3 4.8 %all-to-all-start = ((f32[4,1,384]{2,1,0:T(1,128)}), f32[4,1,384]{2,1,0:T(1,128)S(1)}, u32[]{:S(2)}, u32[]{:S(2)}) async-start(f32[4,1,384]{2,1,0:T(1,128)} %reshape.68), calls=%async_computation | async-start | bytes 12288 | tf_op jit(solution)/shard_map/all_to_all | solution.py:221
  102.1 5.6 %all-to-all-done = f32[4,1,384]{2,1,0:T(1,128)S(1)} async-done(((f32[4,1,384]{2,1,0:T(1,128)}), f32[4,1,384]{2,1,0:T(1,128)S(1)}, u32[]{:S(2)}, u32[]{:S(2)}) %all-to-all-start) | async-done | bytes 6176 | tf_op jit(solution)/shard_map/all_to_all | solution.py:221
  107.7 0.5 broadcast.129
  108.2 0.7 reduce
  109.1 0.6 dynamic-slice_bitcast_fusion
  110.1 0.6 fusion.73
  (93 shorter events, 3.6 us)
Async XLA Ops:
  0.6 9.9 %copy-start = (bf16[1,1024,1024]{2,1,0:T(8,128)(2,1)S(1)}, bf16[1,1024,1024]{2,1,0:T(8,128)(2,1)}, u32[]{:S(2)}) copy-start(bf16[1,1024,1024]{2,1,0:T(8,128)(2,1)} %param.3) | copy-start | bytes 6291460
  1.6 12.9 %collective-permute-start.2 = (bf16[1,16,1024]{2,1,0:T(8,128)(2,1)S(1)}, bf16[1,16,1024]{2,1,0:T(8,128)(2,1)S(1)}, u32[]{:S(2)}, u32[]{:S(2)}) collective-permute-start(bf16[1,16,1024]{2,1,0:T(8,128)(2,1)S(1)} %slice_select_fusion), channel_id=1, source_target_pairs={{0,1},{1,0},{2,3},{3,2},{4,5},{5,4},{6,7},{7,6},{8,9},{9,8},{10,11... | collective-permute-start | bytes 98312 | tf_op jit(solution)/shard_map/ppermute | solution.py:67
  2.1 6.1 %collective-permute-start.1 = (bf16[1,16,16]{2,1,0:T(8,128)(2,1)S(1)}, bf16[1,16,16]{2,1,0:T(8,128)(2,1)S(1)}, u32[]{:S(2)}, u32[]{:S(2)}) collective-permute-start(bf16[1,16,16]{2,1,0:T(8,128)(2,1)S(1)} %slice_select_fusion.1), channel_id=1, source_target_pairs={{0,3},{3,0},{1,2},{2,1},{4,7},{7,4},{5,6},{6,5},{8,11},{11,8},{9,1... | collective-permute-start | bytes 1544 | tf_op jit(solution)/shard_map/ppermute | solution.py:69
  6.1 4.0 %collective-permute-start.3 = (bf16[1,16,1024]{2,1,0:T(8,128)(2,1)S(1)}, bf16[1,16,1024]{2,1,0:T(8,128)(2,1)S(1)}, u32[]{:S(2)}, u32[]{:S(2)}) collective-permute-start(bf16[1,16,1024]{2,1,0:T(8,128)(2,1)S(1)} %select_bitcast_fusion.2), channel_id=1, source_target_pairs={{0,2},{2,0},{1,3},{3,1},{4,6},{6,4},{5,7},{7,5},{8,10},{10,8},{9,1... | collective-permute-start | bytes 98312 | tf_op jit(solution)/shard_map/ppermute | solution.py:68
  6.2 23.5 %collective-permute-start = (s32[1,8,8]{2,1,0:T(8,128)}, s32[1,8,8]{2,1,0:T(8,128)S(1)}, u32[]{:S(2)}, u32[]{:S(2)}) collective-permute-start(s32[1,8,8]{2,1,0:T(8,128)} %param.4), channel_id=1, source_target_pairs={{4,0},{8,4},{12,8},{5,1},{9,5},{13,9},{6,2},{10,6},{14,10},{7,3},{... | collective-permute-start | bytes 776 | tf_op jit(solution)/shard_map/ppermute | solution.py:26
  14.7 6.2 %copy-start.2 = (s32[1,8,8]{2,1,0:T(8,128)S(1)}, s32[1,8,8]{2,1,0:T(8,128)}, u32[]{:S(2)}) copy-start(s32[1,8,8]{2,1,0:T(8,128)} %param.5) | copy-start | bytes 772
  14.7 12.9 %copy-start.1 = (s32[1,8,8]{2,1,0:T(8,128)S(1)}, s32[1,8,8]{2,1,0:T(8,128)}, u32[]{:S(2)}) copy-start(s32[1,8,8]{2,1,0:T(8,128)} %param.4) | copy-start | bytes 772
  16.6 18.8 %collective-permute-start.4 = (bf16[288,1056]{1,0:T(8,128)(2,1)S(1)}, bf16[288,1056]{1,0:T(8,128)(2,1)}, u32[]{:S(2)}, u32[]{:S(2)}) collective-permute-start(bf16[288,1056]{1,0:T(8,128)(2,1)S(1)} %get-tuple-element.20.own_ref), channel_id=1, source_target_pairs={{0,4},{4,8},{8,12},{1,5},{5,9},{9,13},{2,6},{6,10},{10,14},{3,7},{... | collective-permute-start | bytes 1824776 | tf_op jit(solution)/shard_map/ppermute | solution.py:26
  20.9 19.8 %collective-permute-start.5 = (bf16[288,1056]{1,0:T(8,128)(2,1)S(1)}, bf16[288,1056]{1,0:T(8,128)(2,1)}, u32[]{:S(2)}, u32[]{:S(2)}) collective-permute-start(bf16[288,1056]{1,0:T(8,128)(2,1)S(1)} %get-tuple-element.20.own_ref), channel_id=1, source_target_pairs={{4,0},{8,4},{12,8},{5,1},{9,5},{13,9},{6,2},{10,6},{14,10},{7,3},{... | collective-permute-start | bytes 1824776 | tf_op jit(solution)/shard_map/ppermute | solution.py:26
  22.2 34.2 %collective-permute-start.6 = (bf16[288,1056]{1,0:T(8,128)(2,1)S(1)}, bf16[288,1056]{1,0:T(8,128)(2,1)}, u32[]{:S(2)}, u32[]{:S(2)}) collective-permute-start(bf16[288,1056]{1,0:T(8,128)(2,1)S(1)} %get-tuple-element.22.own_ref), channel_id=1, source_target_pairs={{0,4},{4,8},{8,12},{1,5},{5,9},{9,13},{2,6},{6,10},{10,14},{3,7},{... | collective-permute-start | bytes 1824776 | tf_op jit(solution)/shard_map/ppermute | solution.py:26
  27.6 30.5 %collective-permute-start.7 = (bf16[288,1056]{1,0:T(8,128)(2,1)S(1)}, bf16[288,1056]{1,0:T(8,128)(2,1)}, u32[]{:S(2)}, u32[]{:S(2)}) collective-permute-start(bf16[288,1056]{1,0:T(8,128)(2,1)S(1)} %get-tuple-element.22.own_ref), channel_id=1, source_target_pairs={{4,0},{8,4},{12,8},{5,1},{9,5},{13,9},{6,2},{10,6},{14,10},{7,3},{... | collective-permute-start | bytes 1824776 | tf_op jit(solution)/shard_map/ppermute | solution.py:26
  29.8 40.7 %collective-permute-start.8 = (bf16[288,1056]{1,0:T(8,128)(2,1)S(1)}, bf16[288,1056]{1,0:T(8,128)(2,1)}, u32[]{:S(2)}, u32[]{:S(2)}) collective-permute-start(bf16[288,1056]{1,0:T(8,128)(2,1)S(1)} %get-tuple-element.21.own_ref), channel_id=1, source_target_pairs={{0,4},{4,8},{8,12},{1,5},{5,9},{9,13},{2,6},{6,10},{10,14},{3,7},{... | collective-permute-start | bytes 1824776 | tf_op jit(solution)/shard_map/ppermute | solution.py:26
  35.4 35.1 %collective-permute-start.9 = (bf16[288,1056]{1,0:T(8,128)(2,1)S(1)}, bf16[288,1056]{1,0:T(8,128)(2,1)}, u32[]{:S(2)}, u32[]{:S(2)}) collective-permute-start(bf16[288,1056]{1,0:T(8,128)(2,1)S(1)} %get-tuple-element.21.own_ref), channel_id=1, source_target_pairs={{4,0},{8,4},{12,8},{5,1},{9,5},{13,9},{6,2},{10,6},{14,10},{7,3},{... | collective-permute-start | bytes 1824776 | tf_op jit(solution)/shard_map/ppermute | solution.py:26
  40.8 42.2 %collective-permute-start.10 = (bf16[288,1056]{1,0:T(8,128)(2,1)S(1)}, bf16[288,1056]{1,0:T(8,128)(2,1)}, u32[]{:S(2)}, u32[]{:S(2)}) collective-permute-start(bf16[288,1056]{1,0:T(8,128)(2,1)S(1)} %get-tuple-element.23.own_ref), channel_id=1, source_target_pairs={{0,4},{4,8},{8,12},{1,5},{5,9},{9,13},{2,6},{6,10},{10,14},{3,7},{... | collective-permute-start | bytes 1824776 | tf_op jit(solution)/shard_map/ppermute | solution.py:26
  56.4 26.6 %collective-permute-start.11 = (bf16[288,1056]{1,0:T(8,128)(2,1)S(1)}, bf16[288,1056]{1,0:T(8,128)(2,1)S(1)}, u32[]{:S(2)}, u32[]{:S(2)}) collective-permute-start(bf16[288,1056]{1,0:T(8,128)(2,1)S(1)} %get-tuple-element.23.own_ref), channel_id=1, source_target_pairs={{4,0},{8,4},{12,8},{5,1},{9,5},{13,9},{6,2},{10,6},{14,10},{7,3},{... | collective-permute-start | bytes 1824776 | tf_op jit(solution)/shard_map/ppermute | solution.py:26
  97.3 10.4 %all-to-all-start = ((f32[4,1,384]{2,1,0:T(1,128)}), f32[4,1,384]{2,1,0:T(1,128)S(1)}, u32[]{:S(2)}, u32[]{:S(2)}) async-start(f32[4,1,384]{2,1,0:T(1,128)} %reshape.68), calls=%async_computation | async-start | bytes 12288 | tf_op jit(solution)/shard_map/all_to_all | solution.py:221

commit v6 on v5

--- a/solution.py
+++ b/solution.py
@@ -96,8 +96,8 @@
 
 
 def _flow_kernel(
-    skip_ref, skip_next_ref, flag_ref, own_ref, prev_ref, next_ref, cs_ref, c_ref, s_ref, out_ref,
-    half_ref, x_ref, y_ref, br_ref, bi_ref,
+    skip_ref, skip_next_ref, flag_ref, own_ref, prev_ref, next_ref, cs_ref, c_ref, s_ref, inv_ref,
+    out_ref, half_ref, x_ref, y_ref, br_ref, bi_ref,
     *, cols, row0,
 ):
     f32, bf16 = jnp.float32, jnp.bfloat16
@@ -107,6 +107,7 @@
     cos_t = c_ref[...]
     sin_t = s_ref[...]
     both_t = cs_ref[...]
+    inverse_t = inv_ref[...]
     size = float(p * p)
 
     def window(ref, j):
@@ -150,10 +151,11 @@
         t_re, t_im = spectrum(2 * c + 1)
         c_re = (o_re * t_re + o_im * t_im).astype(bf16)
         c_im = (o_re * t_im - o_im * t_re).astype(bf16)
-        a = jnp.dot(both_t, c_re, preferred_element_type=f32)
-        b = jnp.dot(both_t, c_im, preferred_element_type=f32)
-        br_ref[p * c : p * (c + 1), :] = (a[:p] + b[p:]).astype(bf16)
-        bi_ref[p * c : p * (c + 1), :] = (b[:p] - a[p:]).astype(bf16)
+        back = jnp.dot(
+            inverse_t, jnp.concatenate([c_re, c_im], axis=0), preferred_element_type=f32
+        ).astype(bf16)
+        br_ref[p * c : p * (c + 1), :] = back[:p]
+        bi_ref[p * c : p * (c + 1), :] = back[p:]
 
     corr = (
         jnp.dot(br_ref[...], cos_t, preferred_element_type=f32)
@@ -185,13 +187,16 @@
     cols = (broad - (PATCH - STRIDE)) // STRIDE
     assert cols % 2 == 0
     height = max(8, -(-cols // 8) * 8)
-    both_t, cos_t, sin_t = tables
+    both_t, cos_t, sin_t, inverse_t = tables
     band = pl.BlockSpec((pl.Element(PATCH), pl.Element(broad)), lambda i, *_: (i * STRIDE, 0))
     table = pl.BlockSpec((PATCH, PATCH), lambda i, *_: (0, 0))
     grid_spec = pltpu.PrefetchScalarGridSpec(
         num_scalar_prefetch=3,
         grid=(rows,),
-        in_specs=[band, band, band, pl.BlockSpec((2 * PATCH, PATCH), lambda i, *_: (0, 0)), table, table],
+        in_specs=[
+            band, band, band, pl.BlockSpec((2 * PATCH, PATCH), lambda i, *_: (0, 0)), table, table,
+            pl.BlockSpec((2 * PATCH, 2 * PATCH), lambda i, *_: (0, 0)),
+        ],
         out_specs=pl.BlockSpec((1, height, 128), lambda i, *_: (i, 0, 0)),
         scratch_shapes=[
             pltpu.VMEM((4 * cols * PATCH, PATCH), jnp.bfloat16),
@@ -208,7 +213,7 @@
         compiler_params=pltpu.CompilerParams(
             dimension_semantics=("arbitrary",), vmem_limit_bytes=48 * 1024 * 1024
         ),
-    )(skip_flat, skip_next_flat, use_own.reshape(1), own_pad, prev_pad, next_pad, both_t, cos_t, sin_t)
+    )(skip_flat, skip_next_flat, use_own.reshape(1), own_pad, prev_pad, next_pad, both_t, cos_t, sin_t, inverse_t)
     half = cols // 2
     first = jnp.repeat(jnp.transpose(out[:, :half, 0:2], (2, 0, 1)), 2, axis=2)
     second = jnp.repeat(jnp.transpose(out[:, half:cols, 0:2], (2, 0, 1)), 2, axis=2)
@@ -263,7 +268,10 @@
     chunks = max(n for n in (1, 2, 4) if rows_count % n == 0)
     per = rows_count // chunks
     cos_t, sin_t = dft_tables(PATCH)
-    tables = (jnp.concatenate([cos_t, sin_t], axis=0), cos_t, sin_t)
+    inverse_t = jnp.concatenate(
+        [jnp.concatenate([cos_t, sin_t], axis=1), jnp.concatenate([-sin_t, cos_t], axis=1)], axis=0
+    )
+    tables = (jnp.concatenate([cos_t, sin_t], axis=0), cos_t, sin_t, inverse_t)
     skip_flat = skipped.reshape(-1)
     skip_next_flat = skip_next.reshape(-1)
     firsts, seconds = [], []

time: 111 us -> 111 us (level)
  waiting for transfers between devices: 11.7 us -> 10.2 us
  other arithmetic: 5.96 us -> 7.42 us
  transfers between devices with their start and end apart: 13 -> 13, of which waited for: 4 -> 3; matrix products, arithmetic and copies ran while one was open for 9% -> 11% of each run, Pallas kernels for 33% -> 32%
where the time goes in v6:
time: 111 us; the launch traced here: 110 us
  Pallas kernels  47.9 us (43%)
  starting transfers between devices  33.7 us (30%)
  waiting for transfers between devices  10.2 us (9%)
  local copies, waits for them, and re-layouts  10.1 us (9%)
  other arithmetic  7.42 us (7%)
    pallas_call x4, Pallas kernels, pair_flows(): pl.pallas_call(functools.partial(_flow_kernel, cols=cols, row0=row0), gri...  47.9 us
    ppermute x9, starting transfers between devices, shifted(): lax.ppermute(value, axis, [(source, source + steps) for source in range(f...  25.7 us
    all_to_all x1, waiting for transfers between devices, gather_sections(): return lax.all_to_all(spread, axis, 0, 0, tiled=True)  5.58 us
    all_to_all x1, starting transfers between devices, gather_sections(): return lax.all_to_all(spread, axis, 0, 0, tiled=True)  4.82 us
    concatenate x1, local copies, waits for them, and re-layouts, extended_pairs(): jnp.concatenate([keep(left, cols_got), block, keep(right, cols_got)], axi...  3.96 us
    ppermute x9, waiting for transfers between devices, shifted(): lax.ppermute(value, axis, [(source, source + steps) for source in range(f...  3.45 us
    ppermute x1, starting transfers between devices, extended_pairs(): lax.ppermute(corner_send, ('tile', 'sub'), [(0, 3), (3, 0), (1, 2), (2, 1)])  2.6 us
  transfers between devices with their start and end apart: 13, of which 3 were waited for; matrix products, arithmetic and copies ran while one was open for 11% of the time, Pallas kernels for 32%

profile of v6, /device:TPU:0, one launch (start us, length us, event | category | flops | bytes accessed | tf_op | source)
XLA Modules:
  0.0 110.4 jit_solution(310658122883976070)
XLA Ops:
  0.6 0.9 slice_select_fusion
  1.6 0.5 collective-permute-start.2
  2.1 2.6 %collective-permute-start.1 = (bf16[1,16,16]{2,1,0:T(8,128)(2,1)S(1)}, bf16[1,16,16]{2,1,0:T(8,128)(2,1)S(1)}, u32[]{:S(2)}, u32[]{:S(2)}) collective-permute-start(bf16[1,16,16]{2,1,0:T(8,128)(2,1)S(1)} %slice_select_fusion.1), channel_id=1, source_target_pairs={{0,3},{3,0},{1,2},{2,1},{4,7},{7,4},{5,6},{6,5},{8,11},{11,8},{9,1... | collective-permute-start | bytes 1544 | tf_op jit(solution)/shard_map/ppermute | solution.py:69
  4.7 1.2 %fusion.84 = (bf16[1,1024,16]{2,1,0:T(8,128)(2,1)S(1)}, bf16[1,1024,16]{2,1,0:T(8,128)(2,1)S(1)}) fusion(bf16[1,1024,1024]{2,1,0:T(8,128)(2,1)} %param.3), kind=kLoop, calls=%fused_computation.165 | loop fusion | bytes 131072 | tf_op jit(solution)/shard_map/slice | solution.py:64
  6.2 1.3 %collective-permute-start = (s32[1,8,8]{2,1,0:T(8,128)}, s32[1,8,8]{2,1,0:T(8,128)S(1)}, u32[]{:S(2)}, u32[]{:S(2)}) collective-permute-start(s32[1,8,8]{2,1,0:T(8,128)} %param.4), channel_id=1, source_target_pairs={{4,0},{8,4},{12,8},{5,1},{9,5},{13,9},{6,2},{10,6},{14,10},{7,3},{... | collective-permute-start | bytes 776 | tf_op jit(solution)/shard_map/ppermute | solution.py:26
  7.5 0.7 select_convert_fusion
  8.2 0.7 convert_multiply_fusion
  8.9 1.2 %collective-permute-done.3 = bf16[1,16,1024]{2,1,0:T(8,128)(2,1)S(1)} collective-permute-done((bf16[1,16,1024]{2,1,0:T(8,128)(2,1)S(1)}, bf16[1,16,1024]{2,1,0:T(8,128)(2,1)S(1)}, u32[]{:S(2)}, u32[]{:S(2)}) %collective-permute-start.3) | collective-permute-done | bytes 32800 | tf_op jit(solution)/shard_map/ppermute | solution.py:68
  10.5 4.0 %concatenate.38 = bf16[1,1024,1056]{2,1,0:T(8,128)(2,1)} concatenate(bf16[1,1024,16]{2,1,0:T(8,128)(2,1)S(1)} %copy.31, bf16[1,1024,1024]{2,1,0:T(8,128)(2,1)S(1)} %copy-done, bf16[1,1024,16]{2,1,0:T(8,128)(2,1)S(1)} %copy.32), dimensions={2} | concatenate | bytes 4325376 | tf_op jit(solution)/shard_map/concatenate | solution.py:76
  14.7 1.9 %fusion.1 = (bf16[288,1056]{1,0:T(8,128)(2,1)S(1)}, bf16[288,1056]{1,0:T(8,128)(2,1)S(1)}, bf16[288,1056]{1,0:T(8,128)(2,1)S(1)}, bf16[288,1056]{1,0:T(8,128)(2,1)S(1)}) fusion(bf16[1,1024,1056]{2,1,0:T(8,128)(2,1)} %concatenate.38, bf16[1,16,1056]{2,1,0:T(8,128)(2,1)S(1)} %concatenate.37, bf16[1,16,1056]{2,1,0:T(8,128)(2,1)S(1)} %concatenate.44), kind=kLoop, calls=%fused_computation.5 | loop fusion | flops 2433024 | bytes 6187008 | tf_op jit(solution)/shard_map/slice | solution.py:280
  16.6 4.3 %collective-permute-start.4 = (bf16[288,1056]{1,0:T(8,128)(2,1)S(1)}, bf16[288,1056]{1,0:T(8,128)(2,1)}, u32[]{:S(2)}, u32[]{:S(2)}) collective-permute-start(bf16[288,1056]{1,0:T(8,128)(2,1)S(1)} %get-tuple-element.20.own_ref), channel_id=1, source_target_pairs={{0,4},{4,8},{8,12},{1,5},{5,9},{9,13},{2,6},{6,10},{10,14},{3,7},{... | collective-permute-start | bytes 1824776 | tf_op jit(solution)/shard_map/ppermute | solution.py:26
  20.9 1.3 %collective-permute-start.5 = (bf16[288,1056]{1,0:T(8,128)(2,1)S(1)}, bf16[288,1056]{1,0:T(8,128)(2,1)}, u32[]{:S(2)}, u32[]{:S(2)}) collective-permute-start(bf16[288,1056]{1,0:T(8,128)(2,1)S(1)} %get-tuple-element.20.own_ref), channel_id=1, source_target_pairs={{4,0},{8,4},{12,8},{5,1},{9,5},{13,9},{6,2},{10,6},{14,10},{7,3},{... | collective-permute-start | bytes 1824776 | tf_op jit(solution)/shard_map/ppermute | solution.py:26
  22.2 5.4 %collective-permute-start.6 = (bf16[288,1056]{1,0:T(8,128)(2,1)S(1)}, bf16[288,1056]{1,0:T(8,128)(2,1)}, u32[]{:S(2)}, u32[]{:S(2)}) collective-permute-start(bf16[288,1056]{1,0:T(8,128)(2,1)S(1)} %get-tuple-element.22.own_ref), channel_id=1, source_target_pairs={{0,4},{4,8},{8,12},{1,5},{5,9},{9,13},{2,6},{6,10},{10,14},{3,7},{... | collective-permute-start | bytes 1824776 | tf_op jit(solution)/shard_map/ppermute | solution.py:26
  27.6 0.7 fusion.70
  28.2 0.7 negate_convert_fusion
  28.9 1.3 %collective-permute-start.7 = (bf16[288,1056]{1,0:T(8,128)(2,1)S(1)}, bf16[288,1056]{1,0:T(8,128)(2,1)}, u32[]{:S(2)}, u32[]{:S(2)}) collective-permute-start(bf16[288,1056]{1,0:T(8,128)(2,1)S(1)} %get-tuple-element.22.own_ref), channel_id=1, source_target_pairs={{4,0},{8,4},{12,8},{5,1},{9,5},{13,9},{6,2},{10,6},{14,10},{7,3},{... | collective-permute-start | bytes 1824776 | tf_op jit(solution)/shard_map/ppermute | solution.py:26
  30.6 5.4 %collective-permute-start.8 = (bf16[288,1056]{1,0:T(8,128)(2,1)S(1)}, bf16[288,1056]{1,0:T(8,128)(2,1)}, u32[]{:S(2)}, u32[]{:S(2)}) collective-permute-start(bf16[288,1056]{1,0:T(8,128)(2,1)S(1)} %get-tuple-element.21.own_ref), channel_id=1, source_target_pairs={{0,4},{4,8},{8,12},{1,5},{5,9},{9,13},{2,6},{6,10},{10,14},{3,7},{... | collective-permute-start | bytes 1824776 | tf_op jit(solution)/shard_map/ppermute | solution.py:26
  36.0 1.3 %collective-permute-start.9 = (bf16[288,1056]{1,0:T(8,128)(2,1)S(1)}, bf16[288,1056]{1,0:T(8,128)(2,1)}, u32[]{:S(2)}, u32[]{:S(2)}) collective-permute-start(bf16[288,1056]{1,0:T(8,128)(2,1)S(1)} %get-tuple-element.21.own_ref), channel_id=1, source_target_pairs={{4,0},{8,4},{12,8},{5,1},{9,5},{13,9},{6,2},{10,6},{14,10},{7,3},{... | collective-permute-start | bytes 1824776 | tf_op jit(solution)/shard_map/ppermute | solution.py:26
  37.3 3.4 %collective-permute-done.5.next_ref = bf16[288,1056]{1,0:T(8,128)(2,1)} collective-permute-done((bf16[288,1056]{1,0:T(8,128)(2,1)S(1)}, bf16[288,1056]{1,0:T(8,128)(2,1)}, u32[]{:S(2)}, u32[]{:S(2)}) %collective-permute-start.5) | collective-permute-done | bytes 608288 | tf_op jit(solution)/shard_map/ppermute | solution.py:26
  40.7 4.0 %collective-permute-start.10 = (bf16[288,1056]{1,0:T(8,128)(2,1)S(1)}, bf16[288,1056]{1,0:T(8,128)(2,1)}, u32[]{:S(2)}, u32[]{:S(2)}) collective-permute-start(bf16[288,1056]{1,0:T(8,128)(2,1)S(1)} %get-tuple-element.23.own_ref), channel_id=1, source_target_pairs={{0,4},{4,8},{8,12},{1,5},{5,9},{9,13},{2,6},{6,10},{10,14},{3,7},{... | collective-permute-start | bytes 1824776 | tf_op jit(solution)/shard_map/ppermute | solution.py:26
  44.7 11.9 %shard_map.50 = f32[2,8,128]{2,1,0:T(8,128)S(1)} custom-call(s32[64]{0:T(128)S(1)} %reshape.54.skip_ref, s32[64]{0:T(128)S(1)} %reshape.55.skip_next_ref, s32[1]{0:T(128)} %bitcast.1.flag_ref, bf16[288,1056]{1,0:T(8,128)(2,1)S(1)} %get-tuple-element.20.own_ref, bf16[288,1056]{1,0:T(8,128)(2,1)} %collective-permute-done.4.prev_ref, ...), custom_call_target="tpu_custom_call" | custom-call | tf_op jit(solution)/shard_map/pallas_call | solution.py:209
  56.6 1.5 %collective-permute-start.11 = (bf16[288,1056]{1,0:T(8,128)(2,1)S(1)}, bf16[288,1056]{1,0:T(8,128)(2,1)S(1)}, u32[]{:S(2)}, u32[]{:S(2)}) collective-permute-start(bf16[288,1056]{1,0:T(8,128)(2,1)S(1)} %get-tuple-element.23.own_ref), channel_id=1, source_target_pairs={{4,0},{8,4},{12,8},{5,1},{9,5},{13,9},{6,2},{10,6},{14,10},{7,3},{... | collective-permute-start | bytes 1824776 | tf_op jit(solution)/shard_map/ppermute | solution.py:26
  58.4 12.0 %shard_map.51 = f32[2,8,128]{2,1,0:T(8,128)S(1)} custom-call(s32[64]{0:T(128)S(1)} %reshape.54.skip_ref, s32[64]{0:T(128)S(1)} %reshape.55.skip_next_ref, s32[1]{0:T(128)} %bitcast.1.flag_ref, bf16[288,1056]{1,0:T(8,128)(2,1)S(1)} %get-tuple-element.22.own_ref, bf16[288,1056]{1,0:T(8,128)(2,1)} %collective-permute-done.6.prev_ref, ...), custom_call_target="tpu_custom_call" | custom-call | tf_op jit(solution)/shard_map/pallas_call | solution.py:209
  70.6 12.0 %shard_map.52 = f32[2,8,128]{2,1,0:T(8,128)S(1)} custom-call(s32[64]{0:T(128)S(1)} %reshape.54.skip_ref, s32[64]{0:T(128)S(1)} %reshape.55.skip_next_ref, s32[1]{0:T(128)} %bitcast.1.flag_ref, bf16[288,1056]{1,0:T(8,128)(2,1)S(1)} %get-tuple-element.21.own_ref, bf16[288,1056]{1,0:T(8,128)(2,1)} %collective-permute-done.8.prev_ref, ...), custom_call_target="tpu_custom_call" | custom-call | tf_op jit(solution)/shard_map/pallas_call | solution.py:209
  82.8 12.0 %shard_map.53 = f32[2,8,128]{2,1,0:T(8,128)S(1)} custom-call(s32[64]{0:T(128)S(1)} %reshape.54.skip_ref, s32[64]{0:T(128)S(1)} %reshape.55.skip_next_ref, s32[1]{0:T(128)} %bitcast.1.flag_ref, bf16[288,1056]{1,0:T(8,128)(2,1)S(1)} %get-tuple-element.23.own_ref, bf16[288,1056]{1,0:T(8,128)(2,1)} %collective-permute-done.10.prev_ref, ...), custom_call_target="tpu_custom_call" | custom-call | tf_op jit(solution)/shard_map/pallas_call | solution.py:209
  96.3 0.7 reshape.68
  97.0 4.8 %all-to-all-start = ((f32[4,1,384]{2,1,0:T(1,128)}), f32[4,1,384]{2,1,0:T(1,128)S(1)}, u32[]{:S(2)}, u32[]{:S(2)}) async-start(f32[4,1,384]{2,1,0:T(1,128)} %reshape.68), calls=%async_computation | async-start | bytes 12288 | tf_op jit(solution)/shard_map/all_to_all | solution.py:226
  101.8 5.6 %all-to-all-done = f32[4,1,384]{2,1,0:T(1,128)S(1)} async-done(((f32[4,1,384]{2,1,0:T(1,128)}), f32[4,1,384]{2,1,0:T(1,128)S(1)}, u32[]{:S(2)}, u32[]{:S(2)}) %all-to-all-start) | async-done | bytes 6176 | tf_op jit(solution)/shard_map/all_to_all | solution.py:226
  107.4 0.5 broadcast.129
  107.9 0.7 reduce
  108.8 0.6 dynamic-slice_bitcast_fusion
  109.8 0.6 fusion.74
  (93 shorter events, 3.8 us)
Async XLA Ops:
  0.6 9.9 %copy-start = (bf16[1,1024,1024]{2,1,0:T(8,128)(2,1)S(1)}, bf16[1,1024,1024]{2,1,0:T(8,128)(2,1)}, u32[]{:S(2)}) copy-start(bf16[1,1024,1024]{2,1,0:T(8,128)(2,1)} %param.3) | copy-start | bytes 6291460
  1.6 12.9 %collective-permute-start.2 = (bf16[1,16,1024]{2,1,0:T(8,128)(2,1)S(1)}, bf16[1,16,1024]{2,1,0:T(8,128)(2,1)S(1)}, u32[]{:S(2)}, u32[]{:S(2)}) collective-permute-start(bf16[1,16,1024]{2,1,0:T(8,128)(2,1)S(1)} %slice_select_fusion), channel_id=1, source_target_pairs={{0,1},{1,0},{2,3},{3,2},{4,5},{5,4},{6,7},{7,6},{8,9},{9,8},{10,11... | collective-permute-start | bytes 98312 | tf_op jit(solution)/shard_map/ppermute | solution.py:67
  2.1 6.8 %collective-permute-start.1 = (bf16[1,16,16]{2,1,0:T(8,128)(2,1)S(1)}, bf16[1,16,16]{2,1,0:T(8,128)(2,1)S(1)}, u32[]{:S(2)}, u32[]{:S(2)}) collective-permute-start(bf16[1,16,16]{2,1,0:T(8,128)(2,1)S(1)} %slice_select_fusion.1), channel_id=1, source_target_pairs={{0,3},{3,0},{1,2},{2,1},{4,7},{7,4},{5,6},{6,5},{8,11},{11,8},{9,1... | collective-permute-start | bytes 1544 | tf_op jit(solution)/shard_map/ppermute | solution.py:69
  6.1 4.0 %collective-permute-start.3 = (bf16[1,16,1024]{2,1,0:T(8,128)(2,1)S(1)}, bf16[1,16,1024]{2,1,0:T(8,128)(2,1)S(1)}, u32[]{:S(2)}, u32[]{:S(2)}) collective-permute-start(bf16[1,16,1024]{2,1,0:T(8,128)(2,1)S(1)} %select_bitcast_fusion.2), channel_id=1, source_target_pairs={{0,2},{2,0},{1,3},{3,1},{4,6},{6,4},{5,7},{7,5},{8,10},{10,8},{9,1... | collective-permute-start | bytes 98312 | tf_op jit(solution)/shard_map/ppermute | solution.py:68
  6.2 24.3 %collective-permute-start = (s32[1,8,8]{2,1,0:T(8,128)}, s32[1,8,8]{2,1,0:T(8,128)S(1)}, u32[]{:S(2)}, u32[]{:S(2)}) collective-permute-start(s32[1,8,8]{2,1,0:T(8,128)} %param.4), channel_id=1, source_target_pairs={{4,0},{8,4},{12,8},{5,1},{9,5},{13,9},{6,2},{10,6},{14,10},{7,3},{... | collective-permute-start | bytes 776 | tf_op jit(solution)/shard_map/ppermute | solution.py:26
  14.7 6.2 %copy-start.1 = (s32[1,8,8]{2,1,0:T(8,128)S(1)}, s32[1,8,8]{2,1,0:T(8,128)}, u32[]{:S(2)}) copy-start(s32[1,8,8]{2,1,0:T(8,128)} %param.4) | copy-start | bytes 772
  16.6 19.4 %collective-permute-start.4 = (bf16[288,1056]{1,0:T(8,128)(2,1)S(1)}, bf16[288,1056]{1,0:T(8,128)(2,1)}, u32[]{:S(2)}, u32[]{:S(2)}) collective-permute-start(bf16[288,1056]{1,0:T(8,128)(2,1)S(1)} %get-tuple-element.20.own_ref), channel_id=1, source_target_pairs={{0,4},{4,8},{8,12},{1,5},{5,9},{9,13},{2,6},{6,10},{10,14},{3,7},{... | collective-permute-start | bytes 1824776 | tf_op jit(solution)/shard_map/ppermute | solution.py:26
  20.9 19.8 %collective-permute-start.5 = (bf16[288,1056]{1,0:T(8,128)(2,1)S(1)}, bf16[288,1056]{1,0:T(8,128)(2,1)}, u32[]{:S(2)}, u32[]{:S(2)}) collective-permute-start(bf16[288,1056]{1,0:T(8,128)(2,1)S(1)} %get-tuple-element.20.own_ref), channel_id=1, source_target_pairs={{4,0},{8,4},{12,8},{5,1},{9,5},{13,9},{6,2},{10,6},{14,10},{7,3},{... | collective-permute-start | bytes 1824776 | tf_op jit(solution)/shard_map/ppermute | solution.py:26
  22.2 34.4 %collective-permute-start.6 = (bf16[288,1056]{1,0:T(8,128)(2,1)S(1)}, bf16[288,1056]{1,0:T(8,128)(2,1)}, u32[]{:S(2)}, u32[]{:S(2)}) collective-permute-start(bf16[288,1056]{1,0:T(8,128)(2,1)S(1)} %get-tuple-element.22.own_ref), channel_id=1, source_target_pairs={{0,4},{4,8},{8,12},{1,5},{5,9},{9,13},{2,6},{6,10},{10,14},{3,7},{... | collective-permute-start | bytes 1824776 | tf_op jit(solution)/shard_map/ppermute | solution.py:26
  28.9 29.4 %collective-permute-start.7 = (bf16[288,1056]{1,0:T(8,128)(2,1)S(1)}, bf16[288,1056]{1,0:T(8,128)(2,1)}, u32[]{:S(2)}, u32[]{:S(2)}) collective-permute-start(bf16[288,1056]{1,0:T(8,128)(2,1)S(1)} %get-tuple-element.22.own_ref), channel_id=1, source_target_pairs={{4,0},{8,4},{12,8},{5,1},{9,5},{13,9},{6,2},{10,6},{14,10},{7,3},{... | collective-permute-start | bytes 1824776 | tf_op jit(solution)/shard_map/ppermute | solution.py:26
  30.6 40.0 %collective-permute-start.8 = (bf16[288,1056]{1,0:T(8,128)(2,1)S(1)}, bf16[288,1056]{1,0:T(8,128)(2,1)}, u32[]{:S(2)}, u32[]{:S(2)}) collective-permute-start(bf16[288,1056]{1,0:T(8,128)(2,1)S(1)} %get-tuple-element.21.own_ref), channel_id=1, source_target_pairs={{0,4},{4,8},{8,12},{1,5},{5,9},{9,13},{2,6},{6,10},{10,14},{3,7},{... | collective-permute-start | bytes 1824776 | tf_op jit(solution)/shard_map/ppermute | solution.py:26
  36.0 34.6 %collective-permute-start.9 = (bf16[288,1056]{1,0:T(8,128)(2,1)S(1)}, bf16[288,1056]{1,0:T(8,128)(2,1)}, u32[]{:S(2)}, u32[]{:S(2)}) collective-permute-start(bf16[288,1056]{1,0:T(8,128)(2,1)S(1)} %get-tuple-element.21.own_ref), channel_id=1, source_target_pairs={{4,0},{8,4},{12,8},{5,1},{9,5},{13,9},{6,2},{10,6},{14,10},{7,3},{... | collective-permute-start | bytes 1824776 | tf_op jit(solution)/shard_map/ppermute | solution.py:26
  40.7 42.1 %collective-permute-start.10 = (bf16[288,1056]{1,0:T(8,128)(2,1)S(1)}, bf16[288,1056]{1,0:T(8,128)(2,1)}, u32[]{:S(2)}, u32[]{:S(2)}) collective-permute-start(bf16[288,1056]{1,0:T(8,128)(2,1)S(1)} %get-tuple-element.23.own_ref), channel_id=1, source_target_pairs={{0,4},{4,8},{8,12},{1,5},{5,9},{9,13},{2,6},{6,10},{10,14},{3,7},{... | collective-permute-start | bytes 1824776 | tf_op jit(solution)/shard_map/ppermute | solution.py:26
  56.6 26.2 %collective-permute-start.11 = (bf16[288,1056]{1,0:T(8,128)(2,1)S(1)}, bf16[288,1056]{1,0:T(8,128)(2,1)S(1)}, u32[]{:S(2)}, u32[]{:S(2)}) collective-permute-start(bf16[288,1056]{1,0:T(8,128)(2,1)S(1)} %get-tuple-element.23.own_ref), channel_id=1, source_target_pairs={{4,0},{8,4},{12,8},{5,1},{9,5},{13,9},{6,2},{10,6},{14,10},{7,3},{... | collective-permute-start | bytes 1824776 | tf_op jit(solution)/shard_map/ppermute | solution.py:26
  97.0 10.4 %all-to-all-start = ((f32[4,1,384]{2,1,0:T(1,128)}), f32[4,1,384]{2,1,0:T(1,128)S(1)}, u32[]{:S(2)}, u32[]{:S(2)}) async-start(f32[4,1,384]{2,1,0:T(1,128)} %reshape.68), calls=%async_computation | async-start | bytes 12288 | tf_op jit(solution)/shard_map/all_to_all | solution.py:226

commit v7 on v6

--- a/solution.py
+++ b/solution.py
@@ -265,8 +265,12 @@
     skip_next = shifted(skipped, "sec", -1)
     use_own = (index == 0).astype(jnp.int32)
     rows_count = (own_pad.shape[0] - (PATCH - STRIDE)) // STRIDE
-    chunks = max(n for n in (1, 2, 4) if rows_count % n == 0)
-    per = rows_count // chunks
+    if rows_count >= 8:
+        extra = rows_count - 8
+        sizes = [1, 2, 2, 3 + extra]
+    else:
+        sizes = [rows_count]
+    offsets = [sum(sizes[:n]) for n in range(len(sizes))]
     cos_t, sin_t = dft_tables(PATCH)
     inverse_t = jnp.concatenate(
         [jnp.concatenate([cos_t, sin_t], axis=1), jnp.concatenate([-sin_t, cos_t], axis=1)], axis=0
@@ -275,13 +279,13 @@
     skip_flat = skipped.reshape(-1)
     skip_next_flat = skip_next.reshape(-1)
     firsts, seconds = [], []
-    for c in range(chunks):
-        start = c * per * STRIDE
-        own_c = own_pad[start : start + per * STRIDE + PATCH - STRIDE]
+    for first_row, count in zip(offsets, sizes):
+        start = first_row * STRIDE
+        own_c = own_pad[start : start + count * STRIDE + PATCH - STRIDE]
         prev_c = shifted(own_c, "sec", 1)
         next_c = shifted(own_c, "sec", -1)
         first_c, second_c = pair_flows(
-            own_c, prev_c, next_c, skip_flat, skip_next_flat, use_own, c * per, tables
+            own_c, prev_c, next_c, skip_flat, skip_next_flat, use_own, first_row, tables
         )
         firsts.append(first_c)
         seconds.append(second_c)

time: 111 us -> 121 us (1.090)
  waiting for transfers between devices: 10.2 us -> 17.2 us
  local copies, waits for them, and re-layouts: 10.1 us -> 12.1 us
    ppermute x9, waiting for transfers between devices: 3.45 us -> 10 us  [shifted(): lax.ppermute(value, axis, [(source, source + steps) for source in range(f...]
    ppermute x9, starting transfers between devices: 25.7 us -> 27.4 us  [shifted(): lax.ppermute(value, axis, [(source, source + steps) for source in range(f...]
    all_to_all x1, starting transfers between devices: 4.82 us -> 3.25 us  [gather_sections(): return lax.all_to_all(spread, axis, 0, 0, tiled=True)]
    slice x0 -> x1, local copies, waits for them, and re-layouts: none -> 1.39 us  [body(): own_c = own_pad[start:start + count * STRIDE + PATCH - STRIDE]]
  transfers between devices with their start and end apart: 13 -> 13, of which waited for: 3 -> 3; matrix products, arithmetic and copies ran while one was open for 11% -> 13% of each run, Pallas kernels for 32% -> 26%
where the time goes in v7:
time: 121 us; the launch traced here: 120 us
  Pallas kernels  48.2 us (40%)
  starting transfers between devices  33.8 us (28%)
  waiting for transfers between devices  17.2 us (14%)
  local copies, waits for them, and re-layouts  12.1 us (10%)
  other arithmetic  7.65 us (6%)
    pallas_call x4, Pallas kernels, pair_flows(): pl.pallas_call(functools.partial(_flow_kernel, cols=cols, row0=row0), gri...  48.2 us
    ppermute x9, starting transfers between devices, shifted(): lax.ppermute(value, axis, [(source, source + steps) for source in range(f...  27.4 us
    ppermute x9, waiting for transfers between devices, shifted(): lax.ppermute(value, axis, [(source, source + steps) for source in range(f...  10 us
    all_to_all x1, waiting for transfers between devices, gather_sections(): return lax.all_to_all(spread, axis, 0, 0, tiled=True)  5.55 us
    concatenate x1, local copies, waits for them, and re-layouts, extended_pairs(): jnp.concatenate([keep(left, cols_got), block, keep(right, cols_got)], axi...  3.97 us
    all_to_all x1, starting transfers between devices, gather_sections(): return lax.all_to_all(spread, axis, 0, 0, tiled=True)  3.25 us
    ppermute x1, starting transfers between devices, extended_pairs(): lax.ppermute(corner_send, ('tile', 'sub'), [(0, 3), (3, 0), (1, 2), (2, 1)])  2.6 us
  transfers between devices with their start and end apart: 13, of which 3 were waited for; matrix products, arithmetic and copies ran while one was open for 13% of the time, Pallas kernels for 26%

profile of v7, /device:TPU:0, one launch (start us, length us, event | category | flops | bytes accessed | tf_op | source)
XLA Modules:
  0.0 120.1 jit_solution(17208873169765695047)
XLA Ops:
  0.7 1.4 %collective-permute-start = (s32[1,8,8]{2,0,1:T(1,128)}, s32[1,8,8]{2,0,1:T(1,128)S(1)}, u32[]{:S(2)}, u32[]{:S(2)}) collective-permute-start(s32[1,8,8]{2,0,1:T(1,128)} %bitcast.75), channel_id=1, source_target_pairs={{4,0},{8,4},{12,8},{5,1},{9,5},{13,9},{6,2},{10,6},{14,10},{7,3},{... | collective-permute-start | bytes 776 | tf_op jit(solution)/shard_map/ppermute | solution.py:26
  2.1 0.8 slice_select_fusion
  3.4 2.6 %collective-permute-start.1 = (bf16[1,16,16]{2,1,0:T(8,128)(2,1)S(1)}, bf16[1,16,16]{2,1,0:T(8,128)(2,1)S(1)}, u32[]{:S(2)}, u32[]{:S(2)}) collective-permute-start(bf16[1,16,16]{2,1,0:T(8,128)(2,1)S(1)} %slice_select_fusion.1), channel_id=1, source_target_pairs={{0,3},{3,0},{1,2},{2,1},{4,7},{7,4},{5,6},{6,5},{8,11},{11,8},{9,1... | collective-permute-start | bytes 1544 | tf_op jit(solution)/shard_map/ppermute | solution.py:69
  6.0 1.2 fusion.85
  7.5 0.7 compare_bitcast_fusion
  8.2 0.7 fusion.70
  8.9 0.7 negate_convert_fusion
  9.8 1.6 %collective-permute-done.3 = bf16[1,16,1024]{2,1,0:T(8,128)(2,1)S(1)} collective-permute-done((bf16[1,16,1024]{2,1,0:T(8,128)(2,1)S(1)}, bf16[1,16,1024]{2,1,0:T(8,128)(2,1)S(1)}, u32[]{:S(2)}, u32[]{:S(2)}) %collective-permute-start.3) | collective-permute-done | bytes 32800 | tf_op jit(solution)/shard_map/ppermute | solution.py:68
  11.8 4.0 %concatenate.38 = bf16[1,1024,1056]{2,1,0:T(8,128)(2,1)} concatenate(bf16[1,1024,16]{2,1,0:T(8,128)(2,1)S(1)} %copy.83, bf16[1,1024,1024]{2,1,0:T(8,128)(2,1)S(1)} %copy-done, bf16[1,1024,16]{2,1,0:T(8,128)(2,1)S(1)} %copy.84), dimensions={2} | concatenate | bytes 4325376 | tf_op jit(solution)/shard_map/concatenate | solution.py:76
  15.8 1.4 %slice_bitcast_fusion.1 = (bf16[288,1056]{1,0:T(8,128)(2,1)S(1)}, bf16[288,1056]{1,0:T(8,128)(2,1)S(1)}) fusion(bf16[1,1024,1056]{2,1,0:T(8,128)(2,1)} %concatenate.38), kind=kLoop, calls=%fused_computation.3 | loop fusion | bytes 2433024 | tf_op jit(solution)/shard_map/slice | solution.py:284
  17.2 1.3 %collective-permute-start.7 = (bf16[288,1056]{1,0:T(8,128)(2,1)S(1)}, bf16[288,1056]{1,0:T(8,128)(2,1)}, u32[]{:S(2)}, u32[]{:S(2)}) collective-permute-start(bf16[288,1056]{1,0:T(8,128)(2,1)S(1)} %get-tuple-element.22.own_ref), channel_id=1, source_target_pairs={{4,0},{8,4},{12,8},{5,1},{9,5},{13,9},{6,2},{10,6},{14,10},{7,3},{... | collective-permute-start | bytes 1824776 | tf_op jit(solution)/shard_map/ppermute | solution.py:26
  18.6 1.0 fusion.1.own_ref
  19.6 1.3 %collective-permute-start.5 = (bf16[160,1056]{1,0:T(8,128)(2,1)S(1)}, bf16[160,1056]{1,0:T(8,128)(2,1)}, u32[]{:S(2)}, u32[]{:S(2)}) collective-permute-start(bf16[160,1056]{1,0:T(8,128)(2,1)S(1)} %fusion.1.own_ref), channel_id=1, source_target_pairs={{4,0},{8,4},{12,8},{5,1},{9,5},{13,9},{6,2},{10,6},{14,10},{7,3},{... | collective-permute-start | bytes 1013768 | tf_op jit(solution)/shard_map/ppermute | solution.py:26
  20.9 6.6 %collective-permute-start.4 = (bf16[160,1056]{1,0:T(8,128)(2,1)S(1)}, bf16[160,1056]{1,0:T(8,128)(2,1)}, u32[]{:S(2)}, u32[]{:S(2)}) collective-permute-start(bf16[160,1056]{1,0:T(8,128)(2,1)S(1)} %fusion.1.own_ref), channel_id=1, source_target_pairs={{0,4},{4,8},{8,12},{1,5},{5,9},{9,13},{2,6},{6,10},{10,14},{3,7},{... | collective-permute-start | bytes 1013768 | tf_op jit(solution)/shard_map/ppermute | solution.py:26
  28.1 0.7 reduce.3
  28.8 4.0 %collective-permute-start.6 = (bf16[288,1056]{1,0:T(8,128)(2,1)S(1)}, bf16[288,1056]{1,0:T(8,128)(2,1)}, u32[]{:S(2)}, u32[]{:S(2)}) collective-permute-start(bf16[288,1056]{1,0:T(8,128)(2,1)S(1)} %get-tuple-element.22.own_ref), channel_id=1, source_target_pairs={{0,4},{4,8},{8,12},{1,5},{5,9},{9,13},{2,6},{6,10},{10,14},{3,7},{... | collective-permute-start | bytes 1824776 | tf_op jit(solution)/shard_map/ppermute | solution.py:26
  32.9 1.3 %collective-permute-start.9 = (bf16[288,1056]{1,0:T(8,128)(2,1)S(1)}, bf16[288,1056]{1,0:T(8,128)(2,1)}, u32[]{:S(2)}, u32[]{:S(2)}) collective-permute-start(bf16[288,1056]{1,0:T(8,128)(2,1)S(1)} %get-tuple-element.23.own_ref), channel_id=1, source_target_pairs={{4,0},{8,4},{12,8},{5,1},{9,5},{13,9},{6,2},{10,6},{14,10},{7,3},{... | collective-permute-start | bytes 1824776 | tf_op jit(solution)/shard_map/ppermute | solution.py:26
  34.3 1.3 %fusion.own_ref = bf16[416,1056]{1,0:T(8,128)(2,1)S(1)} fusion(bf16[1,16,1056]{2,1,0:T(8,128)(2,1)S(1)} %concatenate.44, bf16[1,1024,1056]{2,1,0:T(8,128)(2,1)} %concatenate.38), kind=kLoop, calls=%fused_computation.1 | loop fusion | flops 1757184 | bytes 3075072 | tf_op jit(solution)/shard_map/slice | solution.py:284
  35.5 10.0 %collective-permute-done.5.next_ref = bf16[160,1056]{1,0:T(8,128)(2,1)} collective-permute-done((bf16[160,1056]{1,0:T(8,128)(2,1)S(1)}, bf16[160,1056]{1,0:T(8,128)(2,1)}, u32[]{:S(2)}, u32[]{:S(2)}) %collective-permute-start.5) | collective-permute-done | bytes 337952 | tf_op jit(solution)/shard_map/ppermute | solution.py:26
  45.5 4.8 %collective-permute-start.8 = (bf16[288,1056]{1,0:T(8,128)(2,1)S(1)}, bf16[288,1056]{1,0:T(8,128)(2,1)}, u32[]{:S(2)}, u32[]{:S(2)}) collective-permute-start(bf16[288,1056]{1,0:T(8,128)(2,1)S(1)} %get-tuple-element.23.own_ref), channel_id=1, source_target_pairs={{0,4},{4,8},{8,12},{1,5},{5,9},{9,13},{2,6},{6,10},{10,14},{3,7},{... | collective-permute-start | bytes 1824776 | tf_op jit(solution)/shard_map/ppermute | solution.py:26
  50.3 1.3 %collective-permute-start.11 = (bf16[416,1056]{1,0:T(8,128)(2,1)S(1)}, bf16[416,1056]{1,0:T(8,128)(2,1)}, u32[]{:S(2)}, u32[]{:S(2)}) collective-permute-start(bf16[416,1056]{1,0:T(8,128)(2,1)S(1)} %fusion.own_ref), channel_id=1, source_target_pairs={{4,0},{8,4},{12,8},{5,1},{9,5},{13,9},{6,2},{10,6},{14,10},{7,3},{... | collective-permute-start | bytes 2635784 | tf_op jit(solution)/shard_map/ppermute | solution.py:26
  51.6 5.5 %collective-permute-start.10 = (bf16[416,1056]{1,0:T(8,128)(2,1)S(1)}, bf16[416,1056]{1,0:T(8,128)(2,1)}, u32[]{:S(2)}, u32[]{:S(2)}) collective-permute-start(bf16[416,1056]{1,0:T(8,128)(2,1)S(1)} %fusion.own_ref), channel_id=1, source_target_pairs={{0,4},{4,8},{8,12},{1,5},{5,9},{9,13},{2,6},{6,10},{10,14},{3,7},{... | collective-permute-start | bytes 2635784 | tf_op jit(solution)/shard_map/ppermute | solution.py:26
  57.1 6.8 %shard_map.50 = f32[1,8,128]{2,1,0:T(8,128)S(1)} custom-call(s32[64]{0:T(128)S(1)} %reshape.58.skip_ref, s32[64]{0:T(128)S(1)} %reshape.59.skip_next_ref, s32[1]{0:T(128)} %bitcast.2.flag_ref, bf16[160,1056]{1,0:T(8,128)(2,1)S(1)} %fusion.1.own_ref, bf16[160,1056]{1,0:T(8,128)(2,1)} %collective-permute-done.4.prev_ref, ...), custom_call_target="tpu_custom_call" | custom-call | tf_op jit(solution)/shard_map/pallas_call | solution.py:209
  64.4 12.2 %shard_map.51 = f32[2,8,128]{2,1,0:T(8,128)S(1)} custom-call(s32[64]{0:T(128)S(1)} %reshape.58.skip_ref, s32[64]{0:T(128)S(1)} %reshape.59.skip_next_ref, s32[1]{0:T(128)} %bitcast.2.flag_ref, bf16[288,1056]{1,0:T(8,128)(2,1)S(1)} %get-tuple-element.22.own_ref, bf16[288,1056]{1,0:T(8,128)(2,1)} %collective-permute-done.6.prev_ref, ...), custom_call_target="tpu_custom_call" | custom-call | tf_op jit(solution)/shard_map/pallas_call | solution.py:209
  77.1 11.9 %shard_map.52 = f32[2,8,128]{2,1,0:T(8,128)S(1)} custom-call(s32[64]{0:T(128)S(1)} %reshape.58.skip_ref, s32[64]{0:T(128)S(1)} %reshape.59.skip_next_ref, s32[1]{0:T(128)} %bitcast.2.flag_ref, bf16[288,1056]{1,0:T(8,128)(2,1)S(1)} %get-tuple-element.23.own_ref, bf16[288,1056]{1,0:T(8,128)(2,1)} %collective-permute-done.8.prev_ref, ...), custom_call_target="tpu_custom_call" | custom-call | tf_op jit(solution)/shard_map/pallas_call | solution.py:209
  89.6 17.3 %shard_map.53 = f32[3,8,128]{2,1,0:T(8,128)S(1)} custom-call(s32[64]{0:T(128)S(1)} %reshape.58.skip_ref, s32[64]{0:T(128)S(1)} %reshape.59.skip_next_ref, s32[1]{0:T(128)} %bitcast.2.flag_ref, bf16[416,1056]{1,0:T(8,128)(2,1)S(1)} %fusion.own_ref, bf16[416,1056]{1,0:T(8,128)(2,1)} %collective-permute-done.10.prev_ref, ...), custom_call_target="tpu_custom_call" | custom-call | tf_op jit(solution)/shard_map/pallas_call | solution.py:209
  107.6 0.7 reshape.79
  108.3 3.2 %all-to-all-start = ((f32[4,1,384]{2,1,0:T(1,128)}), f32[4,1,384]{2,1,0:T(1,128)S(1)}, u32[]{:S(2)}, u32[]{:S(2)}) async-start(f32[4,1,384]{2,1,0:T(1,128)} %reshape.79), calls=%async_computation | async-start | bytes 12288 | tf_op jit(solution)/shard_map/all_to_all | solution.py:226
  111.6 5.6 %all-to-all-done = f32[4,1,384]{2,1,0:T(1,128)S(1)} async-done(((f32[4,1,384]{2,1,0:T(1,128)}), f32[4,1,384]{2,1,0:T(1,128)S(1)}, u32[]{:S(2)}, u32[]{:S(2)}) %all-to-all-start) | async-done | bytes 6176 | tf_op jit(solution)/shard_map/all_to_all | solution.py:226
  117.6 0.7 reduce.4
  118.5 0.6 dynamic-slice_bitcast_fusion
  119.5 0.6 fusion.74
  (106 shorter events, 5.4 us)
Async XLA Ops:
  0.6 9.0 %copy-start.1 = (s32[1,8,8]{2,1,0:T(8,128)S(1)}, s32[1,8,8]{2,1,0:T(8,128)}, u32[]{:S(2)}) copy-start(s32[1,8,8]{2,1,0:T(8,128)} %param.4) | copy-start | bytes 772
  0.6 11.2 %copy-start = (bf16[1,1024,1024]{2,1,0:T(8,128)(2,1)S(1)}, bf16[1,1024,1024]{2,1,0:T(8,128)(2,1)}, u32[]{:S(2)}) copy-start(bf16[1,1024,1024]{2,1,0:T(8,128)(2,1)} %param.3) | copy-start | bytes 6291460
  0.7 8.9 %copy-start.2 = (s32[1,8,8]{2,1,0:T(8,128)S(1)}, s32[1,8,8]{2,1,0:T(8,128)}, u32[]{:S(2)}) copy-start(s32[1,8,8]{2,1,0:T(8,128)} %param.5) | copy-start | bytes 772
  0.7 26.9 %collective-permute-start = (s32[1,8,8]{2,0,1:T(1,128)}, s32[1,8,8]{2,0,1:T(1,128)S(1)}, u32[]{:S(2)}, u32[]{:S(2)}) collective-permute-start(s32[1,8,8]{2,0,1:T(1,128)} %bitcast.75), channel_id=1, source_target_pairs={{4,0},{8,4},{12,8},{5,1},{9,5},{13,9},{6,2},{10,6},{14,10},{7,3},{... | collective-permute-start | bytes 776 | tf_op jit(solution)/shard_map/ppermute | solution.py:26
  2.9 15.6 %collective-permute-start.2 = (bf16[1,16,1024]{2,1,0:T(8,128)(2,1)S(1)}, bf16[1,16,1024]{2,1,0:T(8,128)(2,1)S(1)}, u32[]{:S(2)}, u32[]{:S(2)}) collective-permute-start(bf16[1,16,1024]{2,1,0:T(8,128)(2,1)S(1)} %slice_select_fusion), channel_id=1, source_target_pairs={{0,1},{1,0},{2,3},{3,2},{4,5},{5,4},{6,7},{7,6},{8,9},{9,8},{10,11... | collective-permute-start | bytes 98312 | tf_op jit(solution)/shard_map/ppermute | solution.py:67
  3.4 6.4 %collective-permute-start.1 = (bf16[1,16,16]{2,1,0:T(8,128)(2,1)S(1)}, bf16[1,16,16]{2,1,0:T(8,128)(2,1)S(1)}, u32[]{:S(2)}, u32[]{:S(2)}) collective-permute-start(bf16[1,16,16]{2,1,0:T(8,128)(2,1)S(1)} %slice_select_fusion.1), channel_id=1, source_target_pairs={{0,3},{3,0},{1,2},{2,1},{4,7},{7,4},{5,6},{6,5},{8,11},{11,8},{9,1... | collective-permute-start | bytes 1544 | tf_op jit(solution)/shard_map/ppermute | solution.py:69
  7.4 4.0 %collective-permute-start.3 = (bf16[1,16,1024]{2,1,0:T(8,128)(2,1)S(1)}, bf16[1,16,1024]{2,1,0:T(8,128)(2,1)S(1)}, u32[]{:S(2)}, u32[]{:S(2)}) collective-permute-start(bf16[1,16,1024]{2,1,0:T(8,128)(2,1)S(1)} %select_bitcast_fusion.2), channel_id=1, source_target_pairs={{0,2},{2,0},{1,3},{3,1},{4,6},{6,4},{5,7},{7,5},{8,10},{10,8},{9,1... | collective-permute-start | bytes 98312 | tf_op jit(solution)/shard_map/ppermute | solution.py:68
  17.2 34.4 %collective-permute-start.7 = (bf16[288,1056]{1,0:T(8,128)(2,1)S(1)}, bf16[288,1056]{1,0:T(8,128)(2,1)}, u32[]{:S(2)}, u32[]{:S(2)}) collective-permute-start(bf16[288,1056]{1,0:T(8,128)(2,1)S(1)} %get-tuple-element.22.own_ref), channel_id=1, source_target_pairs={{4,0},{8,4},{12,8},{5,1},{9,5},{13,9},{6,2},{10,6},{14,10},{7,3},{... | collective-permute-start | bytes 1824776 | tf_op jit(solution)/shard_map/ppermute | solution.py:26
  19.6 25.9 %collective-permute-start.5 = (bf16[160,1056]{1,0:T(8,128)(2,1)S(1)}, bf16[160,1056]{1,0:T(8,128)(2,1)}, u32[]{:S(2)}, u32[]{:S(2)}) collective-permute-start(bf16[160,1056]{1,0:T(8,128)(2,1)S(1)} %fusion.1.own_ref), channel_id=1, source_target_pairs={{4,0},{8,4},{12,8},{5,1},{9,5},{13,9},{6,2},{10,6},{14,10},{7,3},{... | collective-permute-start | bytes 1013768 | tf_op jit(solution)/shard_map/ppermute | solution.py:26
  20.9 29.4 %collective-permute-start.4 = (bf16[160,1056]{1,0:T(8,128)(2,1)S(1)}, bf16[160,1056]{1,0:T(8,128)(2,1)}, u32[]{:S(2)}, u32[]{:S(2)}) collective-permute-start(bf16[160,1056]{1,0:T(8,128)(2,1)S(1)} %fusion.1.own_ref), channel_id=1, source_target_pairs={{0,4},{4,8},{8,12},{1,5},{5,9},{9,13},{2,6},{6,10},{10,14},{3,7},{... | collective-permute-start | bytes 1013768 | tf_op jit(solution)/shard_map/ppermute | solution.py:26
  28.8 35.6 %collective-permute-start.6 = (bf16[288,1056]{1,0:T(8,128)(2,1)S(1)}, bf16[288,1056]{1,0:T(8,128)(2,1)}, u32[]{:S(2)}, u32[]{:S(2)}) collective-permute-start(bf16[288,1056]{1,0:T(8,128)(2,1)S(1)} %get-tuple-element.22.own_ref), channel_id=1, source_target_pairs={{0,4},{4,8},{8,12},{1,5},{5,9},{9,13},{2,6},{6,10},{10,14},{3,7},{... | collective-permute-start | bytes 1824776 | tf_op jit(solution)/shard_map/ppermute | solution.py:26
  32.9 44.3 %collective-permute-start.9 = (bf16[288,1056]{1,0:T(8,128)(2,1)S(1)}, bf16[288,1056]{1,0:T(8,128)(2,1)}, u32[]{:S(2)}, u32[]{:S(2)}) collective-permute-start(bf16[288,1056]{1,0:T(8,128)(2,1)S(1)} %get-tuple-element.23.own_ref), channel_id=1, source_target_pairs={{4,0},{8,4},{12,8},{5,1},{9,5},{13,9},{6,2},{10,6},{14,10},{7,3},{... | collective-permute-start | bytes 1824776 | tf_op jit(solution)/shard_map/ppermute | solution.py:26
  45.5 31.6 %collective-permute-start.8 = (bf16[288,1056]{1,0:T(8,128)(2,1)S(1)}, bf16[288,1056]{1,0:T(8,128)(2,1)}, u32[]{:S(2)}, u32[]{:S(2)}) collective-permute-start(bf16[288,1056]{1,0:T(8,128)(2,1)S(1)} %get-tuple-element.23.own_ref), channel_id=1, source_target_pairs={{0,4},{4,8},{8,12},{1,5},{5,9},{9,13},{2,6},{6,10},{10,14},{3,7},{... | collective-permute-start | bytes 1824776 | tf_op jit(solution)/shard_map/ppermute | solution.py:26
  50.3 39.3 %collective-permute-start.11 = (bf16[416,1056]{1,0:T(8,128)(2,1)S(1)}, bf16[416,1056]{1,0:T(8,128)(2,1)}, u32[]{:S(2)}, u32[]{:S(2)}) collective-permute-start(bf16[416,1056]{1,0:T(8,128)(2,1)S(1)} %fusion.own_ref), channel_id=1, source_target_pairs={{4,0},{8,4},{12,8},{5,1},{9,5},{13,9},{6,2},{10,6},{14,10},{7,3},{... | collective-permute-start | bytes 2635784 | tf_op jit(solution)/shard_map/ppermute | solution.py:26
  51.6 38.0 %collective-permute-start.10 = (bf16[416,1056]{1,0:T(8,128)(2,1)S(1)}, bf16[416,1056]{1,0:T(8,128)(2,1)}, u32[]{:S(2)}, u32[]{:S(2)}) collective-permute-start(bf16[416,1056]{1,0:T(8,128)(2,1)S(1)} %fusion.own_ref), channel_id=1, source_target_pairs={{0,4},{4,8},{8,12},{1,5},{5,9},{9,13},{2,6},{6,10},{10,14},{3,7},{... | collective-permute-start | bytes 2635784 | tf_op jit(solution)/shard_map/ppermute | solution.py:26
  108.3 8.8 %all-to-all-start = ((f32[4,1,384]{2,1,0:T(1,128)}), f32[4,1,384]{2,1,0:T(1,128)S(1)}, u32[]{:S(2)}, u32[]{:S(2)}) async-start(f32[4,1,384]{2,1,0:T(1,128)} %reshape.79), calls=%async_computation | async-start | bytes 12288 | tf_op jit(solution)/shard_map/all_to_all | solution.py:226

commit v8 on v7

--- a/solution.py
+++ b/solution.py
@@ -266,8 +266,7 @@
     use_own = (index == 0).astype(jnp.int32)
     rows_count = (own_pad.shape[0] - (PATCH - STRIDE)) // STRIDE
     if rows_count >= 8:
-        extra = rows_count - 8
-        sizes = [1, 2, 2, 3 + extra]
+        sizes = [2, (rows_count - 2) // 2, rows_count - 2 - (rows_count - 2) // 2]
     else:
         sizes = [rows_count]
     offsets = [sum(sizes[:n]) for n in range(len(sizes))]

time: 121 us -> 112 us (0.926)
  starting transfers between devices: 33.8 us -> 28.2 us
  local copies, waits for them, and re-layouts: 12.1 us -> 10.2 us
  other arithmetic: 7.65 us -> 8.97 us
    ppermute x9 -> x7, starting transfers between devices: 27.4 us -> 21.8 us  [shifted(): lax.ppermute(value, axis, [(source, source + steps) for source in range(f...]
    ppermute x1, waiting for transfers between devices: 1.62 us -> 0.01 us  [extended_pairs(): cols_got = jnp.swapaxes(lax.ppermute(cols_send, 'tile', swap), 1, 2)]
    slice x1 -> x0, local copies, waits for them, and re-layouts: 1.39 us -> none  [body(): own_c = own_pad[start:start + count * STRIDE + PATCH - STRIDE]]
    pallas_call x4 -> x3, Pallas kernels: 48.2 us -> 47 us  [pair_flows(): pl.pallas_call(functools.partial(_flow_kernel, cols=cols, row0=row0), gri...]
    ppermute x9 -> x7, waiting for transfers between devices: 10 us -> 10.7 us  [shifted(): lax.ppermute(value, axis, [(source, source + steps) for source in range(f...]
  transfers between devices with their start and end apart: 13 -> 11, of which waited for: 3 -> 5; matrix products, arithmetic and copies ran while one was open for 13% -> 12% of each run, Pallas kernels for 26% -> 26%
where the time goes in v8:
time: 112 us
  Pallas kernels  47 us (42%)
  starting transfers between devices  28.2 us (25%)
  waiting for transfers between devices  16.2 us (14%)
  local copies, waits for them, and re-layouts  10.2 us (9%)
  other arithmetic  8.97 us (8%)
  between operations  1.13 us (1%)
    pallas_call x3, Pallas kernels, pair_flows(): pl.pallas_call(functools.partial(_flow_kernel, cols=cols, row0=row0), gri...  47 us
    ppermute x7, starting transfers between devices, shifted(): lax.ppermute(value, axis, [(source, source + steps) for source in range(f...  21.8 us
    ppermute x7, waiting for transfers between devices, shifted(): lax.ppermute(value, axis, [(source, source + steps) for source in range(f...  10.7 us
    all_to_all x1, waiting for transfers between devices, gather_sections(): return lax.all_to_all(spread, axis, 0, 0, tiled=True)  5.55 us
    concatenate x1, local copies, waits for them, and re-layouts, extended_pairs(): jnp.concatenate([keep(left, cols_got), block, keep(right, cols_got)], axi...  3.99 us
    all_to_all x1, starting transfers between devices, gather_sections(): return lax.all_to_all(spread, axis, 0, 0, tiled=True)  3.25 us
    slice x2, other arithmetic, body(): own_c = own_pad[start:start + count * STRIDE + PATCH - STRIDE]  2.76 us
    ppermute x1, starting transfers between devices, extended_pairs(): lax.ppermute(corner_send, ('tile', 'sub'), [(0, 3), (3, 0), (1, 2), (2, 1)])  2.6 us
  transfers between devices with their start and end apart: 11, of which 5 were waited for; matrix products, arithmetic and copies ran while one was open for 12% of the time, Pallas kernels for 26%

profile of v8, /device:TPU:0, one launch (start us, length us, event | category | flops | bytes accessed | tf_op | source)
XLA Modules:
  0.0 111.8 jit_solution(4128191888940226852)
XLA Ops:
  0.6 0.9 slice_select_fusion
  2.1 2.6 %collective-permute-start.1 = (bf16[1,16,16]{2,1,0:T(8,128)(2,1)S(1)}, bf16[1,16,16]{2,1,0:T(8,128)(2,1)S(1)}, u32[]{:S(2)}, u32[]{:S(2)}) collective-permute-start(bf16[1,16,16]{2,1,0:T(8,128)(2,1)S(1)} %slice_select_fusion.1), channel_id=1, source_target_pairs={{0,3},{3,0},{1,2},{2,1},{4,7},{7,4},{5,6},{6,5},{8,11},{11,8},{9,1... | collective-permute-start | bytes 1544 | tf_op jit(solution)/shard_map/ppermute | solution.py:69
  4.7 1.2 %fusion.85 = (bf16[1,1024,16]{2,1,0:T(8,128)(2,1)S(1)}, bf16[1,1024,16]{2,1,0:T(8,128)(2,1)S(1)}) fusion(bf16[1,1024,1024]{2,1,0:T(8,128)(2,1)} %param.3), kind=kLoop, calls=%fused_computation.164 | loop fusion | bytes 131072 | tf_op jit(solution)/shard_map/slice | solution.py:64
  6.2 1.3 %collective-permute-start = (s32[1,8,8]{2,0,1:T(1,128)}, s32[1,8,8]{2,0,1:T(1,128)S(1)}, u32[]{:S(2)}, u32[]{:S(2)}) collective-permute-start(s32[1,8,8]{2,0,1:T(1,128)} %bitcast.71), channel_id=1, source_target_pairs={{4,0},{8,4},{12,8},{5,1},{9,5},{13,9},{6,2},{10,6},{14,10},{7,3},{... | collective-permute-start | bytes 776 | tf_op jit(solution)/shard_map/ppermute | solution.py:26
  7.5 0.7 negate_convert_fusion
  8.2 0.7 fusion.77
  8.9 0.7 convert_multiply_fusion
  9.6 0.7 fusion.70
  10.7 4.0 %concatenate.38 = bf16[1,1024,1056]{2,1,0:T(8,128)(2,1)} concatenate(bf16[1,1024,16]{2,1,0:T(8,128)(2,1)S(1)} %copy.71, bf16[1,1024,1024]{2,1,0:T(8,128)(2,1)S(1)} %copy-done, bf16[1,1024,16]{2,1,0:T(8,128)(2,1)S(1)} %copy.72), dimensions={2} | concatenate | bytes 4325376 | tf_op jit(solution)/shard_map/concatenate | solution.py:76
  14.8 1.1 %fusion.1.own_ref = bf16[288,1056]{1,0:T(8,128)(2,1)S(1)} fusion(bf16[1,1024,1056]{2,1,0:T(8,128)(2,1)} %concatenate.38, bf16[1,16,1056]{2,1,0:T(8,128)(2,1)S(1)} %concatenate.37), kind=kLoop, calls=%fused_computation.4 | loop fusion | flops 1216512 | bytes 2804736 | tf_op jit(solution)/shard_map/slice | solution.py:283
  16.0 5.5 %collective-permute-start.4 = (bf16[288,1056]{1,0:T(8,128)(2,1)S(1)}, bf16[288,1056]{1,0:T(8,128)(2,1)}, u32[]{:S(2)}, u32[]{:S(2)}) collective-permute-start(bf16[288,1056]{1,0:T(8,128)(2,1)S(1)} %fusion.1.own_ref), channel_id=1, source_target_pairs={{0,4},{4,8},{8,12},{1,5},{5,9},{9,13},{2,6},{6,10},{10,14},{3,7},{... | collective-permute-start | bytes 1824776 | tf_op jit(solution)/shard_map/ppermute | solution.py:26
  21.4 1.3 %collective-permute-start.5 = (bf16[288,1056]{1,0:T(8,128)(2,1)S(1)}, bf16[288,1056]{1,0:T(8,128)(2,1)}, u32[]{:S(2)}, u32[]{:S(2)}) collective-permute-start(bf16[288,1056]{1,0:T(8,128)(2,1)S(1)} %fusion.1.own_ref), channel_id=1, source_target_pairs={{4,0},{8,4},{12,8},{5,1},{9,5},{13,9},{6,2},{10,6},{14,10},{7,3},{... | collective-permute-start | bytes 1824776 | tf_op jit(solution)/shard_map/ppermute | solution.py:26
  22.8 1.6 %slice_bitcast_fusion = (bf16[416,1056]{1,0:T(8,128)(2,1)S(1)}, bf16[416,1056]{1,0:T(8,128)(2,1)S(1)}) fusion(bf16[1,1024,1056]{2,1,0:T(8,128)(2,1)} %concatenate.38, bf16[1,16,1056]{2,1,0:T(8,128)(2,1)S(1)} %concatenate.44), kind=kLoop, calls=%fused_computation.2 | loop fusion | flops 1757184 | bytes 5108736 | tf_op jit(solution)/shard_map/slice | solution.py:283
  24.5 5.5 %collective-permute-start.6 = (bf16[416,1056]{1,0:T(8,128)(2,1)S(1)}, bf16[416,1056]{1,0:T(8,128)(2,1)}, u32[]{:S(2)}, u32[]{:S(2)}) collective-permute-start(bf16[416,1056]{1,0:T(8,128)(2,1)S(1)} %get-tuple-element.22.own_ref), channel_id=1, source_target_pairs={{0,4},{4,8},{8,12},{1,5},{5,9},{9,13},{2,6},{6,10},{10,14},{3,7},{... | collective-permute-start | bytes 2635784 | tf_op jit(solution)/shard_map/ppermute | solution.py:26
  30.0 1.3 %collective-permute-start.7 = (bf16[416,1056]{1,0:T(8,128)(2,1)S(1)}, bf16[416,1056]{1,0:T(8,128)(2,1)}, u32[]{:S(2)}, u32[]{:S(2)}) collective-permute-start(bf16[416,1056]{1,0:T(8,128)(2,1)S(1)} %get-tuple-element.22.own_ref), channel_id=1, source_target_pairs={{4,0},{8,4},{12,8},{5,1},{9,5},{13,9},{6,2},{10,6},{14,10},{7,3},{... | collective-permute-start | bytes 2635784 | tf_op jit(solution)/shard_map/ppermute | solution.py:26
  31.5 5.5 %collective-permute-start.8 = (bf16[416,1056]{1,0:T(8,128)(2,1)S(1)}, bf16[416,1056]{1,0:T(8,128)(2,1)}, u32[]{:S(2)}, u32[]{:S(2)}) collective-permute-start(bf16[416,1056]{1,0:T(8,128)(2,1)S(1)} %get-tuple-element.23.own_ref), channel_id=1, source_target_pairs={{0,4},{4,8},{8,12},{1,5},{5,9},{9,13},{2,6},{6,10},{10,14},{3,7},{... | collective-permute-start | bytes 2635784 | tf_op jit(solution)/shard_map/ppermute | solution.py:26
  37.0 1.5 %collective-permute-start.9 = (bf16[416,1056]{1,0:T(8,128)(2,1)S(1)}, bf16[416,1056]{1,0:T(8,128)(2,1)}, u32[]{:S(2)}, u32[]{:S(2)}) collective-permute-start(bf16[416,1056]{1,0:T(8,128)(2,1)S(1)} %get-tuple-element.23.own_ref), channel_id=1, source_target_pairs={{4,0},{8,4},{12,8},{5,1},{9,5},{13,9},{6,2},{10,6},{14,10},{7,3},{... | collective-permute-start | bytes 2635784 | tf_op jit(solution)/shard_map/ppermute | solution.py:26
  38.5 0.5 broadcast.129
  39.0 0.7 reduce.3
  39.8 1.5 %collective-permute-done.5.next_ref = bf16[288,1056]{1,0:T(8,128)(2,1)} collective-permute-done((bf16[288,1056]{1,0:T(8,128)(2,1)S(1)}, bf16[288,1056]{1,0:T(8,128)(2,1)}, u32[]{:S(2)}, u32[]{:S(2)}) %collective-permute-start.5) | collective-permute-done | bytes 608288 | tf_op jit(solution)/shard_map/ppermute | solution.py:26
  41.3 12.1 %shard_map.50 = f32[2,8,128]{2,1,0:T(8,128)S(1)} custom-call(s32[64]{0:T(128)S(1)} %reshape.46.skip_ref, s32[64]{0:T(128)S(1)} %reshape.47.skip_next_ref, s32[1]{0:T(128)} %bitcast.2.flag_ref, bf16[288,1056]{1,0:T(8,128)(2,1)S(1)} %fusion.1.own_ref, bf16[288,1056]{1,0:T(8,128)(2,1)} %collective-permute-done.4.prev_ref, ...), custom_call_target="tpu_custom_call" | custom-call | tf_op jit(solution)/shard_map/pallas_call | solution.py:209
  53.9 2.5 %collective-permute-done.6.prev_ref = bf16[416,1056]{1,0:T(8,128)(2,1)} collective-permute-done((bf16[416,1056]{1,0:T(8,128)(2,1)S(1)}, bf16[416,1056]{1,0:T(8,128)(2,1)}, u32[]{:S(2)}, u32[]{:S(2)}) %collective-permute-start.6) | collective-permute-done | bytes 878624 | tf_op jit(solution)/shard_map/ppermute | solution.py:26
  56.4 5.4 %collective-permute-done.7.next_ref = bf16[416,1056]{1,0:T(8,128)(2,1)} collective-permute-done((bf16[416,1056]{1,0:T(8,128)(2,1)S(1)}, bf16[416,1056]{1,0:T(8,128)(2,1)}, u32[]{:S(2)}, u32[]{:S(2)}) %collective-permute-start.7) | collective-permute-done | bytes 878624 | tf_op jit(solution)/shard_map/ppermute | solution.py:26
  61.8 17.3 %shard_map.51 = f32[3,8,128]{2,1,0:T(8,128)S(1)} custom-call(s32[64]{0:T(128)S(1)} %reshape.46.skip_ref, s32[64]{0:T(128)S(1)} %reshape.47.skip_next_ref, s32[1]{0:T(128)} %bitcast.2.flag_ref, bf16[416,1056]{1,0:T(8,128)(2,1)S(1)} %get-tuple-element.22.own_ref, bf16[416,1056]{1,0:T(8,128)(2,1)} %collective-permute-done.6.prev_ref, ...), custom_call_target="tpu_custom_call" | custom-call | tf_op jit(solution)/shard_map/pallas_call | solution.py:209
  79.4 1.3 %collective-permute-done.9.next_ref = bf16[416,1056]{1,0:T(8,128)(2,1)} collective-permute-done((bf16[416,1056]{1,0:T(8,128)(2,1)S(1)}, bf16[416,1056]{1,0:T(8,128)(2,1)}, u32[]{:S(2)}, u32[]{:S(2)}) %collective-permute-start.9) | collective-permute-done | bytes 878624 | tf_op jit(solution)/shard_map/ppermute | solution.py:26
  80.8 17.6 %shard_map.52 = f32[3,8,128]{2,1,0:T(8,128)S(1)} custom-call(s32[64]{0:T(128)S(1)} %reshape.46.skip_ref, s32[64]{0:T(128)S(1)} %reshape.47.skip_next_ref, s32[1]{0:T(128)} %bitcast.2.flag_ref, bf16[416,1056]{1,0:T(8,128)(2,1)S(1)} %get-tuple-element.23.own_ref, bf16[416,1056]{1,0:T(8,128)(2,1)} %collective-permute-done.8.prev_ref, ...), custom_call_target="tpu_custom_call" | custom-call | tf_op jit(solution)/shard_map/pallas_call | solution.py:209
  99.3 0.7 reshape.67
  100.0 3.2 %all-to-all-start = ((f32[4,1,384]{2,1,0:T(1,128)}), f32[4,1,384]{2,1,0:T(1,128)S(1)}, u32[]{:S(2)}, u32[]{:S(2)}) async-start(f32[4,1,384]{2,1,0:T(1,128)} %reshape.67), calls=%async_computation | async-start | bytes 12288 | tf_op jit(solution)/shard_map/all_to_all | solution.py:226
  103.2 5.6 %all-to-all-done = f32[4,1,384]{2,1,0:T(1,128)S(1)} async-done(((f32[4,1,384]{2,1,0:T(1,128)}), f32[4,1,384]{2,1,0:T(1,128)S(1)}, u32[]{:S(2)}, u32[]{:S(2)}) %all-to-all-start) | async-done | bytes 6176 | tf_op jit(solution)/shard_map/all_to_all | solution.py:226
  109.3 0.7 reduce.4
  110.2 0.6 dynamic-slice_bitcast_fusion
  111.2 0.6 fusion.74
  (89 shorter events, 4.4 us)
Async XLA Ops:
  0.6 10.1 %copy-start = (bf16[1,1024,1024]{2,1,0:T(8,128)(2,1)S(1)}, bf16[1,1024,1024]{2,1,0:T(8,128)(2,1)}, u32[]{:S(2)}) copy-start(bf16[1,1024,1024]{2,1,0:T(8,128)(2,1)} %param.3) | copy-start | bytes 6291460
  1.6 13.1 %collective-permute-start.2 = (bf16[1,16,1024]{2,1,0:T(8,128)(2,1)S(1)}, bf16[1,16,1024]{2,1,0:T(8,128)(2,1)S(1)}, u32[]{:S(2)}, u32[]{:S(2)}) collective-permute-start(bf16[1,16,1024]{2,1,0:T(8,128)(2,1)S(1)} %slice_select_fusion), channel_id=1, source_target_pairs={{0,1},{1,0},{2,3},{3,2},{4,5},{5,4},{6,7},{7,6},{8,9},{9,8},{10,11... | collective-permute-start | bytes 98312 | tf_op jit(solution)/shard_map/ppermute | solution.py:67
  2.1 8.2 %collective-permute-start.1 = (bf16[1,16,16]{2,1,0:T(8,128)(2,1)S(1)}, bf16[1,16,16]{2,1,0:T(8,128)(2,1)S(1)}, u32[]{:S(2)}, u32[]{:S(2)}) collective-permute-start(bf16[1,16,16]{2,1,0:T(8,128)(2,1)S(1)} %slice_select_fusion.1), channel_id=1, source_target_pairs={{0,3},{3,0},{1,2},{2,1},{4,7},{7,4},{5,6},{6,5},{8,11},{11,8},{9,1... | collective-permute-start | bytes 1544 | tf_op jit(solution)/shard_map/ppermute | solution.py:69
  6.1 4.2 %collective-permute-start.3 = (bf16[1,16,1024]{2,1,0:T(8,128)(2,1)S(1)}, bf16[1,16,1024]{2,1,0:T(8,128)(2,1)S(1)}, u32[]{:S(2)}, u32[]{:S(2)}) collective-permute-start(bf16[1,16,1024]{2,1,0:T(8,128)(2,1)S(1)} %select_bitcast_fusion.2), channel_id=1, source_target_pairs={{0,2},{2,0},{1,3},{3,1},{4,6},{6,4},{5,7},{7,5},{8,10},{10,8},{9,1... | collective-permute-start | bytes 98312 | tf_op jit(solution)/shard_map/ppermute | solution.py:68
  6.2 25.3 %collective-permute-start = (s32[1,8,8]{2,0,1:T(1,128)}, s32[1,8,8]{2,0,1:T(1,128)S(1)}, u32[]{:S(2)}, u32[]{:S(2)}) collective-permute-start(s32[1,8,8]{2,0,1:T(1,128)} %bitcast.71), channel_id=1, source_target_pairs={{4,0},{8,4},{12,8},{5,1},{9,5},{13,9},{6,2},{10,6},{14,10},{7,3},{... | collective-permute-start | bytes 776 | tf_op jit(solution)/shard_map/ppermute | solution.py:26
  16.0 21.1 %collective-permute-start.4 = (bf16[288,1056]{1,0:T(8,128)(2,1)S(1)}, bf16[288,1056]{1,0:T(8,128)(2,1)}, u32[]{:S(2)}, u32[]{:S(2)}) collective-permute-start(bf16[288,1056]{1,0:T(8,128)(2,1)S(1)} %fusion.1.own_ref), channel_id=1, source_target_pairs={{0,4},{4,8},{8,12},{1,5},{5,9},{9,13},{2,6},{6,10},{10,14},{3,7},{... | collective-permute-start | bytes 1824776 | tf_op jit(solution)/shard_map/ppermute | solution.py:26
  21.4 19.8 %collective-permute-start.5 = (bf16[288,1056]{1,0:T(8,128)(2,1)S(1)}, bf16[288,1056]{1,0:T(8,128)(2,1)}, u32[]{:S(2)}, u32[]{:S(2)}) collective-permute-start(bf16[288,1056]{1,0:T(8,128)(2,1)S(1)} %fusion.1.own_ref), channel_id=1, source_target_pairs={{4,0},{8,4},{12,8},{5,1},{9,5},{13,9},{6,2},{10,6},{14,10},{7,3},{... | collective-permute-start | bytes 1824776 | tf_op jit(solution)/shard_map/ppermute | solution.py:26
  22.8 8.6 %copy-start.1 = (s32[1,8,8]{2,1,0:T(8,128)S(1)}, s32[1,8,8]{2,1,0:T(8,128)}, u32[]{:S(2)}) copy-start(s32[1,8,8]{2,1,0:T(8,128)} %param.4) | copy-start | bytes 772
  24.5 32.0 %collective-permute-start.6 = (bf16[416,1056]{1,0:T(8,128)(2,1)S(1)}, bf16[416,1056]{1,0:T(8,128)(2,1)}, u32[]{:S(2)}, u32[]{:S(2)}) collective-permute-start(bf16[416,1056]{1,0:T(8,128)(2,1)S(1)} %get-tuple-element.22.own_ref), channel_id=1, source_target_pairs={{0,4},{4,8},{8,12},{1,5},{5,9},{9,13},{2,6},{6,10},{10,14},{3,7},{... | collective-permute-start | bytes 2635784 | tf_op jit(solution)/shard_map/ppermute | solution.py:26
  30.0 31.8 %collective-permute-start.7 = (bf16[416,1056]{1,0:T(8,128)(2,1)S(1)}, bf16[416,1056]{1,0:T(8,128)(2,1)}, u32[]{:S(2)}, u32[]{:S(2)}) collective-permute-start(bf16[416,1056]{1,0:T(8,128)(2,1)S(1)} %get-tuple-element.22.own_ref), channel_id=1, source_target_pairs={{4,0},{8,4},{12,8},{5,1},{9,5},{13,9},{6,2},{10,6},{14,10},{7,3},{... | collective-permute-start | bytes 2635784 | tf_op jit(solution)/shard_map/ppermute | solution.py:26
  31.5 47.9 %collective-permute-start.8 = (bf16[416,1056]{1,0:T(8,128)(2,1)S(1)}, bf16[416,1056]{1,0:T(8,128)(2,1)}, u32[]{:S(2)}, u32[]{:S(2)}) collective-permute-start(bf16[416,1056]{1,0:T(8,128)(2,1)S(1)} %get-tuple-element.23.own_ref), channel_id=1, source_target_pairs={{0,4},{4,8},{8,12},{1,5},{5,9},{9,13},{2,6},{6,10},{10,14},{3,7},{... | collective-permute-start | bytes 2635784 | tf_op jit(solution)/shard_map/ppermute | solution.py:26
  37.0 43.7 %collective-permute-start.9 = (bf16[416,1056]{1,0:T(8,128)(2,1)S(1)}, bf16[416,1056]{1,0:T(8,128)(2,1)}, u32[]{:S(2)}, u32[]{:S(2)}) collective-permute-start(bf16[416,1056]{1,0:T(8,128)(2,1)S(1)} %get-tuple-element.23.own_ref), channel_id=1, source_target_pairs={{4,0},{8,4},{12,8},{5,1},{9,5},{13,9},{6,2},{10,6},{14,10},{7,3},{... | collective-permute-start | bytes 2635784 | tf_op jit(solution)/shard_map/ppermute | solution.py:26
  100.0 8.8 %all-to-all-start = ((f32[4,1,384]{2,1,0:T(1,128)}), f32[4,1,384]{2,1,0:T(1,128)S(1)}, u32[]{:S(2)}, u32[]{:S(2)}) async-start(f32[4,1,384]{2,1,0:T(1,128)} %reshape.67), calls=%async_computation | async-start | bytes 12288 | tf_op jit(solution)/shard_map/all_to_all | solution.py:226

commit v9 on v6

--- a/solution.py
+++ b/solution.py
@@ -262,7 +262,6 @@
         own_pad = extended_pairs(images, RIM)[0]
     else:
         own_pad = extended(images, (("sub", 1), ("tile", 2)), RIM)[0]
-    skip_next = shifted(skipped, "sec", -1)
     use_own = (index == 0).astype(jnp.int32)
     rows_count = (own_pad.shape[0] - (PATCH - STRIDE)) // STRIDE
     chunks = max(n for n in (1, 2, 4) if rows_count % n == 0)
@@ -273,13 +272,25 @@
     )
     tables = (jnp.concatenate([cos_t, sin_t], axis=0), cos_t, sin_t, inverse_t)
     skip_flat = skipped.reshape(-1)
-    skip_next_flat = skip_next.reshape(-1)
+    broad = own_pad.shape[1]
+    cols_count = (broad - (PATCH - STRIDE)) // STRIDE
+    riding = rows_count <= 16
+    if not riding:
+        skip_next = shifted(skipped, "sec", -1)
     firsts, seconds = [], []
     for c in range(chunks):
         start = c * per * STRIDE
         own_c = own_pad[start : start + per * STRIDE + PATCH - STRIDE]
+        if c == 0 and riding:
+            flags = jnp.zeros((16, broad), jnp.bfloat16)
+            flags = lax.dynamic_update_slice(flags, skipped[0].astype(jnp.bfloat16), (0, 0))
+            own_c = jnp.concatenate([own_c, flags], axis=0)
         prev_c = shifted(own_c, "sec", 1)
         next_c = shifted(own_c, "sec", -1)
+        if c == 0 and riding:
+            tall_c = own_c.shape[0] - 16
+            skip_next = next_c[tall_c : tall_c + rows_count, :cols_count].astype(jnp.int32)[None]
+        skip_next_flat = skip_next.reshape(-1)
         first_c, second_c = pair_flows(
             own_c, prev_c, next_c, skip_flat, skip_next_flat, use_own, c * per, tables
         )

time: 111 us -> 112 us (level)
  other arithmetic: 7.42 us -> 8.92 us
    ppermute x1, waiting for transfers between devices: 1.2 us -> 2.42 us  [extended_pairs(): cols_got = jnp.swapaxes(lax.ppermute(cols_send, 'tile', swap), 1, 2)]
    ppermute x9 -> x8, starting transfers between devices: 25.7 us -> 24.6 us  [shifted(): lax.ppermute(value, axis, [(source, source + steps) for source in range(f...]
    ppermute x9 -> x8, waiting for transfers between devices: 3.45 us -> 2.36 us  [shifted(): lax.ppermute(value, axis, [(source, source + steps) for source in range(f...]
  transfers between devices with their start and end apart: 13 -> 12, of which waited for: 3 -> 4; matrix products, arithmetic and copies ran while one was open for 11% -> 9% of each run, Pallas kernels for 32% -> 32%
where the time goes in v9:
time: 112 us
  Pallas kernels  48.2 us (43%)
  starting transfers between devices  32.8 us (29%)
  waiting for transfers between devices  10.4 us (9%)
  local copies, waits for them, and re-layouts  10.1 us (9%)
  other arithmetic  8.92 us (8%)
    pallas_call x4, Pallas kernels, pair_flows(): pl.pallas_call(functools.partial(_flow_kernel, cols=cols, row0=row0), gri...  48.2 us
    ppermute x8, starting transfers between devices, shifted(): lax.ppermute(value, axis, [(source, source + steps) for source in range(f...  24.6 us
    all_to_all x1, waiting for transfers between devices, gather_sections(): return lax.all_to_all(spread, axis, 0, 0, tiled=True)  5.58 us
    all_to_all x1, starting transfers between devices, gather_sections(): return lax.all_to_all(spread, axis, 0, 0, tiled=True)  5.09 us
    concatenate x1, local copies, waits for them, and re-layouts, extended_pairs(): jnp.concatenate([keep(left, cols_got), block, keep(right, cols_got)], axi...  3.96 us
    ppermute x1, starting transfers between devices, extended_pairs(): lax.ppermute(corner_send, ('tile', 'sub'), [(0, 3), (3, 0), (1, 2), (2, 1)])  2.6 us
    ppermute x1, waiting for transfers between devices, extended_pairs(): cols_got = jnp.swapaxes(lax.ppermute(cols_send, 'tile', swap), 1, 2)  2.42 us
    ppermute x8, waiting for transfers between devices, shifted(): lax.ppermute(value, axis, [(source, source + steps) for source in range(f...  2.36 us
  transfers between devices with their start and end apart: 12, of which 4 were waited for; matrix products, arithmetic and copies ran while one was open for 9% of the time, Pallas kernels for 32%

profile of v9, /device:TPU:0, one launch (start us, length us, event | category | flops | bytes accessed | tf_op | source)
XLA Modules:
  0.0 111.6 jit_solution(2068479675354546230)
XLA Ops:
  0.6 0.9 slice_select_fusion
  2.1 2.6 %collective-permute-start = (bf16[1,16,16]{2,1,0:T(8,128)(2,1)S(1)}, bf16[1,16,16]{2,1,0:T(8,128)(2,1)S(1)}, u32[]{:S(2)}, u32[]{:S(2)}) collective-permute-start(bf16[1,16,16]{2,1,0:T(8,128)(2,1)S(1)} %slice_select_fusion.1), channel_id=1, source_target_pairs={{0,3},{3,0},{1,2},{2,1},{4,7},{7,4},{5,6},{6,5},{8,11},{11,8},{9,1... | collective-permute-start | bytes 1544 | tf_op jit(solution)/shard_map/ppermute | solution.py:69
  4.7 1.2 %fusion.86 = (bf16[1,1024,16]{2,1,0:T(8,128)(2,1)S(1)}, bf16[1,1024,16]{2,1,0:T(8,128)(2,1)S(1)}) fusion(bf16[1,1024,1024]{2,1,0:T(8,128)(2,1)} %param.3), kind=kLoop, calls=%fused_computation.170 | loop fusion | bytes 131072 | tf_op jit(solution)/shard_map/slice | solution.py:64
  6.2 0.7 convert_multiply_fusion
  6.9 0.8 convert_bitcast_fusion.1
  7.7 2.4 %collective-permute-done.2 = bf16[1,16,1024]{2,1,0:T(8,128)(2,1)S(1)} collective-permute-done((bf16[1,16,1024]{2,1,0:T(8,128)(2,1)S(1)}, bf16[1,16,1024]{2,1,0:T(8,128)(2,1)S(1)}, u32[]{:S(2)}, u32[]{:S(2)}) %collective-permute-start.2) | collective-permute-done | bytes 32800 | tf_op jit(solution)/shard_map/ppermute | solution.py:68
  10.5 4.0 %concatenate.41 = bf16[1,1024,1056]{2,1,0:T(8,128)(2,1)} concatenate(bf16[1,1024,16]{2,1,0:T(8,128)(2,1)S(1)} %copy.31, bf16[1,1024,1024]{2,1,0:T(8,128)(2,1)S(1)} %copy-done, bf16[1,1024,16]{2,1,0:T(8,128)(2,1)S(1)} %copy.32), dimensions={2} | concatenate | bytes 4325376 | tf_op jit(solution)/shard_map/concatenate | solution.py:76
  14.7 1.9 %slice_bitcast_fusion.1 = (bf16[288,1056]{1,0:T(8,128)(2,1)S(1)}, bf16[288,1056]{1,0:T(8,128)(2,1)S(1)}, bf16[288,1056]{1,0:T(8,128)(2,1)S(1)}, bf16[288,1056]{1,0:T(8,128)(2,1)S(1)}) fusion(bf16[1,1024,1056]{2,1,0:T(8,128)(2,1)} %concatenate.41, bf16[1,16,1056]{2,1,0:T(8,128)(2,1)S(1)} %concatenate.40, bf16[1,16,1056]{2,1,0:T(8,128)(2,1)S(1)} %concatenate.48), kind=kLoop, calls=%fused_computation.6 | loop fusion | flops 2433024 | bytes 6187008 | tf_op jit(solution)/shard_map/slice | solution.py:283
  16.6 1.3 %collective-permute-start.3 = (bf16[304,1056]{1,0:T(8,128)(2,1)S(1)}, bf16[304,1056]{1,0:T(8,128)(2,1)}, u32[]{:S(2)}, u32[]{:S(2)}) collective-permute-start(bf16[304,1056]{1,0:T(8,128)(2,1)S(1)} %fusion.1.own_ref), channel_id=1, source_target_pairs={{4,0},{8,4},{12,8},{5,1},{9,5},{13,9},{6,2},{10,6},{14,10},{7,3},{... | collective-permute-start | bytes 1926152 | tf_op jit(solution)/shard_map/ppermute | solution.py:26
  18.0 5.4 %collective-permute-start.4 = (bf16[304,1056]{1,0:T(8,128)(2,1)S(1)}, bf16[304,1056]{1,0:T(8,128)(2,1)}, u32[]{:S(2)}, u32[]{:S(2)}) collective-permute-start(bf16[304,1056]{1,0:T(8,128)(2,1)S(1)} %fusion.1.own_ref), channel_id=1, source_target_pairs={{0,4},{4,8},{8,12},{1,5},{5,9},{9,13},{2,6},{6,10},{10,14},{3,7},{... | collective-permute-start | bytes 1926152 | tf_op jit(solution)/shard_map/ppermute | solution.py:26
  23.4 3.4 %collective-permute-start.5 = (bf16[288,1056]{1,0:T(8,128)(2,1)S(1)}, bf16[288,1056]{1,0:T(8,128)(2,1)}, u32[]{:S(2)}, u32[]{:S(2)}) collective-permute-start(bf16[288,1056]{1,0:T(8,128)(2,1)S(1)} %get-tuple-element.20.own_ref), channel_id=1, source_target_pairs={{0,4},{4,8},{8,12},{1,5},{5,9},{9,13},{2,6},{6,10},{10,14},{3,7},{... | collective-permute-start | bytes 1824776 | tf_op jit(solution)/shard_map/ppermute | solution.py:26
  26.8 0.7 negate_convert_fusion
  27.6 1.3 %collective-permute-start.6 = (bf16[288,1056]{1,0:T(8,128)(2,1)S(1)}, bf16[288,1056]{1,0:T(8,128)(2,1)}, u32[]{:S(2)}, u32[]{:S(2)}) collective-permute-start(bf16[288,1056]{1,0:T(8,128)(2,1)S(1)} %get-tuple-element.20.own_ref), channel_id=1, source_target_pairs={{4,0},{8,4},{12,8},{5,1},{9,5},{13,9},{6,2},{10,6},{14,10},{7,3},{... | collective-permute-start | bytes 1824776 | tf_op jit(solution)/shard_map/ppermute | solution.py:26
  28.9 0.7 fusion.72
  29.7 5.4 %collective-permute-start.7 = (bf16[288,1056]{1,0:T(8,128)(2,1)S(1)}, bf16[288,1056]{1,0:T(8,128)(2,1)}, u32[]{:S(2)}, u32[]{:S(2)}) collective-permute-start(bf16[288,1056]{1,0:T(8,128)(2,1)S(1)} %get-tuple-element.22.own_ref), channel_id=1, source_target_pairs={{0,4},{4,8},{8,12},{1,5},{5,9},{9,13},{2,6},{6,10},{10,14},{3,7},{... | collective-permute-start | bytes 1824776 | tf_op jit(solution)/shard_map/ppermute | solution.py:26
  35.1 2.1 %collective-permute-done.3.next_ref = bf16[304,1056]{1,0:T(8,128)(2,1)} collective-permute-done((bf16[304,1056]{1,0:T(8,128)(2,1)S(1)}, bf16[304,1056]{1,0:T(8,128)(2,1)}, u32[]{:S(2)}, u32[]{:S(2)}) %collective-permute-start.3) | collective-permute-done | bytes 642080 | tf_op jit(solution)/shard_map/ppermute | solution.py:26
  37.3 1.3 %collective-permute-start.8 = (bf16[288,1056]{1,0:T(8,128)(2,1)S(1)}, bf16[288,1056]{1,0:T(8,128)(2,1)}, u32[]{:S(2)}, u32[]{:S(2)}) collective-permute-start(bf16[288,1056]{1,0:T(8,128)(2,1)S(1)} %get-tuple-element.22.own_ref), channel_id=1, source_target_pairs={{4,0},{8,4},{12,8},{5,1},{9,5},{13,9},{6,2},{10,6},{14,10},{7,3},{... | collective-permute-start | bytes 1824776 | tf_op jit(solution)/shard_map/ppermute | solution.py:26
  38.6 0.7 slice_convert_fusion
  39.3 1.3 %collective-permute-start.10 = (bf16[288,1056]{1,0:T(8,128)(2,1)S(1)}, bf16[288,1056]{1,0:T(8,128)(2,1)}, u32[]{:S(2)}, u32[]{:S(2)}) collective-permute-start(bf16[288,1056]{1,0:T(8,128)(2,1)S(1)} %get-tuple-element.23.own_ref), channel_id=1, source_target_pairs={{4,0},{8,4},{12,8},{5,1},{9,5},{13,9},{6,2},{10,6},{14,10},{7,3},{... | collective-permute-start | bytes 1824776 | tf_op jit(solution)/shard_map/ppermute | solution.py:26
  40.6 12.0 %shard_map.50 = f32[2,8,128]{2,1,0:T(8,128)S(1)} custom-call(s32[64]{0:T(128)S(1)} %reshape.50.skip_ref, s32[64]{0:T(128)S(1)} %reshape_broadcast_in_dim.2.skip_next_ref, s32[1]{0:T(128)} %bitcast.6.flag_ref, bf16[304,1056]{1,0:T(8,128)(2,1)S(1)} %fusion.1.own_ref, bf16[304,1056]{1,0:T(8,128)(2,1)} %collective-permute-done.4.prev_ref, ...), custom_call_target="tpu_custom_call" | custom-call | tf_op jit(solution)/shard_map/pallas_call | solution.py:209
  52.9 5.2 %collective-permute-start.9 = (bf16[288,1056]{1,0:T(8,128)(2,1)S(1)}, bf16[288,1056]{1,0:T(8,128)(2,1)S(1)}, u32[]{:S(2)}, u32[]{:S(2)}) collective-permute-start(bf16[288,1056]{1,0:T(8,128)(2,1)S(1)} %get-tuple-element.23.own_ref), channel_id=1, source_target_pairs={{0,4},{4,8},{8,12},{1,5},{5,9},{9,13},{2,6},{6,10},{10,14},{3,7},{... | collective-permute-start | bytes 1824776 | tf_op jit(solution)/shard_map/ppermute | solution.py:26
  58.3 12.0 %shard_map.51 = f32[2,8,128]{2,1,0:T(8,128)S(1)} custom-call(s32[64]{0:T(128)S(1)} %reshape.50.skip_ref, s32[64]{0:T(128)S(1)} %reshape_broadcast_in_dim.2.skip_next_ref, s32[1]{0:T(128)} %bitcast.6.flag_ref, bf16[288,1056]{1,0:T(8,128)(2,1)S(1)} %get-tuple-element.20.own_ref, bf16[288,1056]{1,0:T(8,128)(2,1)} %collective-permute-done.5.prev_ref, ...), custom_call_target="tpu_custom_call" | custom-call | tf_op jit(solution)/shard_map/pallas_call | solution.py:209
  70.6 12.1 %shard_map.52 = f32[2,8,128]{2,1,0:T(8,128)S(1)} custom-call(s32[64]{0:T(128)S(1)} %reshape.50.skip_ref, s32[64]{0:T(128)S(1)} %reshape_broadcast_in_dim.2.skip_next_ref, s32[1]{0:T(128)} %bitcast.6.flag_ref, bf16[288,1056]{1,0:T(8,128)(2,1)S(1)} %get-tuple-element.22.own_ref, bf16[288,1056]{1,0:T(8,128)(2,1)} %collective-permute-done.7.prev_ref, ...), custom_call_target="tpu_custom_call" | custom-call | tf_op jit(solution)/shard_map/pallas_call | solution.py:209
  83.0 12.1 %shard_map.53 = f32[2,8,128]{2,1,0:T(8,128)S(1)} custom-call(s32[64]{0:T(128)S(1)} %reshape.50.skip_ref, s32[64]{0:T(128)S(1)} %reshape_broadcast_in_dim.2.skip_next_ref, s32[1]{0:T(128)} %bitcast.6.flag_ref, bf16[288,1056]{1,0:T(8,128)(2,1)S(1)} %get-tuple-element.23.own_ref, bf16[288,1056]{1,0:T(8,128)(2,1)S(1)} %collective-permute-done.9.prev_ref, ...), custom_call_target="tpu_custom_call" | custom-call | tf_op jit(solution)/shard_map/pallas_call | solution.py:209
  96.4 0.7 broadcast_compare_fusion
  97.2 0.7 reshape.63
  97.9 5.1 %all-to-all-start = ((f32[4,1,384]{2,1,0:T(1,128)}), f32[4,1,384]{2,1,0:T(1,128)S(1)}, u32[]{:S(2)}, u32[]{:S(2)}) async-start(f32[4,1,384]{2,1,0:T(1,128)} %reshape.63), calls=%async_computation | async-start | bytes 12288 | tf_op jit(solution)/shard_map/all_to_all | solution.py:226
  103.0 5.6 %all-to-all-done = f32[4,1,384]{2,1,0:T(1,128)S(1)} async-done(((f32[4,1,384]{2,1,0:T(1,128)}), f32[4,1,384]{2,1,0:T(1,128)S(1)}, u32[]{:S(2)}, u32[]{:S(2)}) %all-to-all-start) | async-done | bytes 6176 | tf_op jit(solution)/shard_map/all_to_all | solution.py:226
  108.6 0.5 broadcast.133
  109.1 0.7 reduce
  110.0 0.6 dynamic-slice_bitcast_fusion
  111.0 0.6 fusion.76
  (93 shorter events, 4.6 us)
Async XLA Ops:
  0.6 9.9 %copy-start = (bf16[1,1024,1024]{2,1,0:T(8,128)(2,1)S(1)}, bf16[1,1024,1024]{2,1,0:T(8,128)(2,1)}, u32[]{:S(2)}) copy-start(bf16[1,1024,1024]{2,1,0:T(8,128)(2,1)} %param.3) | copy-start | bytes 6291460
  1.6 12.9 %collective-permute-start.1 = (bf16[1,16,1024]{2,1,0:T(8,128)(2,1)S(1)}, bf16[1,16,1024]{2,1,0:T(8,128)(2,1)S(1)}, u32[]{:S(2)}, u32[]{:S(2)}) collective-permute-start(bf16[1,16,1024]{2,1,0:T(8,128)(2,1)S(1)} %slice_select_fusion), channel_id=1, source_target_pairs={{0,1},{1,0},{2,3},{3,2},{4,5},{5,4},{6,7},{7,6},{8,9},{9,8},{10,11... | collective-permute-start | bytes 98312 | tf_op jit(solution)/shard_map/ppermute | solution.py:67
  2.1 5.6 %collective-permute-start = (bf16[1,16,16]{2,1,0:T(8,128)(2,1)S(1)}, bf16[1,16,16]{2,1,0:T(8,128)(2,1)S(1)}, u32[]{:S(2)}, u32[]{:S(2)}) collective-permute-start(bf16[1,16,16]{2,1,0:T(8,128)(2,1)S(1)} %slice_select_fusion.1), channel_id=1, source_target_pairs={{0,3},{3,0},{1,2},{2,1},{4,7},{7,4},{5,6},{6,5},{8,11},{11,8},{9,1... | collective-permute-start | bytes 1544 | tf_op jit(solution)/shard_map/ppermute | solution.py:69
  6.1 4.0 %collective-permute-start.2 = (bf16[1,16,1024]{2,1,0:T(8,128)(2,1)S(1)}, bf16[1,16,1024]{2,1,0:T(8,128)(2,1)S(1)}, u32[]{:S(2)}, u32[]{:S(2)}) collective-permute-start(bf16[1,16,1024]{2,1,0:T(8,128)(2,1)S(1)} %select_bitcast_fusion.2), channel_id=1, source_target_pairs={{0,2},{2,0},{1,3},{3,1},{4,6},{6,4},{5,7},{7,5},{8,10},{10,8},{9,1... | collective-permute-start | bytes 98312 | tf_op jit(solution)/shard_map/ppermute | solution.py:68
  14.7 3.3 %copy-start.1 = (s32[1,8,8]{2,1,0:T(8,128)S(1)}, s32[1,8,8]{2,1,0:T(8,128)}, u32[]{:S(2)}) copy-start(s32[1,8,8]{2,1,0:T(8,128)} %param.4) | copy-start | bytes 772
  16.6 20.6 %collective-permute-start.3 = (bf16[304,1056]{1,0:T(8,128)(2,1)S(1)}, bf16[304,1056]{1,0:T(8,128)(2,1)}, u32[]{:S(2)}, u32[]{:S(2)}) collective-permute-start(bf16[304,1056]{1,0:T(8,128)(2,1)S(1)} %fusion.1.own_ref), channel_id=1, source_target_pairs={{4,0},{8,4},{12,8},{5,1},{9,5},{13,9},{6,2},{10,6},{14,10},{7,3},{... | collective-permute-start | bytes 1926152 | tf_op jit(solution)/shard_map/ppermute | solution.py:26
  18.0 21.4 %collective-permute-start.4 = (bf16[304,1056]{1,0:T(8,128)(2,1)S(1)}, bf16[304,1056]{1,0:T(8,128)(2,1)}, u32[]{:S(2)}, u32[]{:S(2)}) collective-permute-start(bf16[304,1056]{1,0:T(8,128)(2,1)S(1)} %fusion.1.own_ref), channel_id=1, source_target_pairs={{0,4},{4,8},{8,12},{1,5},{5,9},{9,13},{2,6},{6,10},{10,14},{3,7},{... | collective-permute-start | bytes 1926152 | tf_op jit(solution)/shard_map/ppermute | solution.py:26
  23.4 29.5 %collective-permute-start.5 = (bf16[288,1056]{1,0:T(8,128)(2,1)S(1)}, bf16[288,1056]{1,0:T(8,128)(2,1)}, u32[]{:S(2)}, u32[]{:S(2)}) collective-permute-start(bf16[288,1056]{1,0:T(8,128)(2,1)S(1)} %get-tuple-element.20.own_ref), channel_id=1, source_target_pairs={{0,4},{4,8},{8,12},{1,5},{5,9},{9,13},{2,6},{6,10},{10,14},{3,7},{... | collective-permute-start | bytes 1824776 | tf_op jit(solution)/shard_map/ppermute | solution.py:26
  27.6 30.8 %collective-permute-start.6 = (bf16[288,1056]{1,0:T(8,128)(2,1)S(1)}, bf16[288,1056]{1,0:T(8,128)(2,1)}, u32[]{:S(2)}, u32[]{:S(2)}) collective-permute-start(bf16[288,1056]{1,0:T(8,128)(2,1)S(1)} %get-tuple-element.20.own_ref), channel_id=1, source_target_pairs={{4,0},{8,4},{12,8},{5,1},{9,5},{13,9},{6,2},{10,6},{14,10},{7,3},{... | collective-permute-start | bytes 1824776 | tf_op jit(solution)/shard_map/ppermute | solution.py:26
  29.7 40.9 %collective-permute-start.7 = (bf16[288,1056]{1,0:T(8,128)(2,1)S(1)}, bf16[288,1056]{1,0:T(8,128)(2,1)}, u32[]{:S(2)}, u32[]{:S(2)}) collective-permute-start(bf16[288,1056]{1,0:T(8,128)(2,1)S(1)} %get-tuple-element.22.own_ref), channel_id=1, source_target_pairs={{0,4},{4,8},{8,12},{1,5},{5,9},{9,13},{2,6},{6,10},{10,14},{3,7},{... | collective-permute-start | bytes 1824776 | tf_op jit(solution)/shard_map/ppermute | solution.py:26
  37.3 33.4 %collective-permute-start.8 = (bf16[288,1056]{1,0:T(8,128)(2,1)S(1)}, bf16[288,1056]{1,0:T(8,128)(2,1)}, u32[]{:S(2)}, u32[]{:S(2)}) collective-permute-start(bf16[288,1056]{1,0:T(8,128)(2,1)S(1)} %get-tuple-element.22.own_ref), channel_id=1, source_target_pairs={{4,0},{8,4},{12,8},{5,1},{9,5},{13,9},{6,2},{10,6},{14,10},{7,3},{... | collective-permute-start | bytes 1824776 | tf_op jit(solution)/shard_map/ppermute | solution.py:26
  39.3 43.6 %collective-permute-start.10 = (bf16[288,1056]{1,0:T(8,128)(2,1)S(1)}, bf16[288,1056]{1,0:T(8,128)(2,1)}, u32[]{:S(2)}, u32[]{:S(2)}) collective-permute-start(bf16[288,1056]{1,0:T(8,128)(2,1)S(1)} %get-tuple-element.23.own_ref), channel_id=1, source_target_pairs={{4,0},{8,4},{12,8},{5,1},{9,5},{13,9},{6,2},{10,6},{14,10},{7,3},{... | collective-permute-start | bytes 1824776 | tf_op jit(solution)/shard_map/ppermute | solution.py:26
  52.9 30.1 %collective-permute-start.9 = (bf16[288,1056]{1,0:T(8,128)(2,1)S(1)}, bf16[288,1056]{1,0:T(8,128)(2,1)S(1)}, u32[]{:S(2)}, u32[]{:S(2)}) collective-permute-start(bf16[288,1056]{1,0:T(8,128)(2,1)S(1)} %get-tuple-element.23.own_ref), channel_id=1, source_target_pairs={{0,4},{4,8},{8,12},{1,5},{5,9},{9,13},{2,6},{6,10},{10,14},{3,7},{... | collective-permute-start | bytes 1824776 | tf_op jit(solution)/shard_map/ppermute | solution.py:26
  97.9 10.7 %all-to-all-start = ((f32[4,1,384]{2,1,0:T(1,128)}), f32[4,1,384]{2,1,0:T(1,128)S(1)}, u32[]{:S(2)}, u32[]{:S(2)}) async-start(f32[4,1,384]{2,1,0:T(1,128)} %reshape.63), calls=%async_computation | async-start | bytes 12288 | tf_op jit(solution)/shard_map/all_to_all | solution.py:226

commit v10 on v6

--- a/solution.py
+++ b/solution.py
@@ -97,7 +97,7 @@
 
 def _flow_kernel(
     skip_ref, skip_next_ref, flag_ref, own_ref, prev_ref, next_ref, cs_ref, c_ref, s_ref, inv_ref,
-    out_ref, half_ref, x_ref, y_ref, br_ref, bi_ref,
+    out_ref, half_ref, imag_ref, x_ref, y_ref, br_ref, bi_ref,
     *, cols, row0,
 ):
     f32, bf16 = jnp.float32, jnp.bfloat16
@@ -133,18 +133,20 @@
         centered = x - _sum_all(x) / size
         spread = _sum_all(centered * centered) / size
         normed = (centered * lax.rsqrt(spread + EPSILON)).astype(bf16)
-        half_ref[2 * p * t : 2 * p * (t + 1), :] = jnp.dot(
-            both_t, normed, preferred_element_type=f32
-        ).astype(bf16)
-    halves = half_ref[...]
-    x_ref[...] = jnp.dot(halves, cos_t, preferred_element_type=f32)
-    y_ref[...] = jnp.dot(halves, sin_t, preferred_element_type=f32)
+        half = jnp.dot(both_t, normed, preferred_element_type=f32).astype(bf16)
+        half_ref[p * t : p * (t + 1), :] = half[:p]
+        imag_ref[p * t : p * (t + 1), :] = half[p:]
+    h_re = half_ref[...]
+    h_im = imag_ref[...]
+    x_ref[...] = jnp.dot(h_re, cos_t, preferred_element_type=f32) - jnp.dot(
+        h_im, sin_t, preferred_element_type=f32
+    )
+    y_ref[...] = jnp.dot(h_re, sin_t, preferred_element_type=f32) + jnp.dot(
+        h_im, cos_t, preferred_element_type=f32
+    )
 
     def spectrum(t):
-        base = 2 * p * t
-        re = x_ref[base : base + p, :] - y_ref[base + p : base + 2 * p, :]
-        im = y_ref[base : base + p, :] + x_ref[base + p : base + 2 * p, :]
-        return re, im
+        return x_ref[p * t : p * (t + 1), :], y_ref[p * t : p * (t + 1), :]
 
     for c in range(cols):
         o_re, o_im = spectrum(2 * c)
@@ -199,9 +201,10 @@
         ],
         out_specs=pl.BlockSpec((1, height, 128), lambda i, *_: (i, 0, 0)),
         scratch_shapes=[
-            pltpu.VMEM((4 * cols * PATCH, PATCH), jnp.bfloat16),
-            pltpu.VMEM((4 * cols * PATCH, PATCH), jnp.float32),
-            pltpu.VMEM((4 * cols * PATCH, PATCH), jnp.float32),
+            pltpu.VMEM((2 * cols * PATCH, PATCH), jnp.bfloat16),
+            pltpu.VMEM((2 * cols * PATCH, PATCH), jnp.bfloat16),
+            pltpu.VMEM((2 * cols * PATCH, PATCH), jnp.float32),
+            pltpu.VMEM((2 * cols * PATCH, PATCH), jnp.float32),
             pltpu.VMEM((cols * PATCH, PATCH), jnp.bfloat16),
             pltpu.VMEM((cols * PATCH, PATCH), jnp.bfloat16),
         ],

time: 111 us -> 112 us (level)
  Pallas kernels: 47.9 us -> 49.3 us
    pallas_call x4, Pallas kernels: 47.9 us -> 49.3 us  [pair_flows(): pl.pallas_call(functools.partial(_flow_kernel, cols=cols, row0=row0), gri...]
  transfers between devices with their start and end apart: 13 -> 13, of which waited for: 3 -> 3; matrix products, arithmetic and copies ran while one was open for 11% -> 10% of each run, Pallas kernels for 32% -> 33%
where the time goes in v10:
time: 112 us
  Pallas kernels  49.3 us (44%)
  starting transfers between devices  33.7 us (30%)
  waiting for transfers between devices  10.2 us (9%)
  local copies, waits for them, and re-layouts  10.1 us (9%)
  other arithmetic  7.42 us (7%)
    pallas_call x4, Pallas kernels, pair_flows(): pl.pallas_call(functools.partial(_flow_kernel, cols=cols, row0=row0), gri...  49.3 us
    ppermute x9, starting transfers between devices, shifted(): lax.ppermute(value, axis, [(source, source + steps) for source in range(f...  25.7 us
    all_to_all x1, waiting for transfers between devices, gather_sections(): return lax.all_to_all(spread, axis, 0, 0, tiled=True)  5.58 us
    all_to_all x1, starting transfers between devices, gather_sections(): return lax.all_to_all(spread, axis, 0, 0, tiled=True)  4.82 us
    concatenate x1, local copies, waits for them, and re-layouts, extended_pairs(): jnp.concatenate([keep(left, cols_got), block, keep(right, cols_got)], axi...  3.96 us
    ppermute x9, waiting for transfers between devices, shifted(): lax.ppermute(value, axis, [(source, source + steps) for source in range(f...  3.45 us
    ppermute x1, starting transfers between devices, extended_pairs(): lax.ppermute(corner_send, ('tile', 'sub'), [(0, 3), (3, 0), (1, 2), (2, 1)])  2.6 us
  transfers between devices with their start and end apart: 13, of which 3 were waited for; matrix products, arithmetic and copies ran while one was open for 10% of the time, Pallas kernels for 33%

profile of v10, /device:TPU:0, one launch (start us, length us, event | category | flops | bytes accessed | tf_op | source)
XLA Modules:
  0.0 111.8 jit_solution(18333745986596740226)
XLA Ops:
  0.6 0.9 slice_select_fusion
  1.6 0.5 collective-permute-start.2
  2.1 2.6 %collective-permute-start.1 = (bf16[1,16,16]{2,1,0:T(8,128)(2,1)S(1)}, bf16[1,16,16]{2,1,0:T(8,128)(2,1)S(1)}, u32[]{:S(2)}, u32[]{:S(2)}) collective-permute-start(bf16[1,16,16]{2,1,0:T(8,128)(2,1)S(1)} %slice_select_fusion.1), channel_id=1, source_target_pairs={{0,3},{3,0},{1,2},{2,1},{4,7},{7,4},{5,6},{6,5},{8,11},{11,8},{9,1... | collective-permute-start | bytes 1544 | tf_op jit(solution)/shard_map/ppermute | solution.py:69
  4.7 1.2 %fusion.84 = (bf16[1,1024,16]{2,1,0:T(8,128)(2,1)S(1)}, bf16[1,1024,16]{2,1,0:T(8,128)(2,1)S(1)}) fusion(bf16[1,1024,1024]{2,1,0:T(8,128)(2,1)} %param.3), kind=kLoop, calls=%fused_computation.165 | loop fusion | bytes 131072 | tf_op jit(solution)/shard_map/slice | solution.py:64
  6.2 1.3 %collective-permute-start = (s32[1,8,8]{2,1,0:T(8,128)}, s32[1,8,8]{2,1,0:T(8,128)S(1)}, u32[]{:S(2)}, u32[]{:S(2)}) collective-permute-start(s32[1,8,8]{2,1,0:T(8,128)} %param.4), channel_id=1, source_target_pairs={{4,0},{8,4},{12,8},{5,1},{9,5},{13,9},{6,2},{10,6},{14,10},{7,3},{... | collective-permute-start | bytes 776 | tf_op jit(solution)/shard_map/ppermute | solution.py:26
  7.5 0.7 select_convert_fusion
  8.2 0.7 convert_multiply_fusion
  8.9 1.2 %collective-permute-done.3 = bf16[1,16,1024]{2,1,0:T(8,128)(2,1)S(1)} collective-permute-done((bf16[1,16,1024]{2,1,0:T(8,128)(2,1)S(1)}, bf16[1,16,1024]{2,1,0:T(8,128)(2,1)S(1)}, u32[]{:S(2)}, u32[]{:S(2)}) %collective-permute-start.3) | collective-permute-done | bytes 32800 | tf_op jit(solution)/shard_map/ppermute | solution.py:68
  10.5 4.0 %concatenate.38 = bf16[1,1024,1056]{2,1,0:T(8,128)(2,1)} concatenate(bf16[1,1024,16]{2,1,0:T(8,128)(2,1)S(1)} %copy.31, bf16[1,1024,1024]{2,1,0:T(8,128)(2,1)S(1)} %copy-done, bf16[1,1024,16]{2,1,0:T(8,128)(2,1)S(1)} %copy.32), dimensions={2} | concatenate | bytes 4325376 | tf_op jit(solution)/shard_map/concatenate | solution.py:76
  14.7 1.9 %fusion.1 = (bf16[288,1056]{1,0:T(8,128)(2,1)S(1)}, bf16[288,1056]{1,0:T(8,128)(2,1)S(1)}, bf16[288,1056]{1,0:T(8,128)(2,1)S(1)}, bf16[288,1056]{1,0:T(8,128)(2,1)S(1)}) fusion(bf16[1,1024,1056]{2,1,0:T(8,128)(2,1)} %concatenate.38, bf16[1,16,1056]{2,1,0:T(8,128)(2,1)S(1)} %concatenate.37, bf16[1,16,1056]{2,1,0:T(8,128)(2,1)S(1)} %concatenate.44), kind=kLoop, calls=%fused_computation.5 | loop fusion | flops 2433024 | bytes 6187008 | tf_op jit(solution)/shard_map/slice | solution.py:283
  16.6 4.3 %collective-permute-start.4 = (bf16[288,1056]{1,0:T(8,128)(2,1)S(1)}, bf16[288,1056]{1,0:T(8,128)(2,1)}, u32[]{:S(2)}, u32[]{:S(2)}) collective-permute-start(bf16[288,1056]{1,0:T(8,128)(2,1)S(1)} %get-tuple-element.20.own_ref), channel_id=1, source_target_pairs={{0,4},{4,8},{8,12},{1,5},{5,9},{9,13},{2,6},{6,10},{10,14},{3,7},{... | collective-permute-start | bytes 1824776 | tf_op jit(solution)/shard_map/ppermute | solution.py:26
  20.9 1.3 %collective-permute-start.5 = (bf16[288,1056]{1,0:T(8,128)(2,1)S(1)}, bf16[288,1056]{1,0:T(8,128)(2,1)}, u32[]{:S(2)}, u32[]{:S(2)}) collective-permute-start(bf16[288,1056]{1,0:T(8,128)(2,1)S(1)} %get-tuple-element.20.own_ref), channel_id=1, source_target_pairs={{4,0},{8,4},{12,8},{5,1},{9,5},{13,9},{6,2},{10,6},{14,10},{7,3},{... | collective-permute-start | bytes 1824776 | tf_op jit(solution)/shard_map/ppermute | solution.py:26
  22.2 5.4 %collective-permute-start.6 = (bf16[288,1056]{1,0:T(8,128)(2,1)S(1)}, bf16[288,1056]{1,0:T(8,128)(2,1)}, u32[]{:S(2)}, u32[]{:S(2)}) collective-permute-start(bf16[288,1056]{1,0:T(8,128)(2,1)S(1)} %get-tuple-element.22.own_ref), channel_id=1, source_target_pairs={{0,4},{4,8},{8,12},{1,5},{5,9},{9,13},{2,6},{6,10},{10,14},{3,7},{... | collective-permute-start | bytes 1824776 | tf_op jit(solution)/shard_map/ppermute | solution.py:26
  27.6 0.7 fusion.70
  28.2 0.7 negate_convert_fusion
  28.9 1.3 %collective-permute-start.7 = (bf16[288,1056]{1,0:T(8,128)(2,1)S(1)}, bf16[288,1056]{1,0:T(8,128)(2,1)}, u32[]{:S(2)}, u32[]{:S(2)}) collective-permute-start(bf16[288,1056]{1,0:T(8,128)(2,1)S(1)} %get-tuple-element.22.own_ref), channel_id=1, source_target_pairs={{4,0},{8,4},{12,8},{5,1},{9,5},{13,9},{6,2},{10,6},{14,10},{7,3},{... | collective-permute-start | bytes 1824776 | tf_op jit(solution)/shard_map/ppermute | solution.py:26
  30.6 5.4 %collective-permute-start.8 = (bf16[288,1056]{1,0:T(8,128)(2,1)S(1)}, bf16[288,1056]{1,0:T(8,128)(2,1)}, u32[]{:S(2)}, u32[]{:S(2)}) collective-permute-start(bf16[288,1056]{1,0:T(8,128)(2,1)S(1)} %get-tuple-element.21.own_ref), channel_id=1, source_target_pairs={{0,4},{4,8},{8,12},{1,5},{5,9},{9,13},{2,6},{6,10},{10,14},{3,7},{... | collective-permute-start | bytes 1824776 | tf_op jit(solution)/shard_map/ppermute | solution.py:26
  36.0 1.3 %collective-permute-start.9 = (bf16[288,1056]{1,0:T(8,128)(2,1)S(1)}, bf16[288,1056]{1,0:T(8,128)(2,1)}, u32[]{:S(2)}, u32[]{:S(2)}) collective-permute-start(bf16[288,1056]{1,0:T(8,128)(2,1)S(1)} %get-tuple-element.21.own_ref), channel_id=1, source_target_pairs={{4,0},{8,4},{12,8},{5,1},{9,5},{13,9},{6,2},{10,6},{14,10},{7,3},{... | collective-permute-start | bytes 1824776 | tf_op jit(solution)/shard_map/ppermute | solution.py:26
  37.3 3.4 %collective-permute-done.5.next_ref = bf16[288,1056]{1,0:T(8,128)(2,1)} collective-permute-done((bf16[288,1056]{1,0:T(8,128)(2,1)S(1)}, bf16[288,1056]{1,0:T(8,128)(2,1)}, u32[]{:S(2)}, u32[]{:S(2)}) %collective-permute-start.5) | collective-permute-done | bytes 608288 | tf_op jit(solution)/shard_map/ppermute | solution.py:26
  40.7 4.0 %collective-permute-start.10 = (bf16[288,1056]{1,0:T(8,128)(2,1)S(1)}, bf16[288,1056]{1,0:T(8,128)(2,1)}, u32[]{:S(2)}, u32[]{:S(2)}) collective-permute-start(bf16[288,1056]{1,0:T(8,128)(2,1)S(1)} %get-tuple-element.23.own_ref), channel_id=1, source_target_pairs={{0,4},{4,8},{8,12},{1,5},{5,9},{9,13},{2,6},{6,10},{10,14},{3,7},{... | collective-permute-start | bytes 1824776 | tf_op jit(solution)/shard_map/ppermute | solution.py:26
  44.7 12.3 %shard_map.50 = f32[2,8,128]{2,1,0:T(8,128)S(1)} custom-call(s32[64]{0:T(128)S(1)} %reshape.54.skip_ref, s32[64]{0:T(128)S(1)} %reshape.55.skip_next_ref, s32[1]{0:T(128)} %bitcast.1.flag_ref, bf16[288,1056]{1,0:T(8,128)(2,1)S(1)} %get-tuple-element.20.own_ref, bf16[288,1056]{1,0:T(8,128)(2,1)} %collective-permute-done.4.prev_ref, ...), custom_call_target="tpu_custom_call" | custom-call | tf_op jit(solution)/shard_map/pallas_call | solution.py:212
  57.0 1.5 %collective-permute-start.11 = (bf16[288,1056]{1,0:T(8,128)(2,1)S(1)}, bf16[288,1056]{1,0:T(8,128)(2,1)S(1)}, u32[]{:S(2)}, u32[]{:S(2)}) collective-permute-start(bf16[288,1056]{1,0:T(8,128)(2,1)S(1)} %get-tuple-element.23.own_ref), channel_id=1, source_target_pairs={{4,0},{8,4},{12,8},{5,1},{9,5},{13,9},{6,2},{10,6},{14,10},{7,3},{... | collective-permute-start | bytes 1824776 | tf_op jit(solution)/shard_map/ppermute | solution.py:26
  58.7 12.3 %shard_map.51 = f32[2,8,128]{2,1,0:T(8,128)S(1)} custom-call(s32[64]{0:T(128)S(1)} %reshape.54.skip_ref, s32[64]{0:T(128)S(1)} %reshape.55.skip_next_ref, s32[1]{0:T(128)} %bitcast.1.flag_ref, bf16[288,1056]{1,0:T(8,128)(2,1)S(1)} %get-tuple-element.22.own_ref, bf16[288,1056]{1,0:T(8,128)(2,1)} %collective-permute-done.6.prev_ref, ...), custom_call_target="tpu_custom_call" | custom-call | tf_op jit(solution)/shard_map/pallas_call | solution.py:212
  71.3 12.3 %shard_map.52 = f32[2,8,128]{2,1,0:T(8,128)S(1)} custom-call(s32[64]{0:T(128)S(1)} %reshape.54.skip_ref, s32[64]{0:T(128)S(1)} %reshape.55.skip_next_ref, s32[1]{0:T(128)} %bitcast.1.flag_ref, bf16[288,1056]{1,0:T(8,128)(2,1)S(1)} %get-tuple-element.21.own_ref, bf16[288,1056]{1,0:T(8,128)(2,1)} %collective-permute-done.8.prev_ref, ...), custom_call_target="tpu_custom_call" | custom-call | tf_op jit(solution)/shard_map/pallas_call | solution.py:212
  83.9 12.4 %shard_map.53 = f32[2,8,128]{2,1,0:T(8,128)S(1)} custom-call(s32[64]{0:T(128)S(1)} %reshape.54.skip_ref, s32[64]{0:T(128)S(1)} %reshape.55.skip_next_ref, s32[1]{0:T(128)} %bitcast.1.flag_ref, bf16[288,1056]{1,0:T(8,128)(2,1)S(1)} %get-tuple-element.23.own_ref, bf16[288,1056]{1,0:T(8,128)(2,1)} %collective-permute-done.10.prev_ref, ...), custom_call_target="tpu_custom_call" | custom-call | tf_op jit(solution)/shard_map/pallas_call | solution.py:212
  97.7 0.7 reshape.68
  98.4 4.8 %all-to-all-start = ((f32[4,1,384]{2,1,0:T(1,128)}), f32[4,1,384]{2,1,0:T(1,128)S(1)}, u32[]{:S(2)}, u32[]{:S(2)}) async-start(f32[4,1,384]{2,1,0:T(1,128)} %reshape.68), calls=%async_computation | async-start | bytes 12288 | tf_op jit(solution)/shard_map/all_to_all | solution.py:229
  103.2 5.6 %all-to-all-done = f32[4,1,384]{2,1,0:T(1,128)S(1)} async-done(((f32[4,1,384]{2,1,0:T(1,128)}), f32[4,1,384]{2,1,0:T(1,128)S(1)}, u32[]{:S(2)}, u32[]{:S(2)}) %all-to-all-start) | async-done | bytes 6176 | tf_op jit(solution)/shard_map/all_to_all | solution.py:229
  108.8 0.5 broadcast.129
  109.3 0.7 reduce
  110.2 0.6 dynamic-slice_bitcast_fusion
  111.2 0.6 fusion.74
  (93 shorter events, 3.8 us)
Async XLA Ops:
  0.6 9.9 %copy-start = (bf16[1,1024,1024]{2,1,0:T(8,128)(2,1)S(1)}, bf16[1,1024,1024]{2,1,0:T(8,128)(2,1)}, u32[]{:S(2)}) copy-start(bf16[1,1024,1024]{2,1,0:T(8,128)(2,1)} %param.3) | copy-start | bytes 6291460
  1.6 12.9 %collective-permute-start.2 = (bf16[1,16,1024]{2,1,0:T(8,128)(2,1)S(1)}, bf16[1,16,1024]{2,1,0:T(8,128)(2,1)S(1)}, u32[]{:S(2)}, u32[]{:S(2)}) collective-permute-start(bf16[1,16,1024]{2,1,0:T(8,128)(2,1)S(1)} %slice_select_fusion), channel_id=1, source_target_pairs={{0,1},{1,0},{2,3},{3,2},{4,5},{5,4},{6,7},{7,6},{8,9},{9,8},{10,11... | collective-permute-start | bytes 98312 | tf_op jit(solution)/shard_map/ppermute | solution.py:67
  2.1 6.8 %collective-permute-start.1 = (bf16[1,16,16]{2,1,0:T(8,128)(2,1)S(1)}, bf16[1,16,16]{2,1,0:T(8,128)(2,1)S(1)}, u32[]{:S(2)}, u32[]{:S(2)}) collective-permute-start(bf16[1,16,16]{2,1,0:T(8,128)(2,1)S(1)} %slice_select_fusion.1), channel_id=1, source_target_pairs={{0,3},{3,0},{1,2},{2,1},{4,7},{7,4},{5,6},{6,5},{8,11},{11,8},{9,1... | collective-permute-start | bytes 1544 | tf_op jit(solution)/shard_map/ppermute | solution.py:69
  6.1 4.0 %collective-permute-start.3 = (bf16[1,16,1024]{2,1,0:T(8,128)(2,1)S(1)}, bf16[1,16,1024]{2,1,0:T(8,128)(2,1)S(1)}, u32[]{:S(2)}, u32[]{:S(2)}) collective-permute-start(bf16[1,16,1024]{2,1,0:T(8,128)(2,1)S(1)} %select_bitcast_fusion.2), channel_id=1, source_target_pairs={{0,2},{2,0},{1,3},{3,1},{4,6},{6,4},{5,7},{7,5},{8,10},{10,8},{9,1... | collective-permute-start | bytes 98312 | tf_op jit(solution)/shard_map/ppermute | solution.py:68
  6.2 24.3 %collective-permute-start = (s32[1,8,8]{2,1,0:T(8,128)}, s32[1,8,8]{2,1,0:T(8,128)S(1)}, u32[]{:S(2)}, u32[]{:S(2)}) collective-permute-start(s32[1,8,8]{2,1,0:T(8,128)} %param.4), channel_id=1, source_target_pairs={{4,0},{8,4},{12,8},{5,1},{9,5},{13,9},{6,2},{10,6},{14,10},{7,3},{... | collective-permute-start | bytes 776 | tf_op jit(solution)/shard_map/ppermute | solution.py:26
  14.7 6.2 %copy-start.1 = (s32[1,8,8]{2,1,0:T(8,128)S(1)}, s32[1,8,8]{2,1,0:T(8,128)}, u32[]{:S(2)}) copy-start(s32[1,8,8]{2,1,0:T(8,128)} %param.4) | copy-start | bytes 772
  16.6 19.4 %collective-permute-start.4 = (bf16[288,1056]{1,0:T(8,128)(2,1)S(1)}, bf16[288,1056]{1,0:T(8,128)(2,1)}, u32[]{:S(2)}, u32[]{:S(2)}) collective-permute-start(bf16[288,1056]{1,0:T(8,128)(2,1)S(1)} %get-tuple-element.20.own_ref), channel_id=1, source_target_pairs={{0,4},{4,8},{8,12},{1,5},{5,9},{9,13},{2,6},{6,10},{10,14},{3,7},{... | collective-permute-start | bytes 1824776 | tf_op jit(solution)/shard_map/ppermute | solution.py:26
  20.9 19.8 %collective-permute-start.5 = (bf16[288,1056]{1,0:T(8,128)(2,1)S(1)}, bf16[288,1056]{1,0:T(8,128)(2,1)}, u32[]{:S(2)}, u32[]{:S(2)}) collective-permute-start(bf16[288,1056]{1,0:T(8,128)(2,1)S(1)} %get-tuple-element.20.own_ref), channel_id=1, source_target_pairs={{4,0},{8,4},{12,8},{5,1},{9,5},{13,9},{6,2},{10,6},{14,10},{7,3},{... | collective-permute-start | bytes 1824776 | tf_op jit(solution)/shard_map/ppermute | solution.py:26
  22.2 34.8 %collective-permute-start.6 = (bf16[288,1056]{1,0:T(8,128)(2,1)S(1)}, bf16[288,1056]{1,0:T(8,128)(2,1)}, u32[]{:S(2)}, u32[]{:S(2)}) collective-permute-start(bf16[288,1056]{1,0:T(8,128)(2,1)S(1)} %get-tuple-element.22.own_ref), channel_id=1, source_target_pairs={{0,4},{4,8},{8,12},{1,5},{5,9},{9,13},{2,6},{6,10},{10,14},{3,7},{... | collective-permute-start | bytes 1824776 | tf_op jit(solution)/shard_map/ppermute | solution.py:26
  28.9 29.8 %collective-permute-start.7 = (bf16[288,1056]{1,0:T(8,128)(2,1)S(1)}, bf16[288,1056]{1,0:T(8,128)(2,1)}, u32[]{:S(2)}, u32[]{:S(2)}) collective-permute-start(bf16[288,1056]{1,0:T(8,128)(2,1)S(1)} %get-tuple-element.22.own_ref), channel_id=1, source_target_pairs={{4,0},{8,4},{12,8},{5,1},{9,5},{13,9},{6,2},{10,6},{14,10},{7,3},{... | collective-permute-start | bytes 1824776 | tf_op jit(solution)/shard_map/ppermute | solution.py:26
  30.6 40.7 %collective-permute-start.8 = (bf16[288,1056]{1,0:T(8,128)(2,1)S(1)}, bf16[288,1056]{1,0:T(8,128)(2,1)}, u32[]{:S(2)}, u32[]{:S(2)}) collective-permute-start(bf16[288,1056]{1,0:T(8,128)(2,1)S(1)} %get-tuple-element.21.own_ref), channel_id=1, source_target_pairs={{0,4},{4,8},{8,12},{1,5},{5,9},{9,13},{2,6},{6,10},{10,14},{3,7},{... | collective-permute-start | bytes 1824776 | tf_op jit(solution)/shard_map/ppermute | solution.py:26
  36.0 35.3 %collective-permute-start.9 = (bf16[288,1056]{1,0:T(8,128)(2,1)S(1)}, bf16[288,1056]{1,0:T(8,128)(2,1)}, u32[]{:S(2)}, u32[]{:S(2)}) collective-permute-start(bf16[288,1056]{1,0:T(8,128)(2,1)S(1)} %get-tuple-element.21.own_ref), channel_id=1, source_target_pairs={{4,0},{8,4},{12,8},{5,1},{9,5},{13,9},{6,2},{10,6},{14,10},{7,3},{... | collective-permute-start | bytes 1824776 | tf_op jit(solution)/shard_map/ppermute | solution.py:26
  40.7 43.2 %collective-permute-start.10 = (bf16[288,1056]{1,0:T(8,128)(2,1)S(1)}, bf16[288,1056]{1,0:T(8,128)(2,1)}, u32[]{:S(2)}, u32[]{:S(2)}) collective-permute-start(bf16[288,1056]{1,0:T(8,128)(2,1)S(1)} %get-tuple-element.23.own_ref), channel_id=1, source_target_pairs={{0,4},{4,8},{8,12},{1,5},{5,9},{9,13},{2,6},{6,10},{10,14},{3,7},{... | collective-permute-start | bytes 1824776 | tf_op jit(solution)/shard_map/ppermute | solution.py:26
  57.0 26.9 %collective-permute-start.11 = (bf16[288,1056]{1,0:T(8,128)(2,1)S(1)}, bf16[288,1056]{1,0:T(8,128)(2,1)S(1)}, u32[]{:S(2)}, u32[]{:S(2)}) collective-permute-start(bf16[288,1056]{1,0:T(8,128)(2,1)S(1)} %get-tuple-element.23.own_ref), channel_id=1, source_target_pairs={{4,0},{8,4},{12,8},{5,1},{9,5},{13,9},{6,2},{10,6},{14,10},{7,3},{... | collective-permute-start | bytes 1824776 | tf_op jit(solution)/shard_map/ppermute | solution.py:26
  98.4 10.4 %all-to-all-start = ((f32[4,1,384]{2,1,0:T(1,128)}), f32[4,1,384]{2,1,0:T(1,128)S(1)}, u32[]{:S(2)}, u32[]{:S(2)}) async-start(f32[4,1,384]{2,1,0:T(1,128)} %reshape.68), calls=%async_computation | async-start | bytes 12288 | tf_op jit(solution)/shard_map/all_to_all | solution.py:229

commit v11 on v6

--- a/solution.py
+++ b/solution.py
@@ -97,7 +97,7 @@
 
 def _flow_kernel(
     skip_ref, skip_next_ref, flag_ref, own_ref, prev_ref, next_ref, cs_ref, c_ref, s_ref, inv_ref,
-    out_ref, half_ref, x_ref, y_ref, br_ref, bi_ref,
+    out_ref, half_ref, x_ref, y_ref, br_ref, bi_ref, blk_ref,
     *, cols, row0,
 ):
     f32, bf16 = jnp.float32, jnp.bfloat16
@@ -129,24 +129,30 @@
         blocks.append(jnp.where(use_own, col_own, col_prev))
 
     for t, blk in enumerate(blocks):
-        x = blk.astype(f32)
+        blk_ref[p * t : p * (t + 1), :] = blk
+
+    def first_dft(t, carry):
+        x = blk_ref[pl.ds(pl.multiple_of(t * p, 16), p), :].astype(f32)
         centered = x - _sum_all(x) / size
         spread = _sum_all(centered * centered) / size
         normed = (centered * lax.rsqrt(spread + EPSILON)).astype(bf16)
-        half_ref[2 * p * t : 2 * p * (t + 1), :] = jnp.dot(
+        half_ref[pl.ds(pl.multiple_of(t * 2 * p, 16), 2 * p), :] = jnp.dot(
             both_t, normed, preferred_element_type=f32
         ).astype(bf16)
+        return carry
+
+    lax.fori_loop(0, len(blocks), first_dft, 0)
     halves = half_ref[...]
     x_ref[...] = jnp.dot(halves, cos_t, preferred_element_type=f32)
     y_ref[...] = jnp.dot(halves, sin_t, preferred_element_type=f32)
 
     def spectrum(t):
-        base = 2 * p * t
-        re = x_ref[base : base + p, :] - y_ref[base + p : base + 2 * p, :]
-        im = y_ref[base : base + p, :] + x_ref[base + p : base + 2 * p, :]
+        base = pl.multiple_of(2 * p * t, 16)
+        re = x_ref[pl.ds(base, p), :] - y_ref[pl.ds(base + p, p), :]
+        im = y_ref[pl.ds(base, p), :] + x_ref[pl.ds(base + p, p), :]
         return re, im
 
-    for c in range(cols):
+    def inverse(c, carry):
         o_re, o_im = spectrum(2 * c)
         t_re, t_im = spectrum(2 * c + 1)
         c_re = (o_re * t_re + o_im * t_im).astype(bf16)
@@ -154,8 +160,12 @@
         back = jnp.dot(
             inverse_t, jnp.concatenate([c_re, c_im], axis=0), preferred_element_type=f32
         ).astype(bf16)
-        br_ref[p * c : p * (c + 1), :] = back[:p]
-        bi_ref[p * c : p * (c + 1), :] = back[p:]
+        base = pl.multiple_of(p * c, 16)
+        br_ref[pl.ds(base, p), :] = back[:p]
+        bi_ref[pl.ds(base, p), :] = back[p:]
+        return carry
+
+    lax.fori_loop(0, cols, inverse, 0)
 
     corr = (
         jnp.dot(br_ref[...], cos_t, preferred_element_type=f32)
@@ -204,6 +214,7 @@
             pltpu.VMEM((4 * cols * PATCH, PATCH), jnp.float32),
             pltpu.VMEM((cols * PATCH, PATCH), jnp.bfloat16),
             pltpu.VMEM((cols * PATCH, PATCH), jnp.bfloat16),
+            pltpu.VMEM((2 * cols * PATCH, PATCH), jnp.bfloat16),
         ],
     )
     out = pl.pallas_call(

time: 111 us -> 162 us (1.46)
  Pallas kernels: 47.9 us -> 98.4 us
    pallas_call x4, Pallas kernels: 47.9 us -> 98.4 us  [pair_flows(): pl.pallas_call(functools.partial(_flow_kernel, cols=cols, row0=row0), gri...]
  transfers between devices with their start and end apart: 13 -> 13, of which waited for: 3 -> 3; matrix products, arithmetic and copies ran while one was open for 11% -> 7% of each run, Pallas kernels for 32% -> 46%
where the time goes in v11:
time: 162 us; the launch traced here: 161 us
  Pallas kernels  98.4 us (61%)
  starting transfers between devices  33.7 us (21%)
  waiting for transfers between devices  10.2 us (6%)
  local copies, waits for them, and re-layouts  10.1 us (6%)
  other arithmetic  7.42 us (5%)
    pallas_call x4, Pallas kernels, pair_flows(): pl.pallas_call(functools.partial(_flow_kernel, cols=cols, row0=row0), gri...  98.4 us
    ppermute x9, starting transfers between devices, shifted(): lax.ppermute(value, axis, [(source, source + steps) for source in range(f...  25.7 us
    all_to_all x1, waiting for transfers between devices, gather_sections(): return lax.all_to_all(spread, axis, 0, 0, tiled=True)  5.58 us
    all_to_all x1, starting transfers between devices, gather_sections(): return lax.all_to_all(spread, axis, 0, 0, tiled=True)  4.82 us
    concatenate x1, local copies, waits for them, and re-layouts, extended_pairs(): jnp.concatenate([keep(left, cols_got), block, keep(right, cols_got)], axi...  3.96 us
    ppermute x9, waiting for transfers between devices, shifted(): lax.ppermute(value, axis, [(source, source + steps) for source in range(f...  3.45 us
  transfers between devices with their start and end apart: 13, of which 3 were waited for; matrix products, arithmetic and copies ran while one was open for 7% of the time, Pallas kernels for 46%

profile of v11, /device:TPU:0, one launch (start us, length us, event | category | flops | bytes accessed | tf_op | source)
XLA Modules:
  0.0 160.9 jit_solution(2910129559770267453)
XLA Ops:
  0.6 0.9 slice_select_fusion
  1.6 0.5 collective-permute-start.2
  2.1 2.6 %collective-permute-start.1 = (bf16[1,16,16]{2,1,0:T(8,128)(2,1)S(1)}, bf16[1,16,16]{2,1,0:T(8,128)(2,1)S(1)}, u32[]{:S(2)}, u32[]{:S(2)}) collective-permute-start(bf16[1,16,16]{2,1,0:T(8,128)(2,1)S(1)} %slice_select_fusion.1), channel_id=1, source_target_pairs={{0,3},{3,0},{1,2},{2,1},{4,7},{7,4},{5,6},{6,5},{8,11},{11,8},{9,1... | collective-permute-start | bytes 1544 | tf_op jit(solution)/shard_map/ppermute | solution.py:69
  4.7 1.2 fusion.84
  6.2 1.3 collective-permute-start
  7.5 0.7 select_convert_fusion
  8.2 0.7 convert_multiply_fusion
  8.9 1.2 collective-permute-done.3
  10.5 4.0 %concatenate.38 = bf16[1,1024,1056]{2,1,0:T(8,128)(2,1)} concatenate(bf16[1,1024,16]{2,1,0:T(8,128)(2,1)S(1)} %copy.31, bf16[1,1024,1024]{2,1,0:T(8,128)(2,1)S(1)} %copy-done, bf16[1,1024,16]{2,1,0:T(8,128)(2,1)S(1)} %copy.32), dimensions={2} | concatenate | bytes 4325376 | tf_op jit(solution)/shard_map/concatenate | solution.py:76
  14.7 1.9 %fusion.1 = (bf16[288,1056]{1,0:T(8,128)(2,1)S(1)}, bf16[288,1056]{1,0:T(8,128)(2,1)S(1)}, bf16[288,1056]{1,0:T(8,128)(2,1)S(1)}, bf16[288,1056]{1,0:T(8,128)(2,1)S(1)}) fusion(bf16[1,1024,1056]{2,1,0:T(8,128)(2,1)} %concatenate.38, bf16[1,16,1056]{2,1,0:T(8,128)(2,1)S(1)} %concatenate.37, bf16[1,16,1056]{2,1,0:T(8,128)(2,1)S(1)} %concatenate.44), kind=kLoop, calls=%fused_computation.5 | loop fusion | flops 2433024 | bytes 6187008 | tf_op jit(solution)/shard_map/slice | solution.py:291
  16.6 4.3 %collective-permute-start.4 = (bf16[288,1056]{1,0:T(8,128)(2,1)S(1)}, bf16[288,1056]{1,0:T(8,128)(2,1)}, u32[]{:S(2)}, u32[]{:S(2)}) collective-permute-start(bf16[288,1056]{1,0:T(8,128)(2,1)S(1)} %get-tuple-element.20.own_ref), channel_id=1, source_target_pairs={{0,4},{4,8},{8,12},{1,5},{5,9},{9,13},{2,6},{6,10},{10,14},{3,7},{... | collective-permute-start | bytes 1824776 | tf_op jit(solution)/shard_map/ppermute | solution.py:26
  20.9 1.3 collective-permute-start.5
  22.2 5.4 %collective-permute-start.6 = (bf16[288,1056]{1,0:T(8,128)(2,1)S(1)}, bf16[288,1056]{1,0:T(8,128)(2,1)}, u32[]{:S(2)}, u32[]{:S(2)}) collective-permute-start(bf16[288,1056]{1,0:T(8,128)(2,1)S(1)} %get-tuple-element.22.own_ref), channel_id=1, source_target_pairs={{0,4},{4,8},{8,12},{1,5},{5,9},{9,13},{2,6},{6,10},{10,14},{3,7},{... | collective-permute-start | bytes 1824776 | tf_op jit(solution)/shard_map/ppermute | solution.py:26
  27.6 0.7 fusion.70
  28.2 0.7 negate_convert_fusion
  28.9 1.3 collective-permute-start.7
  30.6 5.4 %collective-permute-start.8 = (bf16[288,1056]{1,0:T(8,128)(2,1)S(1)}, bf16[288,1056]{1,0:T(8,128)(2,1)}, u32[]{:S(2)}, u32[]{:S(2)}) collective-permute-start(bf16[288,1056]{1,0:T(8,128)(2,1)S(1)} %get-tuple-element.21.own_ref), channel_id=1, source_target_pairs={{0,4},{4,8},{8,12},{1,5},{5,9},{9,13},{2,6},{6,10},{10,14},{3,7},{... | collective-permute-start | bytes 1824776 | tf_op jit(solution)/shard_map/ppermute | solution.py:26
  36.0 1.3 collective-permute-start.9
  37.3 3.4 %collective-permute-done.5.next_ref = bf16[288,1056]{1,0:T(8,128)(2,1)} collective-permute-done((bf16[288,1056]{1,0:T(8,128)(2,1)S(1)}, bf16[288,1056]{1,0:T(8,128)(2,1)}, u32[]{:S(2)}, u32[]{:S(2)}) %collective-permute-start.5) | collective-permute-done | bytes 608288 | tf_op jit(solution)/shard_map/ppermute | solution.py:26
  40.7 4.0 %collective-permute-start.10 = (bf16[288,1056]{1,0:T(8,128)(2,1)S(1)}, bf16[288,1056]{1,0:T(8,128)(2,1)}, u32[]{:S(2)}, u32[]{:S(2)}) collective-permute-start(bf16[288,1056]{1,0:T(8,128)(2,1)S(1)} %get-tuple-element.23.own_ref), channel_id=1, source_target_pairs={{0,4},{4,8},{8,12},{1,5},{5,9},{9,13},{2,6},{6,10},{10,14},{3,7},{... | collective-permute-start | bytes 1824776 | tf_op jit(solution)/shard_map/ppermute | solution.py:26
  44.7 24.6 %shard_map.50 = f32[2,8,128]{2,1,0:T(8,128)S(1)} custom-call(s32[64]{0:T(128)S(1)} %reshape.54.skip_ref, s32[64]{0:T(128)S(1)} %reshape.55.skip_next_ref, s32[1]{0:T(128)} %bitcast.1.flag_ref, bf16[288,1056]{1,0:T(8,128)(2,1)S(1)} %get-tuple-element.20.own_ref, bf16[288,1056]{1,0:T(8,128)(2,1)} %collective-permute-done.4.prev_ref, ...), custom_call_target="tpu_custom_call" | custom-call | tf_op jit(solution)/shard_map/pallas_call | solution.py:220
  69.3 1.5 collective-permute-start.11
  71.1 24.6 %shard_map.51 = f32[2,8,128]{2,1,0:T(8,128)S(1)} custom-call(s32[64]{0:T(128)S(1)} %reshape.54.skip_ref, s32[64]{0:T(128)S(1)} %reshape.55.skip_next_ref, s32[1]{0:T(128)} %bitcast.1.flag_ref, bf16[288,1056]{1,0:T(8,128)(2,1)S(1)} %get-tuple-element.22.own_ref, bf16[288,1056]{1,0:T(8,128)(2,1)} %collective-permute-done.6.prev_ref, ...), custom_call_target="tpu_custom_call" | custom-call | tf_op jit(solution)/shard_map/pallas_call | solution.py:220
  96.0 24.6 %shard_map.52 = f32[2,8,128]{2,1,0:T(8,128)S(1)} custom-call(s32[64]{0:T(128)S(1)} %reshape.54.skip_ref, s32[64]{0:T(128)S(1)} %reshape.55.skip_next_ref, s32[1]{0:T(128)} %bitcast.1.flag_ref, bf16[288,1056]{1,0:T(8,128)(2,1)S(1)} %get-tuple-element.21.own_ref, bf16[288,1056]{1,0:T(8,128)(2,1)} %collective-permute-done.8.prev_ref, ...), custom_call_target="tpu_custom_call" | custom-call | tf_op jit(solution)/shard_map/pallas_call | solution.py:220
  120.9 24.5 %shard_map.53 = f32[2,8,128]{2,1,0:T(8,128)S(1)} custom-call(s32[64]{0:T(128)S(1)} %reshape.54.skip_ref, s32[64]{0:T(128)S(1)} %reshape.55.skip_next_ref, s32[1]{0:T(128)} %bitcast.1.flag_ref, bf16[288,1056]{1,0:T(8,128)(2,1)S(1)} %get-tuple-element.23.own_ref, bf16[288,1056]{1,0:T(8,128)(2,1)} %collective-permute-done.10.prev_ref, ...), custom_call_target="tpu_custom_call" | custom-call | tf_op jit(solution)/shard_map/pallas_call | solution.py:220
  146.8 0.7 reshape.68
  147.5 4.8 %all-to-all-start = ((f32[4,1,384]{2,1,0:T(1,128)}), f32[4,1,384]{2,1,0:T(1,128)S(1)}, u32[]{:S(2)}, u32[]{:S(2)}) async-start(f32[4,1,384]{2,1,0:T(1,128)} %reshape.68), calls=%async_computation | async-start | bytes 12288 | tf_op jit(solution)/shard_map/all_to_all | solution.py:237
  152.3 5.6 %all-to-all-done = f32[4,1,384]{2,1,0:T(1,128)S(1)} async-done(((f32[4,1,384]{2,1,0:T(1,128)}), f32[4,1,384]{2,1,0:T(1,128)S(1)}, u32[]{:S(2)}, u32[]{:S(2)}) %all-to-all-start) | async-done | bytes 6176 | tf_op jit(solution)/shard_map/all_to_all | solution.py:237
  157.9 0.5 broadcast.129
  158.4 0.7 reduce
  159.3 0.6 dynamic-slice_bitcast_fusion
  160.3 0.6 fusion.74
  (93 shorter events, 3.8 us)
Async XLA Ops:
  0.6 9.9 %copy-start = (bf16[1,1024,1024]{2,1,0:T(8,128)(2,1)S(1)}, bf16[1,1024,1024]{2,1,0:T(8,128)(2,1)}, u32[]{:S(2)}) copy-start(bf16[1,1024,1024]{2,1,0:T(8,128)(2,1)} %param.3) | copy-start | bytes 6291460
  1.6 12.9 %collective-permute-start.2 = (bf16[1,16,1024]{2,1,0:T(8,128)(2,1)S(1)}, bf16[1,16,1024]{2,1,0:T(8,128)(2,1)S(1)}, u32[]{:S(2)}, u32[]{:S(2)}) collective-permute-start(bf16[1,16,1024]{2,1,0:T(8,128)(2,1)S(1)} %slice_select_fusion), channel_id=1, source_target_pairs={{0,1},{1,0},{2,3},{3,2},{4,5},{5,4},{6,7},{7,6},{8,9},{9,8},{10,11... | collective-permute-start | bytes 98312 | tf_op jit(solution)/shard_map/ppermute | solution.py:67
  2.1 6.8 %collective-permute-start.1 = (bf16[1,16,16]{2,1,0:T(8,128)(2,1)S(1)}, bf16[1,16,16]{2,1,0:T(8,128)(2,1)S(1)}, u32[]{:S(2)}, u32[]{:S(2)}) collective-permute-start(bf16[1,16,16]{2,1,0:T(8,128)(2,1)S(1)} %slice_select_fusion.1), channel_id=1, source_target_pairs={{0,3},{3,0},{1,2},{2,1},{4,7},{7,4},{5,6},{6,5},{8,11},{11,8},{9,1... | collective-permute-start | bytes 1544 | tf_op jit(solution)/shard_map/ppermute | solution.py:69
  6.1 4.0 %collective-permute-start.3 = (bf16[1,16,1024]{2,1,0:T(8,128)(2,1)S(1)}, bf16[1,16,1024]{2,1,0:T(8,128)(2,1)S(1)}, u32[]{:S(2)}, u32[]{:S(2)}) collective-permute-start(bf16[1,16,1024]{2,1,0:T(8,128)(2,1)S(1)} %select_bitcast_fusion.2), channel_id=1, source_target_pairs={{0,2},{2,0},{1,3},{3,1},{4,6},{6,4},{5,7},{7,5},{8,10},{10,8},{9,1... | collective-permute-start | bytes 98312 | tf_op jit(solution)/shard_map/ppermute | solution.py:68
  6.2 24.3 %collective-permute-start = (s32[1,8,8]{2,1,0:T(8,128)}, s32[1,8,8]{2,1,0:T(8,128)S(1)}, u32[]{:S(2)}, u32[]{:S(2)}) collective-permute-start(s32[1,8,8]{2,1,0:T(8,128)} %param.4), channel_id=1, source_target_pairs={{4,0},{8,4},{12,8},{5,1},{9,5},{13,9},{6,2},{10,6},{14,10},{7,3},{... | collective-permute-start | bytes 776 | tf_op jit(solution)/shard_map/ppermute | solution.py:26
  14.7 6.2 %copy-start.1 = (s32[1,8,8]{2,1,0:T(8,128)S(1)}, s32[1,8,8]{2,1,0:T(8,128)}, u32[]{:S(2)}) copy-start(s32[1,8,8]{2,1,0:T(8,128)} %param.4) | copy-start | bytes 772
  16.6 19.4 %collective-permute-start.4 = (bf16[288,1056]{1,0:T(8,128)(2,1)S(1)}, bf16[288,1056]{1,0:T(8,128)(2,1)}, u32[]{:S(2)}, u32[]{:S(2)}) collective-permute-start(bf16[288,1056]{1,0:T(8,128)(2,1)S(1)} %get-tuple-element.20.own_ref), channel_id=1, source_target_pairs={{0,4},{4,8},{8,12},{1,5},{5,9},{9,13},{2,6},{6,10},{10,14},{3,7},{... | collective-permute-start | bytes 1824776 | tf_op jit(solution)/shard_map/ppermute | solution.py:26
  20.9 19.8 %collective-permute-start.5 = (bf16[288,1056]{1,0:T(8,128)(2,1)S(1)}, bf16[288,1056]{1,0:T(8,128)(2,1)}, u32[]{:S(2)}, u32[]{:S(2)}) collective-permute-start(bf16[288,1056]{1,0:T(8,128)(2,1)S(1)} %get-tuple-element.20.own_ref), channel_id=1, source_target_pairs={{4,0},{8,4},{12,8},{5,1},{9,5},{13,9},{6,2},{10,6},{14,10},{7,3},{... | collective-permute-start | bytes 1824776 | tf_op jit(solution)/shard_map/ppermute | solution.py:26
  22.2 47.1 %collective-permute-start.6 = (bf16[288,1056]{1,0:T(8,128)(2,1)S(1)}, bf16[288,1056]{1,0:T(8,128)(2,1)}, u32[]{:S(2)}, u32[]{:S(2)}) collective-permute-start(bf16[288,1056]{1,0:T(8,128)(2,1)S(1)} %get-tuple-element.22.own_ref), channel_id=1, source_target_pairs={{0,4},{4,8},{8,12},{1,5},{5,9},{9,13},{2,6},{6,10},{10,14},{3,7},{... | collective-permute-start | bytes 1824776 | tf_op jit(solution)/shard_map/ppermute | solution.py:26
  28.9 42.1 %collective-permute-start.7 = (bf16[288,1056]{1,0:T(8,128)(2,1)S(1)}, bf16[288,1056]{1,0:T(8,128)(2,1)}, u32[]{:S(2)}, u32[]{:S(2)}) collective-permute-start(bf16[288,1056]{1,0:T(8,128)(2,1)S(1)} %get-tuple-element.22.own_ref), channel_id=1, source_target_pairs={{4,0},{8,4},{12,8},{5,1},{9,5},{13,9},{6,2},{10,6},{14,10},{7,3},{... | collective-permute-start | bytes 1824776 | tf_op jit(solution)/shard_map/ppermute | solution.py:26
  30.6 65.4 %collective-permute-start.8 = (bf16[288,1056]{1,0:T(8,128)(2,1)S(1)}, bf16[288,1056]{1,0:T(8,128)(2,1)}, u32[]{:S(2)}, u32[]{:S(2)}) collective-permute-start(bf16[288,1056]{1,0:T(8,128)(2,1)S(1)} %get-tuple-element.21.own_ref), channel_id=1, source_target_pairs={{0,4},{4,8},{8,12},{1,5},{5,9},{9,13},{2,6},{6,10},{10,14},{3,7},{... | collective-permute-start | bytes 1824776 | tf_op jit(solution)/shard_map/ppermute | solution.py:26
  36.0 60.0 %collective-permute-start.9 = (bf16[288,1056]{1,0:T(8,128)(2,1)S(1)}, bf16[288,1056]{1,0:T(8,128)(2,1)}, u32[]{:S(2)}, u32[]{:S(2)}) collective-permute-start(bf16[288,1056]{1,0:T(8,128)(2,1)S(1)} %get-tuple-element.21.own_ref), channel_id=1, source_target_pairs={{4,0},{8,4},{12,8},{5,1},{9,5},{13,9},{6,2},{10,6},{14,10},{7,3},{... | collective-permute-start | bytes 1824776 | tf_op jit(solution)/shard_map/ppermute | solution.py:26
  40.7 80.1 %collective-permute-start.10 = (bf16[288,1056]{1,0:T(8,128)(2,1)S(1)}, bf16[288,1056]{1,0:T(8,128)(2,1)}, u32[]{:S(2)}, u32[]{:S(2)}) collective-permute-start(bf16[288,1056]{1,0:T(8,128)(2,1)S(1)} %get-tuple-element.23.own_ref), channel_id=1, source_target_pairs={{0,4},{4,8},{8,12},{1,5},{5,9},{9,13},{2,6},{6,10},{10,14},{3,7},{... | collective-permute-start | bytes 1824776 | tf_op jit(solution)/shard_map/ppermute | solution.py:26
  69.3 51.6 %collective-permute-start.11 = (bf16[288,1056]{1,0:T(8,128)(2,1)S(1)}, bf16[288,1056]{1,0:T(8,128)(2,1)S(1)}, u32[]{:S(2)}, u32[]{:S(2)}) collective-permute-start(bf16[288,1056]{1,0:T(8,128)(2,1)S(1)} %get-tuple-element.23.own_ref), channel_id=1, source_target_pairs={{4,0},{8,4},{12,8},{5,1},{9,5},{13,9},{6,2},{10,6},{14,10},{7,3},{... | collective-permute-start | bytes 1824776 | tf_op jit(solution)/shard_map/ppermute | solution.py:26
  147.5 10.4 %all-to-all-start = ((f32[4,1,384]{2,1,0:T(1,128)}), f32[4,1,384]{2,1,0:T(1,128)S(1)}, u32[]{:S(2)}, u32[]{:S(2)}) async-start(f32[4,1,384]{2,1,0:T(1,128)} %reshape.68), calls=%async_computation | async-start | bytes 12288 | tf_op jit(solution)/shard_map/all_to_all | solution.py:237

commit v12 on v6

--- a/solution.py
+++ b/solution.py
@@ -136,19 +136,14 @@
         half_ref[2 * p * t : 2 * p * (t + 1), :] = jnp.dot(
             both_t, normed, preferred_element_type=f32
         ).astype(bf16)
-    halves = half_ref[...]
-    x_ref[...] = jnp.dot(halves, cos_t, preferred_element_type=f32)
-    y_ref[...] = jnp.dot(halves, sin_t, preferred_element_type=f32)
-
-    def spectrum(t):
-        base = 2 * p * t
-        re = x_ref[base : base + p, :] - y_ref[base + p : base + 2 * p, :]
-        im = y_ref[base : base + p, :] + x_ref[base + p : base + 2 * p, :]
-        return re, im
-
     for c in range(cols):
-        o_re, o_im = spectrum(2 * c)
-        t_re, t_im = spectrum(2 * c + 1)
+        pair = half_ref[4 * p * c : 4 * p * (c + 1), :]
+        xs = jnp.dot(pair, cos_t, preferred_element_type=f32)
+        ys = jnp.dot(pair, sin_t, preferred_element_type=f32)
+        o_re = xs[:p] - ys[p : 2 * p]
+        o_im = ys[:p] + xs[p : 2 * p]
+        t_re = xs[2 * p : 3 * p] - ys[3 * p :]
+        t_im = ys[2 * p : 3 * p] + xs[3 * p :]
         c_re = (o_re * t_re + o_im * t_im).astype(bf16)
         c_im = (o_re * t_im - o_im * t_re).astype(bf16)
         back = jnp.dot(

time: 111 us -> 131 us (1.18)
  Pallas kernels: 47.9 us -> 67.8 us
    pallas_call x4, Pallas kernels: 47.9 us -> 67.8 us  [pair_flows(): pl.pallas_call(functools.partial(_flow_kernel, cols=cols, row0=row0), gri...]
  transfers between devices with their start and end apart: 13 -> 13, of which waited for: 3 -> 3; matrix products, arithmetic and copies ran while one was open for 11% -> 9% of each run, Pallas kernels for 32% -> 39%
where the time goes in v12:
time: 131 us; the launch traced here: 130 us
  Pallas kernels  67.8 us (52%)
  starting transfers between devices  33.7 us (26%)
  waiting for transfers between devices  10.2 us (8%)
  local copies, waits for them, and re-layouts  10.1 us (8%)
  other arithmetic  7.42 us (6%)
    pallas_call x4, Pallas kernels, pair_flows(): pl.pallas_call(functools.partial(_flow_kernel, cols=cols, row0=row0), gri...  67.8 us
    ppermute x9, starting transfers between devices, shifted(): lax.ppermute(value, axis, [(source, source + steps) for source in range(f...  25.7 us
    all_to_all x1, waiting for transfers between devices, gather_sections(): return lax.all_to_all(spread, axis, 0, 0, tiled=True)  5.58 us
    all_to_all x1, starting transfers between devices, gather_sections(): return lax.all_to_all(spread, axis, 0, 0, tiled=True)  4.82 us
    concatenate x1, local copies, waits for them, and re-layouts, extended_pairs(): jnp.concatenate([keep(left, cols_got), block, keep(right, cols_got)], axi...  3.96 us
    ppermute x9, waiting for transfers between devices, shifted(): lax.ppermute(value, axis, [(source, source + steps) for source in range(f...  3.45 us
  transfers between devices with their start and end apart: 13, of which 3 were waited for; matrix products, arithmetic and copies ran while one was open for 9% of the time, Pallas kernels for 39%

profile of v12, /device:TPU:0, one launch (start us, length us, event | category | flops | bytes accessed | tf_op | source)
XLA Modules:
  0.0 130.3 jit_solution(12698326575916458954)
XLA Ops:
  0.6 0.9 slice_select_fusion
  1.6 0.5 collective-permute-start.2
  2.1 2.6 %collective-permute-start.1 = (bf16[1,16,16]{2,1,0:T(8,128)(2,1)S(1)}, bf16[1,16,16]{2,1,0:T(8,128)(2,1)S(1)}, u32[]{:S(2)}, u32[]{:S(2)}) collective-permute-start(bf16[1,16,16]{2,1,0:T(8,128)(2,1)S(1)} %slice_select_fusion.1), channel_id=1, source_target_pairs={{0,3},{3,0},{1,2},{2,1},{4,7},{7,4},{5,6},{6,5},{8,11},{11,8},{9,1... | collective-permute-start | bytes 1544 | tf_op jit(solution)/shard_map/ppermute | solution.py:69
  4.7 1.2 fusion.84
  6.2 1.3 collective-permute-start
  7.5 0.7 select_convert_fusion
  8.2 0.7 convert_multiply_fusion
  8.9 1.2 collective-permute-done.3
  10.5 4.0 %concatenate.38 = bf16[1,1024,1056]{2,1,0:T(8,128)(2,1)} concatenate(bf16[1,1024,16]{2,1,0:T(8,128)(2,1)S(1)} %copy.31, bf16[1,1024,1024]{2,1,0:T(8,128)(2,1)S(1)} %copy-done, bf16[1,1024,16]{2,1,0:T(8,128)(2,1)S(1)} %copy.32), dimensions={2} | concatenate | bytes 4325376 | tf_op jit(solution)/shard_map/concatenate | solution.py:76
  14.7 1.9 %fusion.1 = (bf16[288,1056]{1,0:T(8,128)(2,1)S(1)}, bf16[288,1056]{1,0:T(8,128)(2,1)S(1)}, bf16[288,1056]{1,0:T(8,128)(2,1)S(1)}, bf16[288,1056]{1,0:T(8,128)(2,1)S(1)}) fusion(bf16[1,1024,1056]{2,1,0:T(8,128)(2,1)} %concatenate.38, bf16[1,16,1056]{2,1,0:T(8,128)(2,1)S(1)} %concatenate.37, bf16[1,16,1056]{2,1,0:T(8,128)(2,1)S(1)} %concatenate.44), kind=kLoop, calls=%fused_computation.5 | loop fusion | flops 2433024 | bytes 6187008 | tf_op jit(solution)/shard_map/slice | solution.py:275
  16.6 4.3 %collective-permute-start.4 = (bf16[288,1056]{1,0:T(8,128)(2,1)S(1)}, bf16[288,1056]{1,0:T(8,128)(2,1)}, u32[]{:S(2)}, u32[]{:S(2)}) collective-permute-start(bf16[288,1056]{1,0:T(8,128)(2,1)S(1)} %get-tuple-element.20.own_ref), channel_id=1, source_target_pairs={{0,4},{4,8},{8,12},{1,5},{5,9},{9,13},{2,6},{6,10},{10,14},{3,7},{... | collective-permute-start | bytes 1824776 | tf_op jit(solution)/shard_map/ppermute | solution.py:26
  20.9 1.3 collective-permute-start.5
  22.2 5.4 %collective-permute-start.6 = (bf16[288,1056]{1,0:T(8,128)(2,1)S(1)}, bf16[288,1056]{1,0:T(8,128)(2,1)}, u32[]{:S(2)}, u32[]{:S(2)}) collective-permute-start(bf16[288,1056]{1,0:T(8,128)(2,1)S(1)} %get-tuple-element.22.own_ref), channel_id=1, source_target_pairs={{0,4},{4,8},{8,12},{1,5},{5,9},{9,13},{2,6},{6,10},{10,14},{3,7},{... | collective-permute-start | bytes 1824776 | tf_op jit(solution)/shard_map/ppermute | solution.py:26
  27.6 0.7 fusion.70
  28.2 0.7 negate_convert_fusion
  28.9 1.3 collective-permute-start.7
  30.6 5.4 %collective-permute-start.8 = (bf16[288,1056]{1,0:T(8,128)(2,1)S(1)}, bf16[288,1056]{1,0:T(8,128)(2,1)}, u32[]{:S(2)}, u32[]{:S(2)}) collective-permute-start(bf16[288,1056]{1,0:T(8,128)(2,1)S(1)} %get-tuple-element.21.own_ref), channel_id=1, source_target_pairs={{0,4},{4,8},{8,12},{1,5},{5,9},{9,13},{2,6},{6,10},{10,14},{3,7},{... | collective-permute-start | bytes 1824776 | tf_op jit(solution)/shard_map/ppermute | solution.py:26
  36.0 1.3 collective-permute-start.9
  37.3 3.4 %collective-permute-done.5.next_ref = bf16[288,1056]{1,0:T(8,128)(2,1)} collective-permute-done((bf16[288,1056]{1,0:T(8,128)(2,1)S(1)}, bf16[288,1056]{1,0:T(8,128)(2,1)}, u32[]{:S(2)}, u32[]{:S(2)}) %collective-permute-start.5) | collective-permute-done | bytes 608288 | tf_op jit(solution)/shard_map/ppermute | solution.py:26
  40.7 4.0 %collective-permute-start.10 = (bf16[288,1056]{1,0:T(8,128)(2,1)S(1)}, bf16[288,1056]{1,0:T(8,128)(2,1)}, u32[]{:S(2)}, u32[]{:S(2)}) collective-permute-start(bf16[288,1056]{1,0:T(8,128)(2,1)S(1)} %get-tuple-element.23.own_ref), channel_id=1, source_target_pairs={{0,4},{4,8},{8,12},{1,5},{5,9},{9,13},{2,6},{6,10},{10,14},{3,7},{... | collective-permute-start | bytes 1824776 | tf_op jit(solution)/shard_map/ppermute | solution.py:26
  44.7 16.9 %shard_map.50 = f32[2,8,128]{2,1,0:T(8,128)S(1)} custom-call(s32[64]{0:T(128)S(1)} %reshape.54.skip_ref, s32[64]{0:T(128)S(1)} %reshape.55.skip_next_ref, s32[1]{0:T(128)} %bitcast.1.flag_ref, bf16[288,1056]{1,0:T(8,128)(2,1)S(1)} %get-tuple-element.20.own_ref, bf16[288,1056]{1,0:T(8,128)(2,1)} %collective-permute-done.4.prev_ref, ...), custom_call_target="tpu_custom_call" | custom-call | tf_op jit(solution)/shard_map/pallas_call | solution.py:204
  61.6 1.5 %collective-permute-start.11 = (bf16[288,1056]{1,0:T(8,128)(2,1)S(1)}, bf16[288,1056]{1,0:T(8,128)(2,1)S(1)}, u32[]{:S(2)}, u32[]{:S(2)}) collective-permute-start(bf16[288,1056]{1,0:T(8,128)(2,1)S(1)} %get-tuple-element.23.own_ref), channel_id=1, source_target_pairs={{4,0},{8,4},{12,8},{5,1},{9,5},{13,9},{6,2},{10,6},{14,10},{7,3},{... | collective-permute-start | bytes 1824776 | tf_op jit(solution)/shard_map/ppermute | solution.py:26
  63.3 16.9 %shard_map.51 = f32[2,8,128]{2,1,0:T(8,128)S(1)} custom-call(s32[64]{0:T(128)S(1)} %reshape.54.skip_ref, s32[64]{0:T(128)S(1)} %reshape.55.skip_next_ref, s32[1]{0:T(128)} %bitcast.1.flag_ref, bf16[288,1056]{1,0:T(8,128)(2,1)S(1)} %get-tuple-element.22.own_ref, bf16[288,1056]{1,0:T(8,128)(2,1)} %collective-permute-done.6.prev_ref, ...), custom_call_target="tpu_custom_call" | custom-call | tf_op jit(solution)/shard_map/pallas_call | solution.py:204
  80.5 16.9 %shard_map.52 = f32[2,8,128]{2,1,0:T(8,128)S(1)} custom-call(s32[64]{0:T(128)S(1)} %reshape.54.skip_ref, s32[64]{0:T(128)S(1)} %reshape.55.skip_next_ref, s32[1]{0:T(128)} %bitcast.1.flag_ref, bf16[288,1056]{1,0:T(8,128)(2,1)S(1)} %get-tuple-element.21.own_ref, bf16[288,1056]{1,0:T(8,128)(2,1)} %collective-permute-done.8.prev_ref, ...), custom_call_target="tpu_custom_call" | custom-call | tf_op jit(solution)/shard_map/pallas_call | solution.py:204
  97.8 17.0 %shard_map.53 = f32[2,8,128]{2,1,0:T(8,128)S(1)} custom-call(s32[64]{0:T(128)S(1)} %reshape.54.skip_ref, s32[64]{0:T(128)S(1)} %reshape.55.skip_next_ref, s32[1]{0:T(128)} %bitcast.1.flag_ref, bf16[288,1056]{1,0:T(8,128)(2,1)S(1)} %get-tuple-element.23.own_ref, bf16[288,1056]{1,0:T(8,128)(2,1)} %collective-permute-done.10.prev_ref, ...), custom_call_target="tpu_custom_call" | custom-call | tf_op jit(solution)/shard_map/pallas_call | solution.py:204
  116.2 0.7 reshape.68
  116.9 4.8 %all-to-all-start = ((f32[4,1,384]{2,1,0:T(1,128)}), f32[4,1,384]{2,1,0:T(1,128)S(1)}, u32[]{:S(2)}, u32[]{:S(2)}) async-start(f32[4,1,384]{2,1,0:T(1,128)} %reshape.68), calls=%async_computation | async-start | bytes 12288 | tf_op jit(solution)/shard_map/all_to_all | solution.py:221
  121.7 5.6 %all-to-all-done = f32[4,1,384]{2,1,0:T(1,128)S(1)} async-done(((f32[4,1,384]{2,1,0:T(1,128)}), f32[4,1,384]{2,1,0:T(1,128)S(1)}, u32[]{:S(2)}, u32[]{:S(2)}) %all-to-all-start) | async-done | bytes 6176 | tf_op jit(solution)/shard_map/all_to_all | solution.py:221
  127.3 0.5 broadcast.129
  127.8 0.7 reduce
  128.7 0.6 dynamic-slice_bitcast_fusion
  129.7 0.6 fusion.74
  (93 shorter events, 3.8 us)
Async XLA Ops:
  0.6 9.9 %copy-start = (bf16[1,1024,1024]{2,1,0:T(8,128)(2,1)S(1)}, bf16[1,1024,1024]{2,1,0:T(8,128)(2,1)}, u32[]{:S(2)}) copy-start(bf16[1,1024,1024]{2,1,0:T(8,128)(2,1)} %param.3) | copy-start | bytes 6291460
  1.6 12.9 %collective-permute-start.2 = (bf16[1,16,1024]{2,1,0:T(8,128)(2,1)S(1)}, bf16[1,16,1024]{2,1,0:T(8,128)(2,1)S(1)}, u32[]{:S(2)}, u32[]{:S(2)}) collective-permute-start(bf16[1,16,1024]{2,1,0:T(8,128)(2,1)S(1)} %slice_select_fusion), channel_id=1, source_target_pairs={{0,1},{1,0},{2,3},{3,2},{4,5},{5,4},{6,7},{7,6},{8,9},{9,8},{10,11... | collective-permute-start | bytes 98312 | tf_op jit(solution)/shard_map/ppermute | solution.py:67
  2.1 6.8 %collective-permute-start.1 = (bf16[1,16,16]{2,1,0:T(8,128)(2,1)S(1)}, bf16[1,16,16]{2,1,0:T(8,128)(2,1)S(1)}, u32[]{:S(2)}, u32[]{:S(2)}) collective-permute-start(bf16[1,16,16]{2,1,0:T(8,128)(2,1)S(1)} %slice_select_fusion.1), channel_id=1, source_target_pairs={{0,3},{3,0},{1,2},{2,1},{4,7},{7,4},{5,6},{6,5},{8,11},{11,8},{9,1... | collective-permute-start | bytes 1544 | tf_op jit(solution)/shard_map/ppermute | solution.py:69
  6.1 4.0 %collective-permute-start.3 = (bf16[1,16,1024]{2,1,0:T(8,128)(2,1)S(1)}, bf16[1,16,1024]{2,1,0:T(8,128)(2,1)S(1)}, u32[]{:S(2)}, u32[]{:S(2)}) collective-permute-start(bf16[1,16,1024]{2,1,0:T(8,128)(2,1)S(1)} %select_bitcast_fusion.2), channel_id=1, source_target_pairs={{0,2},{2,0},{1,3},{3,1},{4,6},{6,4},{5,7},{7,5},{8,10},{10,8},{9,1... | collective-permute-start | bytes 98312 | tf_op jit(solution)/shard_map/ppermute | solution.py:68
  6.2 24.3 %collective-permute-start = (s32[1,8,8]{2,1,0:T(8,128)}, s32[1,8,8]{2,1,0:T(8,128)S(1)}, u32[]{:S(2)}, u32[]{:S(2)}) collective-permute-start(s32[1,8,8]{2,1,0:T(8,128)} %param.4), channel_id=1, source_target_pairs={{4,0},{8,4},{12,8},{5,1},{9,5},{13,9},{6,2},{10,6},{14,10},{7,3},{... | collective-permute-start | bytes 776 | tf_op jit(solution)/shard_map/ppermute | solution.py:26
  14.7 6.2 %copy-start.1 = (s32[1,8,8]{2,1,0:T(8,128)S(1)}, s32[1,8,8]{2,1,0:T(8,128)}, u32[]{:S(2)}) copy-start(s32[1,8,8]{2,1,0:T(8,128)} %param.4) | copy-start | bytes 772
  16.6 19.4 %collective-permute-start.4 = (bf16[288,1056]{1,0:T(8,128)(2,1)S(1)}, bf16[288,1056]{1,0:T(8,128)(2,1)}, u32[]{:S(2)}, u32[]{:S(2)}) collective-permute-start(bf16[288,1056]{1,0:T(8,128)(2,1)S(1)} %get-tuple-element.20.own_ref), channel_id=1, source_target_pairs={{0,4},{4,8},{8,12},{1,5},{5,9},{9,13},{2,6},{6,10},{10,14},{3,7},{... | collective-permute-start | bytes 1824776 | tf_op jit(solution)/shard_map/ppermute | solution.py:26
  20.9 19.8 %collective-permute-start.5 = (bf16[288,1056]{1,0:T(8,128)(2,1)S(1)}, bf16[288,1056]{1,0:T(8,128)(2,1)}, u32[]{:S(2)}, u32[]{:S(2)}) collective-permute-start(bf16[288,1056]{1,0:T(8,128)(2,1)S(1)} %get-tuple-element.20.own_ref), channel_id=1, source_target_pairs={{4,0},{8,4},{12,8},{5,1},{9,5},{13,9},{6,2},{10,6},{14,10},{7,3},{... | collective-permute-start | bytes 1824776 | tf_op jit(solution)/shard_map/ppermute | solution.py:26
  22.2 39.4 %collective-permute-start.6 = (bf16[288,1056]{1,0:T(8,128)(2,1)S(1)}, bf16[288,1056]{1,0:T(8,128)(2,1)}, u32[]{:S(2)}, u32[]{:S(2)}) collective-permute-start(bf16[288,1056]{1,0:T(8,128)(2,1)S(1)} %get-tuple-element.22.own_ref), channel_id=1, source_target_pairs={{0,4},{4,8},{8,12},{1,5},{5,9},{9,13},{2,6},{6,10},{10,14},{3,7},{... | collective-permute-start | bytes 1824776 | tf_op jit(solution)/shard_map/ppermute | solution.py:26
  28.9 34.4 %collective-permute-start.7 = (bf16[288,1056]{1,0:T(8,128)(2,1)S(1)}, bf16[288,1056]{1,0:T(8,128)(2,1)}, u32[]{:S(2)}, u32[]{:S(2)}) collective-permute-start(bf16[288,1056]{1,0:T(8,128)(2,1)S(1)} %get-tuple-element.22.own_ref), channel_id=1, source_target_pairs={{4,0},{8,4},{12,8},{5,1},{9,5},{13,9},{6,2},{10,6},{14,10},{7,3},{... | collective-permute-start | bytes 1824776 | tf_op jit(solution)/shard_map/ppermute | solution.py:26
  30.6 50.0 %collective-permute-start.8 = (bf16[288,1056]{1,0:T(8,128)(2,1)S(1)}, bf16[288,1056]{1,0:T(8,128)(2,1)}, u32[]{:S(2)}, u32[]{:S(2)}) collective-permute-start(bf16[288,1056]{1,0:T(8,128)(2,1)S(1)} %get-tuple-element.21.own_ref), channel_id=1, source_target_pairs={{0,4},{4,8},{8,12},{1,5},{5,9},{9,13},{2,6},{6,10},{10,14},{3,7},{... | collective-permute-start | bytes 1824776 | tf_op jit(solution)/shard_map/ppermute | solution.py:26
  36.0 44.5 %collective-permute-start.9 = (bf16[288,1056]{1,0:T(8,128)(2,1)S(1)}, bf16[288,1056]{1,0:T(8,128)(2,1)}, u32[]{:S(2)}, u32[]{:S(2)}) collective-permute-start(bf16[288,1056]{1,0:T(8,128)(2,1)S(1)} %get-tuple-element.21.own_ref), channel_id=1, source_target_pairs={{4,0},{8,4},{12,8},{5,1},{9,5},{13,9},{6,2},{10,6},{14,10},{7,3},{... | collective-permute-start | bytes 1824776 | tf_op jit(solution)/shard_map/ppermute | solution.py:26
  40.7 57.0 %collective-permute-start.10 = (bf16[288,1056]{1,0:T(8,128)(2,1)S(1)}, bf16[288,1056]{1,0:T(8,128)(2,1)}, u32[]{:S(2)}, u32[]{:S(2)}) collective-permute-start(bf16[288,1056]{1,0:T(8,128)(2,1)S(1)} %get-tuple-element.23.own_ref), channel_id=1, source_target_pairs={{0,4},{4,8},{8,12},{1,5},{5,9},{9,13},{2,6},{6,10},{10,14},{3,7},{... | collective-permute-start | bytes 1824776 | tf_op jit(solution)/shard_map/ppermute | solution.py:26
  61.6 36.2 %collective-permute-start.11 = (bf16[288,1056]{1,0:T(8,128)(2,1)S(1)}, bf16[288,1056]{1,0:T(8,128)(2,1)S(1)}, u32[]{:S(2)}, u32[]{:S(2)}) collective-permute-start(bf16[288,1056]{1,0:T(8,128)(2,1)S(1)} %get-tuple-element.23.own_ref), channel_id=1, source_target_pairs={{4,0},{8,4},{12,8},{5,1},{9,5},{13,9},{6,2},{10,6},{14,10},{7,3},{... | collective-permute-start | bytes 1824776 | tf_op jit(solution)/shard_map/ppermute | solution.py:26
  116.9 10.4 %all-to-all-start = ((f32[4,1,384]{2,1,0:T(1,128)}), f32[4,1,384]{2,1,0:T(1,128)S(1)}, u32[]{:S(2)}, u32[]{:S(2)}) async-start(f32[4,1,384]{2,1,0:T(1,128)} %reshape.68), calls=%async_computation | async-start | bytes 12288 | tf_op jit(solution)/shard_map/all_to_all | solution.py:221

commit v13 on v6

--- a/solution.py
+++ b/solution.py
@@ -98,12 +98,11 @@
 def _flow_kernel(
     skip_ref, skip_next_ref, flag_ref, own_ref, prev_ref, next_ref, cs_ref, c_ref, s_ref, inv_ref,
     out_ref, half_ref, x_ref, y_ref, br_ref, bi_ref,
-    *, cols, row0,
+    *, cols, row0, count,
 ):
     f32, bf16 = jnp.float32, jnp.bfloat16
     p = PATCH
     pairs = cols // 2
-    i = pl.program_id(0) + row0
     cos_t = c_ref[...]
     sin_t = s_ref[...]
     both_t = cs_ref[...]
@@ -111,9 +110,24 @@
     size = float(p * p)
 
     def window(ref, j):
-        return ref[:, j * STRIDE : j * STRIDE + p]
+        return ref[r0 : r0 + p, j * STRIDE : j * STRIDE + p]
 
     use_own = flag_ref[0] == 1
+    blocks = []
+    for row in range(count):
+        i = row0 + count * pl.program_id(0) + row
+        r0 = row * STRIDE
+        blocks.extend(_row_blocks(skip_ref, skip_next_ref, own_ref, prev_ref, next_ref, use_own, i, r0, cols))
+    _rest(blocks, half_ref, x_ref, y_ref, br_ref, bi_ref, out_ref, cos_t, sin_t, both_t, inverse_t, cols * count, count, cols)
+
+
+def _row_blocks(skip_ref, skip_next_ref, own_ref, prev_ref, next_ref, use_own, i, r0, cols):
+    p = PATCH
+    pairs = cols // 2
+
+    def window(ref, j):
+        return ref[r0 : r0 + p, j * STRIDE : j * STRIDE + p]
+
     blocks = []
     for k in range(pairs):
         left, right = 2 * k, 2 * k + 1
@@ -127,7 +141,14 @@
         col_prev = jnp.where(second_far, window(prev_ref, right), window(prev_ref, left))
         col_own = jnp.where(second_far, window(own_ref, right), window(own_ref, left))
         blocks.append(jnp.where(use_own, col_own, col_prev))
-
+    return blocks
+
+
+def _rest(blocks, half_ref, x_ref, y_ref, br_ref, bi_ref, out_ref, cos_t, sin_t, both_t, inverse_t, total_pairs, count, row_cols):
+    f32, bf16 = jnp.float32, jnp.bfloat16
+    p = PATCH
+    size = float(p * p)
+    cols = total_pairs
     for t, blk in enumerate(blocks):
         x = blk.astype(f32)
         centered = x - _sum_all(x) / size
@@ -176,9 +197,11 @@
     lane = lax.broadcasted_iota(jnp.int32, (cols, 128), 1)
     res = jnp.where(lane == 0, ar, jnp.where(lane == 1, ac, 0.0))
     height = out_ref.shape[1]
-    if height > cols:
-        res = jnp.concatenate([res, jnp.zeros((height - cols, 128), f32)], axis=0)
-    out_ref[0] = res
+    for row in range(count):
+        part = res[row * row_cols : (row + 1) * row_cols]
+        if height > row_cols:
+            part = jnp.concatenate([part, jnp.zeros((height - row_cols, 128), f32)], axis=0)
+        out_ref[row] = part
 
 
 def pair_flows(own_pad, prev_pad, next_pad, skip_flat, skip_next_flat, use_own, row0, tables):
@@ -188,26 +211,30 @@
     assert cols % 2 == 0
     height = max(8, -(-cols // 8) * 8)
     both_t, cos_t, sin_t, inverse_t = tables
-    band = pl.BlockSpec((pl.Element(PATCH), pl.Element(broad)), lambda i, *_: (i * STRIDE, 0))
+    step = 2 if rows % 2 == 0 else 1
+    band = pl.BlockSpec(
+        (pl.Element(step * STRIDE + PATCH - STRIDE), pl.Element(broad)),
+        lambda i, *_: (i * step * STRIDE, 0),
+    )
     table = pl.BlockSpec((PATCH, PATCH), lambda i, *_: (0, 0))
     grid_spec = pltpu.PrefetchScalarGridSpec(
         num_scalar_prefetch=3,
-        grid=(rows,),
+        grid=(rows // step,),
         in_specs=[
             band, band, band, pl.BlockSpec((2 * PATCH, PATCH), lambda i, *_: (0, 0)), table, table,
             pl.BlockSpec((2 * PATCH, 2 * PATCH), lambda i, *_: (0, 0)),
         ],
-        out_specs=pl.BlockSpec((1, height, 128), lambda i, *_: (i, 0, 0)),
+        out_specs=pl.BlockSpec((step, height, 128), lambda i, *_: (i, 0, 0)),
         scratch_shapes=[
-            pltpu.VMEM((4 * cols * PATCH, PATCH), jnp.bfloat16),
-            pltpu.VMEM((4 * cols * PATCH, PATCH), jnp.float32),
-            pltpu.VMEM((4 * cols * PATCH, PATCH), jnp.float32),
-            pltpu.VMEM((cols * PATCH, PATCH), jnp.bfloat16),
-            pltpu.VMEM((cols * PATCH, PATCH), jnp.bfloat16),
+            pltpu.VMEM((4 * step * cols * PATCH, PATCH), jnp.bfloat16),
+            pltpu.VMEM((4 * step * cols * PATCH, PATCH), jnp.float32),
+            pltpu.VMEM((4 * step * cols * PATCH, PATCH), jnp.float32),
+            pltpu.VMEM((step * cols * PATCH, PATCH), jnp.bfloat16),
+            pltpu.VMEM((step * cols * PATCH, PATCH), jnp.bfloat16),
         ],
     )
     out = pl.pallas_call(
-        functools.partial(_flow_kernel, cols=cols, row0=row0),
+        functools.partial(_flow_kernel, cols=cols, row0=row0, count=step),
         grid_spec=grid_spec,
         out_shape=jax.ShapeDtypeStruct((rows, height, 128), jnp.float32),
         compiler_params=pltpu.CompilerParams(
@@ -265,7 +292,7 @@
     skip_next = shifted(skipped, "sec", -1)
     use_own = (index == 0).astype(jnp.int32)
     rows_count = (own_pad.shape[0] - (PATCH - STRIDE)) // STRIDE
-    chunks = max(n for n in (1, 2, 4) if rows_count % n == 0)
+    chunks = 2 if rows_count % 4 == 0 else 1
     per = rows_count // chunks
     cos_t, sin_t = dft_tables(PATCH)
     inverse_t = jnp.concatenate(

time: 111 us -> 113 us (1.018)
  waiting for transfers between devices: 10.2 us -> 32.5 us
  starting transfers between devices: 33.7 us -> 20.6 us
  Pallas kernels: 47.9 us -> 43.8 us
  other arithmetic: 7.42 us -> 6 us
  local copies, waits for them, and re-layouts: 10.1 us -> 8.89 us
    ppermute x9 -> x5, waiting for transfers between devices: 3.45 us -> 24.5 us  [shifted(): lax.ppermute(value, axis, [(source, source + steps) for source in range(f...]
    ppermute x9 -> x5, starting transfers between devices: 25.7 us -> 14.2 us  [shifted(): lax.ppermute(value, axis, [(source, source + steps) for source in range(f...]
    pallas_call x4 -> x2, Pallas kernels: 47.9 us -> 43.8 us  [pair_flows(): pl.pallas_call(functools.partial(_flow_kernel, cols=cols, row0=row0, coun...]
    all_to_all x1, starting transfers between devices: 4.82 us -> 3.25 us  [gather_sections(): return lax.all_to_all(spread, axis, 0, 0, tiled=True)]
    ppermute x1, waiting for transfers between devices: 1.2 us -> 2.45 us  [extended_pairs(): cols_got = jnp.swapaxes(lax.ppermute(cols_send, 'tile', swap), 1, 2)]
  transfers between devices with their start and end apart: 13 -> 9, of which waited for: 3 -> 5; matrix products, arithmetic and copies ran while one was open for 11% -> 9% of each run, Pallas kernels for 32% -> 19%
where the time goes in v13:
time: 113 us
  Pallas kernels  43.8 us (39%)
  waiting for transfers between devices  32.5 us (29%)
  starting transfers between devices  20.6 us (18%)
  local copies, waits for them, and re-layouts  8.89 us (8%)
  other arithmetic  6 us (5%)
    pallas_call x2, Pallas kernels, pair_flows(): pl.pallas_call(functools.partial(_flow_kernel, cols=cols, row0=row0, coun...  43.8 us
    ppermute x5, waiting for transfers between devices, shifted(): lax.ppermute(value, axis, [(source, source + steps) for source in range(f...  24.5 us
    ppermute x5, starting transfers between devices, shifted(): lax.ppermute(value, axis, [(source, source + steps) for source in range(f...  14.2 us
    all_to_all x1, waiting for transfers between devices, gather_sections(): return lax.all_to_all(spread, axis, 0, 0, tiled=True)  5.55 us
    concatenate x1, local copies, waits for them, and re-layouts, extended_pairs(): jnp.concatenate([keep(left, cols_got), block, keep(right, cols_got)], axi...  3.98 us
    all_to_all x1, starting transfers between devices, gather_sections(): return lax.all_to_all(spread, axis, 0, 0, tiled=True)  3.25 us
    ppermute x1, starting transfers between devices, extended_pairs(): lax.ppermute(corner_send, ('tile', 'sub'), [(0, 3), (3, 0), (1, 2), (2, 1)])  2.6 us
    ppermute x1, waiting for transfers between devices, extended_pairs(): cols_got = jnp.swapaxes(lax.ppermute(cols_send, 'tile', swap), 1, 2)  2.45 us
  transfers between devices with their start and end apart: 9, of which 5 were waited for; matrix products, arithmetic and copies ran while one was open for 9% of the time, Pallas kernels for 19%

profile of v13, /device:TPU:0, one launch (start us, length us, event | category | flops | bytes accessed | tf_op | source)
XLA Modules:
  0.0 113.0 jit_solution(12126713436588093310)
XLA Ops:
  0.6 0.8 slice_select_fusion
  1.4 0.5 collective-permute-start.2
  2.0 2.6 %collective-permute-start.1 = (bf16[1,16,16]{2,1,0:T(8,128)(2,1)S(1)}, bf16[1,16,16]{2,1,0:T(8,128)(2,1)S(1)}, u32[]{:S(2)}, u32[]{:S(2)}) collective-permute-start(bf16[1,16,16]{2,1,0:T(8,128)(2,1)S(1)} %slice_select_fusion.1), channel_id=1, source_target_pairs={{0,3},{3,0},{1,2},{2,1},{4,7},{7,4},{5,6},{6,5},{8,11},{11,8},{9,1... | collective-permute-start | bytes 1544 | tf_op jit(solution)/shard_map/ppermute | solution.py:69
  4.6 1.2 %fusion.84 = (bf16[1,1024,16]{2,1,0:T(8,128)(2,1)S(1)}, bf16[1,1024,16]{2,1,0:T(8,128)(2,1)S(1)}) fusion(bf16[1,1024,1024]{2,1,0:T(8,128)(2,1)} %param.3), kind=kLoop, calls=%fused_computation.159 | loop fusion | bytes 131072 | tf_op jit(solution)/shard_map/slice | solution.py:64
  5.9 0.1 copy.42
  6.0 0.1 collective-permute-start.3
  6.2 1.3 %collective-permute-start = (s32[1,8,8]{1,2,0:T(8,128)S(1)}, s32[1,8,8]{1,2,0:T(8,128)S(1)}, u32[]{:S(2)}, u32[]{:S(2)}) collective-permute-start(s32[1,8,8]{1,2,0:T(8,128)S(1)} %copy.22), channel_id=1, source_target_pairs={{4,0},{8,4},{12,8},{5,1},{9,5},{13,9},{6,2},{10,6},{14,10},{7,3},{... | collective-permute-start | bytes 776 | tf_op jit(solution)/shard_map/ppermute | solution.py:26
  7.6 2.5 %collective-permute-done.3 = bf16[1,16,1024]{2,1,0:T(8,128)(2,1)S(1)} collective-permute-done((bf16[1,16,1024]{2,1,0:T(8,128)(2,1)S(1)}, bf16[1,16,1024]{2,1,0:T(8,128)(2,1)S(1)}, u32[]{:S(2)}, u32[]{:S(2)}) %collective-permute-start.3) | collective-permute-done | bytes 32800 | tf_op jit(solution)/shard_map/ppermute | solution.py:68
  10.0 0.2 copy.26
  10.2 0.2 copy.27
  10.4 4.0 %concatenate.38 = bf16[1,1024,1056]{2,1,0:T(8,128)(2,1)} concatenate(bf16[1,1024,16]{2,1,0:T(8,128)(2,1)S(1)} %copy.26, bf16[1,1024,1024]{2,1,0:T(8,128)(2,1)S(1)} %copy-done, bf16[1,1024,16]{2,1,0:T(8,128)(2,1)S(1)} %copy.27), dimensions={2} | concatenate | bytes 4325376 | tf_op jit(solution)/shard_map/concatenate | solution.py:76
  14.6 1.9 %fusion.1 = (bf16[544,1056]{1,0:T(8,128)(2,1)S(1)}, bf16[544,1056]{1,0:T(8,128)(2,1)S(1)}) fusion(bf16[1,1024,1056]{2,1,0:T(8,128)(2,1)} %concatenate.38, bf16[1,16,1056]{2,1,0:T(8,128)(2,1)S(1)} %concatenate.37, bf16[1,16,1056]{2,1,0:T(8,128)(2,1)S(1)} %concatenate.44), kind=kLoop, calls=%fused_computation.3 | loop fusion | flops 4595712 | bytes 4528128 | tf_op jit(solution)/shard_map/slice | solution.py:307
  16.5 4.5 %collective-permute-start.4 = (bf16[544,1056]{1,0:T(8,128)(2,1)S(1)}, bf16[544,1056]{1,0:T(8,128)(2,1)}, u32[]{:S(2)}, u32[]{:S(2)}) collective-permute-start(bf16[544,1056]{1,0:T(8,128)(2,1)S(1)} %get-tuple-element.20.own_ref), channel_id=1, source_target_pairs={{0,4},{4,8},{8,12},{1,5},{5,9},{9,13},{2,6},{6,10},{10,14},{3,7},{... | collective-permute-start | bytes 3446792 | tf_op jit(solution)/shard_map/ppermute | solution.py:26
  21.0 1.3 %collective-permute-start.5 = (bf16[544,1056]{1,0:T(8,128)(2,1)S(1)}, bf16[544,1056]{1,0:T(8,128)(2,1)}, u32[]{:S(2)}, u32[]{:S(2)}) collective-permute-start(bf16[544,1056]{1,0:T(8,128)(2,1)S(1)} %get-tuple-element.20.own_ref), channel_id=1, source_target_pairs={{4,0},{8,4},{12,8},{5,1},{9,5},{13,9},{6,2},{10,6},{14,10},{7,3},{... | collective-permute-start | bytes 3446792 | tf_op jit(solution)/shard_map/ppermute | solution.py:26
  22.3 0.7 negate_convert_fusion
  23.0 5.6 %collective-permute-start.6 = (bf16[544,1056]{1,0:T(8,128)(2,1)S(1)}, bf16[544,1056]{1,0:T(8,128)(2,1)}, u32[]{:S(2)}, u32[]{:S(2)}) collective-permute-start(bf16[544,1056]{1,0:T(8,128)(2,1)S(1)} %get-tuple-element.21.own_ref), channel_id=1, source_target_pairs={{0,4},{4,8},{8,12},{1,5},{5,9},{9,13},{2,6},{6,10},{10,14},{3,7},{... | collective-permute-start | bytes 3446792 | tf_op jit(solution)/shard_map/ppermute | solution.py:26
  28.6 1.5 %collective-permute-start.7 = (bf16[544,1056]{1,0:T(8,128)(2,1)S(1)}, bf16[544,1056]{1,0:T(8,128)(2,1)}, u32[]{:S(2)}, u32[]{:S(2)}) collective-permute-start(bf16[544,1056]{1,0:T(8,128)(2,1)S(1)} %get-tuple-element.21.own_ref), channel_id=1, source_target_pairs={{4,0},{8,4},{12,8},{5,1},{9,5},{13,9},{6,2},{10,6},{14,10},{7,3},{... | collective-permute-start | bytes 3446792 | tf_op jit(solution)/shard_map/ppermute | solution.py:26
  30.1 0.7 fusion.70
  30.8 0.1 maximum_maximum_fusion.inv_ref
  31.4 16.6 %collective-permute-done.4.prev_ref = bf16[544,1056]{1,0:T(8,128)(2,1)} collective-permute-done((bf16[544,1056]{1,0:T(8,128)(2,1)S(1)}, bf16[544,1056]{1,0:T(8,128)(2,1)}, u32[]{:S(2)}, u32[]{:S(2)}) %collective-permute-start.4) | collective-permute-done | bytes 1148960 | tf_op jit(solution)/shard_map/ppermute | solution.py:26
  48.0 5.5 %collective-permute-done.5.next_ref = bf16[544,1056]{1,0:T(8,128)(2,1)} collective-permute-done((bf16[544,1056]{1,0:T(8,128)(2,1)S(1)}, bf16[544,1056]{1,0:T(8,128)(2,1)}, u32[]{:S(2)}, u32[]{:S(2)}) %collective-permute-start.5) | collective-permute-done | bytes 1148960 | tf_op jit(solution)/shard_map/ppermute | solution.py:26
  53.5 21.9 %shard_map.50 = f32[4,8,128]{2,1,0:T(8,128)S(1)} custom-call(s32[64]{0:T(128)S(1)} %reshape.38.skip_ref, s32[64]{0:T(128)S(1)} %reshape.39.skip_next_ref, s32[1]{0:T(128)} %bitcast.1.flag_ref, bf16[544,1056]{1,0:T(8,128)(2,1)S(1)} %get-tuple-element.20.own_ref, bf16[544,1056]{1,0:T(8,128)(2,1)} %collective-permute-done.4.prev_ref, ...), custom_call_target="tpu_custom_call" | custom-call | tf_op jit(solution)/shard_map/pallas_call | solution.py:236
  75.4 0.1 copy.28
  75.5 2.4 %collective-permute-done.7.next_ref = bf16[544,1056]{1,0:T(8,128)(2,1)} collective-permute-done((bf16[544,1056]{1,0:T(8,128)(2,1)S(1)}, bf16[544,1056]{1,0:T(8,128)(2,1)}, u32[]{:S(2)}, u32[]{:S(2)}) %collective-permute-start.7) | collective-permute-done | bytes 1148960 | tf_op jit(solution)/shard_map/ppermute | solution.py:26
  77.9 21.9 %shard_map.51 = f32[4,8,128]{2,1,0:T(8,128)S(1)} custom-call(s32[64]{0:T(128)S(1)} %reshape.38.skip_ref, s32[64]{0:T(128)S(1)} %reshape.39.skip_next_ref, s32[1]{0:T(128)} %bitcast.1.flag_ref, bf16[544,1056]{1,0:T(8,128)(2,1)S(1)} %get-tuple-element.21.own_ref, bf16[544,1056]{1,0:T(8,128)(2,1)} %collective-permute-done.6.prev_ref, ...), custom_call_target="tpu_custom_call" | custom-call | tf_op jit(solution)/shard_map/pallas_call | solution.py:236
  100.4 0.7 reshape.48
  101.2 3.2 %all-to-all-start = ((f32[4,1,384]{2,1,0:T(1,128)}), f32[4,1,384]{2,1,0:T(1,128)S(1)}, u32[]{:S(2)}, u32[]{:S(2)}) async-start(f32[4,1,384]{2,1,0:T(1,128)} %reshape.48), calls=%async_computation | async-start | bytes 12288 | tf_op jit(solution)/shard_map/all_to_all | solution.py:253
  104.4 5.6 %all-to-all-done = f32[4,1,384]{2,1,0:T(1,128)S(1)} async-done(((f32[4,1,384]{2,1,0:T(1,128)}), f32[4,1,384]{2,1,0:T(1,128)S(1)}, u32[]{:S(2)}, u32[]{:S(2)}) %all-to-all-start) | async-done | bytes 6176 | tf_op jit(solution)/shard_map/all_to_all | solution.py:253
  110.0 0.5 broadcast.129
  110.5 0.7 reduce
  111.4 0.6 dynamic-slice_bitcast_fusion
  112.4 0.6 fusion.74
  (72 shorter events, 2.0 us)
Async XLA Ops:
  0.6 5.5 %copy-start.1 = (s32[1,8,8]{2,1,0:T(8,128)S(1)}, s32[1,8,8]{2,1,0:T(8,128)}, u32[]{:S(2)}) copy-start(s32[1,8,8]{2,1,0:T(8,128)} %param.4) | copy-start | bytes 772
  1.4 9.0 %copy-start = (bf16[1,1024,1024]{2,1,0:T(8,128)(2,1)S(1)}, bf16[1,1024,1024]{2,1,0:T(8,128)(2,1)}, u32[]{:S(2)}) copy-start(bf16[1,1024,1024]{2,1,0:T(8,128)(2,1)} %param.3) | copy-start | bytes 6291460
  1.4 13.0 %collective-permute-start.2 = (bf16[1,16,1024]{2,1,0:T(8,128)(2,1)S(1)}, bf16[1,16,1024]{2,1,0:T(8,128)(2,1)S(1)}, u32[]{:S(2)}, u32[]{:S(2)}) collective-permute-start(bf16[1,16,1024]{2,1,0:T(8,128)(2,1)S(1)} %slice_select_fusion), channel_id=1, source_target_pairs={{0,1},{1,0},{2,3},{3,2},{4,5},{5,4},{6,7},{7,6},{8,9},{9,8},{10,11... | collective-permute-start | bytes 98312 | tf_op jit(solution)/shard_map/ppermute | solution.py:67
  2.0 5.5 %collective-permute-start.1 = (bf16[1,16,16]{2,1,0:T(8,128)(2,1)S(1)}, bf16[1,16,16]{2,1,0:T(8,128)(2,1)S(1)}, u32[]{:S(2)}, u32[]{:S(2)}) collective-permute-start(bf16[1,16,16]{2,1,0:T(8,128)(2,1)S(1)} %slice_select_fusion.1), channel_id=1, source_target_pairs={{0,3},{3,0},{1,2},{2,1},{4,7},{7,4},{5,6},{6,5},{8,11},{11,8},{9,1... | collective-permute-start | bytes 1544 | tf_op jit(solution)/shard_map/ppermute | solution.py:69
  6.0 4.0 %collective-permute-start.3 = (bf16[1,16,1024]{2,1,0:T(8,128)(2,1)S(1)}, bf16[1,16,1024]{2,1,0:T(8,128)(2,1)S(1)}, u32[]{:S(2)}, u32[]{:S(2)}) collective-permute-start(bf16[1,16,1024]{2,1,0:T(8,128)(2,1)S(1)} %select_bitcast_fusion.2), channel_id=1, source_target_pairs={{0,2},{2,0},{1,3},{3,1},{4,6},{6,4},{5,7},{7,5},{8,10},{10,8},{9,1... | collective-permute-start | bytes 98312 | tf_op jit(solution)/shard_map/ppermute | solution.py:68
  6.2 25.0 %collective-permute-start = (s32[1,8,8]{1,2,0:T(8,128)S(1)}, s32[1,8,8]{1,2,0:T(8,128)S(1)}, u32[]{:S(2)}, u32[]{:S(2)}) collective-permute-start(s32[1,8,8]{1,2,0:T(8,128)S(1)} %copy.22), channel_id=1, source_target_pairs={{4,0},{8,4},{12,8},{5,1},{9,5},{13,9},{6,2},{10,6},{14,10},{7,3},{... | collective-permute-start | bytes 776 | tf_op jit(solution)/shard_map/ppermute | solution.py:26
  14.6 16.2 %copy-start.2 = (s32[1,8,8]{2,1,0:T(8,128)S(1)}, s32[1,8,8]{2,1,0:T(8,128)}, u32[]{:S(2)}) copy-start(s32[1,8,8]{2,1,0:T(8,128)} %param.5) | copy-start | bytes 772
  16.5 31.5 %collective-permute-start.4 = (bf16[544,1056]{1,0:T(8,128)(2,1)S(1)}, bf16[544,1056]{1,0:T(8,128)(2,1)}, u32[]{:S(2)}, u32[]{:S(2)}) collective-permute-start(bf16[544,1056]{1,0:T(8,128)(2,1)S(1)} %get-tuple-element.20.own_ref), channel_id=1, source_target_pairs={{0,4},{4,8},{8,12},{1,5},{5,9},{9,13},{2,6},{6,10},{10,14},{3,7},{... | collective-permute-start | bytes 3446792 | tf_op jit(solution)/shard_map/ppermute | solution.py:26
  21.0 32.5 %collective-permute-start.5 = (bf16[544,1056]{1,0:T(8,128)(2,1)S(1)}, bf16[544,1056]{1,0:T(8,128)(2,1)}, u32[]{:S(2)}, u32[]{:S(2)}) collective-permute-start(bf16[544,1056]{1,0:T(8,128)(2,1)S(1)} %get-tuple-element.20.own_ref), channel_id=1, source_target_pairs={{4,0},{8,4},{12,8},{5,1},{9,5},{13,9},{6,2},{10,6},{14,10},{7,3},{... | collective-permute-start | bytes 3446792 | tf_op jit(solution)/shard_map/ppermute | solution.py:26
  23.0 52.5 %collective-permute-start.6 = (bf16[544,1056]{1,0:T(8,128)(2,1)S(1)}, bf16[544,1056]{1,0:T(8,128)(2,1)}, u32[]{:S(2)}, u32[]{:S(2)}) collective-permute-start(bf16[544,1056]{1,0:T(8,128)(2,1)S(1)} %get-tuple-element.21.own_ref), channel_id=1, source_target_pairs={{0,4},{4,8},{8,12},{1,5},{5,9},{9,13},{2,6},{6,10},{10,14},{3,7},{... | collective-permute-start | bytes 3446792 | tf_op jit(solution)/shard_map/ppermute | solution.py:26
  28.6 49.3 %collective-permute-start.7 = (bf16[544,1056]{1,0:T(8,128)(2,1)S(1)}, bf16[544,1056]{1,0:T(8,128)(2,1)}, u32[]{:S(2)}, u32[]{:S(2)}) collective-permute-start(bf16[544,1056]{1,0:T(8,128)(2,1)S(1)} %get-tuple-element.21.own_ref), channel_id=1, source_target_pairs={{4,0},{8,4},{12,8},{5,1},{9,5},{13,9},{6,2},{10,6},{14,10},{7,3},{... | collective-permute-start | bytes 3446792 | tf_op jit(solution)/shard_map/ppermute | solution.py:26
  101.2 8.8 %all-to-all-start = ((f32[4,1,384]{2,1,0:T(1,128)}), f32[4,1,384]{2,1,0:T(1,128)S(1)}, u32[]{:S(2)}, u32[]{:S(2)}) async-start(f32[4,1,384]{2,1,0:T(1,128)} %reshape.48), calls=%async_computation | async-start | bytes 12288 | tf_op jit(solution)/shard_map/all_to_all | solution.py:253

commit v14 on v13

--- a/solution.py
+++ b/solution.py
@@ -211,7 +211,7 @@
     assert cols % 2 == 0
     height = max(8, -(-cols // 8) * 8)
     both_t, cos_t, sin_t, inverse_t = tables
-    step = 2 if rows % 2 == 0 else 1
+    step = 2 if rows % 2 == 0 and rows >= 4 else 1
     band = pl.BlockSpec(
         (pl.Element(step * STRIDE + PATCH - STRIDE), pl.Element(broad)),
         lambda i, *_: (i * step * STRIDE, 0),
@@ -292,8 +292,11 @@
     skip_next = shifted(skipped, "sec", -1)
     use_own = (index == 0).astype(jnp.int32)
     rows_count = (own_pad.shape[0] - (PATCH - STRIDE)) // STRIDE
-    chunks = 2 if rows_count % 4 == 0 else 1
-    per = rows_count // chunks
+    if rows_count == 8:
+        sizes = [2, 2, 4]
+    else:
+        sizes = [rows_count]
+    offsets = [sum(sizes[:n]) for n in range(len(sizes))]
     cos_t, sin_t = dft_tables(PATCH)
     inverse_t = jnp.concatenate(
         [jnp.concatenate([cos_t, sin_t], axis=1), jnp.concatenate([-sin_t, cos_t], axis=1)], axis=0
@@ -302,13 +305,13 @@
     skip_flat = skipped.reshape(-1)
     skip_next_flat = skip_next.reshape(-1)
     firsts, seconds = [], []
-    for c in range(chunks):
-        start = c * per * STRIDE
-        own_c = own_pad[start : start + per * STRIDE + PATCH - STRIDE]
+    for first_row, count in zip(offsets, sizes):
+        start = first_row * STRIDE
+        own_c = own_pad[start : start + count * STRIDE + PATCH - STRIDE]
         prev_c = shifted(own_c, "sec", 1)
         next_c = shifted(own_c, "sec", -1)
         first_c, second_c = pair_flows(
-            own_c, prev_c, next_c, skip_flat, skip_next_flat, use_own, c * per, tables
+            own_c, prev_c, next_c, skip_flat, skip_next_flat, use_own, first_row, tables
         )
         firsts.append(first_c)
         seconds.append(second_c)

time: 113 us -> 135 us (1.19)
  starting transfers between devices: 20.6 us -> 31.4 us
  waiting for transfers between devices: 32.5 us -> 38.2 us
  Pallas kernels: 43.8 us -> 46.2 us
  local copies, waits for them, and re-layouts: 8.89 us -> 10.7 us
    ppermute x5 -> x7, starting transfers between devices: 14.2 us -> 20.5 us  [shifted(): lax.ppermute(value, axis, [(source, source + steps) for source in range(f...]
    ppermute x5 -> x7, waiting for transfers between devices: 24.5 us -> 29.5 us  [shifted(): lax.ppermute(value, axis, [(source, source + steps) for source in range(f...]
    all_to_all x1, starting transfers between devices: 3.25 us -> 7.77 us  [gather_sections(): return lax.all_to_all(spread, axis, 0, 0, tiled=True)]
    pallas_call x2 -> x3, Pallas kernels: 43.8 us -> 46.2 us  [pair_flows(): pl.pallas_call(functools.partial(_flow_kernel, cols=cols, row0=row0, coun...]
    unnamed x13 -> x15, local copies, waits for them, and re-layouts: 1.8 us -> 3.76 us
    slice x1 -> x2, other arithmetic: 1.86 us -> 2.77 us  [body(): own_c = own_pad[start:start + count * STRIDE + PATCH - STRIDE]]
  transfers between devices with their start and end apart: 9 -> 11, of which waited for: 5 -> 4; matrix products, arithmetic and copies ran while one was open for 9% -> 9% of each run, Pallas kernels for 19% -> 18%
where the time goes in v14:
time: 135 us; the launch traced here: 134 us
  Pallas kernels  46.2 us (34%)
  waiting for transfers between devices  38.2 us (28%)
  starting transfers between devices  31.4 us (23%)
  local copies, waits for them, and re-layouts  10.7 us (8%)
  other arithmetic  6.91 us (5%)
    pallas_call x3, Pallas kernels, pair_flows(): pl.pallas_call(functools.partial(_flow_kernel, cols=cols, row0=row0, coun...  46.2 us
    ppermute x7, waiting for transfers between devices, shifted(): lax.ppermute(value, axis, [(source, source + steps) for source in range(f...  29.5 us
    ppermute x7, starting transfers between devices, shifted(): lax.ppermute(value, axis, [(source, source + steps) for source in range(f...  20.5 us
    all_to_all x1, starting transfers between devices, gather_sections(): return lax.all_to_all(spread, axis, 0, 0, tiled=True)  7.77 us
    all_to_all x1, waiting for transfers between devices, gather_sections(): return lax.all_to_all(spread, axis, 0, 0, tiled=True)  5.58 us
    concatenate x1, local copies, waits for them, and re-layouts, extended_pairs(): jnp.concatenate([keep(left, cols_got), block, keep(right, cols_got)], axi...  3.98 us
    unnamed x15, local copies, waits for them, and re-layouts  3.76 us
    ppermute x1, waiting for transfers between devices, extended_pairs(): cols_got = jnp.swapaxes(lax.ppermute(cols_send, 'tile', swap), 1, 2)  3.1 us
  transfers between devices with their start and end apart: 11, of which 4 were waited for; matrix products, arithmetic and copies ran while one was open for 9% of the time, Pallas kernels for 18%

profile of v14, /device:TPU:0, one launch (start us, length us, event | category | flops | bytes accessed | tf_op | source)
XLA Modules:
  0.0 134.5 jit_solution(17591313747979130293)
XLA Ops:
  0.6 0.9 copy.50
  1.5 1.3 collective-permute-start
  2.8 0.8 slice_select_fusion
  3.6 0.5 collective-permute-start.2
  4.2 2.6 %collective-permute-start.1 = (bf16[1,16,16]{2,1,0:T(8,128)(2,1)S(1)}, bf16[1,16,16]{2,1,0:T(8,128)(2,1)S(1)}, u32[]{:S(2)}, u32[]{:S(2)}) collective-permute-start(bf16[1,16,16]{2,1,0:T(8,128)(2,1)S(1)} %slice_select_fusion.1), channel_id=1, source_target_pairs={{0,3},{3,0},{1,2},{2,1},{4,7},{7,4},{5,6},{6,5},{8,11},{11,8},{9,1... | collective-permute-start | bytes 1544 | tf_op jit(solution)/shard_map/ppermute | solution.py:69
  6.8 1.2 fusion.84
  8.3 0.8 copy.68
  9.1 3.1 %collective-permute-done.3 = bf16[1,16,1024]{2,1,0:T(8,128)(2,1)S(1)} collective-permute-done((bf16[1,16,1024]{2,1,0:T(8,128)(2,1)S(1)}, bf16[1,16,1024]{2,1,0:T(8,128)(2,1)S(1)}, u32[]{:S(2)}, u32[]{:S(2)}) %collective-permute-start.3) | collective-permute-done | bytes 32800 | tf_op jit(solution)/shard_map/ppermute | solution.py:68
  12.3 0.2 copy.54
  12.5 4.0 %concatenate.38 = bf16[1,1024,1056]{2,1,0:T(8,128)(2,1)} concatenate(bf16[1,1024,16]{2,1,0:T(8,128)(2,1)S(1)} %copy.54, bf16[1,1024,1024]{2,1,0:T(8,128)(2,1)S(1)} %copy-done, bf16[1,1024,16]{2,1,0:T(8,128)(2,1)S(1)} %copy.55), dimensions={2} | concatenate | bytes 4325376 | tf_op jit(solution)/shard_map/concatenate | solution.py:76
  16.6 1.4 %fusion.1 = (bf16[288,1056]{1,0:T(8,128)(2,1)S(1)}, bf16[288,1056]{1,0:T(8,128)(2,1)S(1)}) fusion(bf16[1,1024,1056]{2,1,0:T(8,128)(2,1)} %concatenate.38, bf16[1,16,1056]{2,1,0:T(8,128)(2,1)S(1)} %concatenate.37), kind=kLoop, calls=%fused_computation.4 | loop fusion | flops 1216512 | bytes 4273152 | tf_op jit(solution)/shard_map/slice | solution.py:310
  18.0 1.3 collective-permute-start.5
  19.4 1.4 %fusion.own_ref = bf16[544,1056]{1,0:T(8,128)(2,1)S(1)} fusion(bf16[1,16,1056]{2,1,0:T(8,128)(2,1)S(1)} %concatenate.44, bf16[1,1024,1056]{2,1,0:T(8,128)(2,1)} %concatenate.38), kind=kLoop, calls=%fused_computation.1 | loop fusion | flops 2297856 | bytes 3345408 | tf_op jit(solution)/shard_map/slice | solution.py:310
  20.8 1.3 collective-permute-start.9
  22.1 6.9 %collective-permute-start.8 = (bf16[544,1056]{1,0:T(8,128)(2,1)S(1)}, bf16[544,1056]{1,0:T(8,128)(2,1)}, u32[]{:S(2)}, u32[]{:S(2)}) collective-permute-start(bf16[544,1056]{1,0:T(8,128)(2,1)S(1)} %fusion.own_ref), channel_id=1, source_target_pairs={{0,4},{4,8},{8,12},{1,5},{5,9},{9,13},{2,6},{6,10},{10,14},{3,7},{... | collective-permute-start | bytes 3446792 | tf_op jit(solution)/shard_map/ppermute | solution.py:26
  29.0 3.8 %collective-permute-start.4 = (bf16[288,1056]{1,0:T(8,128)(2,1)S(1)}, bf16[288,1056]{1,0:T(8,128)(2,1)}, u32[]{:S(2)}, u32[]{:S(2)}) collective-permute-start(bf16[288,1056]{1,0:T(8,128)(2,1)S(1)} %get-tuple-element.20.own_ref), channel_id=1, source_target_pairs={{0,4},{4,8},{8,12},{1,5},{5,9},{9,13},{2,6},{6,10},{10,14},{3,7},{... | collective-permute-start | bytes 1824776 | tf_op jit(solution)/shard_map/ppermute | solution.py:26
  32.8 0.7 negate_convert_fusion
  33.5 1.3 collective-permute-start.7
  34.8 3.7 %collective-permute-done.5.next_ref = bf16[288,1056]{1,0:T(8,128)(2,1)} collective-permute-done((bf16[288,1056]{1,0:T(8,128)(2,1)S(1)}, bf16[288,1056]{1,0:T(8,128)(2,1)}, u32[]{:S(2)}, u32[]{:S(2)}) %collective-permute-start.5) | collective-permute-done | bytes 608288 | tf_op jit(solution)/shard_map/ppermute | solution.py:26
  38.5 4.7 %collective-permute-start.6 = (bf16[288,1056]{1,0:T(8,128)(2,1)S(1)}, bf16[288,1056]{1,0:T(8,128)(2,1)}, u32[]{:S(2)}, u32[]{:S(2)}) collective-permute-start(bf16[288,1056]{1,0:T(8,128)(2,1)S(1)} %get-tuple-element.21.own_ref), channel_id=1, source_target_pairs={{0,4},{4,8},{8,12},{1,5},{5,9},{9,13},{2,6},{6,10},{10,14},{3,7},{... | collective-permute-start | bytes 1824776 | tf_op jit(solution)/shard_map/ppermute | solution.py:26
  43.3 0.7 fusion.70
  44.4 25.8 %collective-permute-done.4.prev_ref = bf16[288,1056]{1,0:T(8,128)(2,1)} collective-permute-done((bf16[288,1056]{1,0:T(8,128)(2,1)S(1)}, bf16[288,1056]{1,0:T(8,128)(2,1)}, u32[]{:S(2)}, u32[]{:S(2)}) %collective-permute-start.4) | collective-permute-done | bytes 608288 | tf_op jit(solution)/shard_map/ppermute | solution.py:26
  70.2 12.0 %shard_map.50 = f32[2,8,128]{2,1,0:T(8,128)S(1)} custom-call(s32[64]{0:T(128)S(1)} %reshape.46.skip_ref, s32[64]{0:T(128)S(1)} %reshape.47.skip_next_ref, s32[1]{0:T(128)} %bitcast.1.flag_ref, bf16[288,1056]{1,0:T(8,128)(2,1)S(1)} %get-tuple-element.20.own_ref, bf16[288,1056]{1,0:T(8,128)(2,1)} %collective-permute-done.4.prev_ref, ...), custom_call_target="tpu_custom_call" | custom-call | tf_op jit(solution)/shard_map/pallas_call | solution.py:236
  82.4 12.1 %shard_map.51 = f32[2,8,128]{2,1,0:T(8,128)S(1)} custom-call(s32[64]{0:T(128)S(1)} %reshape.46.skip_ref, s32[64]{0:T(128)S(1)} %reshape.47.skip_next_ref, s32[1]{0:T(128)} %bitcast.1.flag_ref, bf16[288,1056]{1,0:T(8,128)(2,1)S(1)} %get-tuple-element.21.own_ref, bf16[288,1056]{1,0:T(8,128)(2,1)} %collective-permute-done.6.prev_ref, ...), custom_call_target="tpu_custom_call" | custom-call | tf_op jit(solution)/shard_map/pallas_call | solution.py:236
  94.7 22.2 %shard_map.52 = f32[4,8,128]{2,1,0:T(8,128)S(1)} custom-call(s32[64]{0:T(128)S(1)} %reshape.46.skip_ref, s32[64]{0:T(128)S(1)} %reshape.47.skip_next_ref, s32[1]{0:T(128)} %bitcast.1.flag_ref, bf16[544,1056]{1,0:T(8,128)(2,1)S(1)} %fusion.own_ref, bf16[544,1056]{1,0:T(8,128)(2,1)} %collective-permute-done.8.prev_ref, ...), custom_call_target="tpu_custom_call" | custom-call | tf_op jit(solution)/shard_map/pallas_call | solution.py:236
  117.4 0.7 reshape.58
  118.1 7.8 %all-to-all-start = ((f32[4,1,384]{2,1,0:T(1,128)}), f32[4,1,384]{2,1,0:T(1,128)S(1)}, u32[]{:S(2)}, u32[]{:S(2)}) async-start(f32[4,1,384]{2,1,0:T(1,128)} %reshape.58), calls=%async_computation | async-start | bytes 12288 | tf_op jit(solution)/shard_map/all_to_all | solution.py:253
  125.9 5.6 %all-to-all-done = f32[4,1,384]{2,1,0:T(1,128)S(1)} async-done(((f32[4,1,384]{2,1,0:T(1,128)}), f32[4,1,384]{2,1,0:T(1,128)S(1)}, u32[]{:S(2)}, u32[]{:S(2)}) %all-to-all-start) | async-done | bytes 6176 | tf_op jit(solution)/shard_map/all_to_all | solution.py:253
  131.5 0.5 broadcast.129
  132.0 0.7 reduce
  132.9 0.6 dynamic-slice_bitcast_fusion
  133.9 0.6 fusion.74
  (81 shorter events, 2.6 us)
Async XLA Ops:
  0.6 11.9 %copy-start = (bf16[1,1024,1024]{2,1,0:T(8,128)(2,1)S(1)}, bf16[1,1024,1024]{2,1,0:T(8,128)(2,1)}, u32[]{:S(2)}) copy-start(bf16[1,1024,1024]{2,1,0:T(8,128)(2,1)} %param.3) | copy-start | bytes 6291460
  1.5 31.9 %collective-permute-start = (s32[1,8,8]{1,2,0:T(8,128)S(1)}, s32[1,8,8]{1,2,0:T(8,128)S(1)}, u32[]{:S(2)}, u32[]{:S(2)}) collective-permute-start(s32[1,8,8]{1,2,0:T(8,128)S(1)} %copy.50), channel_id=1, source_target_pairs={{4,0},{8,4},{12,8},{5,1},{9,5},{13,9},{6,2},{10,6},{14,10},{7,3},{... | collective-permute-start | bytes 776 | tf_op jit(solution)/shard_map/ppermute | solution.py:26
  3.6 12.9 %collective-permute-start.2 = (bf16[1,16,1024]{2,1,0:T(8,128)(2,1)S(1)}, bf16[1,16,1024]{2,1,0:T(8,128)(2,1)S(1)}, u32[]{:S(2)}, u32[]{:S(2)}) collective-permute-start(bf16[1,16,1024]{2,1,0:T(8,128)(2,1)S(1)} %slice_select_fusion), channel_id=1, source_target_pairs={{0,1},{1,0},{2,3},{3,2},{4,5},{5,4},{6,7},{7,6},{8,9},{9,8},{10,11... | collective-permute-start | bytes 98312 | tf_op jit(solution)/shard_map/ppermute | solution.py:67
  4.2 4.9 %collective-permute-start.1 = (bf16[1,16,16]{2,1,0:T(8,128)(2,1)S(1)}, bf16[1,16,16]{2,1,0:T(8,128)(2,1)S(1)}, u32[]{:S(2)}, u32[]{:S(2)}) collective-permute-start(bf16[1,16,16]{2,1,0:T(8,128)(2,1)S(1)} %slice_select_fusion.1), channel_id=1, source_target_pairs={{0,3},{3,0},{1,2},{2,1},{4,7},{7,4},{5,6},{6,5},{8,11},{11,8},{9,1... | collective-permute-start | bytes 1544 | tf_op jit(solution)/shard_map/ppermute | solution.py:69
  8.2 4.0 %collective-permute-start.3 = (bf16[1,16,1024]{2,1,0:T(8,128)(2,1)S(1)}, bf16[1,16,1024]{2,1,0:T(8,128)(2,1)S(1)}, u32[]{:S(2)}, u32[]{:S(2)}) collective-permute-start(bf16[1,16,1024]{2,1,0:T(8,128)(2,1)S(1)} %select_bitcast_fusion.2), channel_id=1, source_target_pairs={{0,2},{2,0},{1,3},{3,1},{4,6},{6,4},{5,7},{7,5},{8,10},{10,8},{9,1... | collective-permute-start | bytes 98312 | tf_op jit(solution)/shard_map/ppermute | solution.py:68
  18.0 11.0 %copy-start.1 = (s32[1,8,8]{2,1,0:T(8,128)S(1)}, s32[1,8,8]{2,1,0:T(8,128)}, u32[]{:S(2)}) copy-start(s32[1,8,8]{2,1,0:T(8,128)} %param.4) | copy-start | bytes 772
  18.0 20.5 %collective-permute-start.5 = (bf16[288,1056]{1,0:T(8,128)(2,1)S(1)}, bf16[288,1056]{1,0:T(8,128)(2,1)}, u32[]{:S(2)}, u32[]{:S(2)}) collective-permute-start(bf16[288,1056]{1,0:T(8,128)(2,1)S(1)} %get-tuple-element.20.own_ref), channel_id=1, source_target_pairs={{4,0},{8,4},{12,8},{5,1},{9,5},{13,9},{6,2},{10,6},{14,10},{7,3},{... | collective-permute-start | bytes 1824776 | tf_op jit(solution)/shard_map/ppermute | solution.py:26
  20.8 73.9 %collective-permute-start.9 = (bf16[544,1056]{1,0:T(8,128)(2,1)S(1)}, bf16[544,1056]{1,0:T(8,128)(2,1)}, u32[]{:S(2)}, u32[]{:S(2)}) collective-permute-start(bf16[544,1056]{1,0:T(8,128)(2,1)S(1)} %fusion.own_ref), channel_id=1, source_target_pairs={{4,0},{8,4},{12,8},{5,1},{9,5},{13,9},{6,2},{10,6},{14,10},{7,3},{... | collective-permute-start | bytes 3446792 | tf_op jit(solution)/shard_map/ppermute | solution.py:26
  22.1 72.6 %collective-permute-start.8 = (bf16[544,1056]{1,0:T(8,128)(2,1)S(1)}, bf16[544,1056]{1,0:T(8,128)(2,1)}, u32[]{:S(2)}, u32[]{:S(2)}) collective-permute-start(bf16[544,1056]{1,0:T(8,128)(2,1)S(1)} %fusion.own_ref), channel_id=1, source_target_pairs={{0,4},{4,8},{8,12},{1,5},{5,9},{9,13},{2,6},{6,10},{10,14},{3,7},{... | collective-permute-start | bytes 3446792 | tf_op jit(solution)/shard_map/ppermute | solution.py:26
  29.0 41.2 %collective-permute-start.4 = (bf16[288,1056]{1,0:T(8,128)(2,1)S(1)}, bf16[288,1056]{1,0:T(8,128)(2,1)}, u32[]{:S(2)}, u32[]{:S(2)}) collective-permute-start(bf16[288,1056]{1,0:T(8,128)(2,1)S(1)} %get-tuple-element.20.own_ref), channel_id=1, source_target_pairs={{0,4},{4,8},{8,12},{1,5},{5,9},{9,13},{2,6},{6,10},{10,14},{3,7},{... | collective-permute-start | bytes 1824776 | tf_op jit(solution)/shard_map/ppermute | solution.py:26
  33.5 48.9 %collective-permute-start.7 = (bf16[288,1056]{1,0:T(8,128)(2,1)S(1)}, bf16[288,1056]{1,0:T(8,128)(2,1)}, u32[]{:S(2)}, u32[]{:S(2)}) collective-permute-start(bf16[288,1056]{1,0:T(8,128)(2,1)S(1)} %get-tuple-element.21.own_ref), channel_id=1, source_target_pairs={{4,0},{8,4},{12,8},{5,1},{9,5},{13,9},{6,2},{10,6},{14,10},{7,3},{... | collective-permute-start | bytes 1824776 | tf_op jit(solution)/shard_map/ppermute | solution.py:26
  38.5 43.9 %collective-permute-start.6 = (bf16[288,1056]{1,0:T(8,128)(2,1)S(1)}, bf16[288,1056]{1,0:T(8,128)(2,1)}, u32[]{:S(2)}, u32[]{:S(2)}) collective-permute-start(bf16[288,1056]{1,0:T(8,128)(2,1)S(1)} %get-tuple-element.21.own_ref), channel_id=1, source_target_pairs={{0,4},{4,8},{8,12},{1,5},{5,9},{9,13},{2,6},{6,10},{10,14},{3,7},{... | collective-permute-start | bytes 1824776 | tf_op jit(solution)/shard_map/ppermute | solution.py:26
  118.1 13.4 %all-to-all-start = ((f32[4,1,384]{2,1,0:T(1,128)}), f32[4,1,384]{2,1,0:T(1,128)S(1)}, u32[]{:S(2)}, u32[]{:S(2)}) async-start(f32[4,1,384]{2,1,0:T(1,128)} %reshape.58), calls=%async_computation | async-start | bytes 12288 | tf_op jit(solution)/shard_map/all_to_all | solution.py:253

commit v15 on v6

--- a/solution.py
+++ b/solution.py
@@ -262,7 +262,6 @@
         own_pad = extended_pairs(images, RIM)[0]
     else:
         own_pad = extended(images, (("sub", 1), ("tile", 2)), RIM)[0]
-    skip_next = shifted(skipped, "sec", -1)
     use_own = (index == 0).astype(jnp.int32)
     rows_count = (own_pad.shape[0] - (PATCH - STRIDE)) // STRIDE
     chunks = max(n for n in (1, 2, 4) if rows_count % n == 0)
@@ -273,13 +272,15 @@
     )
     tables = (jnp.concatenate([cos_t, sin_t], axis=0), cos_t, sin_t, inverse_t)
     skip_flat = skipped.reshape(-1)
-    skip_next_flat = skip_next.reshape(-1)
     firsts, seconds = [], []
     for c in range(chunks):
         start = c * per * STRIDE
         own_c = own_pad[start : start + per * STRIDE + PATCH - STRIDE]
         prev_c = shifted(own_c, "sec", 1)
         next_c = shifted(own_c, "sec", -1)
+        if c == 0:
+            skip_next = shifted(lax.optimization_barrier((skipped, own_c))[0], "sec", -1)
+            skip_next_flat = skip_next.reshape(-1)
         first_c, second_c = pair_flows(
             own_c, prev_c, next_c, skip_flat, skip_next_flat, use_own, c * per, tables
         )

time: 111 us -> 128 us (1.15)
  waiting for transfers between devices: 10.2 us -> 28.9 us
  starting transfers between devices: 33.7 us -> 32.3 us
    ppermute x9, waiting for transfers between devices: 3.45 us -> 20.8 us  [shifted(): lax.ppermute(value, axis, [(source, source + steps) for source in range(f...]
    ppermute x1, waiting for transfers between devices: 1.2 us -> 2.5 us  [extended_pairs(): cols_got = jnp.swapaxes(lax.ppermute(cols_send, 'tile', swap), 1, 2)]
  transfers between devices with their start and end apart: 13 -> 13, of which waited for: 3 -> 3; matrix products, arithmetic and copies ran while one was open for 11% -> 8% of each run, Pallas kernels for 32% -> 28%
where the time goes in v15:
time: 128 us
  Pallas kernels  47.9 us (37%)
  starting transfers between devices  32.3 us (25%)
  waiting for transfers between devices  28.9 us (23%)
  local copies, waits for them, and re-layouts  10.1 us (8%)
  other arithmetic  7.42 us (6%)
    pallas_call x4, Pallas kernels, pair_flows(): pl.pallas_call(functools.partial(_flow_kernel, cols=cols, row0=row0), gri...  47.9 us
    ppermute x9, starting transfers between devices, shifted(): lax.ppermute(value, axis, [(source, source + steps) for source in range(f...  25.3 us
    ppermute x9, waiting for transfers between devices, shifted(): lax.ppermute(value, axis, [(source, source + steps) for source in range(f...  20.8 us
    all_to_all x1, waiting for transfers between devices, gather_sections(): return lax.all_to_all(spread, axis, 0, 0, tiled=True)  5.58 us
    concatenate x1, local copies, waits for them, and re-layouts, extended_pairs(): jnp.concatenate([keep(left, cols_got), block, keep(right, cols_got)], axi...  3.96 us
    all_to_all x1, starting transfers between devices, gather_sections(): return lax.all_to_all(spread, axis, 0, 0, tiled=True)  3.91 us
    ppermute x1, starting transfers between devices, extended_pairs(): lax.ppermute(corner_send, ('tile', 'sub'), [(0, 3), (3, 0), (1, 2), (2, 1)])  2.6 us
  transfers between devices with their start and end apart: 13, of which 3 were waited for; matrix products, arithmetic and copies ran while one was open for 8% of the time, Pallas kernels for 28%

profile of v15, /device:TPU:0, one launch (start us, length us, event | category | flops | bytes accessed | tf_op | source)
XLA Modules:
  0.0 127.7 jit_solution(472156581451452626)
XLA Ops:
  0.6 0.9 slice_select_fusion
  1.6 0.5 collective-permute-start.1
  2.1 2.6 %collective-permute-start = (bf16[1,16,16]{2,1,0:T(8,128)(2,1)S(1)}, bf16[1,16,16]{2,1,0:T(8,128)(2,1)S(1)}, u32[]{:S(2)}, u32[]{:S(2)}) collective-permute-start(bf16[1,16,16]{2,1,0:T(8,128)(2,1)S(1)} %slice_select_fusion.1), channel_id=1, source_target_pairs={{0,3},{3,0},{1,2},{2,1},{4,7},{7,4},{5,6},{6,5},{8,11},{11,8},{9,1... | collective-permute-start | bytes 1544 | tf_op jit(solution)/shard_map/ppermute | solution.py:69
  4.7 1.2 fusion.84
  6.2 0.7 convert_multiply_fusion
  6.9 0.7 select_convert_fusion
  7.6 2.5 %collective-permute-done.2 = bf16[1,16,1024]{2,1,0:T(8,128)(2,1)S(1)} collective-permute-done((bf16[1,16,1024]{2,1,0:T(8,128)(2,1)S(1)}, bf16[1,16,1024]{2,1,0:T(8,128)(2,1)S(1)}, u32[]{:S(2)}, u32[]{:S(2)}) %collective-permute-start.2) | collective-permute-done | bytes 32800 | tf_op jit(solution)/shard_map/ppermute | solution.py:68
  10.5 4.0 %concatenate.38 = bf16[1,1024,1056]{2,1,0:T(8,128)(2,1)} concatenate(bf16[1,1024,16]{2,1,0:T(8,128)(2,1)S(1)} %copy.31, bf16[1,1024,1024]{2,1,0:T(8,128)(2,1)S(1)} %copy-done, bf16[1,1024,16]{2,1,0:T(8,128)(2,1)S(1)} %copy.32), dimensions={2} | concatenate | bytes 4325376 | tf_op jit(solution)/shard_map/concatenate | solution.py:76
  14.7 1.9 %slice_bitcast_fusion.1 = (bf16[288,1056]{1,0:T(8,128)(2,1)S(1)}, bf16[288,1056]{1,0:T(8,128)(2,1)S(1)}, bf16[288,1056]{1,0:T(8,128)(2,1)S(1)}, bf16[288,1056]{1,0:T(8,128)(2,1)S(1)}) fusion(bf16[1,1024,1056]{2,1,0:T(8,128)(2,1)} %concatenate.38, bf16[1,16,1056]{2,1,0:T(8,128)(2,1)S(1)} %concatenate.37, bf16[1,16,1056]{2,1,0:T(8,128)(2,1)S(1)} %concatenate.44), kind=kLoop, calls=%fused_computation.3 | loop fusion | flops 2433024 | bytes 6187008 | tf_op jit(solution)/shard_map/slice | solution.py:278
  16.6 4.3 %collective-permute-start.4 = (bf16[288,1056]{1,0:T(8,128)(2,1)S(1)}, bf16[288,1056]{1,0:T(8,128)(2,1)}, u32[]{:S(2)}, u32[]{:S(2)}) collective-permute-start(bf16[288,1056]{1,0:T(8,128)(2,1)S(1)} %get-tuple-element.23.own_ref), channel_id=1, source_target_pairs={{0,4},{4,8},{8,12},{1,5},{5,9},{9,13},{2,6},{6,10},{10,14},{3,7},{... | collective-permute-start | bytes 1824776 | tf_op jit(solution)/shard_map/ppermute | solution.py:26
  20.9 1.3 %collective-permute-start.5 = (bf16[288,1056]{1,0:T(8,128)(2,1)S(1)}, bf16[288,1056]{1,0:T(8,128)(2,1)}, u32[]{:S(2)}, u32[]{:S(2)}) collective-permute-start(bf16[288,1056]{1,0:T(8,128)(2,1)S(1)} %get-tuple-element.23.own_ref), channel_id=1, source_target_pairs={{4,0},{8,4},{12,8},{5,1},{9,5},{13,9},{6,2},{10,6},{14,10},{7,3},{... | collective-permute-start | bytes 1824776 | tf_op jit(solution)/shard_map/ppermute | solution.py:26
  22.2 5.4 %collective-permute-start.6 = (bf16[288,1056]{1,0:T(8,128)(2,1)S(1)}, bf16[288,1056]{1,0:T(8,128)(2,1)}, u32[]{:S(2)}, u32[]{:S(2)}) collective-permute-start(bf16[288,1056]{1,0:T(8,128)(2,1)S(1)} %get-tuple-element.22.own_ref), channel_id=1, source_target_pairs={{0,4},{4,8},{8,12},{1,5},{5,9},{9,13},{2,6},{6,10},{10,14},{3,7},{... | collective-permute-start | bytes 1824776 | tf_op jit(solution)/shard_map/ppermute | solution.py:26
  27.6 0.7 fusion.70
  28.2 0.7 negate_convert_fusion
  28.9 1.3 %collective-permute-start.7 = (bf16[288,1056]{1,0:T(8,128)(2,1)S(1)}, bf16[288,1056]{1,0:T(8,128)(2,1)}, u32[]{:S(2)}, u32[]{:S(2)}) collective-permute-start(bf16[288,1056]{1,0:T(8,128)(2,1)S(1)} %get-tuple-element.22.own_ref), channel_id=1, source_target_pairs={{4,0},{8,4},{12,8},{5,1},{9,5},{13,9},{6,2},{10,6},{14,10},{7,3},{... | collective-permute-start | bytes 1824776 | tf_op jit(solution)/shard_map/ppermute | solution.py:26
  30.4 1.3 %collective-permute-start.3 = (s32[1,8,8]{2,1,0:T(8,128)S(1)}, s32[1,8,8]{2,1,0:T(8,128)S(1)}, u32[]{:S(2)}, u32[]{:S(2)}) collective-permute-start(s32[1,8,8]{2,1,0:T(8,128)S(1)} %copy-done.1), channel_id=1, source_target_pairs={{4,0},{8,4},{12,8},{5,1},{9,5},{13,9},{6,2},{10,6},{14,10},{7,3},{... | collective-permute-start | bytes 776 | tf_op jit(solution)/shard_map/ppermute | solution.py:26
  31.8 20.8 %collective-permute-done.3 = s32[1,8,8]{2,1,0:T(8,128)S(1)} collective-permute-done((s32[1,8,8]{2,1,0:T(8,128)S(1)}, s32[1,8,8]{2,1,0:T(8,128)S(1)}, u32[]{:S(2)}, u32[]{:S(2)}) %collective-permute-start.3) | collective-permute-done | bytes 288 | tf_op jit(solution)/shard_map/ppermute | solution.py:26
  52.6 3.6 %collective-permute-start.8 = (bf16[288,1056]{1,0:T(8,128)(2,1)S(1)}, bf16[288,1056]{1,0:T(8,128)(2,1)}, u32[]{:S(2)}, u32[]{:S(2)}) collective-permute-start(bf16[288,1056]{1,0:T(8,128)(2,1)S(1)} %get-tuple-element.24.own_ref), channel_id=1, source_target_pairs={{0,4},{4,8},{8,12},{1,5},{5,9},{9,13},{2,6},{6,10},{10,14},{3,7},{... | collective-permute-start | bytes 1824776 | tf_op jit(solution)/shard_map/ppermute | solution.py:26
  56.2 1.3 %collective-permute-start.9 = (bf16[288,1056]{1,0:T(8,128)(2,1)S(1)}, bf16[288,1056]{1,0:T(8,128)(2,1)}, u32[]{:S(2)}, u32[]{:S(2)}) collective-permute-start(bf16[288,1056]{1,0:T(8,128)(2,1)S(1)} %get-tuple-element.24.own_ref), channel_id=1, source_target_pairs={{4,0},{8,4},{12,8},{5,1},{9,5},{13,9},{6,2},{10,6},{14,10},{7,3},{... | collective-permute-start | bytes 1824776 | tf_op jit(solution)/shard_map/ppermute | solution.py:26
  57.5 5.4 %collective-permute-start.10 = (bf16[288,1056]{1,0:T(8,128)(2,1)S(1)}, bf16[288,1056]{1,0:T(8,128)(2,1)}, u32[]{:S(2)}, u32[]{:S(2)}) collective-permute-start(bf16[288,1056]{1,0:T(8,128)(2,1)S(1)} %get-tuple-element.25.own_ref), channel_id=1, source_target_pairs={{0,4},{4,8},{8,12},{1,5},{5,9},{9,13},{2,6},{6,10},{10,14},{3,7},{... | collective-permute-start | bytes 1824776 | tf_op jit(solution)/shard_map/ppermute | solution.py:26
  62.9 11.9 %shard_map.50 = f32[2,8,128]{2,1,0:T(8,128)S(1)} custom-call(s32[64]{0:T(128)S(1)} %reshape.54.skip_ref, s32[64]{0:T(128)S(1)} %reshape.55.skip_next_ref, s32[1]{0:T(128)} %bitcast.5.flag_ref, bf16[288,1056]{1,0:T(8,128)(2,1)S(1)} %get-tuple-element.23.own_ref, bf16[288,1056]{1,0:T(8,128)(2,1)} %collective-permute-done.4.prev_ref, ...), custom_call_target="tpu_custom_call" | custom-call | tf_op jit(solution)/shard_map/pallas_call | solution.py:209
  74.9 1.5 %collective-permute-start.11 = (bf16[288,1056]{1,0:T(8,128)(2,1)S(1)}, bf16[288,1056]{1,0:T(8,128)(2,1)S(1)}, u32[]{:S(2)}, u32[]{:S(2)}) collective-permute-start(bf16[288,1056]{1,0:T(8,128)(2,1)S(1)} %get-tuple-element.25.own_ref), channel_id=1, source_target_pairs={{4,0},{8,4},{12,8},{5,1},{9,5},{13,9},{6,2},{10,6},{14,10},{7,3},{... | collective-permute-start | bytes 1824776 | tf_op jit(solution)/shard_map/ppermute | solution.py:26
  76.6 11.9 %shard_map.51 = f32[2,8,128]{2,1,0:T(8,128)S(1)} custom-call(s32[64]{0:T(128)S(1)} %reshape.54.skip_ref, s32[64]{0:T(128)S(1)} %reshape.55.skip_next_ref, s32[1]{0:T(128)} %bitcast.5.flag_ref, bf16[288,1056]{1,0:T(8,128)(2,1)S(1)} %get-tuple-element.22.own_ref, bf16[288,1056]{1,0:T(8,128)(2,1)} %collective-permute-done.6.prev_ref, ...), custom_call_target="tpu_custom_call" | custom-call | tf_op jit(solution)/shard_map/pallas_call | solution.py:209
  88.8 12.0 %shard_map.52 = f32[2,8,128]{2,1,0:T(8,128)S(1)} custom-call(s32[64]{0:T(128)S(1)} %reshape.54.skip_ref, s32[64]{0:T(128)S(1)} %reshape.55.skip_next_ref, s32[1]{0:T(128)} %bitcast.5.flag_ref, bf16[288,1056]{1,0:T(8,128)(2,1)S(1)} %get-tuple-element.24.own_ref, bf16[288,1056]{1,0:T(8,128)(2,1)} %collective-permute-done.8.prev_ref, ...), custom_call_target="tpu_custom_call" | custom-call | tf_op jit(solution)/shard_map/pallas_call | solution.py:209
  101.1 12.0 %shard_map.53 = f32[2,8,128]{2,1,0:T(8,128)S(1)} custom-call(s32[64]{0:T(128)S(1)} %reshape.54.skip_ref, s32[64]{0:T(128)S(1)} %reshape.55.skip_next_ref, s32[1]{0:T(128)} %bitcast.5.flag_ref, bf16[288,1056]{1,0:T(8,128)(2,1)S(1)} %get-tuple-element.25.own_ref, bf16[288,1056]{1,0:T(8,128)(2,1)} %collective-permute-done.10.prev_ref, ...), custom_call_target="tpu_custom_call" | custom-call | tf_op jit(solution)/shard_map/pallas_call | solution.py:209
  114.5 0.7 reshape.68
  115.2 3.9 %all-to-all-start = ((f32[4,1,384]{2,1,0:T(1,128)}), f32[4,1,384]{2,1,0:T(1,128)S(1)}, u32[]{:S(2)}, u32[]{:S(2)}) async-start(f32[4,1,384]{2,1,0:T(1,128)} %reshape.68), calls=%async_computation | async-start | bytes 12288 | tf_op jit(solution)/shard_map/all_to_all | solution.py:226
  119.1 5.6 %all-to-all-done = f32[4,1,384]{2,1,0:T(1,128)S(1)} async-done(((f32[4,1,384]{2,1,0:T(1,128)}), f32[4,1,384]{2,1,0:T(1,128)S(1)}, u32[]{:S(2)}, u32[]{:S(2)}) %all-to-all-start) | async-done | bytes 6176 | tf_op jit(solution)/shard_map/all_to_all | solution.py:226
  124.7 0.5 broadcast.129
  125.2 0.7 reduce
  126.1 0.6 dynamic-slice_bitcast_fusion
  127.1 0.6 fusion.74
  (93 shorter events, 3.8 us)
Async XLA Ops:
  0.6 9.9 %copy-start = (bf16[1,1024,1024]{2,1,0:T(8,128)(2,1)S(1)}, bf16[1,1024,1024]{2,1,0:T(8,128)(2,1)}, u32[]{:S(2)}) copy-start(bf16[1,1024,1024]{2,1,0:T(8,128)(2,1)} %param.3) | copy-start | bytes 6291460
  1.6 12.9 %collective-permute-start.1 = (bf16[1,16,1024]{2,1,0:T(8,128)(2,1)S(1)}, bf16[1,16,1024]{2,1,0:T(8,128)(2,1)S(1)}, u32[]{:S(2)}, u32[]{:S(2)}) collective-permute-start(bf16[1,16,1024]{2,1,0:T(8,128)(2,1)S(1)} %slice_select_fusion), channel_id=1, source_target_pairs={{0,1},{1,0},{2,3},{3,2},{4,5},{5,4},{6,7},{7,6},{8,9},{9,8},{10,11... | collective-permute-start | bytes 98312 | tf_op jit(solution)/shard_map/ppermute | solution.py:67
  2.1 5.5 %collective-permute-start = (bf16[1,16,16]{2,1,0:T(8,128)(2,1)S(1)}, bf16[1,16,16]{2,1,0:T(8,128)(2,1)S(1)}, u32[]{:S(2)}, u32[]{:S(2)}) collective-permute-start(bf16[1,16,16]{2,1,0:T(8,128)(2,1)S(1)} %slice_select_fusion.1), channel_id=1, source_target_pairs={{0,3},{3,0},{1,2},{2,1},{4,7},{7,4},{5,6},{6,5},{8,11},{11,8},{9,1... | collective-permute-start | bytes 1544 | tf_op jit(solution)/shard_map/ppermute | solution.py:69
  6.1 4.0 %collective-permute-start.2 = (bf16[1,16,1024]{2,1,0:T(8,128)(2,1)S(1)}, bf16[1,16,1024]{2,1,0:T(8,128)(2,1)S(1)}, u32[]{:S(2)}, u32[]{:S(2)}) collective-permute-start(bf16[1,16,1024]{2,1,0:T(8,128)(2,1)S(1)} %select_bitcast_fusion.2), channel_id=1, source_target_pairs={{0,2},{2,0},{1,3},{3,1},{4,6},{6,4},{5,7},{7,5},{8,10},{10,8},{9,1... | collective-permute-start | bytes 98312 | tf_op jit(solution)/shard_map/ppermute | solution.py:68
  14.7 6.2 %copy-start.1 = (s32[1,8,8]{2,1,0:T(8,128)S(1)}, s32[1,8,8]{2,1,0:T(8,128)}, u32[]{:S(2)}) copy-start(s32[1,8,8]{2,1,0:T(8,128)} %param.4) | copy-start | bytes 772
  16.6 39.6 %collective-permute-start.4 = (bf16[288,1056]{1,0:T(8,128)(2,1)S(1)}, bf16[288,1056]{1,0:T(8,128)(2,1)}, u32[]{:S(2)}, u32[]{:S(2)}) collective-permute-start(bf16[288,1056]{1,0:T(8,128)(2,1)S(1)} %get-tuple-element.23.own_ref), channel_id=1, source_target_pairs={{0,4},{4,8},{8,12},{1,5},{5,9},{9,13},{2,6},{6,10},{10,14},{3,7},{... | collective-permute-start | bytes 1824776 | tf_op jit(solution)/shard_map/ppermute | solution.py:26
  20.9 36.6 %collective-permute-start.5 = (bf16[288,1056]{1,0:T(8,128)(2,1)S(1)}, bf16[288,1056]{1,0:T(8,128)(2,1)}, u32[]{:S(2)}, u32[]{:S(2)}) collective-permute-start(bf16[288,1056]{1,0:T(8,128)(2,1)S(1)} %get-tuple-element.23.own_ref), channel_id=1, source_target_pairs={{4,0},{8,4},{12,8},{5,1},{9,5},{13,9},{6,2},{10,6},{14,10},{7,3},{... | collective-permute-start | bytes 1824776 | tf_op jit(solution)/shard_map/ppermute | solution.py:26
  22.2 52.7 %collective-permute-start.6 = (bf16[288,1056]{1,0:T(8,128)(2,1)S(1)}, bf16[288,1056]{1,0:T(8,128)(2,1)}, u32[]{:S(2)}, u32[]{:S(2)}) collective-permute-start(bf16[288,1056]{1,0:T(8,128)(2,1)S(1)} %get-tuple-element.22.own_ref), channel_id=1, source_target_pairs={{0,4},{4,8},{8,12},{1,5},{5,9},{9,13},{2,6},{6,10},{10,14},{3,7},{... | collective-permute-start | bytes 1824776 | tf_op jit(solution)/shard_map/ppermute | solution.py:26
  28.9 47.7 %collective-permute-start.7 = (bf16[288,1056]{1,0:T(8,128)(2,1)S(1)}, bf16[288,1056]{1,0:T(8,128)(2,1)}, u32[]{:S(2)}, u32[]{:S(2)}) collective-permute-start(bf16[288,1056]{1,0:T(8,128)(2,1)S(1)} %get-tuple-element.22.own_ref), channel_id=1, source_target_pairs={{4,0},{8,4},{12,8},{5,1},{9,5},{13,9},{6,2},{10,6},{14,10},{7,3},{... | collective-permute-start | bytes 1824776 | tf_op jit(solution)/shard_map/ppermute | solution.py:26
  30.4 22.2 %collective-permute-start.3 = (s32[1,8,8]{2,1,0:T(8,128)S(1)}, s32[1,8,8]{2,1,0:T(8,128)S(1)}, u32[]{:S(2)}, u32[]{:S(2)}) collective-permute-start(s32[1,8,8]{2,1,0:T(8,128)S(1)} %copy-done.1), channel_id=1, source_target_pairs={{4,0},{8,4},{12,8},{5,1},{9,5},{13,9},{6,2},{10,6},{14,10},{7,3},{... | collective-permute-start | bytes 776 | tf_op jit(solution)/shard_map/ppermute | solution.py:26
  52.6 36.3 %collective-permute-start.8 = (bf16[288,1056]{1,0:T(8,128)(2,1)S(1)}, bf16[288,1056]{1,0:T(8,128)(2,1)}, u32[]{:S(2)}, u32[]{:S(2)}) collective-permute-start(bf16[288,1056]{1,0:T(8,128)(2,1)S(1)} %get-tuple-element.24.own_ref), channel_id=1, source_target_pairs={{0,4},{4,8},{8,12},{1,5},{5,9},{9,13},{2,6},{6,10},{10,14},{3,7},{... | collective-permute-start | bytes 1824776 | tf_op jit(solution)/shard_map/ppermute | solution.py:26
  56.2 32.6 %collective-permute-start.9 = (bf16[288,1056]{1,0:T(8,128)(2,1)S(1)}, bf16[288,1056]{1,0:T(8,128)(2,1)}, u32[]{:S(2)}, u32[]{:S(2)}) collective-permute-start(bf16[288,1056]{1,0:T(8,128)(2,1)S(1)} %get-tuple-element.24.own_ref), channel_id=1, source_target_pairs={{4,0},{8,4},{12,8},{5,1},{9,5},{13,9},{6,2},{10,6},{14,10},{7,3},{... | collective-permute-start | bytes 1824776 | tf_op jit(solution)/shard_map/ppermute | solution.py:26
  57.5 43.5 %collective-permute-start.10 = (bf16[288,1056]{1,0:T(8,128)(2,1)S(1)}, bf16[288,1056]{1,0:T(8,128)(2,1)}, u32[]{:S(2)}, u32[]{:S(2)}) collective-permute-start(bf16[288,1056]{1,0:T(8,128)(2,1)S(1)} %get-tuple-element.25.own_ref), channel_id=1, source_target_pairs={{0,4},{4,8},{8,12},{1,5},{5,9},{9,13},{2,6},{6,10},{10,14},{3,7},{... | collective-permute-start | bytes 1824776 | tf_op jit(solution)/shard_map/ppermute | solution.py:26
  74.9 26.2 %collective-permute-start.11 = (bf16[288,1056]{1,0:T(8,128)(2,1)S(1)}, bf16[288,1056]{1,0:T(8,128)(2,1)S(1)}, u32[]{:S(2)}, u32[]{:S(2)}) collective-permute-start(bf16[288,1056]{1,0:T(8,128)(2,1)S(1)} %get-tuple-element.25.own_ref), channel_id=1, source_target_pairs={{4,0},{8,4},{12,8},{5,1},{9,5},{13,9},{6,2},{10,6},{14,10},{7,3},{... | collective-permute-start | bytes 1824776 | tf_op jit(solution)/shard_map/ppermute | solution.py:26
  115.2 9.5 %all-to-all-start = ((f32[4,1,384]{2,1,0:T(1,128)}), f32[4,1,384]{2,1,0:T(1,128)S(1)}, u32[]{:S(2)}, u32[]{:S(2)}) async-start(f32[4,1,384]{2,1,0:T(1,128)} %reshape.68), calls=%async_computation | async-start | bytes 12288 | tf_op jit(solution)/shard_map/all_to_all | solution.py:226
